TPU v7x, 256 devices: a whole 4x4x8 slice. The times are simulated.
256 devices in a mesh: gx: 32 (over z, y), gy: 4 (over x), gz: 2 (over core).
Axes of the slice: x: 4, y: 4, z: 8, core: 2. Of those that a mesh axis runs over, the one named last changes fastest.
Arguments:
- volt: float32 [32, 1024, 512], P('gz', 'gx', 'gy'), may hold values from 0 to 1
- recovery: float32 [32, 1024, 512], P('gz', 'gx', 'gy'), may hold values from 0 to 1
- fiber_class: int32 [32, 1024, 512], P('gz', 'gx', 'gy'), may hold values from 0 to 7
- fiber_table: float32 [3, 8], replicated, may hold values from 0.02 to 0.16
- junction_block: int32 [32768], P(('gx', 'gy', 'gz')), may hold values from 0 to 511
- junction_term: int32 [32768], P(('gx', 'gy', 'gz')), may hold values from 0 to 31
- junction_owner: int32 [32768, 1], P(('gx', 'gy', 'gz')), may hold values from 0 to 127; in each aligned block of 128 rows (0 to 127, 128 to 255, ...) at most 2 rows name the same one
- term_volt: float32 [8192, 128], P(('gx', 'gy', 'gz')), may hold values from 0 to 1
- term_recovery: float32 [8192, 128], P(('gx', 'gy', 'gz')), may hold values from 0 to 1
- term_gain: float32 [8192], P(('gx', 'gy', 'gz')), may hold values from 0.5 to 4
- cable_gain: float32 [8192], P(('gx', 'gy', 'gz')), may hold values from 0.05 to 0.45
Outputs:
- volt_out: float32 [32, 1024, 512], P('gz', 'gx', 'gy')
- recovery_out: float32 [32, 1024, 512], P('gz', 'gx', 'gy')
- term_volt_out: float32 [8192, 128], P(('gx', 'gy', 'gz'))
- term_recovery_out: float32 [8192, 128], P(('gx', 'gy', 'gz'))
Inputs may be any that keep to these rules, and one draw needn't show every extreme that they name: `junction_owner`: among the 128 junctions of one device, at most 2 have the same owner, a bound that some block reaches.
All inputs are finite; a program needn't handle non-finite values.
Results may differ from a plain program's by a relative error of at most 0.00002.
Values sent between devices are 32-bit elements; how exact they have to be, the bound alone decides.
No kernel may reach another device: no remote copies, remote signals or barrier semaphores. Data moves between devices by JAX's collectives and lax.ppermute only.
A program may use at most 64 MiB of HBM per device.

v0:
```python
import jax
import jax.numpy as jnp
from jax import lax
from jax.sharding import PartitionSpec as P

NCLASS = 8
STEPS = 4


def cell_kinetics(v, w, drive):
    react = -8.0 * v * (v - 0.15) * (v - 1.0) - v * w
    new_v = 0.1 * (react + drive)
    new_w = w + 0.01 * (-w - 8.0 * v * (v - 1.15))
    return (new_v, new_w)


def neighbours(cells, axis, dim):
    count = lax.axis_size(axis)
    index = lax.axis_index(axis)
    size = cells.shape[dim]
    first = lax.slice_in_dim(cells, 0, 1, axis=dim)
    last = lax.slice_in_dim(cells, size - 1, size, axis=dim)
    from_low = lax.ppermute(last, axis, [(i, i + 1) for i in range(count - 1)])
    from_high = lax.ppermute(first, axis, [(i + 1, i) for i in range(count - 1)])
    low = jnp.where(index == 0, first, from_low)
    high = jnp.where(index == count - 1, last, from_high)
    plus = jnp.concatenate([lax.slice_in_dim(cells, 1, size, axis=dim), high], axis=dim)
    minus = jnp.concatenate([low, lax.slice_in_dim(cells, 0, size - 1, axis=dim)], axis=dim)
    return plus, minus


def on_device(
    volt,
    recovery,
    fiber_class,
    fiber_table,
    junction_block,
    junction_term,
    junction_owner,
    term_volt,
    term_recovery,
    term_gain,
    cable_gain,
):
    depth, rows_x, width = volt.shape
    owners = lax.axis_size("gx") * lax.axis_size("gy")
    jcount = junction_block.shape[0]
    capacity = max(2, 2 * jcount // owners)
    slots_total = owners * capacity
    term_count = term_volt.shape[0]
    coef_z = jnp.zeros(volt.shape, jnp.float32)
    coef_x = jnp.zeros(volt.shape, jnp.float32)
    coef_y = jnp.zeros(volt.shape, jnp.float32)
    for klass in range(NCLASS):
        hit = fiber_class == klass
        coef_z = jnp.where(hit, fiber_table[0, klass], coef_z)
        coef_x = jnp.where(hit, fiber_table[1, klass], coef_x)
        coef_y = jnp.where(hit, fiber_table[2, klass], coef_y)
    coef_z, coef_x, coef_y = lax.optimization_barrier((coef_z, coef_x, coef_y))

    owner = junction_owner[:, 0]
    order = jnp.arange(jcount, dtype=jnp.int32)
    earlier = (owner[:, None] == owner[None, :]) & (order[None, :] < order[:, None])
    rank = jnp.sum(earlier.astype(jnp.int32), axis=1)
    slot = owner * capacity + rank
    hits = slot[None, :] == jnp.arange(slots_total, dtype=jnp.int32)[:, None]
    slot_used = jnp.any(hits, axis=1)
    slot_block = jnp.sum(jnp.where(hits, junction_block[None, :], 0), axis=1)
    slot_term = jnp.sum(jnp.where(hits, junction_term[None, :] + 1, 0), axis=1) - 1

    arrived = lax.all_to_all(slot_term, ("gx", "gy"), split_axis=0, concat_axis=0, tiled=True)
    valid = arrived >= 0
    safe_ids = jnp.where(valid, arrived, 0)
    pick = safe_ids[:, None] == jnp.arange(term_count, dtype=jnp.int32)[None, :]
    gains = jnp.where(valid, jnp.sum(jnp.where(pick, term_gain[None, :], 0.0), axis=1), 0.0)
    gain_rows = jnp.broadcast_to(gains[:, None], (slots_total, width))

    tile_gain = None
    for step in range(STEPS):
        flat_rows = volt.reshape(depth * rows_x, width)
        rows = flat_rows[junction_block]
        out_rows = jnp.where(slot_used[:, None], flat_rows[slot_block], 0.0)
        far_volt = term_volt[safe_ids]
        parts = [out_rows, far_volt] + ([gain_rows] if step == 0 else [])
        sent = jnp.stack(parts, axis=1)
        received = lax.all_to_all(sent, ("gx", "gy"), split_axis=0, concat_axis=0, tiled=True)
        current = gains[:, None] * (far_volt - received[:, 0, :])
        into_term = jax.ops.segment_sum(-current, safe_ids, num_segments=term_count)
        mine = received[slot]
        if step == 0:
            tile_gain = mine[:, 2, :]
        tile_current = tile_gain * (mine[:, 1, :] - rows)
        into_voxel = jax.ops.segment_sum(
            tile_current, junction_block, num_segments=depth * rows_x
        ).reshape(depth, rows_x, width)
        z_plus, z_minus = neighbours(volt, "gz", 0)
        x_plus, x_minus = neighbours(volt, "gx", 1)
        y_plus, y_minus = neighbours(volt, "gy", 2)
        lap_z = z_plus + z_minus - 2.0 * volt
        lap_x = x_plus + x_minus - 2.0 * volt
        lap_y = y_plus + y_minus - 2.0 * volt
        react_v, new_w = cell_kinetics(volt, recovery, into_voxel)
        new_v = volt + (coef_z * lap_z + coef_x * lap_x + coef_y * lap_y) + react_v
        cable = jnp.pad(term_volt, ((0, 0), (1, 1)), mode="edge")
        lap_k = cable[:, 2:] + cable[:, :-2] - 2.0 * term_volt
        react_u, new_r = cell_kinetics(term_volt, term_recovery, 0.1 * into_term)
        new_u = term_volt + cable_gain[:, None] * lap_k + react_u
        volt, recovery, term_volt, term_recovery = (new_v, new_w, new_u, new_r)
    return (volt, recovery, term_volt, term_recovery)


def solution(mesh):
    return jax.shard_map(
        on_device,
        mesh=mesh,
        in_specs=(
            P("gz", "gx", "gy"),
            P("gz", "gx", "gy"),
            P("gz", "gx", "gy"),
            P(),
            P(("gx", "gy", "gz")),
            P(("gx", "gy", "gz")),
            P(("gx", "gy", "gz"), None),
            P(("gx", "gy", "gz"), None),
            P(("gx", "gy", "gz"), None),
            P(("gx", "gy", "gz")),
            P(("gx", "gy", "gz")),
        ),
        out_specs=(
            P("gz", "gx", "gy"),
            P("gz", "gx", "gy"),
            P(("gx", "gy", "gz"), None),
            P(("gx", "gy", "gz"), None),
        ),
        check_vma=False,
    )
```

profile of v0, /device:TPU:128, one launch (start us, length us, event | category | flops | bytes accessed | tf_op | source)
XLA Modules:
  0.0 246.0 jit_solution(8803511261203656579)
XLA Ops:
  3.5 14.0 %all-to-all-start = ((s32[128,2,1]{1,2,0:T(1,128)}), s32[128,2,1]{1,2,0:T(1,128)S(1)}, u32[]{:S(2)}, u32[]{:S(2)}) async-start(s32[128,2,1]{1,2,0:T(1,128)} %bitcast.29), calls=%async_computation | async-start | bytes 131072 | tf_op jit(solution)/shard_map/all_to_all | solution.py:71
  17.5 1.9 fusion.123
  20.7 5.2 %collective-permute-start.5 = (f32[16,32,1]{2,1,0:T(8,128)}, f32[16,32,1]{2,1,0:T(8,128)}, u32[]{:S(2)}, u32[]{:S(2)}) collective-permute-start(f32[16,32,1]{2,1,0:T(8,128)} %get-tuple-element.83), channel_id=1, source_target_pairs={{0,2},{2,4},{4,6},{1,3},{3,5},{5,7},{8,10},{10,12},{12,14},{9,11},... | collective-permute-start | bytes 6152 | tf_op jit(solution)/shard_map/ppermute | solution.py:23
  27.9 3.6 %collective-permute-start.1 = (f32[1,32,128]{2,1,0:T(8,128)}, f32[1,32,128]{2,1,0:T(8,128)}, u32[]{:S(2)}, u32[]{:S(2)}) collective-permute-start(f32[1,32,128]{2,1,0:T(8,128)} %get-tuple-element.95), channel_id=1, source_target_pairs={{0,1},{2,3},{4,5},{6,7},{8,9},{10,11},{12,13},{14,15},{16,17},{18,... | collective-permute-start | bytes 49160 | tf_op jit(solution)/shard_map/ppermute | solution.py:23
  32.1 4.5 %collective-permute-start.2 = (f32[16,1,128]{2,1,0:T(1,128)}, f32[16,1,128]{2,1,0:T(1,128)}, u32[]{:S(2)}, u32[]{:S(2)}) collective-permute-start(f32[16,1,128]{2,1,0:T(1,128)} %get-tuple-element.90), channel_id=1, source_target_pairs={{8,0},{16,8},{24,16},{32,24},{40,32},{48,40},{56,48},{64,56},{72,6... | collective-permute-start | bytes 24584 | tf_op jit(solution)/shard_map/ppermute | solution.py:24
  41.6 5.2 %select_select_fusion = (f32[16,32,128]{2,1,0:T(8,128)S(1)}, pred[16,32,128]{2,1,0:T(8,128)(4,1)S(1)}, pred[16,32,128]{2,1,0:T(8,128)(4,1)S(1)}, pred[16,32,128]...) fusion(f32[]{:T(128)} %bitcast.23, f32[]{:T(128)} %bitcast.22, ...), kind=kLoop, calls=%fused_computation.84 | loop fusion | flops 1048576 | bytes 1048608 | tf_op jit(solution)/shard_map/jit(_where)/select_n | solution.py:58
  46.8 5.3 %select_select_fusion.1 = f32[16,32,128]{2,1,0:T(8,128)S(1)} fusion(pred[16,32,128]{2,1,0:T(8,128)(4,1)S(1)} %get-tuple-element.26, pred[16,32,128]{2,1,0:T(8,128)(4,1)S(1)} %get-tuple-element.25, pred[16,32,128]{2,1,0:T(8,128)(4,1)S(1)} %get-tuple-element.24, pred[16,32,128]{2,1,0:T(8,128)(4,1)S(1)} %get-tuple-element.23, ...), kind=kLoop, calls=%fused_computation.85 | loop fusion | flops 524288 | bytes 786464 | tf_op jit(solution)/shard_map/jit(_where)/select_n | solution.py:57
  52.1 5.1 %select_select_fusion.2 = f32[16,32,128]{2,1,0:T(8,128)S(1)} fusion(pred[16,32,128]{2,1,0:T(8,128)(4,1)S(1)} %get-tuple-element.26, pred[16,32,128]{2,1,0:T(8,128)(4,1)S(1)} %get-tuple-element.25, pred[16,32,128]{2,1,0:T(8,128)(4,1)S(1)} %get-tuple-element.24, pred[16,32,128]{2,1,0:T(8,128)(4,1)S(1)} %get-tuple-element.23, ...), kind=kLoop, calls=%fused_computation.86 | loop fusion | flops 524288 | bytes 786464 | tf_op jit(solution)/shard_map/jit(_where)/select_n | solution.py:56
  62.2 11.8 %all-to-all-start.1 = ((f32[256,3,128]{2,1,0:T(4,128)}), f32[256,3,128]{2,1,0:T(4,128)S(1)}, u32[]{:S(2)}, u32[]{:S(2)}) async-start(f32[256,3,128]{2,1,0:T(4,128)} %copy.37), calls=%async_computation.1 | async-start | bytes 1048576 | tf_op jit(solution)/shard_map/all_to_all | solution.py:86
  74.8 3.4 %collective-permute-start.3 = (f32[16,1,128]{2,1,0:T(1,128)S(1)}, f32[16,1,128]{2,1,0:T(1,128)S(1)}, u32[]{:S(2)}, u32[]{:S(2)}) collective-permute-start(f32[16,1,128]{2,1,0:T(1,128)S(1)} %copy-done.21), channel_id=1, source_target_pairs={{0,8},{8,16},{16,24},{24,32},{32,40},{40,48},{48,56},{56,64},{64,7... | collective-permute-start | bytes 24584 | tf_op jit(solution)/shard_map/ppermute | solution.py:23
  78.2 1.8 broadcast_select_fusion.3
  80.0 6.1 %collective-permute-done.3 = f32[16,1,128]{2,1,0:T(1,128)S(1)} collective-permute-done((f32[16,1,128]{2,1,0:T(1,128)S(1)}, f32[16,1,128]{2,1,0:T(1,128)S(1)}, u32[]{:S(2)}, u32[]{:S(2)}) %collective-permute-start.3) | collective-permute-done | bytes 8224 | tf_op jit(solution)/shard_map/ppermute | solution.py:23
  87.8 1.7 scatter_custom_fusion.1
  92.7 1.9 scatter_custom_fusion
  94.6 1.6 fusion.5
  99.0 1.3 collective-permute-start.10
  100.3 5.3 %collective-permute-start.11 = (f32[16,32,1]{2,1,0:T(8,128)}, f32[16,32,1]{2,1,0:T(8,128)}, u32[]{:S(2)}, u32[]{:S(2)}) collective-permute-start(f32[16,32,1]{2,1,0:T(8,128)} %get-tuple-element.63), channel_id=1, source_target_pairs={{0,2},{2,4},{4,6},{1,3},{3,5},{5,7},{8,10},{10,12},{12,14},{9,11},... | collective-permute-start | bytes 6152 | tf_op jit(solution)/shard_map/ppermute | solution.py:23
  106.5 12.1 %all-to-all-start.2 = ((f32[256,2,128]{2,1,0:T(2,128)}), f32[256,2,128]{2,1,0:T(2,128)S(1)}, u32[]{:S(2)}, u32[]{:S(2)}) async-start(f32[256,2,128]{2,1,0:T(2,128)} %copy.40), calls=%async_computation.2 | async-start | bytes 524288 | tf_op jit(solution)/shard_map/all_to_all | solution.py:86
  118.6 4.6 %collective-permute-start.8 = (f32[16,1,128]{2,1,0:T(1,128)S(1)}, f32[16,1,128]{2,1,0:T(1,128)S(1)}, u32[]{:S(2)}, u32[]{:S(2)}) collective-permute-start(f32[16,1,128]{2,1,0:T(1,128)S(1)} %get-tuple-element.70), channel_id=1, source_target_pairs={{8,0},{16,8},{24,16},{32,24},{40,32},{48,40},{56,48},{64,56},{72,6... | collective-permute-start | bytes 24584 | tf_op jit(solution)/shard_map/ppermute | solution.py:24
  123.1 1.9 collective-permute-start.9
  125.1 1.3 collective-permute-start.6
  126.4 3.0 %collective-permute-start.7 = (f32[1,32,128]{2,1,0:T(8,128)S(1)}, f32[1,32,128]{2,1,0:T(8,128)S(1)}, u32[]{:S(2)}, u32[]{:S(2)}) collective-permute-start(f32[1,32,128]{2,1,0:T(8,128)S(1)} %get-tuple-element.75), channel_id=1, source_target_pairs={{0,1},{2,3},{4,5},{6,7},{8,9},{10,11},{12,13},{14,15},{16,17},{18,... | collective-permute-start | bytes 49160 | tf_op jit(solution)/shard_map/ppermute | solution.py:23
  129.4 1.8 broadcast_select_fusion.2
  132.2 2.0 scatter_custom_fusion.3
  136.7 1.8 scatter_custom_fusion.2
  138.5 1.8 fusion.14
  144.3 1.3 collective-permute-start.16
  145.6 5.3 %collective-permute-start.17 = (f32[16,32,1]{2,1,0:T(8,128)S(1)}, f32[16,32,1]{2,1,0:T(8,128)}, u32[]{:S(2)}, u32[]{:S(2)}) collective-permute-start(f32[16,32,1]{2,1,0:T(8,128)S(1)} %get-tuple-element.60), channel_id=1, source_target_pairs={{0,2},{2,4},{4,6},{1,3},{3,5},{5,7},{8,10},{10,12},{12,14},{9,11},... | collective-permute-start | bytes 6152 | tf_op jit(solution)/shard_map/ppermute | solution.py:23
  151.8 14.3 %all-to-all-start.3 = ((f32[256,2,128]{2,1,0:T(2,128)}), f32[256,2,128]{2,1,0:T(2,128)S(1)}, u32[]{:S(2)}, u32[]{:S(2)}) async-start(f32[256,2,128]{2,1,0:T(2,128)} %copy.43), calls=%async_computation.3 | async-start | bytes 524288 | tf_op jit(solution)/shard_map/all_to_all | solution.py:86
  166.1 1.3 collective-permute-start.12
  167.4 3.0 %collective-permute-start.13 = (f32[1,32,128]{2,1,0:T(8,128)S(1)}, f32[1,32,128]{2,1,0:T(8,128)S(1)}, u32[]{:S(2)}, u32[]{:S(2)}) collective-permute-start(f32[1,32,128]{2,1,0:T(8,128)S(1)} %get-tuple-element.48), channel_id=1, source_target_pairs={{0,1},{2,3},{4,5},{6,7},{8,9},{10,11},{12,13},{14,15},{16,17},{18,... | collective-permute-start | bytes 49160 | tf_op jit(solution)/shard_map/ppermute | solution.py:23
  170.5 4.6 %collective-permute-start.14 = (f32[16,1,128]{2,1,0:T(1,128)S(1)}, f32[16,1,128]{2,1,0:T(1,128)S(1)}, u32[]{:S(2)}, u32[]{:S(2)}) collective-permute-start(f32[16,1,128]{2,1,0:T(1,128)S(1)} %get-tuple-element.53), channel_id=1, source_target_pairs={{8,0},{16,8},{24,16},{32,24},{40,32},{48,40},{56,48},{64,56},{72,6... | collective-permute-start | bytes 24584 | tf_op jit(solution)/shard_map/ppermute | solution.py:24
  175.0 1.9 collective-permute-start.15
  177.0 1.8 broadcast_select_fusion.5
  178.8 5.1 %collective-permute-done.15 = f32[16,1,128]{2,1,0:T(1,128)S(1)} collective-permute-done((f32[16,1,128]{2,1,0:T(1,128)S(1)}, f32[16,1,128]{2,1,0:T(1,128)S(1)}, u32[]{:S(2)}, u32[]{:S(2)}) %collective-permute-start.15) | collective-permute-done | bytes 8224 | tf_op jit(solution)/shard_map/ppermute | solution.py:23
  184.9 1.8 scatter_custom_fusion.4
  186.7 2.7 %multiply_add_fusion = (f32[16,32,128]{2,1,0:T(8,128)}, f32[16,32,128]{2,1,0:T(8,128)S(1)}, f32[16,32,128]{2,1,0:T(8,128)S(1)}) fusion(f32[16,32,128]{2,1,0:T(8,128)S(1)} %fusion.14, f32[16,32,128]{2,1,0:T(8,128)S(1)} %bitcast.101, f32[16,32,128]{2,1,0:T(8,128)S(1)} %get-tuple-element.9, f32[16,32,127]{2,1,0:T(8,128)} %get-tuple-element.56, ...), kind=kLoop, calls=%fused_computation.80 | loop fusion | flops 3735552 | bytes 4456448 | tf_op jit(solution)/shard_map/add | solution.py:13
  192.6 1.9 scatter_custom_fusion.5
  196.2 4.0 %collective-permute-start.23 = (f32[16,32,1]{2,1,0:T(8,128)S(1)}, f32[16,32,1]{2,1,0:T(8,128)}, u32[]{:S(2)}, u32[]{:S(2)}) collective-permute-start(f32[16,32,1]{2,1,0:T(8,128)S(1)} %copy-done.4), channel_id=1, source_target_pairs={{0,2},{2,4},{4,6},{1,3},{3,5},{5,7},{8,10},{10,12},{12,14},{9,11},... | collective-permute-start | bytes 6152 | tf_op jit(solution)/shard_map/ppermute | solution.py:23
  204.0 1.5 collective-permute-start.22
  206.5 15.5 %all-to-all-start.4 = ((f32[256,2,128]{2,1,0:T(2,128)}), f32[256,2,128]{2,1,0:T(2,128)S(1)}, u32[]{:S(2)}, u32[]{:S(2)}) async-start(f32[256,2,128]{2,1,0:T(2,128)} %copy.46), calls=%async_computation.4 | async-start | bytes 524288 | tf_op jit(solution)/shard_map/all_to_all | solution.py:86
  222.0 4.6 %collective-permute-start.20 = (f32[16,1,128]{2,1,0:T(1,128)S(1)}, f32[16,1,128]{2,1,0:T(1,128)S(1)}, u32[]{:S(2)}, u32[]{:S(2)}) collective-permute-start(f32[16,1,128]{2,1,0:T(1,128)S(1)} %copy-done.23), channel_id=1, source_target_pairs={{8,0},{16,8},{24,16},{32,24},{40,32},{48,40},{56,48},{64,56},{72,6... | collective-permute-start | bytes 24584 | tf_op jit(solution)/shard_map/ppermute | solution.py:24
  226.5 1.9 collective-permute-start.21
  229.8 3.0 %collective-permute-start.19 = (f32[1,32,128]{2,1,0:T(8,128)S(1)}, f32[1,32,128]{2,1,0:T(8,128)S(1)}, u32[]{:S(2)}, u32[]{:S(2)}) collective-permute-start(f32[1,32,128]{2,1,0:T(8,128)S(1)} %copy-done.11), channel_id=1, source_target_pairs={{0,1},{2,3},{4,5},{6,7},{8,9},{10,11},{12,13},{14,15},{16,17},{18,... | collective-permute-start | bytes 49160 | tf_op jit(solution)/shard_map/ppermute | solution.py:23
  232.8 1.8 broadcast_select_fusion.4
  236.8 2.1 scatter_custom_fusion.7
  239.8 1.8 scatter_custom_fusion.6
  243.7 2.4 fusion.32
  (186 shorter events, 50.9 us)
Async XLA Ops:
  3.5 54.3 %all-to-all-start = ((s32[128,2,1]{1,2,0:T(1,128)}), s32[128,2,1]{1,2,0:T(1,128)S(1)}, u32[]{:S(2)}, u32[]{:S(2)}) async-start(s32[128,2,1]{1,2,0:T(1,128)} %bitcast.29), calls=%async_computation | async-start | bytes 131072 | tf_op jit(solution)/shard_map/all_to_all | solution.py:71
  17.5 8.5 %copy-start = (f32[16,32,128]{2,1,0:T(8,128)S(1)}, f32[16,32,128]{2,1,0:T(8,128)}, u32[]{:S(2)}) copy-start(f32[16,32,128]{2,1,0:T(8,128)} %param.11) | copy-start | bytes 786436
  19.5 54.6 %collective-permute-start.4 = (f32[16,32,1]{2,1,0:T(8,128)}, f32[16,32,1]{2,1,0:T(8,128)}, u32[]{:S(2)}, u32[]{:S(2)}) collective-permute-start(f32[16,32,1]{2,1,0:T(8,128)} %get-tuple-element.84), channel_id=1, source_target_pairs={{2,0},{4,2},{6,4},{3,1},{5,3},{7,5},{10,8},{12,10},{14,12},{11,9},... | collective-permute-start | bytes 6152 | tf_op jit(solution)/shard_map/ppermute | solution.py:24
  20.7 57.4 %collective-permute-start.5 = (f32[16,32,1]{2,1,0:T(8,128)}, f32[16,32,1]{2,1,0:T(8,128)}, u32[]{:S(2)}, u32[]{:S(2)}) collective-permute-start(f32[16,32,1]{2,1,0:T(8,128)} %get-tuple-element.83), channel_id=1, source_target_pairs={{0,2},{2,4},{4,6},{1,3},{3,5},{5,7},{8,10},{10,12},{12,14},{9,11},... | collective-permute-start | bytes 6152 | tf_op jit(solution)/shard_map/ppermute | solution.py:23
  26.6 60.2 %collective-permute-start = (f32[1,32,128]{2,1,0:T(8,128)}, f32[1,32,128]{2,1,0:T(8,128)S(1)}, u32[]{:S(2)}, u32[]{:S(2)}) collective-permute-start(f32[1,32,128]{2,1,0:T(8,128)} %get-tuple-element.96), channel_id=1, source_target_pairs={{1,0},{3,2},{5,4},{7,6},{9,8},{11,10},{13,12},{15,14},{17,16},{19,... | collective-permute-start | bytes 49160 | tf_op jit(solution)/shard_map/ppermute | solution.py:24
  27.9 59.0 %collective-permute-start.1 = (f32[1,32,128]{2,1,0:T(8,128)}, f32[1,32,128]{2,1,0:T(8,128)}, u32[]{:S(2)}, u32[]{:S(2)}) collective-permute-start(f32[1,32,128]{2,1,0:T(8,128)} %get-tuple-element.95), channel_id=1, source_target_pairs={{0,1},{2,3},{4,5},{6,7},{8,9},{10,11},{12,13},{14,15},{16,17},{18,... | collective-permute-start | bytes 49160 | tf_op jit(solution)/shard_map/ppermute | solution.py:23
  31.5 5.2 %copy-start.7 = (f32[3,8]{1,0:T(4,128)S(1)}, f32[3,8]{1,0:T(4,128)}, u32[]{:S(2)}) copy-start(f32[3,8]{1,0:T(4,128)} %param.14) | copy-start | bytes 292
  32.1 47.9 %collective-permute-start.2 = (f32[16,1,128]{2,1,0:T(1,128)}, f32[16,1,128]{2,1,0:T(1,128)}, u32[]{:S(2)}, u32[]{:S(2)}) collective-permute-start(f32[16,1,128]{2,1,0:T(1,128)} %get-tuple-element.90), channel_id=1, source_target_pairs={{8,0},{16,8},{24,16},{32,24},{40,32},{48,40},{56,48},{64,56},{72,6... | collective-permute-start | bytes 24584 | tf_op jit(solution)/shard_map/ppermute | solution.py:24
  38.2 2.4 copy-start.17
  38.9 0.9 copy-start.1
  40.6 1.0 copy-start.5
  60.2 27.5 %copy-start.24 = (s32[256,1]{0,1:T(1,128)}, s32[256,1]{0,1:T(1,128)S(1)}, u32[]{:S(2)}) copy-start(s32[256,1]{0,1:T(1,128)S(1)} %get-tuple-element.131) | copy-start | bytes 3076
  62.2 11.8 %copy-start.29 = (s32[128]{0:T(128)S(1)}, s32[128]{0:T(128)}, u32[]{:S(2)}) copy-start(s32[128]{0:T(128)} %compare_select_fusion.3) | copy-start | bytes 1540
  62.2 25.4 %all-to-all-start.1 = ((f32[256,3,128]{2,1,0:T(4,128)}), f32[256,3,128]{2,1,0:T(4,128)S(1)}, u32[]{:S(2)}, u32[]{:S(2)}) async-start(f32[256,3,128]{2,1,0:T(4,128)} %copy.37), calls=%async_computation.1 | async-start | bytes 1048576 | tf_op jit(solution)/shard_map/all_to_all | solution.py:86
  74.8 11.4 %collective-permute-start.3 = (f32[16,1,128]{2,1,0:T(1,128)S(1)}, f32[16,1,128]{2,1,0:T(1,128)S(1)}, u32[]{:S(2)}, u32[]{:S(2)}) collective-permute-start(f32[16,1,128]{2,1,0:T(1,128)S(1)} %copy-done.21), channel_id=1, source_target_pairs={{0,8},{8,16},{16,24},{24,32},{32,40},{40,48},{48,56},{56,64},{64,7... | collective-permute-start | bytes 24584 | tf_op jit(solution)/shard_map/ppermute | solution.py:23
  87.8 1.8 copy-start.6
  92.6 1.9 copy-start.2
  92.7 1.9 copy-start.3
  98.2 0.7 copy-start.18
  99.0 27.3 %collective-permute-start.10 = (f32[16,32,1]{2,1,0:T(8,128)}, f32[16,32,1]{2,1,0:T(8,128)}, u32[]{:S(2)}, u32[]{:S(2)}) collective-permute-start(f32[16,32,1]{2,1,0:T(8,128)} %get-tuple-element.64), channel_id=1, source_target_pairs={{2,0},{4,2},{6,4},{3,1},{5,3},{7,5},{10,8},{12,10},{14,12},{11,9},... | collective-permute-start | bytes 6152 | tf_op jit(solution)/shard_map/ppermute | solution.py:24
  100.3 29.1 %collective-permute-start.11 = (f32[16,32,1]{2,1,0:T(8,128)}, f32[16,32,1]{2,1,0:T(8,128)}, u32[]{:S(2)}, u32[]{:S(2)}) collective-permute-start(f32[16,32,1]{2,1,0:T(8,128)} %get-tuple-element.63), channel_id=1, source_target_pairs={{0,2},{2,4},{4,6},{1,3},{3,5},{5,7},{8,10},{10,12},{12,14},{9,11},... | collective-permute-start | bytes 6152 | tf_op jit(solution)/shard_map/ppermute | solution.py:23
  106.5 25.6 %all-to-all-start.2 = ((f32[256,2,128]{2,1,0:T(2,128)}), f32[256,2,128]{2,1,0:T(2,128)S(1)}, u32[]{:S(2)}, u32[]{:S(2)}) async-start(f32[256,2,128]{2,1,0:T(2,128)} %copy.40), calls=%async_computation.2 | async-start | bytes 524288 | tf_op jit(solution)/shard_map/all_to_all | solution.py:86
  118.6 12.7 %collective-permute-start.8 = (f32[16,1,128]{2,1,0:T(1,128)S(1)}, f32[16,1,128]{2,1,0:T(1,128)S(1)}, u32[]{:S(2)}, u32[]{:S(2)}) collective-permute-start(f32[16,1,128]{2,1,0:T(1,128)S(1)} %get-tuple-element.70), channel_id=1, source_target_pairs={{8,0},{16,8},{24,16},{32,24},{40,32},{48,40},{56,48},{64,56},{72,6... | collective-permute-start | bytes 24584 | tf_op jit(solution)/shard_map/ppermute | solution.py:24
  123.1 8.9 %collective-permute-start.9 = (f32[16,1,128]{2,1,0:T(1,128)S(1)}, f32[16,1,128]{2,1,0:T(1,128)S(1)}, u32[]{:S(2)}, u32[]{:S(2)}) collective-permute-start(f32[16,1,128]{2,1,0:T(1,128)S(1)} %get-tuple-element.69), channel_id=1, source_target_pairs={{0,8},{8,16},{16,24},{24,32},{32,40},{40,48},{48,56},{56,64},{64,7... | collective-permute-start | bytes 24584 | tf_op jit(solution)/shard_map/ppermute | solution.py:23
  125.1 7.0 %collective-permute-start.6 = (f32[1,32,128]{2,1,0:T(8,128)S(1)}, f32[1,32,128]{2,1,0:T(8,128)S(1)}, u32[]{:S(2)}, u32[]{:S(2)}) collective-permute-start(f32[1,32,128]{2,1,0:T(8,128)S(1)} %get-tuple-element.76), channel_id=1, source_target_pairs={{1,0},{3,2},{5,4},{7,6},{9,8},{11,10},{13,12},{15,14},{17,16},{19,... | collective-permute-start | bytes 49160 | tf_op jit(solution)/shard_map/ppermute | solution.py:24
  126.4 5.7 %collective-permute-start.7 = (f32[1,32,128]{2,1,0:T(8,128)S(1)}, f32[1,32,128]{2,1,0:T(8,128)S(1)}, u32[]{:S(2)}, u32[]{:S(2)}) collective-permute-start(f32[1,32,128]{2,1,0:T(8,128)S(1)} %get-tuple-element.75), channel_id=1, source_target_pairs={{0,1},{2,3},{4,5},{6,7},{8,9},{10,11},{12,13},{14,15},{16,17},{18,... | collective-permute-start | bytes 49160 | tf_op jit(solution)/shard_map/ppermute | solution.py:23
  132.2 2.0 copy-start.8
  132.2 2.0 copy-start.9
  144.3 30.7 %collective-permute-start.16 = (f32[16,32,1]{2,1,0:T(8,128)}, f32[16,32,1]{2,1,0:T(8,128)}, u32[]{:S(2)}, u32[]{:S(2)}) collective-permute-start(f32[16,32,1]{2,1,0:T(8,128)} %get-tuple-element.59), channel_id=1, source_target_pairs={{2,0},{4,2},{6,4},{3,1},{5,3},{7,5},{10,8},{12,10},{14,12},{11,9},... | collective-permute-start | bytes 6152 | tf_op jit(solution)/shard_map/ppermute | solution.py:24
  145.6 31.3 %collective-permute-start.17 = (f32[16,32,1]{2,1,0:T(8,128)S(1)}, f32[16,32,1]{2,1,0:T(8,128)}, u32[]{:S(2)}, u32[]{:S(2)}) collective-permute-start(f32[16,32,1]{2,1,0:T(8,128)S(1)} %get-tuple-element.60), channel_id=1, source_target_pairs={{0,2},{2,4},{4,6},{1,3},{3,5},{5,7},{8,10},{10,12},{12,14},{9,11},... | collective-permute-start | bytes 6152 | tf_op jit(solution)/shard_map/ppermute | solution.py:23
  151.8 32.1 %all-to-all-start.3 = ((f32[256,2,128]{2,1,0:T(2,128)}), f32[256,2,128]{2,1,0:T(2,128)S(1)}, u32[]{:S(2)}, u32[]{:S(2)}) async-start(f32[256,2,128]{2,1,0:T(2,128)} %copy.43), calls=%async_computation.3 | async-start | bytes 524288 | tf_op jit(solution)/shard_map/all_to_all | solution.py:86
  166.1 17.8 %collective-permute-start.12 = (f32[1,32,128]{2,1,0:T(8,128)S(1)}, f32[1,32,128]{2,1,0:T(8,128)S(1)}, u32[]{:S(2)}, u32[]{:S(2)}) collective-permute-start(f32[1,32,128]{2,1,0:T(8,128)S(1)} %get-tuple-element.47), channel_id=1, source_target_pairs={{1,0},{3,2},{5,4},{7,6},{9,8},{11,10},{13,12},{15,14},{17,16},{19,... | collective-permute-start | bytes 49160 | tf_op jit(solution)/shard_map/ppermute | solution.py:24
  167.4 16.5 %collective-permute-start.13 = (f32[1,32,128]{2,1,0:T(8,128)S(1)}, f32[1,32,128]{2,1,0:T(8,128)S(1)}, u32[]{:S(2)}, u32[]{:S(2)}) collective-permute-start(f32[1,32,128]{2,1,0:T(8,128)S(1)} %get-tuple-element.48), channel_id=1, source_target_pairs={{0,1},{2,3},{4,5},{6,7},{8,9},{10,11},{12,13},{14,15},{16,17},{18,... | collective-permute-start | bytes 49160 | tf_op jit(solution)/shard_map/ppermute | solution.py:23
  170.5 8.4 %collective-permute-start.14 = (f32[16,1,128]{2,1,0:T(1,128)S(1)}, f32[16,1,128]{2,1,0:T(1,128)S(1)}, u32[]{:S(2)}, u32[]{:S(2)}) collective-permute-start(f32[16,1,128]{2,1,0:T(1,128)S(1)} %get-tuple-element.53), channel_id=1, source_target_pairs={{8,0},{16,8},{24,16},{32,24},{40,32},{48,40},{56,48},{64,56},{72,6... | collective-permute-start | bytes 24584 | tf_op jit(solution)/shard_map/ppermute | solution.py:24
  175.0 8.9 %collective-permute-start.15 = (f32[16,1,128]{2,1,0:T(1,128)S(1)}, f32[16,1,128]{2,1,0:T(1,128)S(1)}, u32[]{:S(2)}, u32[]{:S(2)}) collective-permute-start(f32[16,1,128]{2,1,0:T(1,128)S(1)} %get-tuple-element.54), channel_id=1, source_target_pairs={{0,8},{8,16},{16,24},{24,32},{32,40},{40,48},{48,56},{56,64},{64,7... | collective-permute-start | bytes 24584 | tf_op jit(solution)/shard_map/ppermute | solution.py:23
  194.5 0.7 copy-start.20
  195.2 1.0 copy-start.4
  196.2 7.1 %collective-permute-start.23 = (f32[16,32,1]{2,1,0:T(8,128)S(1)}, f32[16,32,1]{2,1,0:T(8,128)}, u32[]{:S(2)}, u32[]{:S(2)}) collective-permute-start(f32[16,32,1]{2,1,0:T(8,128)S(1)} %copy-done.4), channel_id=1, source_target_pairs={{0,2},{2,4},{4,6},{1,3},{3,5},{5,7},{8,10},{10,12},{12,14},{9,11},... | collective-permute-start | bytes 6152 | tf_op jit(solution)/shard_map/ppermute | solution.py:23
  204.0 28.8 %collective-permute-start.22 = (f32[16,32,1]{2,1,0:T(8,128)}, f32[16,32,1]{2,1,0:T(8,128)}, u32[]{:S(2)}, u32[]{:S(2)}) collective-permute-start(f32[16,32,1]{2,1,0:T(8,128)} %get-tuple-element.28), channel_id=1, source_target_pairs={{2,0},{4,2},{6,4},{3,1},{5,3},{7,5},{10,8},{12,10},{14,12},{11,9},... | collective-permute-start | bytes 6152 | tf_op jit(solution)/shard_map/ppermute | solution.py:24
  206.5 15.5 %copy-start.23 = (f32[16,1,128]{2,1,0:T(1,128)S(1)}, f32[16,1,128]{2,1,0:T(1,128)}, u32[]{:S(2)}) copy-start(f32[16,1,128]{2,1,0:T(1,128)} %get-tuple-element.34) | copy-start | bytes 24580
  206.5 20.0 %copy-start.22 = (f32[16,1,128]{2,1,0:T(1,128)S(1)}, f32[16,1,128]{2,1,0:T(1,128)}, u32[]{:S(2)}) copy-start(f32[16,1,128]{2,1,0:T(1,128)} %get-tuple-element.33) | copy-start | bytes 24580
  206.5 22.0 %copy-start.12 = (f32[1,32,128]{2,1,0:T(8,128)S(1)}, f32[1,32,128]{2,1,0:T(8,128)}, u32[]{:S(2)}) copy-start(f32[1,32,128]{2,1,0:T(8,128)} %get-tuple-element.40) | copy-start | bytes 49156
  206.5 23.3 %copy-start.11 = (f32[1,32,128]{2,1,0:T(8,128)S(1)}, f32[1,32,128]{2,1,0:T(8,128)}, u32[]{:S(2)}) copy-start(f32[1,32,128]{2,1,0:T(8,128)} %get-tuple-element.39) | copy-start | bytes 49156
  206.5 29.5 %all-to-all-start.4 = ((f32[256,2,128]{2,1,0:T(2,128)}), f32[256,2,128]{2,1,0:T(2,128)S(1)}, u32[]{:S(2)}, u32[]{:S(2)}) async-start(f32[256,2,128]{2,1,0:T(2,128)} %copy.46), calls=%async_computation.4 | async-start | bytes 524288 | tf_op jit(solution)/shard_map/all_to_all | solution.py:86
  222.0 12.7 %collective-permute-start.20 = (f32[16,1,128]{2,1,0:T(1,128)S(1)}, f32[16,1,128]{2,1,0:T(1,128)S(1)}, u32[]{:S(2)}, u32[]{:S(2)}) collective-permute-start(f32[16,1,128]{2,1,0:T(1,128)S(1)} %copy-done.23), channel_id=1, source_target_pairs={{8,0},{16,8},{24,16},{32,24},{40,32},{48,40},{56,48},{64,56},{72,6... | collective-permute-start | bytes 24584 | tf_op jit(solution)/shard_map/ppermute | solution.py:24
  226.5 8.9 %collective-permute-start.21 = (f32[16,1,128]{2,1,0:T(1,128)S(1)}, f32[16,1,128]{2,1,0:T(1,128)S(1)}, u32[]{:S(2)}, u32[]{:S(2)}) collective-permute-start(f32[16,1,128]{2,1,0:T(1,128)S(1)} %copy-done.22), channel_id=1, source_target_pairs={{0,8},{8,16},{16,24},{24,32},{32,40},{40,48},{48,56},{56,64},{64,7... | collective-permute-start | bytes 24584 | tf_op jit(solution)/shard_map/ppermute | solution.py:23
  228.5 7.5 %collective-permute-start.18 = (f32[1,32,128]{2,1,0:T(8,128)S(1)}, f32[1,32,128]{2,1,0:T(8,128)S(1)}, u32[]{:S(2)}, u32[]{:S(2)}) collective-permute-start(f32[1,32,128]{2,1,0:T(8,128)S(1)} %copy-done.12), channel_id=1, source_target_pairs={{1,0},{3,2},{5,4},{7,6},{9,8},{11,10},{13,12},{15,14},{17,16},{19,... | collective-permute-start | bytes 49160 | tf_op jit(solution)/shard_map/ppermute | solution.py:24
  229.8 6.2 %collective-permute-start.19 = (f32[1,32,128]{2,1,0:T(8,128)S(1)}, f32[1,32,128]{2,1,0:T(8,128)S(1)}, u32[]{:S(2)}, u32[]{:S(2)}) collective-permute-start(f32[1,32,128]{2,1,0:T(8,128)S(1)} %copy-done.11), channel_id=1, source_target_pairs={{0,1},{2,3},{4,5},{6,7},{8,9},{10,11},{12,13},{14,15},{16,17},{18,... | collective-permute-start | bytes 49160 | tf_op jit(solution)/shard_map/ppermute | solution.py:23
  (11 other events, 7.4 us)
where the time goes:
time: 250 us; the launch traced here: 246 us
  starting transfers between devices  138 us (55%)
  other arithmetic  53 us (21%)
  local copies, waits for them, and re-layouts  39 us (16%)
  waiting for transfers between devices  14.5 us (6%)
    all_to_all x4, starting transfers between devices, on_device(): lax.all_to_all(sent, ('gx', 'gy'), split_axis=0, concat_axis=0, tiled=True)  53.6 us
    ppermute x12, starting transfers between devices, neighbours(): from_low = lax.ppermute(last, axis, [(i, i + 1) for i in range(count - 1)])  41.6 us
    ppermute x12, starting transfers between devices, neighbours(): lax.ppermute(first, axis, [(i + 1, i) for i in range(count - 1)])  28.7 us
    all_to_all x1, starting transfers between devices, on_device(): lax.all_to_all(slot_term, ('gx', 'gy'), split_axis=0, concat_axis=0, tile...  14 us
    ppermute x12, waiting for transfers between devices, neighbours(): from_low = lax.ppermute(last, axis, [(i, i + 1) for i in range(count - 1)])  13.7 us
    unnamed x60, local copies, waits for them, and re-layouts  8.13 us
    scatter-add x4, other arithmetic, on_device(): into_term = jax.ops.segment_sum(-current, safe_ids, num_segments=term_count)  7.66 us
    scatter-add x4, other arithmetic, on_device(): jax.ops.segment_sum(tile_current, junction_block, num_segments=depth * ro...  7.21 us
  transfers between devices with their start and end apart: 29, of which 6 were waited for; matrix products, arithmetic and copies ran while one was open for 16% of the time, Pallas kernels for 0%

commit v1 on v0

--- a/solution.py
+++ b/solution.py
@@ -20,8 +20,12 @@
     size = cells.shape[dim]
     first = lax.slice_in_dim(cells, 0, 1, axis=dim)
     last = lax.slice_in_dim(cells, size - 1, size, axis=dim)
+    face = first.shape
+    if dim == cells.ndim - 1:
+        first, last = (x.reshape(-1, 128) for x in (first, last))
     from_low = lax.ppermute(last, axis, [(i, i + 1) for i in range(count - 1)])
     from_high = lax.ppermute(first, axis, [(i + 1, i) for i in range(count - 1)])
+    first, last, from_low, from_high = (x.reshape(face) for x in (first, last, from_low, from_high))
     low = jnp.where(index == 0, first, from_low)
     high = jnp.where(index == count - 1, last, from_high)
     plus = jnp.concatenate([lax.slice_in_dim(cells, 1, size, axis=dim), high], axis=dim)

time: 250 us -> 240 us (0.960)
  starting transfers between devices: 138 us -> 132 us
  other arithmetic: 53 us -> 49.6 us
    reshape x0 -> x16, local copies, waits for them, and re-layouts: none -> 5.08 us  [the longest x8 4.46 us: neighbours(): x.reshape(face)]
    all_to_all x4, starting transfers between devices: 53.6 us -> 49.8 us  [on_device(): lax.all_to_all(sent, ('gx', 'gy'), split_axis=0, concat_axis=0, tiled=True)]
    slice x9 -> x10, local copies, waits for them, and re-layouts: 6.13 us -> 2.44 us  [neighbours(): last = lax.slice_in_dim(cells, size - 1, size, axis=dim)]
    select_n x4 -> x3, other arithmetic: 3.68 us -> 0.92 us  [neighbours(): high = jnp.where(index == count - 1, last, from_high)]
    unnamed x60 -> x40, local copies, waits for them, and re-layouts: 8.13 us -> 5.95 us
  transfers between devices with their start and end apart: 29 -> 29, of which waited for: 6 -> 3; matrix products, arithmetic and copies ran while one was open for 16% -> 16% of each run, Pallas kernels for 0% -> 0%
where the time goes in v1:
time: 240 us; the launch traced here: 235 us
  starting transfers between devices  132 us (55%)
  other arithmetic  49.6 us (21%)
  local copies, waits for them, and re-layouts  36.9 us (15%)
  waiting for transfers between devices  15.1 us (6%)
    all_to_all x4, starting transfers between devices, on_device(): lax.all_to_all(sent, ('gx', 'gy'), split_axis=0, concat_axis=0, tiled=True)  49.8 us
    ppermute x12, starting transfers between devices, neighbours(): from_low = lax.ppermute(last, axis, [(i, i + 1) for i in range(count - 1)])  39.6 us
    ppermute x12, starting transfers between devices, neighbours(): lax.ppermute(first, axis, [(i + 1, i) for i in range(count - 1)])  28.5 us
    all_to_all x1, starting transfers between devices, on_device(): lax.all_to_all(slot_term, ('gx', 'gy'), split_axis=0, concat_axis=0, tile...  14 us
    ppermute x12, waiting for transfers between devices, neighbours(): from_low = lax.ppermute(last, axis, [(i, i + 1) for i in range(count - 1)])  13.6 us
    scatter-add x4, other arithmetic, on_device(): into_term = jax.ops.segment_sum(-current, safe_ids, num_segments=term_count)  7.86 us
    scatter-add x4, other arithmetic, on_device(): jax.ops.segment_sum(tile_current, junction_block, num_segments=depth * ro...  7.39 us
    unnamed x40, local copies, waits for them, and re-layouts  5.95 us
  transfers between devices with their start and end apart: 29, of which 3 were waited for; matrix products, arithmetic and copies ran while one was open for 16% of the time, Pallas kernels for 0%

profile of v1, /device:TPU:128, one launch (start us, length us, event | category | flops | bytes accessed | tf_op | source)
XLA Modules:
  0.0 235.1 jit_solution(9546726062214619200)
XLA Ops:
  3.5 14.0 %all-to-all-start = ((s32[128,2,1]{1,2,0:T(1,128)}), s32[128,2,1]{1,2,0:T(1,128)S(1)}, u32[]{:S(2)}, u32[]{:S(2)}) async-start(s32[128,2,1]{1,2,0:T(1,128)} %bitcast.33), calls=%async_computation | async-start | bytes 131072 | tf_op jit(solution)/shard_map/all_to_all | solution.py:75
  17.5 1.4 slice_reduce_fusion.7
  19.0 1.3 collective-permute-start.4
  20.4 4.5 %collective-permute-start.5 = (f32[4,128]{1,0:T(4,128)S(1)}, f32[4,128]{1,0:T(4,128)S(1)}, u32[]{:S(2)}, u32[]{:S(2)}) collective-permute-start(f32[4,128]{1,0:T(4,128)S(1)} %reshape.261), channel_id=1, source_target_pairs={{0,2},{2,4},{4,6},{1,3},{3,5},{5,7},{8,10},{10,12},{12,14},{9,11},... | collective-permute-start | bytes 6152 | tf_op jit(solution)/shard_map/ppermute | solution.py:26
  24.9 1.3 collective-permute-start
  26.2 3.0 %collective-permute-start.1 = (f32[1,32,128]{2,1,0:T(8,128)S(1)}, f32[1,32,128]{2,1,0:T(8,128)S(1)}, u32[]{:S(2)}, u32[]{:S(2)}) collective-permute-start(f32[1,32,128]{2,1,0:T(8,128)S(1)} %get-tuple-element.113), channel_id=1, source_target_pairs={{0,1},{2,3},{4,5},{6,7},{8,9},{10,11},{12,13},{14,15},{16,17},{18,... | collective-permute-start | bytes 49160 | tf_op jit(solution)/shard_map/ppermute | solution.py:26
  29.3 4.6 %collective-permute-start.2 = (f32[16,1,128]{2,0,1:T(8,128)S(1)}, f32[16,1,128]{2,0,1:T(8,128)S(1)}, u32[]{:S(2)}, u32[]{:S(2)}) collective-permute-start(f32[16,1,128]{2,0,1:T(8,128)S(1)} %bitcast.138), channel_id=1, source_target_pairs={{8,0},{16,8},{24,16},{32,24},{40,32},{48,40},{56,48},{64,56},{72,6... | collective-permute-start | bytes 24584 | tf_op jit(solution)/shard_map/ppermute | solution.py:27
  38.2 5.3 %select_select_fusion = (f32[16,32,128]{2,1,0:T(8,128)S(1)}, pred[16,32,128]{2,1,0:T(8,128)(4,1)S(1)}, pred[16,32,128]{2,1,0:T(8,128)(4,1)S(1)}, pred[16,32,128]...) fusion(f32[]{:T(128)} %bitcast.23, f32[]{:T(128)} %bitcast.22, ...), kind=kLoop, calls=%fused_computation.84 | loop fusion | flops 1048576 | bytes 1048608 | tf_op jit(solution)/shard_map/jit(_where)/select_n | solution.py:62
  43.6 5.2 %select_select_fusion.1 = f32[16,32,128]{2,1,0:T(8,128)S(1)} fusion(pred[16,32,128]{2,1,0:T(8,128)(4,1)S(1)} %get-tuple-element.50, pred[16,32,128]{2,1,0:T(8,128)(4,1)S(1)} %get-tuple-element.49, pred[16,32,128]{2,1,0:T(8,128)(4,1)S(1)} %get-tuple-element.48, pred[16,32,128]{2,1,0:T(8,128)(4,1)S(1)} %get-tuple-element.47, ...), kind=kLoop, calls=%fused_computation.85 | loop fusion | flops 524288 | bytes 786464 | tf_op jit(solution)/shard_map/jit(_where)/select_n | solution.py:61
  48.7 5.2 %select_select_fusion.2 = f32[16,32,128]{2,1,0:T(8,128)S(1)} fusion(pred[16,32,128]{2,1,0:T(8,128)(4,1)S(1)} %get-tuple-element.50, pred[16,32,128]{2,1,0:T(8,128)(4,1)S(1)} %get-tuple-element.49, pred[16,32,128]{2,1,0:T(8,128)(4,1)S(1)} %get-tuple-element.48, pred[16,32,128]{2,1,0:T(8,128)(4,1)S(1)} %get-tuple-element.47, ...), kind=kLoop, calls=%fused_computation.86 | loop fusion | flops 524288 | bytes 786464 | tf_op jit(solution)/shard_map/jit(_where)/select_n | solution.py:60
  58.3 11.7 %all-to-all-start.1 = ((f32[256,3,128]{2,1,0:T(4,128)}), f32[256,3,128]{2,1,0:T(4,128)S(1)}, u32[]{:S(2)}, u32[]{:S(2)}) async-start(f32[256,3,128]{2,1,0:T(4,128)} %copy.324), calls=%async_computation.1 | async-start | bytes 1048576 | tf_op jit(solution)/shard_map/all_to_all | solution.py:90
  70.0 3.4 %collective-permute-start.3 = (f32[16,1,128]{2,0,1:T(8,128)S(1)}, f32[16,1,128]{2,0,1:T(8,128)S(1)}, u32[]{:S(2)}, u32[]{:S(2)}) collective-permute-start(f32[16,1,128]{2,0,1:T(8,128)S(1)} %bitcast.137), channel_id=1, source_target_pairs={{0,8},{8,16},{16,24},{24,32},{32,40},{40,48},{48,56},{56,64},{64,7... | collective-permute-start | bytes 24584 | tf_op jit(solution)/shard_map/ppermute | solution.py:26
  74.7 7.9 %collective-permute-done.3 = f32[16,1,128]{2,0,1:T(8,128)S(1)} collective-permute-done((f32[16,1,128]{2,0,1:T(8,128)S(1)}, f32[16,1,128]{2,0,1:T(8,128)S(1)}, u32[]{:S(2)}, u32[]{:S(2)}) %collective-permute-start.3) | collective-permute-done | bytes 8224 | tf_op jit(solution)/shard_map/ppermute | solution.py:26
  82.7 1.5 all-to-all-done.1
  84.3 1.7 scatter_custom_fusion.1
  88.5 1.6 scatter_custom_fusion
  90.2 1.7 fusion.5
  95.6 4.7 %collective-permute-start.11 = (f32[4,128]{1,0:T(4,128)S(1)}, f32[4,128]{1,0:T(4,128)S(1)}, u32[]{:S(2)}, u32[]{:S(2)}) collective-permute-start(f32[4,128]{1,0:T(4,128)S(1)} %reshape.267), channel_id=1, source_target_pairs={{0,2},{2,4},{4,6},{1,3},{3,5},{5,7},{8,10},{10,12},{12,14},{9,11},... | collective-permute-start | bytes 6152 | tf_op jit(solution)/shard_map/ppermute | solution.py:26
  101.2 11.9 %all-to-all-start.2 = ((f32[256,2,128]{2,1,0:T(2,128)}), f32[256,2,128]{2,1,0:T(2,128)S(1)}, u32[]{:S(2)}, u32[]{:S(2)}) async-start(f32[256,2,128]{2,1,0:T(2,128)} %copy.333), calls=%async_computation.2 | async-start | bytes 524288 | tf_op jit(solution)/shard_map/all_to_all | solution.py:90
  113.1 4.6 %collective-permute-start.8 = (f32[16,1,128]{2,0,1:T(8,128)S(1)}, f32[16,1,128]{2,0,1:T(8,128)S(1)}, u32[]{:S(2)}, u32[]{:S(2)}) collective-permute-start(f32[16,1,128]{2,0,1:T(8,128)S(1)} %bitcast.143), channel_id=1, source_target_pairs={{8,0},{16,8},{24,16},{32,24},{40,32},{48,40},{56,48},{64,56},{72,6... | collective-permute-start | bytes 24584 | tf_op jit(solution)/shard_map/ppermute | solution.py:27
  117.6 1.9 collective-permute-start.9
  119.6 1.3 collective-permute-start.6
  120.9 3.0 %collective-permute-start.7 = (f32[1,32,128]{2,1,0:T(8,128)S(1)}, f32[1,32,128]{2,1,0:T(8,128)S(1)}, u32[]{:S(2)}, u32[]{:S(2)}) collective-permute-start(f32[1,32,128]{2,1,0:T(8,128)S(1)} %get-tuple-element.95), channel_id=1, source_target_pairs={{0,1},{2,3},{4,5},{6,7},{8,9},{10,11},{12,13},{14,15},{16,17},{18,... | collective-permute-start | bytes 49160 | tf_op jit(solution)/shard_map/ppermute | solution.py:26
  125.7 1.8 slice_select_fusion.4
  127.7 1.9 scatter_custom_fusion.3
  131.3 1.8 scatter_custom_fusion.2
  133.1 1.8 fusion.14
  139.9 4.5 %collective-permute-start.17 = (f32[4,128]{1,0:T(4,128)S(1)}, f32[4,128]{1,0:T(4,128)S(1)}, u32[]{:S(2)}, u32[]{:S(2)}) collective-permute-start(f32[4,128]{1,0:T(4,128)S(1)} %reshape.273), channel_id=1, source_target_pairs={{0,2},{2,4},{4,6},{1,3},{3,5},{5,7},{8,10},{10,12},{12,14},{9,11},... | collective-permute-start | bytes 6152 | tf_op jit(solution)/shard_map/ppermute | solution.py:26
  145.3 15.0 %all-to-all-start.3 = ((f32[256,2,128]{2,1,0:T(2,128)}), f32[256,2,128]{2,1,0:T(2,128)S(1)}, u32[]{:S(2)}, u32[]{:S(2)}) async-start(f32[256,2,128]{2,1,0:T(2,128)} %copy.342), calls=%async_computation.3 | async-start | bytes 524288 | tf_op jit(solution)/shard_map/all_to_all | solution.py:90
  160.3 1.3 collective-permute-start.12
  161.6 3.0 %collective-permute-start.13 = (f32[1,32,128]{2,1,0:T(8,128)S(1)}, f32[1,32,128]{2,1,0:T(8,128)S(1)}, u32[]{:S(2)}, u32[]{:S(2)}) collective-permute-start(f32[1,32,128]{2,1,0:T(8,128)S(1)} %get-tuple-element.72), channel_id=1, source_target_pairs={{0,1},{2,3},{4,5},{6,7},{8,9},{10,11},{12,13},{14,15},{16,17},{18,... | collective-permute-start | bytes 49160 | tf_op jit(solution)/shard_map/ppermute | solution.py:26
  164.7 4.6 %collective-permute-start.14 = (f32[16,1,128]{2,0,1:T(8,128)}, f32[16,1,128]{2,0,1:T(8,128)S(1)}, u32[]{:S(2)}, u32[]{:S(2)}) collective-permute-start(f32[16,1,128]{2,0,1:T(8,128)} %bitcast.52), channel_id=1, source_target_pairs={{8,0},{16,8},{24,16},{32,24},{40,32},{48,40},{56,48},{64,56},{72,6... | collective-permute-start | bytes 24584 | tf_op jit(solution)/shard_map/ppermute | solution.py:27
  169.2 1.9 collective-permute-start.15
  172.5 5.6 %collective-permute-done.15 = f32[16,1,128]{2,0,1:T(8,128)S(1)} collective-permute-done((f32[16,1,128]{2,0,1:T(8,128)S(1)}, f32[16,1,128]{2,0,1:T(8,128)S(1)}, u32[]{:S(2)}, u32[]{:S(2)}) %collective-permute-start.15) | collective-permute-done | bytes 8224 | tf_op jit(solution)/shard_map/ppermute | solution.py:26
  178.3 1.9 scatter_custom_fusion.5
  183.8 2.0 scatter_custom_fusion.4
  185.8 2.6 %multiply_add_fusion = (f32[16,32,128]{2,1,0:T(8,128)}, f32[16,32,128]{2,1,0:T(8,128)S(1)}, f32[16,32,128]{2,1,0:T(8,128)S(1)}) fusion(f32[16,32,128]{2,1,0:T(8,128)S(1)} %fusion.14, f32[16,32,128]{2,1,0:T(8,128)S(1)} %bitcast.117, f32[16,32,128]{2,1,0:T(8,128)S(1)} %get-tuple-element.9, f32[16,32,127]{2,1,0:T(8,128)} %get-tuple-element.80, ...), kind=kLoop, calls=%fused_computation.80 | loop fusion | flops 3735552 | bytes 4456448 | tf_op jit(solution)/shard_map/add | solution.py:13
  192.1 4.5 %collective-permute-start.23 = (f32[4,128]{1,0:T(4,128)S(1)}, f32[4,128]{1,0:T(4,128)S(1)}, u32[]{:S(2)}, u32[]{:S(2)}) collective-permute-start(f32[4,128]{1,0:T(4,128)S(1)} %reshape.279), channel_id=1, source_target_pairs={{0,2},{2,4},{4,6},{1,3},{3,5},{5,7},{8,10},{10,12},{12,14},{9,11},... | collective-permute-start | bytes 6152 | tf_op jit(solution)/shard_map/ppermute | solution.py:26
  197.6 11.2 %all-to-all-start.4 = ((f32[256,2,128]{2,1,0:T(2,128)}), f32[256,2,128]{2,1,0:T(2,128)S(1)}, u32[]{:S(2)}, u32[]{:S(2)}) async-start(f32[256,2,128]{2,1,0:T(2,128)} %copy.351), calls=%async_computation.4 | async-start | bytes 524288 | tf_op jit(solution)/shard_map/all_to_all | solution.py:90
  208.9 4.6 %collective-permute-start.20 = (f32[16,1,128]{2,0,1:T(8,128)S(1)}, f32[16,1,128]{2,0,1:T(8,128)S(1)}, u32[]{:S(2)}, u32[]{:S(2)}) collective-permute-start(f32[16,1,128]{2,0,1:T(8,128)S(1)} %bitcast.140), channel_id=1, source_target_pairs={{8,0},{16,8},{24,16},{32,24},{40,32},{48,40},{56,48},{64,56},{72,6... | collective-permute-start | bytes 24584 | tf_op jit(solution)/shard_map/ppermute | solution.py:27
  213.4 1.9 collective-permute-start.21
  215.3 1.3 collective-permute-start.18
  216.7 3.0 %collective-permute-start.19 = (f32[1,32,128]{2,1,0:T(8,128)S(1)}, f32[1,32,128]{2,1,0:T(8,128)S(1)}, u32[]{:S(2)}, u32[]{:S(2)}) collective-permute-start(f32[1,32,128]{2,1,0:T(8,128)S(1)} %get-tuple-element.63), channel_id=1, source_target_pairs={{0,1},{2,3},{4,5},{6,7},{8,9},{10,11},{12,13},{14,15},{16,17},{18,... | collective-permute-start | bytes 49160 | tf_op jit(solution)/shard_map/ppermute | solution.py:26
  221.5 1.8 slice_select_fusion
  224.1 2.4 %scatter_custom_fusion.7 = f32[32,128]{1,0:T(8,128)} fusion(s32[256]{0:T(256)} %bitcast.150, f32[256,128]{1,0:T(8,128)S(1)} %gather_fusion.10, f32[256,128]{1,0:T(8,128)S(1)} %bitcast.121, f32[256]{0:T(256)S(1)} %compare_select_fusion.5, f32[]{:T(128)} %constant.38.clone.1), kind=kCustom, calls=%fused_computation.107 | custom fusion | flops 131072 | bytes 280064 | tf_op jit(solution)/shard_map/scatter-add | solution.py:92
  228.1 2.0 scatter_custom_fusion.6
  230.7 1.5 fusion.78
  232.9 2.2 fusion.32
  (181 shorter events, 44.7 us)
Async XLA Ops:
  0.6 0.7 copy-start.17
  1.3 0.7 copy-start.16
  3.5 50.4 %all-to-all-start = ((s32[128,2,1]{1,2,0:T(1,128)}), s32[128,2,1]{1,2,0:T(1,128)S(1)}, u32[]{:S(2)}, u32[]{:S(2)}) async-start(s32[128,2,1]{1,2,0:T(1,128)} %bitcast.33), calls=%async_computation | async-start | bytes 131072 | tf_op jit(solution)/shard_map/all_to_all | solution.py:75
  17.5 7.4 %copy-start = (f32[16,32,128]{2,1,0:T(8,128)S(1)}, f32[16,32,128]{2,1,0:T(8,128)}, u32[]{:S(2)}) copy-start(f32[16,32,128]{2,1,0:T(8,128)} %param.11) | copy-start | bytes 786436
  19.0 51.0 %collective-permute-start.4 = (f32[4,128]{1,0:T(4,128)S(1)}, f32[4,128]{1,0:T(4,128)S(1)}, u32[]{:S(2)}, u32[]{:S(2)}) collective-permute-start(f32[4,128]{1,0:T(4,128)S(1)} %reshape.259), channel_id=1, source_target_pairs={{2,0},{4,2},{6,4},{3,1},{5,3},{7,5},{10,8},{12,10},{14,12},{11,9},... | collective-permute-start | bytes 6152 | tf_op jit(solution)/shard_map/ppermute | solution.py:27
  20.4 53.2 %collective-permute-start.5 = (f32[4,128]{1,0:T(4,128)S(1)}, f32[4,128]{1,0:T(4,128)S(1)}, u32[]{:S(2)}, u32[]{:S(2)}) collective-permute-start(f32[4,128]{1,0:T(4,128)S(1)} %reshape.261), channel_id=1, source_target_pairs={{0,2},{2,4},{4,6},{1,3},{3,5},{5,7},{8,10},{10,12},{12,14},{9,11},... | collective-permute-start | bytes 6152 | tf_op jit(solution)/shard_map/ppermute | solution.py:26
  24.9 57.7 %collective-permute-start = (f32[1,32,128]{2,1,0:T(8,128)S(1)}, f32[1,32,128]{2,1,0:T(8,128)S(1)}, u32[]{:S(2)}, u32[]{:S(2)}) collective-permute-start(f32[1,32,128]{2,1,0:T(8,128)S(1)} %get-tuple-element.114), channel_id=1, source_target_pairs={{1,0},{3,2},{5,4},{7,6},{9,8},{11,10},{13,12},{15,14},{17,16},{19,... | collective-permute-start | bytes 49160 | tf_op jit(solution)/shard_map/ppermute | solution.py:27
  26.2 56.4 %collective-permute-start.1 = (f32[1,32,128]{2,1,0:T(8,128)S(1)}, f32[1,32,128]{2,1,0:T(8,128)S(1)}, u32[]{:S(2)}, u32[]{:S(2)}) collective-permute-start(f32[1,32,128]{2,1,0:T(8,128)S(1)} %get-tuple-element.113), channel_id=1, source_target_pairs={{0,1},{2,3},{4,5},{6,7},{8,9},{10,11},{12,13},{14,15},{16,17},{18,... | collective-permute-start | bytes 49160 | tf_op jit(solution)/shard_map/ppermute | solution.py:26
  29.3 4.6 %copy-start.6 = (f32[3,8]{1,0:T(4,128)S(1)}, f32[3,8]{1,0:T(4,128)}, u32[]{:S(2)}) copy-start(f32[3,8]{1,0:T(4,128)} %param.14) | copy-start | bytes 292
  29.3 45.4 %collective-permute-start.2 = (f32[16,1,128]{2,0,1:T(8,128)S(1)}, f32[16,1,128]{2,0,1:T(8,128)S(1)}, u32[]{:S(2)}, u32[]{:S(2)}) collective-permute-start(f32[16,1,128]{2,0,1:T(8,128)S(1)} %bitcast.138), channel_id=1, source_target_pairs={{8,0},{16,8},{24,16},{32,24},{40,32},{48,40},{56,48},{64,56},{72,6... | collective-permute-start | bytes 24584 | tf_op jit(solution)/shard_map/ppermute | solution.py:27
  35.4 58.6 %copy-start.12 = (pred[256]{0:T(512)(128)(4,1)}, pred[256]{0:T(512)(128)(4,1)S(1)}, u32[]{:S(2)}) copy-start(pred[256]{0:T(512)(128)(4,1)S(1)} %fusion.52) | copy-start | bytes 772
  35.6 0.9 copy-start.1
  37.3 1.0 copy-start.4
  54.0 76.5 %copy-start.8 = (s32[1024]{0:T(1024)}, s32[1024]{0:T(1024)S(1)}, u32[]{:S(2)}) copy-start(s32[1024]{0:T(1024)S(1)} %pad_clamp_fusion.1) | copy-start | bytes 12292
  54.1 0.7 copy-start.18
  56.3 28.0 %copy-start.15 = (s32[256,1]{0,1:T(1,128)}, s32[256,1]{0,1:T(1,128)S(1)}, u32[]{:S(2)}) copy-start(s32[256,1]{0,1:T(1,128)S(1)} %get-tuple-element.149) | copy-start | bytes 3076
  58.3 25.9 %all-to-all-start.1 = ((f32[256,3,128]{2,1,0:T(4,128)}), f32[256,3,128]{2,1,0:T(4,128)S(1)}, u32[]{:S(2)}, u32[]{:S(2)}) async-start(f32[256,3,128]{2,1,0:T(4,128)} %copy.324), calls=%async_computation.1 | async-start | bytes 1048576 | tf_op jit(solution)/shard_map/all_to_all | solution.py:90
  70.0 12.7 %collective-permute-start.3 = (f32[16,1,128]{2,0,1:T(8,128)S(1)}, f32[16,1,128]{2,0,1:T(8,128)S(1)}, u32[]{:S(2)}, u32[]{:S(2)}) collective-permute-start(f32[16,1,128]{2,0,1:T(8,128)S(1)} %bitcast.137), channel_id=1, source_target_pairs={{0,8},{8,16},{16,24},{24,32},{32,40},{40,48},{48,56},{56,64},{64,7... | collective-permute-start | bytes 24584 | tf_op jit(solution)/shard_map/ppermute | solution.py:26
  84.3 1.8 copy-start.5
  86.1 0.7 copy-start.9
  88.5 1.7 copy-start.2
  94.2 26.7 %collective-permute-start.10 = (f32[4,128]{1,0:T(4,128)S(1)}, f32[4,128]{1,0:T(4,128)S(1)}, u32[]{:S(2)}, u32[]{:S(2)}) collective-permute-start(f32[4,128]{1,0:T(4,128)S(1)} %reshape.265), channel_id=1, source_target_pairs={{2,0},{4,2},{6,4},{3,1},{5,3},{7,5},{10,8},{12,10},{14,12},{11,9},... | collective-permute-start | bytes 6152 | tf_op jit(solution)/shard_map/ppermute | solution.py:27
  95.6 29.3 %collective-permute-start.11 = (f32[4,128]{1,0:T(4,128)S(1)}, f32[4,128]{1,0:T(4,128)S(1)}, u32[]{:S(2)}, u32[]{:S(2)}) collective-permute-start(f32[4,128]{1,0:T(4,128)S(1)} %reshape.267), channel_id=1, source_target_pairs={{0,2},{2,4},{4,6},{1,3},{3,5},{5,7},{8,10},{10,12},{12,14},{9,11},... | collective-permute-start | bytes 6152 | tf_op jit(solution)/shard_map/ppermute | solution.py:26
  101.2 26.4 %all-to-all-start.2 = ((f32[256,2,128]{2,1,0:T(2,128)}), f32[256,2,128]{2,1,0:T(2,128)S(1)}, u32[]{:S(2)}, u32[]{:S(2)}) async-start(f32[256,2,128]{2,1,0:T(2,128)} %copy.333), calls=%async_computation.2 | async-start | bytes 524288 | tf_op jit(solution)/shard_map/all_to_all | solution.py:90
  113.1 14.5 %collective-permute-start.8 = (f32[16,1,128]{2,0,1:T(8,128)S(1)}, f32[16,1,128]{2,0,1:T(8,128)S(1)}, u32[]{:S(2)}, u32[]{:S(2)}) collective-permute-start(f32[16,1,128]{2,0,1:T(8,128)S(1)} %bitcast.143), channel_id=1, source_target_pairs={{8,0},{16,8},{24,16},{32,24},{40,32},{48,40},{56,48},{64,56},{72,6... | collective-permute-start | bytes 24584 | tf_op jit(solution)/shard_map/ppermute | solution.py:27
  117.6 9.9 %collective-permute-start.9 = (f32[16,1,128]{2,0,1:T(8,128)S(1)}, f32[16,1,128]{2,0,1:T(8,128)S(1)}, u32[]{:S(2)}, u32[]{:S(2)}) collective-permute-start(f32[16,1,128]{2,0,1:T(8,128)S(1)} %bitcast.141), channel_id=1, source_target_pairs={{0,8},{8,16},{16,24},{24,32},{32,40},{40,48},{48,56},{56,64},{64,7... | collective-permute-start | bytes 24584 | tf_op jit(solution)/shard_map/ppermute | solution.py:26
  119.6 8.0 %collective-permute-start.6 = (f32[1,32,128]{2,1,0:T(8,128)S(1)}, f32[1,32,128]{2,1,0:T(8,128)S(1)}, u32[]{:S(2)}, u32[]{:S(2)}) collective-permute-start(f32[1,32,128]{2,1,0:T(8,128)S(1)} %get-tuple-element.96), channel_id=1, source_target_pairs={{1,0},{3,2},{5,4},{7,6},{9,8},{11,10},{13,12},{15,14},{17,16},{19,... | collective-permute-start | bytes 49160 | tf_op jit(solution)/shard_map/ppermute | solution.py:27
  120.9 6.7 %collective-permute-start.7 = (f32[1,32,128]{2,1,0:T(8,128)S(1)}, f32[1,32,128]{2,1,0:T(8,128)S(1)}, u32[]{:S(2)}, u32[]{:S(2)}) collective-permute-start(f32[1,32,128]{2,1,0:T(8,128)S(1)} %get-tuple-element.95), channel_id=1, source_target_pairs={{0,1},{2,3},{4,5},{6,7},{8,9},{10,11},{12,13},{14,15},{16,17},{18,... | collective-permute-start | bytes 49160 | tf_op jit(solution)/shard_map/ppermute | solution.py:26
  137.6 0.7 copy-start.13
  138.5 30.7 %collective-permute-start.16 = (f32[4,128]{1,0:T(4,128)S(1)}, f32[4,128]{1,0:T(4,128)S(1)}, u32[]{:S(2)}, u32[]{:S(2)}) collective-permute-start(f32[4,128]{1,0:T(4,128)S(1)} %reshape.271), channel_id=1, source_target_pairs={{2,0},{4,2},{6,4},{3,1},{5,3},{7,5},{10,8},{12,10},{14,12},{11,9},... | collective-permute-start | bytes 6152 | tf_op jit(solution)/shard_map/ppermute | solution.py:27
  139.9 31.5 %collective-permute-start.17 = (f32[4,128]{1,0:T(4,128)S(1)}, f32[4,128]{1,0:T(4,128)S(1)}, u32[]{:S(2)}, u32[]{:S(2)}) collective-permute-start(f32[4,128]{1,0:T(4,128)S(1)} %reshape.273), channel_id=1, source_target_pairs={{0,2},{2,4},{4,6},{1,3},{3,5},{5,7},{8,10},{10,12},{12,14},{9,11},... | collective-permute-start | bytes 6152 | tf_op jit(solution)/shard_map/ppermute | solution.py:26
  145.3 32.8 %all-to-all-start.3 = ((f32[256,2,128]{2,1,0:T(2,128)}), f32[256,2,128]{2,1,0:T(2,128)S(1)}, u32[]{:S(2)}, u32[]{:S(2)}) async-start(f32[256,2,128]{2,1,0:T(2,128)} %copy.342), calls=%async_computation.3 | async-start | bytes 524288 | tf_op jit(solution)/shard_map/all_to_all | solution.py:90
  160.3 17.8 %collective-permute-start.12 = (f32[1,32,128]{2,1,0:T(8,128)S(1)}, f32[1,32,128]{2,1,0:T(8,128)S(1)}, u32[]{:S(2)}, u32[]{:S(2)}) collective-permute-start(f32[1,32,128]{2,1,0:T(8,128)S(1)} %get-tuple-element.71), channel_id=1, source_target_pairs={{1,0},{3,2},{5,4},{7,6},{9,8},{11,10},{13,12},{15,14},{17,16},{19,... | collective-permute-start | bytes 49160 | tf_op jit(solution)/shard_map/ppermute | solution.py:27
  161.6 16.5 %collective-permute-start.13 = (f32[1,32,128]{2,1,0:T(8,128)S(1)}, f32[1,32,128]{2,1,0:T(8,128)S(1)}, u32[]{:S(2)}, u32[]{:S(2)}) collective-permute-start(f32[1,32,128]{2,1,0:T(8,128)S(1)} %get-tuple-element.72), channel_id=1, source_target_pairs={{0,1},{2,3},{4,5},{6,7},{8,9},{10,11},{12,13},{14,15},{16,17},{18,... | collective-permute-start | bytes 49160 | tf_op jit(solution)/shard_map/ppermute | solution.py:26
  164.7 7.8 %collective-permute-start.14 = (f32[16,1,128]{2,0,1:T(8,128)}, f32[16,1,128]{2,0,1:T(8,128)S(1)}, u32[]{:S(2)}, u32[]{:S(2)}) collective-permute-start(f32[16,1,128]{2,0,1:T(8,128)} %bitcast.52), channel_id=1, source_target_pairs={{8,0},{16,8},{24,16},{32,24},{40,32},{48,40},{56,48},{64,56},{72,6... | collective-permute-start | bytes 24584 | tf_op jit(solution)/shard_map/ppermute | solution.py:27
  169.2 8.9 %collective-permute-start.15 = (f32[16,1,128]{2,0,1:T(8,128)S(1)}, f32[16,1,128]{2,0,1:T(8,128)S(1)}, u32[]{:S(2)}, u32[]{:S(2)}) collective-permute-start(f32[16,1,128]{2,0,1:T(8,128)S(1)} %bitcast.142), channel_id=1, source_target_pairs={{0,8},{8,16},{16,24},{24,32},{32,40},{40,48},{48,56},{56,64},{64,7... | collective-permute-start | bytes 24584 | tf_op jit(solution)/shard_map/ppermute | solution.py:26
  180.1 0.7 copy-start.10
  189.9 0.7 copy-start.14
  190.8 25.9 %collective-permute-start.22 = (f32[4,128]{1,0:T(4,128)S(1)}, f32[4,128]{1,0:T(4,128)S(1)}, u32[]{:S(2)}, u32[]{:S(2)}) collective-permute-start(f32[4,128]{1,0:T(4,128)S(1)} %reshape.277), channel_id=1, source_target_pairs={{2,0},{4,2},{6,4},{3,1},{5,3},{7,5},{10,8},{12,10},{14,12},{11,9},... | collective-permute-start | bytes 6152 | tf_op jit(solution)/shard_map/ppermute | solution.py:27
  192.1 28.5 %collective-permute-start.23 = (f32[4,128]{1,0:T(4,128)S(1)}, f32[4,128]{1,0:T(4,128)S(1)}, u32[]{:S(2)}, u32[]{:S(2)}) collective-permute-start(f32[4,128]{1,0:T(4,128)S(1)} %reshape.279), channel_id=1, source_target_pairs={{0,2},{2,4},{4,6},{1,3},{3,5},{5,7},{8,10},{10,12},{12,14},{9,11},... | collective-permute-start | bytes 6152 | tf_op jit(solution)/shard_map/ppermute | solution.py:26
  197.6 26.3 %all-to-all-start.4 = ((f32[256,2,128]{2,1,0:T(2,128)}), f32[256,2,128]{2,1,0:T(2,128)S(1)}, u32[]{:S(2)}, u32[]{:S(2)}) async-start(f32[256,2,128]{2,1,0:T(2,128)} %copy.351), calls=%async_computation.4 | async-start | bytes 524288 | tf_op jit(solution)/shard_map/all_to_all | solution.py:90
  208.9 14.5 %collective-permute-start.20 = (f32[16,1,128]{2,0,1:T(8,128)S(1)}, f32[16,1,128]{2,0,1:T(8,128)S(1)}, u32[]{:S(2)}, u32[]{:S(2)}) collective-permute-start(f32[16,1,128]{2,0,1:T(8,128)S(1)} %bitcast.140), channel_id=1, source_target_pairs={{8,0},{16,8},{24,16},{32,24},{40,32},{48,40},{56,48},{64,56},{72,6... | collective-permute-start | bytes 24584 | tf_op jit(solution)/shard_map/ppermute | solution.py:27
  213.4 9.9 %collective-permute-start.21 = (f32[16,1,128]{2,0,1:T(8,128)S(1)}, f32[16,1,128]{2,0,1:T(8,128)S(1)}, u32[]{:S(2)}, u32[]{:S(2)}) collective-permute-start(f32[16,1,128]{2,0,1:T(8,128)S(1)} %bitcast.139), channel_id=1, source_target_pairs={{0,8},{8,16},{16,24},{24,32},{32,40},{40,48},{48,56},{56,64},{64,7... | collective-permute-start | bytes 24584 | tf_op jit(solution)/shard_map/ppermute | solution.py:26
  215.3 8.6 %collective-permute-start.18 = (f32[1,32,128]{2,1,0:T(8,128)S(1)}, f32[1,32,128]{2,1,0:T(8,128)S(1)}, u32[]{:S(2)}, u32[]{:S(2)}) collective-permute-start(f32[1,32,128]{2,1,0:T(8,128)S(1)} %get-tuple-element.64), channel_id=1, source_target_pairs={{1,0},{3,2},{5,4},{7,6},{9,8},{11,10},{13,12},{15,14},{17,16},{19,... | collective-permute-start | bytes 49160 | tf_op jit(solution)/shard_map/ppermute | solution.py:27
  216.7 7.3 %collective-permute-start.19 = (f32[1,32,128]{2,1,0:T(8,128)S(1)}, f32[1,32,128]{2,1,0:T(8,128)S(1)}, u32[]{:S(2)}, u32[]{:S(2)}) collective-permute-start(f32[1,32,128]{2,1,0:T(8,128)S(1)} %get-tuple-element.63), channel_id=1, source_target_pairs={{0,1},{2,3},{4,5},{6,7},{8,9},{10,11},{12,13},{14,15},{16,17},{18,... | collective-permute-start | bytes 49160 | tf_op jit(solution)/shard_map/ppermute | solution.py:26
  228.0 4.1 %copy-start.3 = (f32[16,32,1]{2,1,0:T(8,128)S(1)}, f32[16,32,1]{2,1,0:T(8,128)}, u32[]{:S(2)}) copy-start(f32[16,32,1]{2,1,0:T(8,128)} %get-tuple-element.52) | copy-start | bytes 6148
  230.0 0.7 copy-start.11
  232.2 0.7 copy-start.7
  (1 other events, 0.7 us)

commit v2 on v1

--- a/solution.py
+++ b/solution.py
@@ -23,8 +23,12 @@
     face = first.shape
     if dim == cells.ndim - 1:
         first, last = (x.reshape(-1, 128) for x in (first, last))
-    from_low = lax.ppermute(last, axis, [(i, i + 1) for i in range(count - 1)])
-    from_high = lax.ppermute(first, axis, [(i + 1, i) for i in range(count - 1)])
+    if count == 2:
+        swapped = lax.ppermute(jnp.where(index == 0, last, first), axis, [(0, 1), (1, 0)])
+        from_low, from_high = swapped, swapped
+    else:
+        from_low = lax.ppermute(last, axis, [(i, i + 1) for i in range(count - 1)])
+        from_high = lax.ppermute(first, axis, [(i + 1, i) for i in range(count - 1)])
     first, last, from_low, from_high = (x.reshape(face) for x in (first, last, from_low, from_high))
     low = jnp.where(index == 0, first, from_low)
     high = jnp.where(index == count - 1, last, from_high)

time: 240 us -> 232 us (0.967); the launches traced: 235 us -> 230 us
  starting transfers between devices: 132 us -> 114 us
  waiting for transfers between devices: 15.1 us -> 25.8 us
    ppermute x12 -> x8, starting transfers between devices: 39.6 us -> 26 us  [neighbours(): from_low = lax.ppermute(last, axis, [(i, i + 1) for i in range(count - 1)])]
    all_to_all x4, waiting for transfers between devices: 1.5 us -> 13.1 us  [on_device(): lax.all_to_all(sent, ('gx', 'gy'), split_axis=0, concat_axis=0, tiled=True)]
    ppermute x12 -> x8, starting transfers between devices: 28.5 us -> 23.3 us  [neighbours(): lax.ppermute(first, axis, [(i + 1, i) for i in range(count - 1)])]
    ppermute x12 -> x8, waiting for transfers between devices: 13.6 us -> 12.7 us  [neighbours(): from_low = lax.ppermute(last, axis, [(i, i + 1) for i in range(count - 1)])]
    unnamed x40 -> x36, local copies, waits for them, and re-layouts: 5.95 us -> 5.44 us
  transfers between devices with their start and end apart: 29 -> 25, of which waited for: 3 -> 4; matrix products, arithmetic and copies ran while one was open for 16% -> 16% of each run, Pallas kernels for 0% -> 0%
where the time goes in v2:
time: 232 us; the launch traced here: 230 us
  starting transfers between devices  114 us (49%)
  other arithmetic  50.9 us (22%)
  local copies, waits for them, and re-layouts  37.3 us (16%)
  waiting for transfers between devices  25.8 us (11%)
    all_to_all x4, starting transfers between devices, on_device(): lax.all_to_all(sent, ('gx', 'gy'), split_axis=0, concat_axis=0, tiled=True)  50.5 us
    ppermute x8, starting transfers between devices, neighbours(): from_low = lax.ppermute(last, axis, [(i, i + 1) for i in range(count - 1)])  26 us
    ppermute x8, starting transfers between devices, neighbours(): lax.ppermute(first, axis, [(i + 1, i) for i in range(count - 1)])  23.3 us
    all_to_all x1, starting transfers between devices, on_device(): lax.all_to_all(slot_term, ('gx', 'gy'), split_axis=0, concat_axis=0, tile...  14 us
    all_to_all x4, waiting for transfers between devices, on_device(): lax.all_to_all(sent, ('gx', 'gy'), split_axis=0, concat_axis=0, tiled=True)  13.1 us
    ppermute x8, waiting for transfers between devices, neighbours(): from_low = lax.ppermute(last, axis, [(i, i + 1) for i in range(count - 1)])  12.7 us
    scatter-add x4, other arithmetic, on_device(): into_term = jax.ops.segment_sum(-current, safe_ids, num_segments=term_count)  7.79 us
    scatter-add x4, other arithmetic, on_device(): jax.ops.segment_sum(tile_current, junction_block, num_segments=depth * ro...  7.31 us
  transfers between devices with their start and end apart: 25, of which 4 were waited for; matrix products, arithmetic and copies ran while one was open for 16% of the time, Pallas kernels for 0%

profile of v2, /device:TPU:128, one launch (start us, length us, event | category | flops | bytes accessed | tf_op | source)
XLA Modules:
  0.0 229.7 jit_solution(5218942464746347308)
XLA Ops:
  3.7 14.0 %all-to-all-start = ((s32[128,2,1]{1,2,0:T(1,128)}), s32[128,2,1]{1,2,0:T(1,128)S(1)}, u32[]{:S(2)}, u32[]{:S(2)}) async-start(s32[128,2,1]{1,2,0:T(1,128)} %bitcast.33), calls=%async_computation | async-start | bytes 131072 | tf_op jit(solution)/shard_map/all_to_all | solution.py:79
  18.8 1.3 collective-permute-start.3
  20.2 4.5 %collective-permute-start.4 = (f32[4,128]{1,0:T(4,128)S(1)}, f32[4,128]{1,0:T(4,128)S(1)}, u32[]{:S(2)}, u32[]{:S(2)}) collective-permute-start(f32[4,128]{1,0:T(4,128)S(1)} %reshape.261), channel_id=1, source_target_pairs={{0,2},{2,4},{4,6},{1,3},{3,5},{5,7},{8,10},{10,12},{12,14},{9,11},... | collective-permute-start | bytes 6152 | tf_op jit(solution)/shard_map/ppermute | solution.py:30
  24.8 4.6 %collective-permute-start.1 = (f32[16,1,128]{2,0,1:T(8,128)S(1)}, f32[16,1,128]{2,0,1:T(8,128)S(1)}, u32[]{:S(2)}, u32[]{:S(2)}) collective-permute-start(f32[16,1,128]{2,0,1:T(8,128)S(1)} %bitcast.138), channel_id=1, source_target_pairs={{8,0},{16,8},{24,16},{32,24},{40,32},{48,40},{56,48},{64,56},{72,6... | collective-permute-start | bytes 24584 | tf_op jit(solution)/shard_map/ppermute | solution.py:31
  29.4 1.9 collective-permute-start.2
  36.3 5.3 %select_select_fusion = (f32[16,32,128]{2,1,0:T(8,128)S(1)}, pred[16,32,128]{2,1,0:T(8,128)(4,1)S(1)}, pred[16,32,128]{2,1,0:T(8,128)(4,1)S(1)}, pred[16,32,128]...) fusion(f32[]{:T(128)} %bitcast.23, f32[]{:T(128)} %bitcast.22, ...), kind=kLoop, calls=%fused_computation.84 | loop fusion | flops 1048576 | bytes 1048608 | tf_op jit(solution)/shard_map/jit(_where)/select_n | solution.py:66
  41.6 5.3 %select_select_fusion.1 = f32[16,32,128]{2,1,0:T(8,128)S(1)} fusion(pred[16,32,128]{2,1,0:T(8,128)(4,1)S(1)} %get-tuple-element.50, pred[16,32,128]{2,1,0:T(8,128)(4,1)S(1)} %get-tuple-element.49, pred[16,32,128]{2,1,0:T(8,128)(4,1)S(1)} %get-tuple-element.48, pred[16,32,128]{2,1,0:T(8,128)(4,1)S(1)} %get-tuple-element.47, ...), kind=kLoop, calls=%fused_computation.85 | loop fusion | flops 524288 | bytes 786464 | tf_op jit(solution)/shard_map/jit(_where)/select_n | solution.py:65
  46.9 5.2 %select_select_fusion.2 = f32[16,32,128]{2,1,0:T(8,128)S(1)} fusion(pred[16,32,128]{2,1,0:T(8,128)(4,1)S(1)} %get-tuple-element.50, pred[16,32,128]{2,1,0:T(8,128)(4,1)S(1)} %get-tuple-element.49, pred[16,32,128]{2,1,0:T(8,128)(4,1)S(1)} %get-tuple-element.48, pred[16,32,128]{2,1,0:T(8,128)(4,1)S(1)} %get-tuple-element.47, ...), kind=kLoop, calls=%fused_computation.86 | loop fusion | flops 524288 | bytes 786464 | tf_op jit(solution)/shard_map/jit(_where)/select_n | solution.py:64
  55.4 1.1 copy.324
  56.5 15.0 %all-to-all-start.1 = ((f32[256,3,128]{2,1,0:T(4,128)}), f32[256,3,128]{2,1,0:T(4,128)S(1)}, u32[]{:S(2)}, u32[]{:S(2)}) async-start(f32[256,3,128]{2,1,0:T(4,128)} %copy.324), calls=%async_computation.1 | async-start | bytes 1048576 | tf_op jit(solution)/shard_map/all_to_all | solution.py:94
  72.9 13.0 %all-to-all-done.1 = f32[256,3,128]{2,1,0:T(4,128)S(1)} async-done(((f32[256,3,128]{2,1,0:T(4,128)}), f32[256,3,128]{2,1,0:T(4,128)S(1)}, u32[]{:S(2)}, u32[]{:S(2)}) %all-to-all-start.1) | async-done | bytes 393248 | tf_op jit(solution)/shard_map/all_to_all | solution.py:94
  86.0 1.7 scatter_custom_fusion.1
  90.2 1.8 scatter_custom_fusion
  92.0 1.7 fusion.5
  96.0 1.3 collective-permute-start.8
  97.4 4.5 %collective-permute-start.9 = (f32[4,128]{1,0:T(4,128)S(1)}, f32[4,128]{1,0:T(4,128)S(1)}, u32[]{:S(2)}, u32[]{:S(2)}) collective-permute-start(f32[4,128]{1,0:T(4,128)S(1)} %reshape.267), channel_id=1, source_target_pairs={{0,2},{2,4},{4,6},{1,3},{3,5},{5,7},{8,10},{10,12},{12,14},{9,11},... | collective-permute-start | bytes 6152 | tf_op jit(solution)/shard_map/ppermute | solution.py:30
  102.9 11.9 %all-to-all-start.2 = ((f32[256,2,128]{2,1,0:T(2,128)}), f32[256,2,128]{2,1,0:T(2,128)S(1)}, u32[]{:S(2)}, u32[]{:S(2)}) async-start(f32[256,2,128]{2,1,0:T(2,128)} %copy.333), calls=%async_computation.2 | async-start | bytes 524288 | tf_op jit(solution)/shard_map/all_to_all | solution.py:94
  114.8 4.6 %collective-permute-start.6 = (f32[16,1,128]{2,0,1:T(8,128)S(1)}, f32[16,1,128]{2,0,1:T(8,128)S(1)}, u32[]{:S(2)}, u32[]{:S(2)}) collective-permute-start(f32[16,1,128]{2,0,1:T(8,128)S(1)} %bitcast.142), channel_id=1, source_target_pairs={{8,0},{16,8},{24,16},{32,24},{40,32},{48,40},{56,48},{64,56},{72,6... | collective-permute-start | bytes 24584 | tf_op jit(solution)/shard_map/ppermute | solution.py:31
  119.4 1.9 collective-permute-start.7
  121.4 0.9 reshape.485
  122.3 0.9 reshape.486
  123.2 1.8 slice_select_fusion.4
  125.1 3.2 %collective-permute-done.7 = f32[16,1,128]{2,0,1:T(8,128)S(1)} collective-permute-done((f32[16,1,128]{2,0,1:T(8,128)S(1)}, f32[16,1,128]{2,0,1:T(8,128)S(1)}, u32[]{:S(2)}, u32[]{:S(2)}) %collective-permute-start.7) | collective-permute-done | bytes 8224 | tf_op jit(solution)/shard_map/ppermute | solution.py:30
  128.4 1.8 scatter_custom_fusion.3
  132.0 1.8 scatter_custom_fusion.2
  133.7 1.8 fusion.14
  138.6 1.3 collective-permute-start.13
  139.9 4.5 %collective-permute-start.14 = (f32[4,128]{1,0:T(4,128)S(1)}, f32[4,128]{1,0:T(4,128)S(1)}, u32[]{:S(2)}, u32[]{:S(2)}) collective-permute-start(f32[4,128]{1,0:T(4,128)S(1)} %reshape.273), channel_id=1, source_target_pairs={{0,2},{2,4},{4,6},{1,3},{3,5},{5,7},{8,10},{10,12},{12,14},{9,11},... | collective-permute-start | bytes 6152 | tf_op jit(solution)/shard_map/ppermute | solution.py:30
  145.4 11.9 %all-to-all-start.3 = ((f32[256,2,128]{2,1,0:T(2,128)}), f32[256,2,128]{2,1,0:T(2,128)S(1)}, u32[]{:S(2)}, u32[]{:S(2)}) async-start(f32[256,2,128]{2,1,0:T(2,128)} %copy.342), calls=%async_computation.3 | async-start | bytes 524288 | tf_op jit(solution)/shard_map/all_to_all | solution.py:94
  157.4 4.6 %collective-permute-start.11 = (f32[16,1,128]{2,0,1:T(8,128)S(1)}, f32[16,1,128]{2,0,1:T(8,128)S(1)}, u32[]{:S(2)}, u32[]{:S(2)}) collective-permute-start(f32[16,1,128]{2,0,1:T(8,128)S(1)} %bitcast.141), channel_id=1, source_target_pairs={{8,0},{16,8},{24,16},{32,24},{40,32},{48,40},{56,48},{64,56},{72,6... | collective-permute-start | bytes 24584 | tf_op jit(solution)/shard_map/ppermute | solution.py:31
  162.0 2.1 collective-permute-start.12
  165.4 5.4 %collective-permute-done.12 = f32[16,1,128]{2,0,1:T(8,128)S(1)} collective-permute-done((f32[16,1,128]{2,0,1:T(8,128)S(1)}, f32[16,1,128]{2,0,1:T(8,128)S(1)}, u32[]{:S(2)}, u32[]{:S(2)}) %collective-permute-start.12) | collective-permute-done | bytes 8224 | tf_op jit(solution)/shard_map/ppermute | solution.py:30
  171.0 1.8 scatter_custom_fusion.5
  176.5 1.8 scatter_custom_fusion.4
  178.3 2.6 %multiply_add_fusion = (f32[16,32,128]{2,1,0:T(8,128)}, f32[16,32,128]{2,1,0:T(8,128)S(1)}, f32[16,32,128]{2,1,0:T(8,128)S(1)}) fusion(f32[16,32,128]{2,1,0:T(8,128)S(1)} %fusion.14, f32[16,32,128]{2,1,0:T(8,128)S(1)} %bitcast.117, f32[16,32,128]{2,1,0:T(8,128)S(1)} %get-tuple-element.9, f32[16,32,127]{2,1,0:T(8,128)} %get-tuple-element.80, ...), kind=kLoop, calls=%fused_computation.80 | loop fusion | flops 3735552 | bytes 4456448 | tf_op jit(solution)/shard_map/add | solution.py:13
  183.8 1.3 collective-permute-start.18
  185.2 4.5 %collective-permute-start.19 = (f32[4,128]{1,0:T(4,128)S(1)}, f32[4,128]{1,0:T(4,128)S(1)}, u32[]{:S(2)}, u32[]{:S(2)}) collective-permute-start(f32[4,128]{1,0:T(4,128)S(1)} %reshape.279), channel_id=1, source_target_pairs={{0,2},{2,4},{4,6},{1,3},{3,5},{5,7},{8,10},{10,12},{12,14},{9,11},... | collective-permute-start | bytes 6152 | tf_op jit(solution)/shard_map/ppermute | solution.py:30
  190.7 11.8 %all-to-all-start.4 = ((f32[256,2,128]{2,1,0:T(2,128)}), f32[256,2,128]{2,1,0:T(2,128)}, u32[]{:S(2)}, u32[]{:S(2)}) async-start(f32[256,2,128]{2,1,0:T(2,128)} %copy.351), calls=%async_computation.4 | async-start | bytes 524288 | tf_op jit(solution)/shard_map/all_to_all | solution.py:94
  202.5 4.6 %collective-permute-start.16 = (f32[16,1,128]{2,0,1:T(8,128)}, f32[16,1,128]{2,0,1:T(8,128)S(1)}, u32[]{:S(2)}, u32[]{:S(2)}) collective-permute-start(f32[16,1,128]{2,0,1:T(8,128)} %bitcast.62), channel_id=1, source_target_pairs={{8,0},{16,8},{24,16},{32,24},{40,32},{48,40},{56,48},{64,56},{72,6... | collective-permute-start | bytes 24584 | tf_op jit(solution)/shard_map/ppermute | solution.py:31
  207.0 1.9 collective-permute-start.17
  210.9 1.1 slice_select_fusion
  212.0 4.1 %collective-permute-done.17 = f32[16,1,128]{2,0,1:T(8,128)S(1)} collective-permute-done((f32[16,1,128]{2,0,1:T(8,128)}, f32[16,1,128]{2,0,1:T(8,128)S(1)}, u32[]{:S(2)}, u32[]{:S(2)}) %collective-permute-start.17) | collective-permute-done | bytes 8224 | tf_op jit(solution)/shard_map/ppermute | solution.py:30
  216.7 1.0 slice.480
  217.8 2.4 %scatter_custom_fusion.7 = f32[32,128]{1,0:T(8,128)} fusion(s32[256]{0:T(256)} %bitcast.149, f32[256,128]{1,0:T(8,128)S(1)} %gather_fusion.10, f32[256,128]{1,0:T(8,128)S(1)} %bitcast.121, f32[256]{0:T(256)S(1)} %compare_select_fusion.5, f32[]{:T(128)} %constant.38.clone.1), kind=kCustom, calls=%fused_computation.107 | custom fusion | flops 131072 | bytes 280064 | tf_op jit(solution)/shard_map/scatter-add | solution.py:96
  220.2 1.8 gather_fusion.11
  222.7 1.9 scatter_custom_fusion.6
  225.3 1.5 fusion.78
  227.5 2.2 fusion.32
  (169 shorter events, 39.2 us)
Async XLA Ops:
  0.6 0.7 copy-start.15
  0.6 17.8 %copy-start = (f32[16,32,128]{2,1,0:T(8,128)S(1)}, f32[16,32,128]{2,1,0:T(8,128)}, u32[]{:S(2)}) copy-start(f32[16,32,128]{2,1,0:T(8,128)} %param.11) | copy-start | bytes 786436
  3.7 48.4 %all-to-all-start = ((s32[128,2,1]{1,2,0:T(1,128)}), s32[128,2,1]{1,2,0:T(1,128)S(1)}, u32[]{:S(2)}, u32[]{:S(2)}) async-start(s32[128,2,1]{1,2,0:T(1,128)} %bitcast.33), calls=%async_computation | async-start | bytes 131072 | tf_op jit(solution)/shard_map/all_to_all | solution.py:79
  18.4 54.4 %collective-permute-start = (f32[1,32,128]{2,1,0:T(8,128)S(1)}, f32[1,32,128]{2,1,0:T(8,128)S(1)}, u32[]{:S(2)}, u32[]{:S(2)}) collective-permute-start(f32[1,32,128]{2,1,0:T(8,128)S(1)} %slice_select_fusion.18), channel_id=1, source_target_pairs={{0,1},{1,0},{2,3},{3,2},{4,5},{5,4},{6,7},{7,6},{8,9},{9,8},{10,11... | collective-permute-start | bytes 49160 | tf_op jit(solution)/shard_map/ppermute | solution.py:27
  18.8 52.6 %collective-permute-start.3 = (f32[4,128]{1,0:T(4,128)S(1)}, f32[4,128]{1,0:T(4,128)S(1)}, u32[]{:S(2)}, u32[]{:S(2)}) collective-permute-start(f32[4,128]{1,0:T(4,128)S(1)} %reshape.259), channel_id=1, source_target_pairs={{2,0},{4,2},{6,4},{3,1},{5,3},{7,5},{10,8},{12,10},{14,12},{11,9},... | collective-permute-start | bytes 6152 | tf_op jit(solution)/shard_map/ppermute | solution.py:31
  20.2 51.5 %collective-permute-start.4 = (f32[4,128]{1,0:T(4,128)S(1)}, f32[4,128]{1,0:T(4,128)S(1)}, u32[]{:S(2)}, u32[]{:S(2)}) collective-permute-start(f32[4,128]{1,0:T(4,128)S(1)} %reshape.261), channel_id=1, source_target_pairs={{0,2},{2,4},{4,6},{1,3},{3,5},{5,7},{8,10},{10,12},{12,14},{9,11},... | collective-permute-start | bytes 6152 | tf_op jit(solution)/shard_map/ppermute | solution.py:30
  24.8 6.5 %copy-start.5 = (f32[3,8]{1,0:T(4,128)S(1)}, f32[3,8]{1,0:T(4,128)}, u32[]{:S(2)}) copy-start(f32[3,8]{1,0:T(4,128)} %param.14) | copy-start | bytes 292
  24.8 48.0 %collective-permute-start.1 = (f32[16,1,128]{2,0,1:T(8,128)S(1)}, f32[16,1,128]{2,0,1:T(8,128)S(1)}, u32[]{:S(2)}, u32[]{:S(2)}) collective-permute-start(f32[16,1,128]{2,0,1:T(8,128)S(1)} %bitcast.138), channel_id=1, source_target_pairs={{8,0},{16,8},{24,16},{32,24},{40,32},{48,40},{56,48},{64,56},{72,6... | collective-permute-start | bytes 24584 | tf_op jit(solution)/shard_map/ppermute | solution.py:31
  29.4 43.5 %collective-permute-start.2 = (f32[16,1,128]{2,0,1:T(8,128)S(1)}, f32[16,1,128]{2,0,1:T(8,128)S(1)}, u32[]{:S(2)}, u32[]{:S(2)}) collective-permute-start(f32[16,1,128]{2,0,1:T(8,128)S(1)} %bitcast.137), channel_id=1, source_target_pairs={{0,8},{8,16},{16,24},{24,32},{32,40},{40,48},{48,56},{56,64},{64,7... | collective-permute-start | bytes 24584 | tf_op jit(solution)/shard_map/ppermute | solution.py:30
  32.8 63.0 %copy-start.11 = (pred[256]{0:T(512)(128)(4,1)}, pred[256]{0:T(512)(128)(4,1)S(1)}, u32[]{:S(2)}) copy-start(pred[256]{0:T(512)(128)(4,1)S(1)} %fusion.52) | copy-start | bytes 772
  32.8 0.7 copy-start.17
  33.7 0.9 copy-start.1
  35.4 1.0 copy-start.3
  52.1 79.0 %copy-start.7 = (s32[1024]{0:T(1024)}, s32[1024]{0:T(1024)S(1)}, u32[]{:S(2)}) copy-start(s32[1024]{0:T(1024)S(1)} %pad_clamp_fusion.1) | copy-start | bytes 12292
  52.3 0.7 copy-start.16
  54.5 31.5 %copy-start.14 = (s32[256,1]{0,1:T(1,128)}, s32[256,1]{0,1:T(1,128)S(1)}, u32[]{:S(2)}) copy-start(s32[256,1]{0,1:T(1,128)S(1)} %get-tuple-element.141) | copy-start | bytes 3076
  56.5 29.4 %all-to-all-start.1 = ((f32[256,3,128]{2,1,0:T(4,128)}), f32[256,3,128]{2,1,0:T(4,128)S(1)}, u32[]{:S(2)}, u32[]{:S(2)}) async-start(f32[256,3,128]{2,1,0:T(4,128)} %copy.324), calls=%async_computation.1 | async-start | bytes 1048576 | tf_op jit(solution)/shard_map/all_to_all | solution.py:94
  86.0 1.7 copy-start.4
  87.7 0.7 copy-start.8
  90.2 1.8 copy-start.2
  96.0 25.4 %collective-permute-start.8 = (f32[4,128]{1,0:T(4,128)S(1)}, f32[4,128]{1,0:T(4,128)S(1)}, u32[]{:S(2)}, u32[]{:S(2)}) collective-permute-start(f32[4,128]{1,0:T(4,128)S(1)} %reshape.265), channel_id=1, source_target_pairs={{2,0},{4,2},{6,4},{3,1},{5,3},{7,5},{10,8},{12,10},{14,12},{11,9},... | collective-permute-start | bytes 6152 | tf_op jit(solution)/shard_map/ppermute | solution.py:31
  97.4 24.9 %collective-permute-start.9 = (f32[4,128]{1,0:T(4,128)S(1)}, f32[4,128]{1,0:T(4,128)S(1)}, u32[]{:S(2)}, u32[]{:S(2)}) collective-permute-start(f32[4,128]{1,0:T(4,128)S(1)} %reshape.267), channel_id=1, source_target_pairs={{0,2},{2,4},{4,6},{1,3},{3,5},{5,7},{8,10},{10,12},{12,14},{9,11},... | collective-permute-start | bytes 6152 | tf_op jit(solution)/shard_map/ppermute | solution.py:30
  102.9 25.4 %all-to-all-start.2 = ((f32[256,2,128]{2,1,0:T(2,128)}), f32[256,2,128]{2,1,0:T(2,128)S(1)}, u32[]{:S(2)}, u32[]{:S(2)}) async-start(f32[256,2,128]{2,1,0:T(2,128)} %copy.333), calls=%async_computation.2 | async-start | bytes 524288 | tf_op jit(solution)/shard_map/all_to_all | solution.py:94
  114.8 10.3 %collective-permute-start.6 = (f32[16,1,128]{2,0,1:T(8,128)S(1)}, f32[16,1,128]{2,0,1:T(8,128)S(1)}, u32[]{:S(2)}, u32[]{:S(2)}) collective-permute-start(f32[16,1,128]{2,0,1:T(8,128)S(1)} %bitcast.142), channel_id=1, source_target_pairs={{8,0},{16,8},{24,16},{32,24},{40,32},{48,40},{56,48},{64,56},{72,6... | collective-permute-start | bytes 24584 | tf_op jit(solution)/shard_map/ppermute | solution.py:31
  119.4 8.9 %collective-permute-start.7 = (f32[16,1,128]{2,0,1:T(8,128)S(1)}, f32[16,1,128]{2,0,1:T(8,128)S(1)}, u32[]{:S(2)}, u32[]{:S(2)}) collective-permute-start(f32[16,1,128]{2,0,1:T(8,128)S(1)} %bitcast.140), channel_id=1, source_target_pairs={{0,8},{8,16},{16,24},{24,32},{32,40},{40,48},{48,56},{56,64},{64,7... | collective-permute-start | bytes 24584 | tf_op jit(solution)/shard_map/ppermute | solution.py:30
  121.3 7.0 %collective-permute-start.5 = (f32[1,32,128]{2,1,0:T(8,128)S(1)}, f32[1,32,128]{2,1,0:T(8,128)S(1)}, u32[]{:S(2)}, u32[]{:S(2)}) collective-permute-start(f32[1,32,128]{2,1,0:T(8,128)S(1)} %slice_select_fusion.15), channel_id=1, source_target_pairs={{0,1},{1,0},{2,3},{3,2},{4,5},{5,4},{6,7},{7,6},{8,9},{9,8},{10,11... | collective-permute-start | bytes 49160 | tf_op jit(solution)/shard_map/ppermute | solution.py:27
  137.6 0.7 copy-start.12
  138.6 25.5 %collective-permute-start.13 = (f32[4,128]{1,0:T(4,128)S(1)}, f32[4,128]{1,0:T(4,128)S(1)}, u32[]{:S(2)}, u32[]{:S(2)}) collective-permute-start(f32[4,128]{1,0:T(4,128)S(1)} %reshape.271), channel_id=1, source_target_pairs={{2,0},{4,2},{6,4},{3,1},{5,3},{7,5},{10,8},{12,10},{14,12},{11,9},... | collective-permute-start | bytes 6152 | tf_op jit(solution)/shard_map/ppermute | solution.py:31
  139.9 24.4 %collective-permute-start.14 = (f32[4,128]{1,0:T(4,128)S(1)}, f32[4,128]{1,0:T(4,128)S(1)}, u32[]{:S(2)}, u32[]{:S(2)}) collective-permute-start(f32[4,128]{1,0:T(4,128)S(1)} %reshape.273), channel_id=1, source_target_pairs={{0,2},{2,4},{4,6},{1,3},{3,5},{5,7},{8,10},{10,12},{12,14},{9,11},... | collective-permute-start | bytes 6152 | tf_op jit(solution)/shard_map/ppermute | solution.py:30
  145.4 25.5 %all-to-all-start.3 = ((f32[256,2,128]{2,1,0:T(2,128)}), f32[256,2,128]{2,1,0:T(2,128)S(1)}, u32[]{:S(2)}, u32[]{:S(2)}) async-start(f32[256,2,128]{2,1,0:T(2,128)} %copy.342), calls=%async_computation.3 | async-start | bytes 524288 | tf_op jit(solution)/shard_map/all_to_all | solution.py:94
  157.3 13.6 %collective-permute-start.10 = (f32[1,32,128]{2,1,0:T(8,128)S(1)}, f32[1,32,128]{2,1,0:T(8,128)S(1)}, u32[]{:S(2)}, u32[]{:S(2)}) collective-permute-start(f32[1,32,128]{2,1,0:T(8,128)S(1)} %slice_select_fusion.12), channel_id=1, source_target_pairs={{0,1},{1,0},{2,3},{3,2},{4,5},{5,4},{6,7},{7,6},{8,9},{9,8},{10,11... | collective-permute-start | bytes 49160 | tf_op jit(solution)/shard_map/ppermute | solution.py:27
  157.4 8.0 %collective-permute-start.11 = (f32[16,1,128]{2,0,1:T(8,128)S(1)}, f32[16,1,128]{2,0,1:T(8,128)S(1)}, u32[]{:S(2)}, u32[]{:S(2)}) collective-permute-start(f32[16,1,128]{2,0,1:T(8,128)S(1)} %bitcast.141), channel_id=1, source_target_pairs={{8,0},{16,8},{24,16},{32,24},{40,32},{48,40},{56,48},{64,56},{72,6... | collective-permute-start | bytes 24584 | tf_op jit(solution)/shard_map/ppermute | solution.py:31
  162.0 8.9 %collective-permute-start.12 = (f32[16,1,128]{2,0,1:T(8,128)S(1)}, f32[16,1,128]{2,0,1:T(8,128)S(1)}, u32[]{:S(2)}, u32[]{:S(2)}) collective-permute-start(f32[16,1,128]{2,0,1:T(8,128)S(1)} %bitcast.139), channel_id=1, source_target_pairs={{0,8},{8,16},{16,24},{24,32},{32,40},{40,48},{48,56},{56,64},{64,7... | collective-permute-start | bytes 24584 | tf_op jit(solution)/shard_map/ppermute | solution.py:30
  172.8 0.7 copy-start.9
  182.9 0.7 copy-start.13
  183.8 25.2 %collective-permute-start.18 = (f32[4,128]{1,0:T(4,128)S(1)}, f32[4,128]{1,0:T(4,128)S(1)}, u32[]{:S(2)}, u32[]{:S(2)}) collective-permute-start(f32[4,128]{1,0:T(4,128)S(1)} %reshape.277), channel_id=1, source_target_pairs={{2,0},{4,2},{6,4},{3,1},{5,3},{7,5},{10,8},{12,10},{14,12},{11,9},... | collective-permute-start | bytes 6152 | tf_op jit(solution)/shard_map/ppermute | solution.py:31
  185.2 24.8 %collective-permute-start.19 = (f32[4,128]{1,0:T(4,128)S(1)}, f32[4,128]{1,0:T(4,128)S(1)}, u32[]{:S(2)}, u32[]{:S(2)}) collective-permute-start(f32[4,128]{1,0:T(4,128)S(1)} %reshape.279), channel_id=1, source_target_pairs={{0,2},{2,4},{4,6},{1,3},{3,5},{5,7},{8,10},{10,12},{12,14},{9,11},... | collective-permute-start | bytes 6152 | tf_op jit(solution)/shard_map/ppermute | solution.py:30
  190.7 26.0 %all-to-all-start.4 = ((f32[256,2,128]{2,1,0:T(2,128)}), f32[256,2,128]{2,1,0:T(2,128)}, u32[]{:S(2)}, u32[]{:S(2)}) async-start(f32[256,2,128]{2,1,0:T(2,128)} %copy.351), calls=%async_computation.4 | async-start | bytes 524288 | tf_op jit(solution)/shard_map/all_to_all | solution.py:94
  202.5 9.5 %collective-permute-start.16 = (f32[16,1,128]{2,0,1:T(8,128)}, f32[16,1,128]{2,0,1:T(8,128)S(1)}, u32[]{:S(2)}, u32[]{:S(2)}) collective-permute-start(f32[16,1,128]{2,0,1:T(8,128)} %bitcast.62), channel_id=1, source_target_pairs={{8,0},{16,8},{24,16},{32,24},{40,32},{48,40},{56,48},{64,56},{72,6... | collective-permute-start | bytes 24584 | tf_op jit(solution)/shard_map/ppermute | solution.py:31
  207.0 9.1 %collective-permute-start.17 = (f32[16,1,128]{2,0,1:T(8,128)}, f32[16,1,128]{2,0,1:T(8,128)S(1)}, u32[]{:S(2)}, u32[]{:S(2)}) collective-permute-start(f32[16,1,128]{2,0,1:T(8,128)} %bitcast.64), channel_id=1, source_target_pairs={{0,8},{8,16},{16,24},{24,32},{32,40},{40,48},{48,56},{56,64},{64,7... | collective-permute-start | bytes 24584 | tf_op jit(solution)/shard_map/ppermute | solution.py:30
  208.9 7.8 %collective-permute-start.15 = (f32[1,32,128]{2,1,0:T(8,128)S(1)}, f32[1,32,128]{2,1,0:T(8,128)S(1)}, u32[]{:S(2)}, u32[]{:S(2)}) collective-permute-start(f32[1,32,128]{2,1,0:T(8,128)S(1)} %slice_select_fusion.9), channel_id=1, source_target_pairs={{0,1},{1,0},{2,3},{3,2},{4,5},{5,4},{6,7},{7,6},{8,9},{9,8},{10,11... | collective-permute-start | bytes 49160 | tf_op jit(solution)/shard_map/ppermute | solution.py:27
  224.7 0.7 copy-start.10
  226.8 0.7 copy-start.6

commit v3 on v0

v3 whole, which is shorter than its diff:
```python
import jax
import jax.numpy as jnp
from jax import lax
from jax.experimental import pallas as pl
from jax.experimental.pallas import tpu as pltpu
from jax.sharding import PartitionSpec as P

NCLASS = 8
STEPS = 4
INTERPRET = False


def cell_kinetics(v, w, drive):
    react = -8.0 * v * (v - 0.15) * (v - 1.0) - v * w
    new_v = 0.1 * (react + drive)
    new_w = w + 0.01 * (-w - 8.0 * v * (v - 1.15))
    return (new_v, new_w)


def shifted(cells, axis):
    size = cells.shape[axis]
    a = pltpu.roll(cells, 1, axis)
    b = pltpu.roll(cells, size - 1, axis)
    pos = lax.broadcasted_iota(jnp.int32, cells.shape, axis)
    moved = pltpu.roll(pos, 1, axis)
    forward = moved == jnp.where(pos == 0, size - 1, pos - 1)
    return jnp.where(forward, a, b), jnp.where(forward, b, a)


def flag(ref, i, shape):
    return jnp.full(shape, ref[i], jnp.int32) > 0


def step_kernel(
    blk_ref, slot_ref, ids_ref, sblk_ref, edge_ref,
    v_ref, w_ref, cz_ref, cx_ref, cy_ref, recv_ref, tg_ref, g_ref,
    tv_ref, tr_ref, cg_ref, zr_ref, xlo_ref, xhi_ref, ylo_ref, yhi_ref,
    nv_ref, nw_ref, ntv_ref, ntr_ref, snd_ref, zs_ref, xf_ref, xl_ref, yf_ref, yl_ref,
    iv_ref, it_ref,
):
    depth, rows_x, width = v_ref.shape
    jcount = blk_ref.shape[0]
    slots = ids_ref.shape[0]
    iv_ref[...] = jnp.zeros(iv_ref.shape, jnp.float32)
    it_ref[...] = jnp.zeros(it_ref.shape, jnp.float32)

    def tile_body(j, carry):
        b = blk_ref[j]
        s = slot_ref[j]
        z = b // rows_x
        x = b % rows_x
        row = v_ref[z, pl.ds(x, 1), :]
        far = recv_ref[pl.ds(s, 1), :][:, width:2 * width]
        cur = tg_ref[pl.ds(j, 1), :] * (far - row)
        iv_ref[z, pl.ds(x, 1), :] = iv_ref[z, pl.ds(x, 1), :] + cur
        return carry

    lax.fori_loop(0, jcount, tile_body, 0)

    def owner_body(k, carry):
        t = ids_ref[k]
        cur = g_ref[pl.ds(k, 1), :] * (tv_ref[pl.ds(t, 1), :] - recv_ref[pl.ds(k, 1), :][:, 0:width])
        it_ref[pl.ds(t, 1), :] = it_ref[pl.ds(t, 1), :] + (-cur)
        return carry

    lax.fori_loop(0, slots, owner_body, 0)

    u = tv_ref[...]
    r = tr_ref[...]
    u_minus, u_plus = shifted(u, 1)
    lane_t = lax.broadcasted_iota(jnp.int32, u.shape, 1)
    u_minus = jnp.where(lane_t == 0, u, u_minus)
    u_plus = jnp.where(lane_t == width - 1, u, u_plus)
    lap_k = u_plus + u_minus - 2.0 * u
    react_u, new_r = cell_kinetics(u, r, 0.1 * it_ref[...])
    ntv_ref[...] = u + cg_ref[...] * lap_k + react_u
    ntr_ref[...] = new_r

    plane = (rows_x, width)
    sub = lax.broadcasted_iota(jnp.int32, plane, 0)
    lane = lax.broadcasted_iota(jnp.int32, plane, 1)
    z_low = flag(edge_ref, 0, plane)
    z_high = flag(edge_ref, 1, plane)
    x_low = flag(edge_ref, 2, (1, width))
    x_high = flag(edge_ref, 3, (1, width))
    y_low = flag(edge_ref, 4, (rows_x, 1))
    y_high = flag(edge_ref, 5, (rows_x, 1))
    per_row = width // rows_x
    y_first = [jnp.zeros((1, width), jnp.float32) for _ in range(yf_ref.shape[0])]
    y_last = [jnp.zeros((1, width), jnp.float32) for _ in range(yf_ref.shape[0])]
    for z in range(depth):
        vz = v_ref[z]
        if z == 0:
            zm = jnp.where(z_low, vz, zr_ref[...])
        else:
            zm = v_ref[z - 1]
        if z == depth - 1:
            zp = jnp.where(z_high, vz, zr_ref[...])
        else:
            zp = v_ref[z + 1]
        xm, xp = shifted(vz, 0)
        x_lo_row = jnp.where(x_low, vz[0:1, :], xlo_ref[z:z + 1, :])
        x_hi_row = jnp.where(x_high, vz[rows_x - 1:rows_x, :], xhi_ref[z:z + 1, :])
        xm = jnp.where(sub == 0, x_lo_row, xm)
        xp = jnp.where(sub == rows_x - 1, x_hi_row, xp)
        ym, yp = shifted(vz, 1)
        row_at, lane_at = z // per_row, (z % per_row) * rows_x
        pick = lane == sub + lane_at
        y_lo_col = jnp.sum(jnp.where(pick, ylo_ref[row_at:row_at + 1, :], 0.0), axis=1, keepdims=True)
        y_hi_col = jnp.sum(jnp.where(pick, yhi_ref[row_at:row_at + 1, :], 0.0), axis=1, keepdims=True)
        y_lo_col = jnp.where(y_low, vz[:, 0:1], y_lo_col)
        y_hi_col = jnp.where(y_high, vz[:, width - 1:width], y_hi_col)
        ym = jnp.where(lane == 0, y_lo_col, ym)
        yp = jnp.where(lane == width - 1, y_hi_col, yp)
        lap_z = zp + zm - 2.0 * vz
        lap_x = xp + xm - 2.0 * vz
        lap_y = yp + ym - 2.0 * vz
        react_v, new_w = cell_kinetics(vz, w_ref[z], iv_ref[z])
        nv = vz + (cz_ref[z] * lap_z + cx_ref[z] * lap_x + cy_ref[z] * lap_y) + react_v
        nv_ref[z] = nv
        nw_ref[z] = new_w
        xf_ref[z:z + 1, :] = nv[0:1, :]
        xl_ref[z:z + 1, :] = nv[rows_x - 1:rows_x, :]
        y_first[row_at] = y_first[row_at] + jnp.sum(
            jnp.where(pick, nv[:, 0:1], 0.0), axis=0, keepdims=True)
        y_last[row_at] = y_last[row_at] + jnp.sum(
            jnp.where(pick, nv[:, width - 1:width], 0.0), axis=0, keepdims=True)
    for i in range(yf_ref.shape[0]):
        yf_ref[i:i + 1, :] = y_first[i]
        yl_ref[i:i + 1, :] = y_last[i]
    zs_ref[...] = jnp.where(z_low, nv_ref[depth - 1], nv_ref[0])

    def pack_body(k, carry):
        b = sblk_ref[k]
        t = ids_ref[k]
        snd_ref[pl.ds(k, 1), :] = jnp.concatenate(
            [nv_ref[b // rows_x, pl.ds(b % rows_x, 1), :], ntv_ref[pl.ds(t, 1), :]], axis=1)
        return carry

    lax.fori_loop(0, slots, pack_body, 0)


def run_step(tables, state, recv, tile_gain, gains_rows, cable_rows, halos):
    volt, recovery, coef_z, coef_x, coef_y, term_volt, term_recovery = state
    depth, rows_x, width = volt.shape
    slots = tables[2].shape[0]
    f32 = jnp.float32
    smem = pl.BlockSpec(memory_space=pltpu.SMEM)
    vmem = pl.BlockSpec(memory_space=pltpu.VMEM)
    out_shape = (
        jax.ShapeDtypeStruct(volt.shape, f32),
        jax.ShapeDtypeStruct(volt.shape, f32),
        jax.ShapeDtypeStruct(term_volt.shape, f32),
        jax.ShapeDtypeStruct(term_volt.shape, f32),
        jax.ShapeDtypeStruct((slots, 2 * width), f32),
        jax.ShapeDtypeStruct((rows_x, width), f32),
        jax.ShapeDtypeStruct((depth, width), f32),
        jax.ShapeDtypeStruct((depth, width), f32),
        jax.ShapeDtypeStruct((depth * rows_x // width, width), f32),
        jax.ShapeDtypeStruct((depth * rows_x // width, width), f32),
    )
    operands = tuple(tables) + (volt, recovery, coef_z, coef_x, coef_y, recv, tile_gain,
                                gains_rows, term_volt, term_recovery, cable_rows) + tuple(halos)
    return pl.pallas_call(
        step_kernel,
        out_shape=out_shape,
        in_specs=[smem] * len(tables) + [vmem] * (len(operands) - len(tables)),
        out_specs=[vmem] * len(out_shape),
        scratch_shapes=[pltpu.VMEM(volt.shape, f32), pltpu.VMEM(term_volt.shape, f32)],
        interpret=INTERPRET,
    )(*operands)


def exchange_halos(faces):
    z_send, x_first, x_last, y_first, y_last = faces
    assert lax.axis_size("gz") == 2
    halos = [lax.ppermute(z_send, "gz", [(0, 1), (1, 0)])]
    for axis, first, last in (("gx", x_first, x_last), ("gy", y_first, y_last)):
        count = lax.axis_size(axis)
        halos.append(lax.ppermute(last, axis, [(i, i + 1) for i in range(count - 1)]))
        halos.append(lax.ppermute(first, axis, [(i + 1, i) for i in range(count - 1)]))
    return halos


def on_device(
    volt,
    recovery,
    fiber_class,
    fiber_table,
    junction_block,
    junction_term,
    junction_owner,
    term_volt,
    term_recovery,
    term_gain,
    cable_gain,
):
    depth, rows_x, width = volt.shape
    owners = lax.axis_size("gx") * lax.axis_size("gy")
    jcount = junction_block.shape[0]
    capacity = max(2, 2 * jcount // owners)
    slots_total = owners * capacity
    term_count = term_volt.shape[0]
    coef_z = jnp.zeros(volt.shape, jnp.float32)
    coef_x = jnp.zeros(volt.shape, jnp.float32)
    coef_y = jnp.zeros(volt.shape, jnp.float32)
    for klass in range(NCLASS):
        hit = fiber_class == klass
        coef_z = jnp.where(hit, fiber_table[0, klass], coef_z)
        coef_x = jnp.where(hit, fiber_table[1, klass], coef_x)
        coef_y = jnp.where(hit, fiber_table[2, klass], coef_y)

    owner = junction_owner[:, 0]
    order = jnp.arange(jcount, dtype=jnp.int32)
    earlier = (owner[:, None] == owner[None, :]) & (order[None, :] < order[:, None])
    rank = jnp.sum(earlier.astype(jnp.int32), axis=1)
    slot = owner * capacity + rank
    hits = slot[None, :] == jnp.arange(slots_total, dtype=jnp.int32)[:, None]
    slot_block = jnp.sum(jnp.where(hits, junction_block[None, :], 0), axis=1)
    slot_term = jnp.sum(jnp.where(hits, junction_term[None, :] + 1, 0), axis=1) - 1

    arrived = lax.all_to_all(slot_term, ("gx", "gy"), split_axis=0, concat_axis=0, tiled=True)
    valid = arrived >= 0
    safe_ids = jnp.where(valid, arrived, 0)
    pick = safe_ids[:, None] == jnp.arange(term_count, dtype=jnp.int32)[None, :]
    gains = jnp.where(valid, jnp.sum(jnp.where(pick, term_gain[None, :], 0.0), axis=1), 0.0)
    gain_rows = jnp.broadcast_to(gains[:, None], (slots_total, width))
    cable_rows = jnp.broadcast_to(cable_gain[:, None], term_volt.shape)

    edges = []
    for axis in ("gz", "gx", "gy"):
        index = lax.axis_index(axis)
        edges += [index == 0, index == lax.axis_size(axis) - 1]
    edges = jnp.stack(edges + edges[:2]).astype(jnp.int32)
    tables = (junction_block, slot, safe_ids, slot_block, edges)

    flat_rows = volt.reshape(depth * rows_x, width)
    sent = jnp.concatenate([flat_rows[slot_block], term_volt[safe_ids], gain_rows], axis=1)
    faces = (
        jnp.where(lax.axis_index("gz") == 0, volt[depth - 1], volt[0]),
        volt[:, 0, :],
        volt[:, rows_x - 1, :],
        volt[:, :, 0].reshape(-1, width),
        volt[:, :, width - 1].reshape(-1, width),
    )
    tile_gain = None
    for step in range(STEPS):
        halos = exchange_halos(faces)
        received = lax.all_to_all(sent, ("gx", "gy"), split_axis=0, concat_axis=0, tiled=True)
        if step == 0:
            tile_gain = received[slot, 2 * width:3 * width]
        state = (volt, recovery, coef_z, coef_x, coef_y, term_volt, term_recovery)
        outs = run_step(tables, state, received, tile_gain, gain_rows, cable_rows, halos)
        volt, recovery, term_volt, term_recovery, sent = outs[:5]
        faces = outs[5:]
    return (volt, recovery, term_volt, term_recovery)


def solution(mesh):
    return jax.shard_map(
        on_device,
        mesh=mesh,
        in_specs=(
            P("gz", "gx", "gy"),
            P("gz", "gx", "gy"),
            P("gz", "gx", "gy"),
            P(),
            P(("gx", "gy", "gz")),
            P(("gx", "gy", "gz")),
            P(("gx", "gy", "gz"), None),
            P(("gx", "gy", "gz"), None),
            P(("gx", "gy", "gz"), None),
            P(("gx", "gy", "gz")),
            P(("gx", "gy", "gz")),
        ),
        out_specs=(
            P("gz", "gx", "gy"),
            P("gz", "gx", "gy"),
            P(("gx", "gy", "gz"), None),
            P(("gx", "gy", "gz"), None),
        ),
        check_vma=False,
    )
```

time: 250 us -> 488 us (1.95)
  local copies, waits for them, and re-layouts: 39 us -> 277 us
  Pallas kernels: 0 us -> 55.6 us
  other arithmetic: 53 us -> 19.5 us
  starting transfers between devices: 138 us -> 116 us
    gather x12 -> x514, local copies, waits for them, and re-layouts: 9.29 us -> 256 us  [the longest x4 3.47 us: on_device(): mine = received[slot]]
    pallas_call x0 -> x4, Pallas kernels: none -> 55.6 us  [run_step(): pl.pallas_call(step_kernel, out_shape=out_shape, in_specs=[smem] * len(ta...]
    scatter-add x8 -> x0, other arithmetic: 14.9 us -> none  [the longest x4 7.66 us: on_device(): into_term = jax.ops.segment_sum(-current, safe_ids, num_segments=term_count)]
    ppermute x24 -> x20, starting transfers between devices: 70.3 us -> 55.9 us  [the longest x8 28.1 us: exchange_halos(): lax.ppermute(first, axis, [(i + 1, i) for i in range(count - 1)])]
    slice x36 -> x2, local copies, waits for them, and re-layouts: 14.7 us -> 1.4 us  [the longest x1 1.38 us: on_device(): volt[:, :, 0].reshape(-1, width)]
    select_n x20 -> x4, other arithmetic: 10.4 us -> 0.02 us  [the longest x1 0.01 us: on_device(): tile_gain = received[slot, 2 * width:3 * width]]
    add x8 -> x1, other arithmetic: 10 us -> 0.01 us  [on_device(): junction_term[None, :] + 1]
    all_to_all x0 -> x8, local copies, waits for them, and re-layouts: none -> 9.29 us  [on_device(): lax.all_to_all(sent, ('gx', 'gy'), split_axis=0, concat_axis=0, tiled=True)]
  transfers between devices with their start and end apart: 29 -> 25, of which waited for: 6 -> 4; matrix products, arithmetic and copies ran while one was open for 16% -> 58% of each run, Pallas kernels for 0% -> 0%
where the time goes in v3:
time: 488 us; the launch traced here: 484 us
  local copies, waits for them, and re-layouts  277 us (57%)
  starting transfers between devices  116 us (24%)
  Pallas kernels  55.6 us (11%)
  other arithmetic  19.5 us (4%)
  waiting for transfers between devices  14.8 us (3%)
    gather x512, local copies, waits for them, and re-layouts  255 us
    pallas_call x4, Pallas kernels, run_step(): pl.pallas_call(step_kernel, out_shape=out_shape, in_specs=[smem] * len(ta...  55.6 us
    all_to_all x4, starting transfers between devices, on_device(): lax.all_to_all(sent, ('gx', 'gy'), split_axis=0, concat_axis=0, tiled=True)  47.2 us
    ppermute x8, starting transfers between devices, exchange_halos(): lax.ppermute(first, axis, [(i + 1, i) for i in range(count - 1)])  28.1 us
    ppermute x8, starting transfers between devices, exchange_halos(): lax.ppermute(last, axis, [(i, i + 1) for i in range(count - 1)])  27.2 us
    all_to_all x1, starting transfers between devices, on_device(): lax.all_to_all(slot_term, ('gx', 'gy'), split_axis=0, concat_axis=0, tile...  12.5 us
    ppermute x8, waiting for transfers between devices, exchange_halos(): lax.ppermute(first, axis, [(i + 1, i) for i in range(count - 1)])  9.87 us
  transfers between devices with their start and end apart: 25, of which 4 were waited for; matrix products, arithmetic and copies ran while one was open for 58% of the time, Pallas kernels for 0%

profile of v3, /device:TPU:128, one launch (start us, length us, event | category | flops | bytes accessed | tf_op | source)
XLA Modules:
  0.0 484.4 jit_solution(7858436188565413328)
XLA Ops:
  0.6 1.4 slice_reduce_fusion
  2.1 3.4 collective-permute-start.3
  6.9 3.5 collective-permute-start.1
  10.4 5.7 %collective-permute-start.2 = (f32[16,128]{1,0:T(8,128)S(1)}, f32[16,128]{1,0:T(8,128)S(1)}, u32[]{:S(2)}, u32[]{:S(2)}) collective-permute-start(f32[16,128]{1,0:T(8,128)S(1)} %bitcast.60), channel_id=1, source_target_pairs={{8,0},{16,8},{24,16},{32,24},{40,32},{48,40},{56,48},{64,56},{72,6... | collective-permute-start | bytes 24584 | tf_op jit(solution)/shard_map/ppermute | solution.py:181
  19.2 12.5 %all-to-all-start = ((s32[128,2,1]{1,2,0:T(1,128)}), s32[128,2,1]{1,2,0:T(1,128)S(1)}, u32[]{:S(2)}, u32[]{:S(2)}) async-start(s32[128,2,1]{1,2,0:T(1,128)} %bitcast.1), calls=%async_computation | async-start | bytes 131072 | tf_op jit(solution)/shard_map/all_to_all | solution.py:222
  33.8 4.9 %all-to-all-done = s32[128,2,1]{1,2,0:T(1,128)S(1)} async-done(((s32[128,2,1]{1,2,0:T(1,128)}), s32[128,2,1]{1,2,0:T(1,128)S(1)}, u32[]{:S(2)}, u32[]{:S(2)}) %all-to-all-start) | async-done | bytes 1056 | tf_op jit(solution)/shard_map/all_to_all | solution.py:222
  44.1 11.0 %all-to-all-start.1 = ((f32[128,2,384]{2,1,0:T(2,128)}), f32[128,2,384]{2,1,0:T(2,128)S(1)}, u32[]{:S(2)}, u32[]{:S(2)}) async-start(f32[128,2,384]{2,1,0:T(2,128)} %all_to_all.39), calls=%async_computation.1 | async-start | bytes 786432 | tf_op jit(solution)/shard_map/all_to_all | solution.py:249
  56.4 6.1 %select_select_fusion = (f32[16,32,128]{2,1,0:T(8,128)}, pred[16,32,128]{2,1,0:T(8,128)(4,1)S(1)}, pred[16,32,128]{2,1,0:T(8,128)(4,1)S(1)}, pred[16,32,128]{2,1...) fusion(f32[]{:T(128)} %bitcast.31, f32[]{:T(128)} %bitcast.30, ...), kind=kLoop, calls=%fused_computation.6 | loop fusion | flops 1048576 | bytes 1048608 | tf_op jit(solution)/shard_map/jit(_where)/select_n | solution.py:211
  62.5 5.8 %select_select_fusion.1.cx_ref = f32[16,32,128]{2,1,0:T(8,128)} fusion(pred[16,32,128]{2,1,0:T(8,128)(4,1)S(1)} %get-tuple-element.100, pred[16,32,128]{2,1,0:T(8,128)(4,1)S(1)} %get-tuple-element.99, pred[16,32,128]{2,1,0:T(8,128)(4,1)S(1)} %get-tuple-element.98, pred[16,32,128]{2,1,0:T(8,128)(4,1)S(1)} %get-tuple-element.97, ...), kind=kLoop, calls=%fused_computation.7 | loop fusion | flops 524288 | bytes 786464 | tf_op jit(solution)/shard_map/jit(_where)/select_n | solution.py:210
  68.3 5.8 %select_select_fusion.2.cz_ref = f32[16,32,128]{2,1,0:T(8,128)} fusion(pred[16,32,128]{2,1,0:T(8,128)(4,1)S(1)} %get-tuple-element.100, pred[16,32,128]{2,1,0:T(8,128)(4,1)S(1)} %get-tuple-element.99, pred[16,32,128]{2,1,0:T(8,128)(4,1)S(1)} %get-tuple-element.98, pred[16,32,128]{2,1,0:T(8,128)(4,1)S(1)} %get-tuple-element.97, ...), kind=kLoop, calls=%fused_computation.8 | loop fusion | flops 524288 | bytes 786464 | tf_op jit(solution)/shard_map/jit(_where)/select_n | solution.py:209
  74.3 255.2 %while.1 = (s32[]{:T(128)}, f32[256,384]{1,0:T(8,128)S(1)}, s32[128,2]{0,1:T(2,128)S(1)}, f32[128,128]{1,0:T(8,128)S(1)}, s32[]{:T(128)}, /*index=5*/s32[]{:T(128)}) while((s32[]{:T(128)}, f32[256,384]{1,0:T(8,128)S(1)}, s32[128,2]{0,1:T(2,128)S(1)}, f32[128,128]{1,0:T(8,128)S(1)}, s32[]{:T(128)}, /*index=5*/s32[]{:T(128)}) %tuple.56), condition=%wide.while_cond, body=%wide.while_body.sunk | while | flops 2 | bytes 2169 | solution.py:251
  75.0 1.4 dynamic-slice.7
  77.0 1.4 dynamic-slice.7
  84.9 1.4 dynamic-slice.7
  86.9 1.4 dynamic-slice.7
  94.9 1.4 dynamic-slice.7
  104.9 1.4 dynamic-slice.7
  112.8 1.4 dynamic-slice.7
  114.8 1.4 dynamic-slice.7
  122.8 1.4 dynamic-slice.7
  124.8 1.4 dynamic-slice.7
  132.8 1.4 dynamic-slice.7
  142.7 1.4 dynamic-slice.7
  150.7 1.4 dynamic-slice.7
  152.7 1.4 dynamic-slice.7
  160.7 1.4 dynamic-slice.7
  330.4 14.0 %shard_map.138 = (f32[16,32,128]{2,1,0:T(8,128)}, f32[16,32,128]{2,1,0:T(8,128)}, f32[32,128]{1,0:T(8,128)}, f32[32,128]{1,0:T(8,128)}, f32[256,256]{1,0:T(8,128...) custom-call(s32[128]{0:T(128)} %blk_ref.7, ...), custom_call_target="tpu_custom_call" | custom-call | tf_op jit(solution)/shard_map/pallas_call | solution.py:164
  344.3 1.8 all_to_all.42
  346.1 13.9 %all-to-all-start.2 = ((f32[128,2,256]{2,1,0:T(2,128)}), f32[128,2,256]{2,1,0:T(2,128)S(1)}, u32[]{:S(2)}, u32[]{:S(2)}) async-start(f32[128,2,256]{2,1,0:T(2,128)} %all_to_all.42), calls=%async_computation.2 | async-start | bytes 524288 | tf_op jit(solution)/shard_map/all_to_all | solution.py:249
  360.3 3.4 collective-permute-start.6
  363.8 5.8 %collective-permute-start.7 = (f32[16,128]{1,0:T(8,128)S(1)}, f32[16,128]{1,0:T(8,128)S(1)}, u32[]{:S(2)}, u32[]{:S(2)}) collective-permute-start(f32[16,128]{1,0:T(8,128)S(1)} %copy-done.38), channel_id=1, source_target_pairs={{8,0},{16,8},{24,16},{32,24},{40,32},{48,40},{56,48},{64,56},{72,6... | collective-permute-start | bytes 24584 | tf_op jit(solution)/shard_map/ppermute | solution.py:181
  369.5 3.4 collective-permute-start.8
  375.1 3.3 collective-permute-done.9.yhi_ref
  379.0 13.9 %shard_map.139 = (f32[16,32,128]{2,1,0:T(8,128)}, f32[16,32,128]{2,1,0:T(8,128)}, f32[32,128]{1,0:T(8,128)}, f32[32,128]{1,0:T(8,128)}, f32[256,256]{1,0:T(8,128...) custom-call(s32[128]{0:T(128)} %blk_ref.7, ...), custom_call_target="tpu_custom_call" | custom-call | tf_op jit(solution)/shard_map/pallas_call | solution.py:164
  393.0 1.8 all_to_all.45
  394.8 11.1 %all-to-all-start.3 = ((f32[128,2,256]{2,1,0:T(2,128)}), f32[128,2,256]{2,1,0:T(2,128)S(1)}, u32[]{:S(2)}, u32[]{:S(2)}) async-start(f32[128,2,256]{2,1,0:T(2,128)} %all_to_all.45), calls=%async_computation.3 | async-start | bytes 524288 | tf_op jit(solution)/shard_map/all_to_all | solution.py:249
  406.0 3.4 collective-permute-start.11
  409.5 5.8 %collective-permute-start.12 = (f32[16,128]{1,0:T(8,128)S(1)}, f32[16,128]{1,0:T(8,128)S(1)}, u32[]{:S(2)}, u32[]{:S(2)}) collective-permute-start(f32[16,128]{1,0:T(8,128)S(1)} %copy-done.34), channel_id=1, source_target_pairs={{8,0},{16,8},{24,16},{32,24},{40,32},{48,40},{56,48},{64,56},{72,6... | collective-permute-start | bytes 24584 | tf_op jit(solution)/shard_map/ppermute | solution.py:181
  415.2 3.4 collective-permute-start.13
  420.8 3.3 collective-permute-done.14.yhi_ref
  424.8 13.9 %shard_map.140 = (f32[16,32,128]{2,1,0:T(8,128)}, f32[16,32,128]{2,1,0:T(8,128)}, f32[32,128]{1,0:T(8,128)}, f32[32,128]{1,0:T(8,128)}, f32[256,256]{1,0:T(8,128...) custom-call(s32[128]{0:T(128)} %blk_ref.7, ...), custom_call_target="tpu_custom_call" | custom-call | tf_op jit(solution)/shard_map/pallas_call | solution.py:164
  438.6 1.8 all_to_all.48
  440.4 11.1 %all-to-all-start.4 = ((f32[128,2,256]{2,1,0:T(2,128)}), f32[128,2,256]{2,1,0:T(2,128)S(1)}, u32[]{:S(2)}, u32[]{:S(2)}) async-start(f32[128,2,256]{2,1,0:T(2,128)} %all_to_all.48), calls=%async_computation.4 | async-start | bytes 524288 | tf_op jit(solution)/shard_map/all_to_all | solution.py:249
  451.7 3.4 collective-permute-start.16
  455.1 5.8 %collective-permute-start.17 = (f32[16,128]{1,0:T(8,128)S(1)}, f32[16,128]{1,0:T(8,128)S(1)}, u32[]{:S(2)}, u32[]{:S(2)}) collective-permute-start(f32[16,128]{1,0:T(8,128)S(1)} %copy-done.35), channel_id=1, source_target_pairs={{8,0},{16,8},{24,16},{32,24},{40,32},{48,40},{56,48},{64,56},{72,6... | collective-permute-start | bytes 24584 | tf_op jit(solution)/shard_map/ppermute | solution.py:181
  460.9 3.4 collective-permute-start.18
  466.5 3.3 collective-permute-done.19.yhi_ref
  470.4 13.9 %shard_map.141 = (f32[16,32,128]{2,1,0:T(8,128)}, f32[16,32,128]{2,1,0:T(8,128)}, f32[32,128]{1,0:T(8,128)}, f32[32,128]{1,0:T(8,128)}, f32[256,256]{1,0:T(8,128...) custom-call(s32[128]{0:T(128)} %blk_ref.7, ...), custom_call_target="tpu_custom_call" | custom-call | tf_op jit(solution)/shard_map/pallas_call | solution.py:164
  (660 shorter events, 257.2 us)
Async XLA Ops:
  0.6 6.2 %copy-start.1 = (f32[16,32,128]{2,1,0:T(8,128)S(1)}, f32[16,32,128]{2,1,0:T(8,128)}, u32[]{:S(2)}) copy-start(f32[16,32,128]{2,1,0:T(8,128)} %v_ref.1) | copy-start | bytes 786436
  2.1 327.4 %collective-permute-start.3 = (f32[4,128]{1,0:T(4,128)S(1)}, f32[4,128]{1,0:T(4,128)S(1)}, u32[]{:S(2)}, u32[]{:S(2)}) collective-permute-start(f32[4,128]{1,0:T(4,128)S(1)} %reshape_squeeze.6), channel_id=1, source_target_pairs={{0,2},{2,4},{4,6},{1,3},{3,5},{5,7},{8,10},{10,12},{12,14},{9,11},... | collective-permute-start | bytes 6152 | tf_op jit(solution)/shard_map/ppermute | solution.py:180
  5.6 324.0 %collective-permute-start.4 = (f32[4,128]{1,0:T(4,128)S(1)}, f32[4,128]{1,0:T(4,128)S(1)}, u32[]{:S(2)}, u32[]{:S(2)}) collective-permute-start(f32[4,128]{1,0:T(4,128)S(1)} %reshape_squeeze.7), channel_id=1, source_target_pairs={{2,0},{4,2},{6,4},{3,1},{5,3},{7,5},{10,8},{12,10},{14,12},{11,9},... | collective-permute-start | bytes 6152 | tf_op jit(solution)/shard_map/ppermute | solution.py:181
  6.9 322.7 %collective-permute-start.1 = (f32[16,128]{1,0:T(8,128)S(1)}, f32[16,128]{1,0:T(8,128)S(1)}, u32[]{:S(2)}, u32[]{:S(2)}) collective-permute-start(f32[16,128]{1,0:T(8,128)S(1)} %bitcast.61), channel_id=1, source_target_pairs={{0,8},{8,16},{16,24},{24,32},{32,40},{40,48},{48,56},{56,64},{64,7... | collective-permute-start | bytes 24584 | tf_op jit(solution)/shard_map/ppermute | solution.py:180
  10.4 319.2 %collective-permute-start.2 = (f32[16,128]{1,0:T(8,128)S(1)}, f32[16,128]{1,0:T(8,128)S(1)}, u32[]{:S(2)}, u32[]{:S(2)}) collective-permute-start(f32[16,128]{1,0:T(8,128)S(1)} %bitcast.60), channel_id=1, source_target_pairs={{8,0},{16,8},{24,16},{32,24},{40,32},{48,40},{56,48},{64,56},{72,6... | collective-permute-start | bytes 24584 | tf_op jit(solution)/shard_map/ppermute | solution.py:181
  16.1 313.5 %collective-permute-start = (f32[32,128]{1,0:T(8,128)S(1)}, f32[32,128]{1,0:T(8,128)S(1)}, u32[]{:S(2)}, u32[]{:S(2)}) collective-permute-start(f32[32,128]{1,0:T(8,128)S(1)} %select_bitcast_fusion), channel_id=1, source_target_pairs={{0,1},{1,0},{2,3},{3,2},{4,5},{5,4},{6,7},{7,6},{8,9},{9,8},{10,11... | collective-permute-start | bytes 49160 | tf_op jit(solution)/shard_map/ppermute | solution.py:177
  18.4 13.3 %copy-start.5 = (s32[256]{0:T(256)}, s32[256]{0:T(256)S(1)}, u32[]{:S(2)}) copy-start(s32[256]{0:T(256)S(1)} %get-tuple-element.82.sblk_ref) | copy-start | bytes 3076
  19.2 19.5 %all-to-all-start = ((s32[128,2,1]{1,2,0:T(1,128)}), s32[128,2,1]{1,2,0:T(1,128)S(1)}, u32[]{:S(2)}, u32[]{:S(2)}) async-start(s32[128,2,1]{1,2,0:T(1,128)} %bitcast.1), calls=%async_computation | async-start | bytes 131072 | tf_op jit(solution)/shard_map/all_to_all | solution.py:222
  40.2 1.4 copy-start
  44.1 12.3 %copy-start.3 = (s32[16,32,128]{2,1,0:T(8,128)S(1)}, s32[16,32,128]{2,1,0:T(8,128)}, u32[]{:S(2)}) copy-start(s32[16,32,128]{2,1,0:T(8,128)} %param.13) | copy-start | bytes 786436
  44.1 30.0 %all-to-all-start.1 = ((f32[128,2,384]{2,1,0:T(2,128)}), f32[128,2,384]{2,1,0:T(2,128)S(1)}, u32[]{:S(2)}, u32[]{:S(2)}) async-start(f32[128,2,384]{2,1,0:T(2,128)} %all_to_all.39), calls=%async_computation.1 | async-start | bytes 786432 | tf_op jit(solution)/shard_map/all_to_all | solution.py:249
  74.3 255.3 %copy-start.30 = (f32[32]{0:T(128)S(1)}, f32[32]{0:T(128)}, u32[]{:S(2)}) copy-start(f32[32]{0:T(128)} %param.21) | copy-start | bytes 388
  346.1 13.9 %copy-start.33 = (f32[32,128]{1,0:T(8,128)S(1)}, f32[32,128]{1,0:T(8,128)}, u32[]{:S(2)}) copy-start(f32[32,128]{1,0:T(8,128)} %get-tuple-element.43) | copy-start | bytes 49156
  346.1 14.2 %copy-start.39 = (f32[16,128]{1,0:T(8,128)S(1)}, f32[16,128]{1,0:T(8,128)}, u32[]{:S(2)}) copy-start(f32[16,128]{1,0:T(8,128)} %get-tuple-element.44) | copy-start | bytes 24580
  346.1 17.6 %copy-start.38 = (f32[16,128]{1,0:T(8,128)S(1)}, f32[16,128]{1,0:T(8,128)}, u32[]{:S(2)}) copy-start(f32[16,128]{1,0:T(8,128)} %get-tuple-element.45) | copy-start | bytes 24580
  346.1 28.1 %all-to-all-start.2 = ((f32[128,2,256]{2,1,0:T(2,128)}), f32[128,2,256]{2,1,0:T(2,128)S(1)}, u32[]{:S(2)}, u32[]{:S(2)}) async-start(f32[128,2,256]{2,1,0:T(2,128)} %all_to_all.42), calls=%async_computation.2 | async-start | bytes 524288 | tf_op jit(solution)/shard_map/all_to_all | solution.py:249
  360.0 18.4 %collective-permute-start.5 = (f32[32,128]{1,0:T(8,128)S(1)}, f32[32,128]{1,0:T(8,128)S(1)}, u32[]{:S(2)}, u32[]{:S(2)}) collective-permute-start(f32[32,128]{1,0:T(8,128)S(1)} %copy-done.33), channel_id=1, source_target_pairs={{0,1},{1,0},{2,3},{3,2},{4,5},{5,4},{6,7},{7,6},{8,9},{9,8},{10,11... | collective-permute-start | bytes 49160 | tf_op jit(solution)/shard_map/ppermute | solution.py:177
  360.3 9.2 %copy-start.45 = (f32[4,128]{1,0:T(4,128)S(1)}, f32[4,128]{1,0:T(4,128)}, u32[]{:S(2)}) copy-start(f32[4,128]{1,0:T(4,128)} %get-tuple-element.46) | copy-start | bytes 6148
  360.3 18.1 %collective-permute-start.6 = (f32[16,128]{1,0:T(8,128)S(1)}, f32[16,128]{1,0:T(8,128)S(1)}, u32[]{:S(2)}, u32[]{:S(2)}) collective-permute-start(f32[16,128]{1,0:T(8,128)S(1)} %copy-done.39), channel_id=1, source_target_pairs={{0,8},{8,16},{16,24},{24,32},{32,40},{40,48},{48,56},{56,64},{64,7... | collective-permute-start | bytes 24584 | tf_op jit(solution)/shard_map/ppermute | solution.py:180
  363.7 9.2 %copy-start.44 = (f32[4,128]{1,0:T(4,128)S(1)}, f32[4,128]{1,0:T(4,128)}, u32[]{:S(2)}) copy-start(f32[4,128]{1,0:T(4,128)} %get-tuple-element.47) | copy-start | bytes 6148
  363.8 14.7 %collective-permute-start.7 = (f32[16,128]{1,0:T(8,128)S(1)}, f32[16,128]{1,0:T(8,128)S(1)}, u32[]{:S(2)}, u32[]{:S(2)}) collective-permute-start(f32[16,128]{1,0:T(8,128)S(1)} %copy-done.38), channel_id=1, source_target_pairs={{8,0},{16,8},{24,16},{32,24},{40,32},{48,40},{56,48},{64,56},{72,6... | collective-permute-start | bytes 24584 | tf_op jit(solution)/shard_map/ppermute | solution.py:181
  369.5 5.6 %collective-permute-start.8 = (f32[4,128]{1,0:T(4,128)S(1)}, f32[4,128]{1,0:T(4,128)S(1)}, u32[]{:S(2)}, u32[]{:S(2)}) collective-permute-start(f32[4,128]{1,0:T(4,128)S(1)} %copy-done.45), channel_id=1, source_target_pairs={{0,2},{2,4},{4,6},{1,3},{3,5},{5,7},{8,10},{10,12},{12,14},{9,11},... | collective-permute-start | bytes 6152 | tf_op jit(solution)/shard_map/ppermute | solution.py:180
  372.9 5.5 %collective-permute-start.9 = (f32[4,128]{1,0:T(4,128)S(1)}, f32[4,128]{1,0:T(4,128)S(1)}, u32[]{:S(2)}, u32[]{:S(2)}) collective-permute-start(f32[4,128]{1,0:T(4,128)S(1)} %copy-done.44), channel_id=1, source_target_pairs={{2,0},{4,2},{6,4},{3,1},{5,3},{7,5},{10,8},{12,10},{14,12},{11,9},... | collective-permute-start | bytes 6152 | tf_op jit(solution)/shard_map/ppermute | solution.py:181
  375.1 3.3 copy-start.25
  394.8 11.1 %copy-start.31 = (f32[32,128]{1,0:T(8,128)S(1)}, f32[32,128]{1,0:T(8,128)}, u32[]{:S(2)}) copy-start(f32[32,128]{1,0:T(8,128)} %get-tuple-element.53) | copy-start | bytes 49156
  394.8 11.3 %copy-start.36 = (f32[16,128]{1,0:T(8,128)S(1)}, f32[16,128]{1,0:T(8,128)}, u32[]{:S(2)}) copy-start(f32[16,128]{1,0:T(8,128)} %get-tuple-element.54) | copy-start | bytes 24580
  394.8 14.7 %copy-start.34 = (f32[16,128]{1,0:T(8,128)S(1)}, f32[16,128]{1,0:T(8,128)}, u32[]{:S(2)}) copy-start(f32[16,128]{1,0:T(8,128)} %get-tuple-element.55) | copy-start | bytes 24580
  394.8 25.2 %all-to-all-start.3 = ((f32[128,2,256]{2,1,0:T(2,128)}), f32[128,2,256]{2,1,0:T(2,128)S(1)}, u32[]{:S(2)}, u32[]{:S(2)}) async-start(f32[128,2,256]{2,1,0:T(2,128)} %all_to_all.45), calls=%async_computation.3 | async-start | bytes 524288 | tf_op jit(solution)/shard_map/all_to_all | solution.py:249
  405.9 18.2 %collective-permute-start.10 = (f32[32,128]{1,0:T(8,128)S(1)}, f32[32,128]{1,0:T(8,128)S(1)}, u32[]{:S(2)}, u32[]{:S(2)}) collective-permute-start(f32[32,128]{1,0:T(8,128)S(1)} %copy-done.31), channel_id=1, source_target_pairs={{0,1},{1,0},{2,3},{3,2},{4,5},{5,4},{6,7},{7,6},{8,9},{9,8},{10,11... | collective-permute-start | bytes 49160 | tf_op jit(solution)/shard_map/ppermute | solution.py:177
  406.0 9.2 %copy-start.42 = (f32[4,128]{1,0:T(4,128)S(1)}, f32[4,128]{1,0:T(4,128)}, u32[]{:S(2)}) copy-start(f32[4,128]{1,0:T(4,128)} %get-tuple-element.56) | copy-start | bytes 6148
  406.0 18.1 %collective-permute-start.11 = (f32[16,128]{1,0:T(8,128)S(1)}, f32[16,128]{1,0:T(8,128)S(1)}, u32[]{:S(2)}, u32[]{:S(2)}) collective-permute-start(f32[16,128]{1,0:T(8,128)S(1)} %copy-done.36), channel_id=1, source_target_pairs={{0,8},{8,16},{16,24},{24,32},{32,40},{40,48},{48,56},{56,64},{64,7... | collective-permute-start | bytes 24584 | tf_op jit(solution)/shard_map/ppermute | solution.py:180
  409.4 9.2 %copy-start.40 = (f32[4,128]{1,0:T(4,128)S(1)}, f32[4,128]{1,0:T(4,128)}, u32[]{:S(2)}) copy-start(f32[4,128]{1,0:T(4,128)} %get-tuple-element.57) | copy-start | bytes 6148
  409.5 14.7 %collective-permute-start.12 = (f32[16,128]{1,0:T(8,128)S(1)}, f32[16,128]{1,0:T(8,128)S(1)}, u32[]{:S(2)}, u32[]{:S(2)}) collective-permute-start(f32[16,128]{1,0:T(8,128)S(1)} %copy-done.34), channel_id=1, source_target_pairs={{8,0},{16,8},{24,16},{32,24},{40,32},{48,40},{56,48},{64,56},{72,6... | collective-permute-start | bytes 24584 | tf_op jit(solution)/shard_map/ppermute | solution.py:181
  415.2 5.6 %collective-permute-start.13 = (f32[4,128]{1,0:T(4,128)S(1)}, f32[4,128]{1,0:T(4,128)S(1)}, u32[]{:S(2)}, u32[]{:S(2)}) collective-permute-start(f32[4,128]{1,0:T(4,128)S(1)} %copy-done.42), channel_id=1, source_target_pairs={{0,2},{2,4},{4,6},{1,3},{3,5},{5,7},{8,10},{10,12},{12,14},{9,11},... | collective-permute-start | bytes 6152 | tf_op jit(solution)/shard_map/ppermute | solution.py:180
  418.6 5.5 %collective-permute-start.14 = (f32[4,128]{1,0:T(4,128)S(1)}, f32[4,128]{1,0:T(4,128)S(1)}, u32[]{:S(2)}, u32[]{:S(2)}) collective-permute-start(f32[4,128]{1,0:T(4,128)S(1)} %copy-done.40), channel_id=1, source_target_pairs={{2,0},{4,2},{6,4},{3,1},{5,3},{7,5},{10,8},{12,10},{14,12},{11,9},... | collective-permute-start | bytes 6152 | tf_op jit(solution)/shard_map/ppermute | solution.py:181
  420.8 3.3 copy-start.26
  440.4 11.1 %copy-start.32 = (f32[32,128]{1,0:T(8,128)S(1)}, f32[32,128]{1,0:T(8,128)}, u32[]{:S(2)}) copy-start(f32[32,128]{1,0:T(8,128)} %get-tuple-element.63) | copy-start | bytes 49156
  440.4 11.3 %copy-start.37 = (f32[16,128]{1,0:T(8,128)S(1)}, f32[16,128]{1,0:T(8,128)}, u32[]{:S(2)}) copy-start(f32[16,128]{1,0:T(8,128)} %get-tuple-element.64) | copy-start | bytes 24580
  440.4 14.7 %copy-start.35 = (f32[16,128]{1,0:T(8,128)S(1)}, f32[16,128]{1,0:T(8,128)}, u32[]{:S(2)}) copy-start(f32[16,128]{1,0:T(8,128)} %get-tuple-element.65) | copy-start | bytes 24580
  440.4 25.2 %all-to-all-start.4 = ((f32[128,2,256]{2,1,0:T(2,128)}), f32[128,2,256]{2,1,0:T(2,128)S(1)}, u32[]{:S(2)}, u32[]{:S(2)}) async-start(f32[128,2,256]{2,1,0:T(2,128)} %all_to_all.48), calls=%async_computation.4 | async-start | bytes 524288 | tf_op jit(solution)/shard_map/all_to_all | solution.py:249
  451.6 18.2 %collective-permute-start.15 = (f32[32,128]{1,0:T(8,128)S(1)}, f32[32,128]{1,0:T(8,128)S(1)}, u32[]{:S(2)}, u32[]{:S(2)}) collective-permute-start(f32[32,128]{1,0:T(8,128)S(1)} %copy-done.32), channel_id=1, source_target_pairs={{0,1},{1,0},{2,3},{3,2},{4,5},{5,4},{6,7},{7,6},{8,9},{9,8},{10,11... | collective-permute-start | bytes 49160 | tf_op jit(solution)/shard_map/ppermute | solution.py:177
  451.7 9.2 %copy-start.43 = (f32[4,128]{1,0:T(4,128)S(1)}, f32[4,128]{1,0:T(4,128)}, u32[]{:S(2)}) copy-start(f32[4,128]{1,0:T(4,128)} %get-tuple-element.66) | copy-start | bytes 6148
  451.7 18.1 %collective-permute-start.16 = (f32[16,128]{1,0:T(8,128)S(1)}, f32[16,128]{1,0:T(8,128)S(1)}, u32[]{:S(2)}, u32[]{:S(2)}) collective-permute-start(f32[16,128]{1,0:T(8,128)S(1)} %copy-done.37), channel_id=1, source_target_pairs={{0,8},{8,16},{16,24},{24,32},{32,40},{40,48},{48,56},{56,64},{64,7... | collective-permute-start | bytes 24584 | tf_op jit(solution)/shard_map/ppermute | solution.py:180
  455.1 9.2 %copy-start.41 = (f32[4,128]{1,0:T(4,128)S(1)}, f32[4,128]{1,0:T(4,128)}, u32[]{:S(2)}) copy-start(f32[4,128]{1,0:T(4,128)} %get-tuple-element.67) | copy-start | bytes 6148
  455.1 14.7 %collective-permute-start.17 = (f32[16,128]{1,0:T(8,128)S(1)}, f32[16,128]{1,0:T(8,128)S(1)}, u32[]{:S(2)}, u32[]{:S(2)}) collective-permute-start(f32[16,128]{1,0:T(8,128)S(1)} %copy-done.35), channel_id=1, source_target_pairs={{8,0},{16,8},{24,16},{32,24},{40,32},{48,40},{56,48},{64,56},{72,6... | collective-permute-start | bytes 24584 | tf_op jit(solution)/shard_map/ppermute | solution.py:181
  460.9 5.6 %collective-permute-start.18 = (f32[4,128]{1,0:T(4,128)S(1)}, f32[4,128]{1,0:T(4,128)S(1)}, u32[]{:S(2)}, u32[]{:S(2)}) collective-permute-start(f32[4,128]{1,0:T(4,128)S(1)} %copy-done.43), channel_id=1, source_target_pairs={{0,2},{2,4},{4,6},{1,3},{3,5},{5,7},{8,10},{10,12},{12,14},{9,11},... | collective-permute-start | bytes 6152 | tf_op jit(solution)/shard_map/ppermute | solution.py:180
  464.3 5.5 %collective-permute-start.19 = (f32[4,128]{1,0:T(4,128)S(1)}, f32[4,128]{1,0:T(4,128)S(1)}, u32[]{:S(2)}, u32[]{:S(2)}) collective-permute-start(f32[4,128]{1,0:T(4,128)S(1)} %copy-done.41), channel_id=1, source_target_pairs={{2,0},{4,2},{6,4},{3,1},{5,3},{7,5},{10,8},{12,10},{14,12},{11,9},... | collective-permute-start | bytes 6152 | tf_op jit(solution)/shard_map/ppermute | solution.py:181
  466.5 3.3 copy-start.23
  (25 other events, 15.8 us)

commit v4 on v3

--- a/solution.py
+++ b/solution.py
@@ -55,7 +55,7 @@
         iv_ref[z, pl.ds(x, 1), :] = iv_ref[z, pl.ds(x, 1), :] + cur
         return carry
 
-    lax.fori_loop(0, jcount, tile_body, 0)
+    lax.fori_loop(0, jcount, tile_body, 0, unroll=8)
 
     def owner_body(k, carry):
         t = ids_ref[k]
@@ -63,7 +63,7 @@
         it_ref[pl.ds(t, 1), :] = it_ref[pl.ds(t, 1), :] + (-cur)
         return carry
 
-    lax.fori_loop(0, slots, owner_body, 0)
+    lax.fori_loop(0, slots, owner_body, 0, unroll=8)
 
     u = tv_ref[...]
     r = tr_ref[...]
@@ -137,7 +137,7 @@
             [nv_ref[b // rows_x, pl.ds(b % rows_x, 1), :], ntv_ref[pl.ds(t, 1), :]], axis=1)
         return carry
 
-    lax.fori_loop(0, slots, pack_body, 0)
+    lax.fori_loop(0, slots, pack_body, 0, unroll=8)
 
 
 def run_step(tables, state, recv, tile_gain, gains_rows, cable_rows, halos):
@@ -248,7 +248,7 @@
         halos = exchange_halos(faces)
         received = lax.all_to_all(sent, ("gx", "gy"), split_axis=0, concat_axis=0, tiled=True)
         if step == 0:
-            tile_gain = received[slot, 2 * width:3 * width]
+            tile_gain = received[:, 2 * width:3 * width][slot]
         state = (volt, recovery, coef_z, coef_x, coef_y, term_volt, term_recovery)
         outs = run_step(tables, state, received, tile_gain, gain_rows, cable_rows, halos)
         volt, recovery, term_volt, term_recovery, sent = outs[:5]

time: 488 us -> 213 us (0.44)
  local copies, waits for them, and re-layouts: 277 us -> 21.5 us
  Pallas kernels: 55.6 us -> 40.4 us
    gather x512 -> x1, local copies, waits for them, and re-layouts: 255 us -> 1.24 us  [on_device(): tile_gain = received[:, 2 * width:3 * width][slot]]
    pallas_call x4, Pallas kernels: 55.6 us -> 40.4 us  [run_step(): pl.pallas_call(step_kernel, out_shape=out_shape, in_specs=[smem] * len(ta...]
    all_to_all x1, waiting for transfers between devices: 4.9 us -> 0.01 us  [on_device(): lax.all_to_all(slot_term, ('gx', 'gy'), split_axis=0, concat_axis=0, tile...]
  transfers between devices with their start and end apart: 25 -> 25, of which waited for: 4 -> 4; matrix products, arithmetic and copies ran while one was open for 58% -> 12% of each run, Pallas kernels for 0% -> 0%
where the time goes in v4:
time: 213 us; the launch traced here: 212 us
  starting transfers between devices  118 us (55%)
  Pallas kernels  40.4 us (19%)
  local copies, waits for them, and re-layouts  21.5 us (10%)
  other arithmetic  19.7 us (9%)
  waiting for transfers between devices  10 us (5%)
    all_to_all x4, starting transfers between devices, on_device(): lax.all_to_all(sent, ('gx', 'gy'), split_axis=0, concat_axis=0, tiled=True)  49.7 us
    pallas_call x4, Pallas kernels, run_step(): pl.pallas_call(step_kernel, out_shape=out_shape, in_specs=[smem] * len(ta...  40.4 us
    ppermute x8, starting transfers between devices, exchange_halos(): lax.ppermute(first, axis, [(i + 1, i) for i in range(count - 1)])  28.1 us
    ppermute x8, starting transfers between devices, exchange_halos(): lax.ppermute(last, axis, [(i, i + 1) for i in range(count - 1)])  27.2 us
    all_to_all x1, starting transfers between devices, on_device(): lax.all_to_all(slot_term, ('gx', 'gy'), split_axis=0, concat_axis=0, tile...  12.6 us
    ppermute x8, waiting for transfers between devices, exchange_halos(): lax.ppermute(first, axis, [(i + 1, i) for i in range(count - 1)])  9.87 us
    all_to_all x8, local copies, waits for them, and re-layouts, on_device(): lax.all_to_all(sent, ('gx', 'gy'), split_axis=0, concat_axis=0, tiled=True)  9.29 us
    select_n x1, other arithmetic, on_device(): coef_y = jnp.where(hit, fiber_table[2, klass], coef_y)  6.13 us
  transfers between devices with their start and end apart: 25, of which 4 were waited for; matrix products, arithmetic and copies ran while one was open for 12% of the time, Pallas kernels for 0%

profile of v4, /device:TPU:128, one launch (start us, length us, event | category | flops | bytes accessed | tf_op | source)
XLA Modules:
  0.0 211.6 jit_solution(12972379933010938606)
XLA Ops:
  0.7 1.4 slice_reduce_fusion
  2.1 3.4 %collective-permute-start.3 = (f32[4,128]{1,0:T(4,128)S(1)}, f32[4,128]{1,0:T(4,128)S(1)}, u32[]{:S(2)}, u32[]{:S(2)}) collective-permute-start(f32[4,128]{1,0:T(4,128)S(1)} %reshape_squeeze.6), channel_id=1, source_target_pairs={{0,2},{2,4},{4,6},{1,3},{3,5},{5,7},{8,10},{10,12},{12,14},{9,11},... | collective-permute-start | bytes 6152 | tf_op jit(solution)/shard_map/ppermute | solution.py:180
  5.6 1.3 collective-permute-start.4
  6.9 3.5 %collective-permute-start.1 = (f32[16,128]{1,0:T(8,128)S(1)}, f32[16,128]{1,0:T(8,128)S(1)}, u32[]{:S(2)}, u32[]{:S(2)}) collective-permute-start(f32[16,128]{1,0:T(8,128)S(1)} %bitcast.57), channel_id=1, source_target_pairs={{0,8},{8,16},{16,24},{24,32},{32,40},{40,48},{48,56},{56,64},{64,7... | collective-permute-start | bytes 24584 | tf_op jit(solution)/shard_map/ppermute | solution.py:180
  10.4 5.7 %collective-permute-start.2 = (f32[16,128]{1,0:T(8,128)S(1)}, f32[16,128]{1,0:T(8,128)S(1)}, u32[]{:S(2)}, u32[]{:S(2)}) collective-permute-start(f32[16,128]{1,0:T(8,128)S(1)} %bitcast.56), channel_id=1, source_target_pairs={{8,0},{16,8},{24,16},{32,24},{40,32},{48,40},{56,48},{64,56},{72,6... | collective-permute-start | bytes 24584 | tf_op jit(solution)/shard_map/ppermute | solution.py:181
  17.1 0.8 sub.7
  17.9 12.6 %all-to-all-start = ((s32[128,2,1]{1,2,0:T(1,128)}), s32[128,2,1]{1,2,0:T(1,128)S(1)}, u32[]{:S(2)}, u32[]{:S(2)}) async-start(s32[128,2,1]{1,2,0:T(1,128)} %bitcast.1), calls=%async_computation | async-start | bytes 131072 | tf_op jit(solution)/shard_map/all_to_all | solution.py:222
  30.5 0.7 fusion.4
  31.2 0.7 fusion.3
  31.9 6.1 %select_select_fusion = (f32[16,32,128]{2,1,0:T(8,128)}, pred[16,32,128]{2,1,0:T(8,128)(4,1)S(1)}, pred[16,32,128]{2,1,0:T(8,128)(4,1)S(1)}, pred[16,32,128]{2,1...) fusion(f32[]{:T(128)} %bitcast.31, f32[]{:T(128)} %bitcast.30, ...), kind=kLoop, calls=%fused_computation.6 | loop fusion | flops 1048576 | bytes 1048608 | tf_op jit(solution)/shard_map/jit(_where)/select_n | solution.py:211
  38.1 0.7 gather_fusion
  39.5 0.8 reduce.9
  40.5 0.6 copy-done.30
  41.7 0.7 gather_fusion.1
  43.2 1.0 all_to_all.39
  44.2 13.7 %all-to-all-start.1 = ((f32[128,2,384]{2,1,0:T(2,128)}), f32[128,2,384]{2,1,0:T(2,128)S(1)}, u32[]{:S(2)}, u32[]{:S(2)}) async-start(f32[128,2,384]{2,1,0:T(2,128)} %all_to_all.39), calls=%async_computation.1 | async-start | bytes 786432 | tf_op jit(solution)/shard_map/all_to_all | solution.py:249
  57.9 5.8 %select_select_fusion.1.cx_ref = f32[16,32,128]{2,1,0:T(8,128)} fusion(pred[16,32,128]{2,1,0:T(8,128)(4,1)S(1)} %get-tuple-element.84, pred[16,32,128]{2,1,0:T(8,128)(4,1)S(1)} %get-tuple-element.83, pred[16,32,128]{2,1,0:T(8,128)(4,1)S(1)} %get-tuple-element.82, pred[16,32,128]{2,1,0:T(8,128)(4,1)S(1)} %get-tuple-element.81, ...), kind=kLoop, calls=%fused_computation.7 | loop fusion | flops 524288 | bytes 786464 | tf_op jit(solution)/shard_map/jit(_where)/select_n | solution.py:210
  63.7 5.9 %select_select_fusion.2.cz_ref = f32[16,32,128]{2,1,0:T(8,128)} fusion(pred[16,32,128]{2,1,0:T(8,128)(4,1)S(1)} %get-tuple-element.84, pred[16,32,128]{2,1,0:T(8,128)(4,1)S(1)} %get-tuple-element.83, pred[16,32,128]{2,1,0:T(8,128)(4,1)S(1)} %get-tuple-element.82, pred[16,32,128]{2,1,0:T(8,128)(4,1)S(1)} %get-tuple-element.81, ...), kind=kLoop, calls=%fused_computation.8 | loop fusion | flops 524288 | bytes 786464 | tf_op jit(solution)/shard_map/jit(_where)/select_n | solution.py:209
  70.7 1.2 gather_fusion.2
  72.1 0.7 broadcast_in_dim.164.cg_ref
  72.8 10.1 %shard_map.138 = (f32[16,32,128]{2,1,0:T(8,128)}, f32[16,32,128]{2,1,0:T(8,128)}, f32[32,128]{1,0:T(8,128)}, f32[32,128]{1,0:T(8,128)}, f32[256,256]{1,0:T(8,128...) custom-call(s32[128]{0:T(128)} %blk_ref.7, ...), custom_call_target="tpu_custom_call" | custom-call | tf_op jit(solution)/shard_map/pallas_call | solution.py:164
  82.9 1.8 all_to_all.42
  84.7 13.8 %all-to-all-start.2 = ((f32[128,2,256]{2,1,0:T(2,128)}), f32[128,2,256]{2,1,0:T(2,128)S(1)}, u32[]{:S(2)}, u32[]{:S(2)}) async-start(f32[128,2,256]{2,1,0:T(2,128)} %all_to_all.42), calls=%async_computation.2 | async-start | bytes 524288 | tf_op jit(solution)/shard_map/all_to_all | solution.py:249
  98.8 3.4 %collective-permute-start.6 = (f32[16,128]{1,0:T(8,128)S(1)}, f32[16,128]{1,0:T(8,128)S(1)}, u32[]{:S(2)}, u32[]{:S(2)}) collective-permute-start(f32[16,128]{1,0:T(8,128)S(1)} %copy-done.40), channel_id=1, source_target_pairs={{0,8},{8,16},{16,24},{24,32},{32,40},{40,48},{48,56},{56,64},{64,7... | collective-permute-start | bytes 24584 | tf_op jit(solution)/shard_map/ppermute | solution.py:180
  102.2 5.8 %collective-permute-start.7 = (f32[16,128]{1,0:T(8,128)S(1)}, f32[16,128]{1,0:T(8,128)S(1)}, u32[]{:S(2)}, u32[]{:S(2)}) collective-permute-start(f32[16,128]{1,0:T(8,128)S(1)} %copy-done.39), channel_id=1, source_target_pairs={{8,0},{16,8},{24,16},{32,24},{40,32},{48,40},{56,48},{64,56},{72,6... | collective-permute-start | bytes 24584 | tf_op jit(solution)/shard_map/ppermute | solution.py:181
  108.0 3.4 %collective-permute-start.8 = (f32[4,128]{1,0:T(4,128)S(1)}, f32[4,128]{1,0:T(4,128)S(1)}, u32[]{:S(2)}, u32[]{:S(2)}) collective-permute-start(f32[4,128]{1,0:T(4,128)S(1)} %copy-done.46), channel_id=1, source_target_pairs={{0,2},{2,4},{4,6},{1,3},{3,5},{5,7},{8,10},{10,12},{12,14},{9,11},... | collective-permute-start | bytes 6152 | tf_op jit(solution)/shard_map/ppermute | solution.py:180
  111.4 1.3 collective-permute-start.9
  112.7 0.9 all_to_all.44.recv_ref
  113.6 3.3 %collective-permute-done.9.yhi_ref = f32[4,128]{1,0:T(4,128)S(1)} collective-permute-done((f32[4,128]{1,0:T(4,128)S(1)}, f32[4,128]{1,0:T(4,128)S(1)}, u32[]{:S(2)}, u32[]{:S(2)}) %collective-permute-start.9) | collective-permute-done | bytes 2080 | tf_op jit(solution)/shard_map/ppermute | solution.py:181
  117.5 10.1 %shard_map.139 = (f32[16,32,128]{2,1,0:T(8,128)}, f32[16,32,128]{2,1,0:T(8,128)}, f32[32,128]{1,0:T(8,128)}, f32[32,128]{1,0:T(8,128)}, f32[256,256]{1,0:T(8,128...) custom-call(s32[128]{0:T(128)} %blk_ref.7, ...), custom_call_target="tpu_custom_call" | custom-call | tf_op jit(solution)/shard_map/pallas_call | solution.py:164
  127.6 1.8 all_to_all.45
  129.5 11.1 %all-to-all-start.3 = ((f32[128,2,256]{2,1,0:T(2,128)}), f32[128,2,256]{2,1,0:T(2,128)S(1)}, u32[]{:S(2)}, u32[]{:S(2)}) async-start(f32[128,2,256]{2,1,0:T(2,128)} %all_to_all.45), calls=%async_computation.3 | async-start | bytes 524288 | tf_op jit(solution)/shard_map/all_to_all | solution.py:249
  140.7 3.4 %collective-permute-start.11 = (f32[16,128]{1,0:T(8,128)S(1)}, f32[16,128]{1,0:T(8,128)S(1)}, u32[]{:S(2)}, u32[]{:S(2)}) collective-permute-start(f32[16,128]{1,0:T(8,128)S(1)} %copy-done.37), channel_id=1, source_target_pairs={{0,8},{8,16},{16,24},{24,32},{32,40},{40,48},{48,56},{56,64},{64,7... | collective-permute-start | bytes 24584 | tf_op jit(solution)/shard_map/ppermute | solution.py:180
  144.1 5.8 %collective-permute-start.12 = (f32[16,128]{1,0:T(8,128)S(1)}, f32[16,128]{1,0:T(8,128)S(1)}, u32[]{:S(2)}, u32[]{:S(2)}) collective-permute-start(f32[16,128]{1,0:T(8,128)S(1)} %copy-done.35), channel_id=1, source_target_pairs={{8,0},{16,8},{24,16},{32,24},{40,32},{48,40},{56,48},{64,56},{72,6... | collective-permute-start | bytes 24584 | tf_op jit(solution)/shard_map/ppermute | solution.py:181
  149.9 3.4 %collective-permute-start.13 = (f32[4,128]{1,0:T(4,128)S(1)}, f32[4,128]{1,0:T(4,128)S(1)}, u32[]{:S(2)}, u32[]{:S(2)}) collective-permute-start(f32[4,128]{1,0:T(4,128)S(1)} %copy-done.43), channel_id=1, source_target_pairs={{0,2},{2,4},{4,6},{1,3},{3,5},{5,7},{8,10},{10,12},{12,14},{9,11},... | collective-permute-start | bytes 6152 | tf_op jit(solution)/shard_map/ppermute | solution.py:180
  153.3 1.3 collective-permute-start.14
  154.6 0.9 all_to_all.47.recv_ref
  155.5 3.3 %collective-permute-done.14.yhi_ref = f32[4,128]{1,0:T(4,128)S(1)} collective-permute-done((f32[4,128]{1,0:T(4,128)S(1)}, f32[4,128]{1,0:T(4,128)S(1)}, u32[]{:S(2)}, u32[]{:S(2)}) %collective-permute-start.14) | collective-permute-done | bytes 2080 | tf_op jit(solution)/shard_map/ppermute | solution.py:181
  159.4 10.1 %shard_map.140 = (f32[16,32,128]{2,1,0:T(8,128)}, f32[16,32,128]{2,1,0:T(8,128)}, f32[32,128]{1,0:T(8,128)}, f32[32,128]{1,0:T(8,128)}, f32[256,256]{1,0:T(8,128...) custom-call(s32[128]{0:T(128)} %blk_ref.7, ...), custom_call_target="tpu_custom_call" | custom-call | tf_op jit(solution)/shard_map/pallas_call | solution.py:164
  169.5 1.8 all_to_all.48
  171.3 11.1 %all-to-all-start.4 = ((f32[128,2,256]{2,1,0:T(2,128)}), f32[128,2,256]{2,1,0:T(2,128)S(1)}, u32[]{:S(2)}, u32[]{:S(2)}) async-start(f32[128,2,256]{2,1,0:T(2,128)} %all_to_all.48), calls=%async_computation.4 | async-start | bytes 524288 | tf_op jit(solution)/shard_map/all_to_all | solution.py:249
  182.6 3.4 %collective-permute-start.16 = (f32[16,128]{1,0:T(8,128)S(1)}, f32[16,128]{1,0:T(8,128)S(1)}, u32[]{:S(2)}, u32[]{:S(2)}) collective-permute-start(f32[16,128]{1,0:T(8,128)S(1)} %copy-done.38), channel_id=1, source_target_pairs={{0,8},{8,16},{16,24},{24,32},{32,40},{40,48},{48,56},{56,64},{64,7... | collective-permute-start | bytes 24584 | tf_op jit(solution)/shard_map/ppermute | solution.py:180
  186.0 5.8 %collective-permute-start.17 = (f32[16,128]{1,0:T(8,128)S(1)}, f32[16,128]{1,0:T(8,128)S(1)}, u32[]{:S(2)}, u32[]{:S(2)}) collective-permute-start(f32[16,128]{1,0:T(8,128)S(1)} %copy-done.36), channel_id=1, source_target_pairs={{8,0},{16,8},{24,16},{32,24},{40,32},{48,40},{56,48},{64,56},{72,6... | collective-permute-start | bytes 24584 | tf_op jit(solution)/shard_map/ppermute | solution.py:181
  191.8 3.4 %collective-permute-start.18 = (f32[4,128]{1,0:T(4,128)S(1)}, f32[4,128]{1,0:T(4,128)S(1)}, u32[]{:S(2)}, u32[]{:S(2)}) collective-permute-start(f32[4,128]{1,0:T(4,128)S(1)} %copy-done.44), channel_id=1, source_target_pairs={{0,2},{2,4},{4,6},{1,3},{3,5},{5,7},{8,10},{10,12},{12,14},{9,11},... | collective-permute-start | bytes 6152 | tf_op jit(solution)/shard_map/ppermute | solution.py:180
  195.2 1.3 collective-permute-start.19
  196.5 0.9 all_to_all.50.recv_ref
  197.4 3.3 %collective-permute-done.19.yhi_ref = f32[4,128]{1,0:T(4,128)S(1)} collective-permute-done((f32[4,128]{1,0:T(4,128)S(1)}, f32[4,128]{1,0:T(4,128)S(1)}, u32[]{:S(2)}, u32[]{:S(2)}) %collective-permute-start.19) | collective-permute-done | bytes 2080 | tf_op jit(solution)/shard_map/ppermute | solution.py:181
  201.3 10.1 %shard_map.141 = (f32[16,32,128]{2,1,0:T(8,128)}, f32[16,32,128]{2,1,0:T(8,128)}, f32[32,128]{1,0:T(8,128)}, f32[32,128]{1,0:T(8,128)}, f32[256,256]{1,0:T(8,128...) custom-call(s32[128]{0:T(128)} %blk_ref.7, ...), custom_call_target="tpu_custom_call" | custom-call | tf_op jit(solution)/shard_map/pallas_call | solution.py:164
  (150 shorter events, 6.8 us)
Async XLA Ops:
  0.6 6.3 %copy-start.1 = (f32[16,32,128]{2,1,0:T(8,128)S(1)}, f32[16,32,128]{2,1,0:T(8,128)}, u32[]{:S(2)}) copy-start(f32[16,32,128]{2,1,0:T(8,128)} %v_ref.1) | copy-start | bytes 786436
  0.6 15.6 %copy-start.48 = (s32[128,1]{0,1:T(1,128)S(1)}, s32[128,1]{0,1:T(1,128)}, u32[]{:S(2)}) copy-start(s32[128,1]{0,1:T(1,128)} %param.17) | copy-start | bytes 1540
  0.7 15.8 %copy-start.47 = (s32[128]{0:T(128)S(1)}, s32[128]{0:T(128)}, u32[]{:S(2)}) copy-start(s32[128]{0:T(128)} %param.16) | copy-start | bytes 1540
  0.7 16.3 %copy-start.12 = (s32[128]{0:T(128)S(1)}, s32[128]{0:T(128)}, u32[]{:S(2)}) copy-start(s32[128]{0:T(128)} %blk_ref.7) | copy-start | bytes 1540
  2.0 29.9 %copy-start.4 = (s32[16,32,128]{2,1,0:T(8,128)S(1)}, s32[16,32,128]{2,1,0:T(8,128)}, u32[]{:S(2)}) copy-start(s32[16,32,128]{2,1,0:T(8,128)} %param.13) | copy-start | bytes 786436
  2.1 69.9 %collective-permute-start.3 = (f32[4,128]{1,0:T(4,128)S(1)}, f32[4,128]{1,0:T(4,128)S(1)}, u32[]{:S(2)}, u32[]{:S(2)}) collective-permute-start(f32[4,128]{1,0:T(4,128)S(1)} %reshape_squeeze.6), channel_id=1, source_target_pairs={{0,2},{2,4},{4,6},{1,3},{3,5},{5,7},{8,10},{10,12},{12,14},{9,11},... | collective-permute-start | bytes 6152 | tf_op jit(solution)/shard_map/ppermute | solution.py:180
  5.6 66.4 %collective-permute-start.4 = (f32[4,128]{1,0:T(4,128)S(1)}, f32[4,128]{1,0:T(4,128)S(1)}, u32[]{:S(2)}, u32[]{:S(2)}) collective-permute-start(f32[4,128]{1,0:T(4,128)S(1)} %reshape_squeeze.7), channel_id=1, source_target_pairs={{2,0},{4,2},{6,4},{3,1},{5,3},{7,5},{10,8},{12,10},{14,12},{11,9},... | collective-permute-start | bytes 6152 | tf_op jit(solution)/shard_map/ppermute | solution.py:181
  6.9 65.1 %collective-permute-start.1 = (f32[16,128]{1,0:T(8,128)S(1)}, f32[16,128]{1,0:T(8,128)S(1)}, u32[]{:S(2)}, u32[]{:S(2)}) collective-permute-start(f32[16,128]{1,0:T(8,128)S(1)} %bitcast.57), channel_id=1, source_target_pairs={{0,8},{8,16},{16,24},{24,32},{32,40},{40,48},{48,56},{56,64},{64,7... | collective-permute-start | bytes 24584 | tf_op jit(solution)/shard_map/ppermute | solution.py:180
  10.4 61.6 %collective-permute-start.2 = (f32[16,128]{1,0:T(8,128)S(1)}, f32[16,128]{1,0:T(8,128)S(1)}, u32[]{:S(2)}, u32[]{:S(2)}) collective-permute-start(f32[16,128]{1,0:T(8,128)S(1)} %bitcast.56), channel_id=1, source_target_pairs={{8,0},{16,8},{24,16},{32,24},{40,32},{48,40},{56,48},{64,56},{72,6... | collective-permute-start | bytes 24584 | tf_op jit(solution)/shard_map/ppermute | solution.py:181
  16.1 55.9 %collective-permute-start = (f32[32,128]{1,0:T(8,128)S(1)}, f32[32,128]{1,0:T(8,128)S(1)}, u32[]{:S(2)}, u32[]{:S(2)}) collective-permute-start(f32[32,128]{1,0:T(8,128)S(1)} %select_bitcast_fusion), channel_id=1, source_target_pairs={{0,1},{1,0},{2,3},{3,2},{4,5},{5,4},{6,7},{7,6},{8,9},{9,8},{10,11... | collective-permute-start | bytes 49160 | tf_op jit(solution)/shard_map/ppermute | solution.py:177
  17.1 14.8 %copy-start.6 = (s32[256]{0:T(256)}, s32[256]{0:T(256)S(1)}, u32[]{:S(2)}) copy-start(s32[256]{0:T(256)S(1)} %get-tuple-element.74.sblk_ref) | copy-start | bytes 3076
  17.9 12.6 %copy-start.5 = (f32[3,8]{1,0:T(4,128)S(1)}, f32[3,8]{1,0:T(4,128)}, u32[]{:S(2)}) copy-start(f32[3,8]{1,0:T(4,128)} %param.14) | copy-start | bytes 292
  17.9 20.9 %all-to-all-start = ((s32[128,2,1]{1,2,0:T(1,128)}), s32[128,2,1]{1,2,0:T(1,128)S(1)}, u32[]{:S(2)}, u32[]{:S(2)}) async-start(s32[128,2,1]{1,2,0:T(1,128)} %bitcast.1), calls=%async_computation | async-start | bytes 131072 | tf_op jit(solution)/shard_map/all_to_all | solution.py:222
  44.2 26.3 %all-to-all-start.1 = ((f32[128,2,384]{2,1,0:T(2,128)}), f32[128,2,384]{2,1,0:T(2,128)S(1)}, u32[]{:S(2)}, u32[]{:S(2)}) async-start(f32[128,2,384]{2,1,0:T(2,128)} %all_to_all.39), calls=%async_computation.1 | async-start | bytes 786432 | tf_op jit(solution)/shard_map/all_to_all | solution.py:249
  84.7 13.8 %copy-start.34 = (f32[32,128]{1,0:T(8,128)S(1)}, f32[32,128]{1,0:T(8,128)}, u32[]{:S(2)}) copy-start(f32[32,128]{1,0:T(8,128)} %get-tuple-element.43) | copy-start | bytes 49156
  84.7 14.1 %copy-start.40 = (f32[16,128]{1,0:T(8,128)S(1)}, f32[16,128]{1,0:T(8,128)}, u32[]{:S(2)}) copy-start(f32[16,128]{1,0:T(8,128)} %get-tuple-element.44) | copy-start | bytes 24580
  84.7 17.5 %copy-start.39 = (f32[16,128]{1,0:T(8,128)S(1)}, f32[16,128]{1,0:T(8,128)}, u32[]{:S(2)}) copy-start(f32[16,128]{1,0:T(8,128)} %get-tuple-element.45) | copy-start | bytes 24580
  84.7 28.0 %all-to-all-start.2 = ((f32[128,2,256]{2,1,0:T(2,128)}), f32[128,2,256]{2,1,0:T(2,128)S(1)}, u32[]{:S(2)}, u32[]{:S(2)}) async-start(f32[128,2,256]{2,1,0:T(2,128)} %all_to_all.42), calls=%async_computation.2 | async-start | bytes 524288 | tf_op jit(solution)/shard_map/all_to_all | solution.py:249
  98.5 18.4 %collective-permute-start.5 = (f32[32,128]{1,0:T(8,128)S(1)}, f32[32,128]{1,0:T(8,128)S(1)}, u32[]{:S(2)}, u32[]{:S(2)}) collective-permute-start(f32[32,128]{1,0:T(8,128)S(1)} %copy-done.34), channel_id=1, source_target_pairs={{0,1},{1,0},{2,3},{3,2},{4,5},{5,4},{6,7},{7,6},{8,9},{9,8},{10,11... | collective-permute-start | bytes 49160 | tf_op jit(solution)/shard_map/ppermute | solution.py:177
  98.8 9.2 %copy-start.46 = (f32[4,128]{1,0:T(4,128)S(1)}, f32[4,128]{1,0:T(4,128)}, u32[]{:S(2)}) copy-start(f32[4,128]{1,0:T(4,128)} %get-tuple-element.46) | copy-start | bytes 6148
  98.8 18.1 %collective-permute-start.6 = (f32[16,128]{1,0:T(8,128)S(1)}, f32[16,128]{1,0:T(8,128)S(1)}, u32[]{:S(2)}, u32[]{:S(2)}) collective-permute-start(f32[16,128]{1,0:T(8,128)S(1)} %copy-done.40), channel_id=1, source_target_pairs={{0,8},{8,16},{16,24},{24,32},{32,40},{40,48},{48,56},{56,64},{64,7... | collective-permute-start | bytes 24584 | tf_op jit(solution)/shard_map/ppermute | solution.py:180
  102.2 9.2 %copy-start.45 = (f32[4,128]{1,0:T(4,128)S(1)}, f32[4,128]{1,0:T(4,128)}, u32[]{:S(2)}) copy-start(f32[4,128]{1,0:T(4,128)} %get-tuple-element.47) | copy-start | bytes 6148
  102.2 14.7 %collective-permute-start.7 = (f32[16,128]{1,0:T(8,128)S(1)}, f32[16,128]{1,0:T(8,128)S(1)}, u32[]{:S(2)}, u32[]{:S(2)}) collective-permute-start(f32[16,128]{1,0:T(8,128)S(1)} %copy-done.39), channel_id=1, source_target_pairs={{8,0},{16,8},{24,16},{32,24},{40,32},{48,40},{56,48},{64,56},{72,6... | collective-permute-start | bytes 24584 | tf_op jit(solution)/shard_map/ppermute | solution.py:181
  108.0 5.6 %collective-permute-start.8 = (f32[4,128]{1,0:T(4,128)S(1)}, f32[4,128]{1,0:T(4,128)S(1)}, u32[]{:S(2)}, u32[]{:S(2)}) collective-permute-start(f32[4,128]{1,0:T(4,128)S(1)} %copy-done.46), channel_id=1, source_target_pairs={{0,2},{2,4},{4,6},{1,3},{3,5},{5,7},{8,10},{10,12},{12,14},{9,11},... | collective-permute-start | bytes 6152 | tf_op jit(solution)/shard_map/ppermute | solution.py:180
  111.4 5.5 %collective-permute-start.9 = (f32[4,128]{1,0:T(4,128)S(1)}, f32[4,128]{1,0:T(4,128)S(1)}, u32[]{:S(2)}, u32[]{:S(2)}) collective-permute-start(f32[4,128]{1,0:T(4,128)S(1)} %copy-done.45), channel_id=1, source_target_pairs={{2,0},{4,2},{6,4},{3,1},{5,3},{7,5},{10,8},{12,10},{14,12},{11,9},... | collective-permute-start | bytes 6152 | tf_op jit(solution)/shard_map/ppermute | solution.py:181
  113.6 3.3 %copy-start.26 = (f32[4,128]{1,0:T(4,128)}, f32[4,128]{1,0:T(4,128)S(1)}, u32[]{:S(2)}) copy-start(f32[4,128]{1,0:T(4,128)S(1)} %collective-permute-done.8.ylo_ref) | copy-start | bytes 6148
  129.4 11.1 %copy-start.32 = (f32[32,128]{1,0:T(8,128)S(1)}, f32[32,128]{1,0:T(8,128)}, u32[]{:S(2)}) copy-start(f32[32,128]{1,0:T(8,128)} %get-tuple-element.53) | copy-start | bytes 49156
  129.4 11.2 %copy-start.37 = (f32[16,128]{1,0:T(8,128)S(1)}, f32[16,128]{1,0:T(8,128)}, u32[]{:S(2)}) copy-start(f32[16,128]{1,0:T(8,128)} %get-tuple-element.54) | copy-start | bytes 24580
  129.4 14.7 %copy-start.35 = (f32[16,128]{1,0:T(8,128)S(1)}, f32[16,128]{1,0:T(8,128)}, u32[]{:S(2)}) copy-start(f32[16,128]{1,0:T(8,128)} %get-tuple-element.55) | copy-start | bytes 24580
  129.5 25.2 %all-to-all-start.3 = ((f32[128,2,256]{2,1,0:T(2,128)}), f32[128,2,256]{2,1,0:T(2,128)S(1)}, u32[]{:S(2)}, u32[]{:S(2)}) async-start(f32[128,2,256]{2,1,0:T(2,128)} %all_to_all.45), calls=%async_computation.3 | async-start | bytes 524288 | tf_op jit(solution)/shard_map/all_to_all | solution.py:249
  140.6 18.2 %collective-permute-start.10 = (f32[32,128]{1,0:T(8,128)S(1)}, f32[32,128]{1,0:T(8,128)S(1)}, u32[]{:S(2)}, u32[]{:S(2)}) collective-permute-start(f32[32,128]{1,0:T(8,128)S(1)} %copy-done.32), channel_id=1, source_target_pairs={{0,1},{1,0},{2,3},{3,2},{4,5},{5,4},{6,7},{7,6},{8,9},{9,8},{10,11... | collective-permute-start | bytes 49160 | tf_op jit(solution)/shard_map/ppermute | solution.py:177
  140.7 9.2 %copy-start.43 = (f32[4,128]{1,0:T(4,128)S(1)}, f32[4,128]{1,0:T(4,128)}, u32[]{:S(2)}) copy-start(f32[4,128]{1,0:T(4,128)} %get-tuple-element.56) | copy-start | bytes 6148
  140.7 18.1 %collective-permute-start.11 = (f32[16,128]{1,0:T(8,128)S(1)}, f32[16,128]{1,0:T(8,128)S(1)}, u32[]{:S(2)}, u32[]{:S(2)}) collective-permute-start(f32[16,128]{1,0:T(8,128)S(1)} %copy-done.37), channel_id=1, source_target_pairs={{0,8},{8,16},{16,24},{24,32},{32,40},{40,48},{48,56},{56,64},{64,7... | collective-permute-start | bytes 24584 | tf_op jit(solution)/shard_map/ppermute | solution.py:180
  144.1 9.2 %copy-start.41 = (f32[4,128]{1,0:T(4,128)S(1)}, f32[4,128]{1,0:T(4,128)}, u32[]{:S(2)}) copy-start(f32[4,128]{1,0:T(4,128)} %get-tuple-element.57) | copy-start | bytes 6148
  144.1 14.7 %collective-permute-start.12 = (f32[16,128]{1,0:T(8,128)S(1)}, f32[16,128]{1,0:T(8,128)S(1)}, u32[]{:S(2)}, u32[]{:S(2)}) collective-permute-start(f32[16,128]{1,0:T(8,128)S(1)} %copy-done.35), channel_id=1, source_target_pairs={{8,0},{16,8},{24,16},{32,24},{40,32},{48,40},{56,48},{64,56},{72,6... | collective-permute-start | bytes 24584 | tf_op jit(solution)/shard_map/ppermute | solution.py:181
  149.9 5.6 %collective-permute-start.13 = (f32[4,128]{1,0:T(4,128)S(1)}, f32[4,128]{1,0:T(4,128)S(1)}, u32[]{:S(2)}, u32[]{:S(2)}) collective-permute-start(f32[4,128]{1,0:T(4,128)S(1)} %copy-done.43), channel_id=1, source_target_pairs={{0,2},{2,4},{4,6},{1,3},{3,5},{5,7},{8,10},{10,12},{12,14},{9,11},... | collective-permute-start | bytes 6152 | tf_op jit(solution)/shard_map/ppermute | solution.py:180
  153.3 5.5 %collective-permute-start.14 = (f32[4,128]{1,0:T(4,128)S(1)}, f32[4,128]{1,0:T(4,128)S(1)}, u32[]{:S(2)}, u32[]{:S(2)}) collective-permute-start(f32[4,128]{1,0:T(4,128)S(1)} %copy-done.41), channel_id=1, source_target_pairs={{2,0},{4,2},{6,4},{3,1},{5,3},{7,5},{10,8},{12,10},{14,12},{11,9},... | collective-permute-start | bytes 6152 | tf_op jit(solution)/shard_map/ppermute | solution.py:181
  171.3 11.1 %copy-start.33 = (f32[32,128]{1,0:T(8,128)S(1)}, f32[32,128]{1,0:T(8,128)}, u32[]{:S(2)}) copy-start(f32[32,128]{1,0:T(8,128)} %get-tuple-element.63) | copy-start | bytes 49156
  171.3 11.2 %copy-start.38 = (f32[16,128]{1,0:T(8,128)S(1)}, f32[16,128]{1,0:T(8,128)}, u32[]{:S(2)}) copy-start(f32[16,128]{1,0:T(8,128)} %get-tuple-element.64) | copy-start | bytes 24580
  171.3 14.7 %copy-start.36 = (f32[16,128]{1,0:T(8,128)S(1)}, f32[16,128]{1,0:T(8,128)}, u32[]{:S(2)}) copy-start(f32[16,128]{1,0:T(8,128)} %get-tuple-element.65) | copy-start | bytes 24580
  171.3 25.2 %all-to-all-start.4 = ((f32[128,2,256]{2,1,0:T(2,128)}), f32[128,2,256]{2,1,0:T(2,128)S(1)}, u32[]{:S(2)}, u32[]{:S(2)}) async-start(f32[128,2,256]{2,1,0:T(2,128)} %all_to_all.48), calls=%async_computation.4 | async-start | bytes 524288 | tf_op jit(solution)/shard_map/all_to_all | solution.py:249
  182.5 18.2 %collective-permute-start.15 = (f32[32,128]{1,0:T(8,128)S(1)}, f32[32,128]{1,0:T(8,128)S(1)}, u32[]{:S(2)}, u32[]{:S(2)}) collective-permute-start(f32[32,128]{1,0:T(8,128)S(1)} %copy-done.33), channel_id=1, source_target_pairs={{0,1},{1,0},{2,3},{3,2},{4,5},{5,4},{6,7},{7,6},{8,9},{9,8},{10,11... | collective-permute-start | bytes 49160 | tf_op jit(solution)/shard_map/ppermute | solution.py:177
  182.6 9.2 %copy-start.44 = (f32[4,128]{1,0:T(4,128)S(1)}, f32[4,128]{1,0:T(4,128)}, u32[]{:S(2)}) copy-start(f32[4,128]{1,0:T(4,128)} %get-tuple-element.66) | copy-start | bytes 6148
  182.6 18.1 %collective-permute-start.16 = (f32[16,128]{1,0:T(8,128)S(1)}, f32[16,128]{1,0:T(8,128)S(1)}, u32[]{:S(2)}, u32[]{:S(2)}) collective-permute-start(f32[16,128]{1,0:T(8,128)S(1)} %copy-done.38), channel_id=1, source_target_pairs={{0,8},{8,16},{16,24},{24,32},{32,40},{40,48},{48,56},{56,64},{64,7... | collective-permute-start | bytes 24584 | tf_op jit(solution)/shard_map/ppermute | solution.py:180
  186.0 9.2 %copy-start.42 = (f32[4,128]{1,0:T(4,128)S(1)}, f32[4,128]{1,0:T(4,128)}, u32[]{:S(2)}) copy-start(f32[4,128]{1,0:T(4,128)} %get-tuple-element.67) | copy-start | bytes 6148
  186.0 14.7 %collective-permute-start.17 = (f32[16,128]{1,0:T(8,128)S(1)}, f32[16,128]{1,0:T(8,128)S(1)}, u32[]{:S(2)}, u32[]{:S(2)}) collective-permute-start(f32[16,128]{1,0:T(8,128)S(1)} %copy-done.36), channel_id=1, source_target_pairs={{8,0},{16,8},{24,16},{32,24},{40,32},{48,40},{56,48},{64,56},{72,6... | collective-permute-start | bytes 24584 | tf_op jit(solution)/shard_map/ppermute | solution.py:181
  191.8 5.6 %collective-permute-start.18 = (f32[4,128]{1,0:T(4,128)S(1)}, f32[4,128]{1,0:T(4,128)S(1)}, u32[]{:S(2)}, u32[]{:S(2)}) collective-permute-start(f32[4,128]{1,0:T(4,128)S(1)} %copy-done.44), channel_id=1, source_target_pairs={{0,2},{2,4},{4,6},{1,3},{3,5},{5,7},{8,10},{10,12},{12,14},{9,11},... | collective-permute-start | bytes 6152 | tf_op jit(solution)/shard_map/ppermute | solution.py:180
  195.2 5.5 %collective-permute-start.19 = (f32[4,128]{1,0:T(4,128)S(1)}, f32[4,128]{1,0:T(4,128)S(1)}, u32[]{:S(2)}, u32[]{:S(2)}) collective-permute-start(f32[4,128]{1,0:T(4,128)S(1)} %copy-done.42), channel_id=1, source_target_pairs={{2,0},{4,2},{6,4},{3,1},{5,3},{7,5},{10,8},{12,10},{14,12},{11,9},... | collective-permute-start | bytes 6152 | tf_op jit(solution)/shard_map/ppermute | solution.py:181
  (26 other events, 23.9 us)

commit v5 on v4

--- a/solution.py
+++ b/solution.py
@@ -31,39 +31,40 @@
     return jnp.full(shape, ref[i], jnp.int32) > 0
 
 
+def split3(x):
+    a = x.astype(jnp.bfloat16)
+    rest = x - a.astype(jnp.float32)
+    b = rest.astype(jnp.bfloat16)
+    c = (rest - b.astype(jnp.float32)).astype(jnp.bfloat16)
+    return a, b, c
+
+
+def one_hot_dot(one_hot, x):
+    a, b, c = split3(x)
+    if INTERPRET:
+        one_hot, a, b, c = (t.astype(jnp.float32) for t in (one_hot, a, b, c))
+    dot = lambda part: jnp.dot(one_hot, part, preferred_element_type=jnp.float32)
+    return (dot(a) + dot(b)) + dot(c)
+
+
 def step_kernel(
-    blk_ref, slot_ref, ids_ref, sblk_ref, edge_ref,
+    edge_ref,
     v_ref, w_ref, cz_ref, cx_ref, cy_ref, recv_ref, tg_ref, g_ref,
     tv_ref, tr_ref, cg_ref, zr_ref, xlo_ref, xhi_ref, ylo_ref, yhi_ref,
+    oh_blk_ref, oh_blk_t_ref, oh_slot_ref, oh_ids_ref, oh_ids_t_ref, oh_sblk_ref,
     nv_ref, nw_ref, ntv_ref, ntr_ref, snd_ref, zs_ref, xf_ref, xl_ref, yf_ref, yl_ref,
-    iv_ref, it_ref,
 ):
     depth, rows_x, width = v_ref.shape
-    jcount = blk_ref.shape[0]
-    slots = ids_ref.shape[0]
-    iv_ref[...] = jnp.zeros(iv_ref.shape, jnp.float32)
-    it_ref[...] = jnp.zeros(it_ref.shape, jnp.float32)
-
-    def tile_body(j, carry):
-        b = blk_ref[j]
-        s = slot_ref[j]
-        z = b // rows_x
-        x = b % rows_x
-        row = v_ref[z, pl.ds(x, 1), :]
-        far = recv_ref[pl.ds(s, 1), :][:, width:2 * width]
-        cur = tg_ref[pl.ds(j, 1), :] * (far - row)
-        iv_ref[z, pl.ds(x, 1), :] = iv_ref[z, pl.ds(x, 1), :] + cur
-        return carry
-
-    lax.fori_loop(0, jcount, tile_body, 0, unroll=8)
-
-    def owner_body(k, carry):
-        t = ids_ref[k]
-        cur = g_ref[pl.ds(k, 1), :] * (tv_ref[pl.ds(t, 1), :] - recv_ref[pl.ds(k, 1), :][:, 0:width])
-        it_ref[pl.ds(t, 1), :] = it_ref[pl.ds(t, 1), :] + (-cur)
-        return carry
-
-    lax.fori_loop(0, slots, owner_body, 0, unroll=8)
+
+    v_flat = v_ref[...].reshape(depth * rows_x, width)
+    rows = one_hot_dot(oh_blk_ref[...], v_flat)
+    far = one_hot_dot(oh_slot_ref[...], recv_ref[:, width:2 * width])
+    tile_current = tg_ref[...] * (far - rows)
+    into_voxel = one_hot_dot(oh_blk_t_ref[...], tile_current)
+
+    far_volt = one_hot_dot(oh_ids_t_ref[...], tv_ref[...])
+    current = g_ref[...] * (far_volt - recv_ref[:, 0:width])
+    into_term = one_hot_dot(oh_ids_ref[...], -current)
 
     u = tv_ref[...]
     r = tr_ref[...]
@@ -72,7 +73,7 @@
     u_minus = jnp.where(lane_t == 0, u, u_minus)
     u_plus = jnp.where(lane_t == width - 1, u, u_plus)
     lap_k = u_plus + u_minus - 2.0 * u
-    react_u, new_r = cell_kinetics(u, r, 0.1 * it_ref[...])
+    react_u, new_r = cell_kinetics(u, r, 0.1 * into_term)
     ntv_ref[...] = u + cg_ref[...] * lap_k + react_u
     ntr_ref[...] = new_r
 
@@ -115,7 +116,7 @@
         lap_z = zp + zm - 2.0 * vz
         lap_x = xp + xm - 2.0 * vz
         lap_y = yp + ym - 2.0 * vz
-        react_v, new_w = cell_kinetics(vz, w_ref[z], iv_ref[z])
+        react_v, new_w = cell_kinetics(vz, w_ref[z], into_voxel[z * rows_x:(z + 1) * rows_x])
         nv = vz + (cz_ref[z] * lap_z + cx_ref[z] * lap_x + cy_ref[z] * lap_y) + react_v
         nv_ref[z] = nv
         nw_ref[z] = new_w
@@ -130,20 +131,14 @@
         yl_ref[i:i + 1, :] = y_last[i]
     zs_ref[...] = jnp.where(z_low, nv_ref[depth - 1], nv_ref[0])
 
-    def pack_body(k, carry):
-        b = sblk_ref[k]
-        t = ids_ref[k]
-        snd_ref[pl.ds(k, 1), :] = jnp.concatenate(
-            [nv_ref[b // rows_x, pl.ds(b % rows_x, 1), :], ntv_ref[pl.ds(t, 1), :]], axis=1)
-        return carry
-
-    lax.fori_loop(0, slots, pack_body, 0, unroll=8)
+    snd_ref[:, 0:width] = one_hot_dot(oh_sblk_ref[...], nv_ref[...].reshape(depth * rows_x, width))
+    snd_ref[:, width:2 * width] = one_hot_dot(oh_ids_t_ref[...], ntv_ref[...])
 
 
 def run_step(tables, state, recv, tile_gain, gains_rows, cable_rows, halos):
     volt, recovery, coef_z, coef_x, coef_y, term_volt, term_recovery = state
     depth, rows_x, width = volt.shape
-    slots = tables[2].shape[0]
+    slots = recv.shape[0]
     f32 = jnp.float32
     smem = pl.BlockSpec(memory_space=pltpu.SMEM)
     vmem = pl.BlockSpec(memory_space=pltpu.VMEM)
@@ -159,14 +154,14 @@
         jax.ShapeDtypeStruct((depth * rows_x // width, width), f32),
         jax.ShapeDtypeStruct((depth * rows_x // width, width), f32),
     )
-    operands = tuple(tables) + (volt, recovery, coef_z, coef_x, coef_y, recv, tile_gain,
-                                gains_rows, term_volt, term_recovery, cable_rows) + tuple(halos)
+    edges, one_hots = tables
+    operands = (edges, volt, recovery, coef_z, coef_x, coef_y, recv, tile_gain,
+                gains_rows, term_volt, term_recovery, cable_rows) + tuple(halos) + tuple(one_hots)
     return pl.pallas_call(
         step_kernel,
         out_shape=out_shape,
-        in_specs=[smem] * len(tables) + [vmem] * (len(operands) - len(tables)),
+        in_specs=[smem] + [vmem] * (len(operands) - 1),
         out_specs=[vmem] * len(out_shape),
-        scratch_shapes=[pltpu.VMEM(volt.shape, f32), pltpu.VMEM(term_volt.shape, f32)],
         interpret=INTERPRET,
     )(*operands)
 
@@ -232,7 +227,14 @@
         index = lax.axis_index(axis)
         edges += [index == 0, index == lax.axis_size(axis) - 1]
     edges = jnp.stack(edges + edges[:2]).astype(jnp.int32)
-    tables = (junction_block, slot, safe_ids, slot_block, edges)
+    bf16 = jnp.bfloat16
+    rows_all = jnp.arange(depth * rows_x, dtype=jnp.int32)
+    oh_blk = (junction_block[:, None] == rows_all[None, :]).astype(bf16)
+    oh_slot = (slot[:, None] == jnp.arange(slots_total, dtype=jnp.int32)[None, :]).astype(bf16)
+    oh_ids = (jnp.arange(term_count, dtype=jnp.int32)[:, None] == safe_ids[None, :]).astype(bf16)
+    oh_sblk = (slot_block[:, None] == rows_all[None, :]).astype(bf16)
+    one_hots = (oh_blk, oh_blk.T, oh_slot, oh_ids, oh_ids.T, oh_sblk)
+    tables = (edges, one_hots)
 
     flat_rows = volt.reshape(depth * rows_x, width)
     sent = jnp.concatenate([flat_rows[slot_block], term_volt[safe_ids], gain_rows], axis=1)

time: 213 us -> 198 us (0.930)
  Pallas kernels: 40.4 us -> 16.5 us
  waiting for transfers between devices: 10 us -> 14.7 us
  other arithmetic: 19.7 us -> 24.1 us
    pallas_call x4, Pallas kernels: 40.4 us -> 16.5 us  [run_step(): pl.pallas_call(step_kernel, out_shape=out_shape, in_specs=[smem] + [vmem]...]
    all_to_all x4, waiting for transfers between devices: 0.12 us -> 4.77 us  [on_device(): lax.all_to_all(sent, ('gx', 'gy'), split_axis=0, concat_axis=0, tiled=True)]
    convert_element_type x0 -> x6, other arithmetic: none -> 4.26 us  [the longest x2 1.42 us: on_device(): oh_blk = (junction_block[:, None] == rows_all[None, :]).astype(bf16)]
    unnamed x98 -> x92, local copies, waits for them, and re-layouts: 4.15 us -> 6.03 us
  transfers between devices with their start and end apart: 25 -> 25, of which waited for: 4 -> 4; matrix products, arithmetic and copies ran while one was open for 12% -> 15% of each run, Pallas kernels for 0% -> 0%
where the time goes in v5:
time: 198 us; the launch traced here: 196 us
  starting transfers between devices  116 us (59%)
  other arithmetic  24.1 us (12%)
  local copies, waits for them, and re-layouts  23.4 us (12%)
  Pallas kernels  16.5 us (8%)
  waiting for transfers between devices  14.7 us (7%)
    all_to_all x4, starting transfers between devices, on_device(): lax.all_to_all(sent, ('gx', 'gy'), split_axis=0, concat_axis=0, tiled=True)  48 us
    ppermute x8, starting transfers between devices, exchange_halos(): lax.ppermute(first, axis, [(i + 1, i) for i in range(count - 1)])  28.1 us
    ppermute x8, starting transfers between devices, exchange_halos(): lax.ppermute(last, axis, [(i, i + 1) for i in range(count - 1)])  27.2 us
    pallas_call x4, Pallas kernels, run_step(): pl.pallas_call(step_kernel, out_shape=out_shape, in_specs=[smem] + [vmem]...  16.5 us
    all_to_all x1, starting transfers between devices, on_device(): lax.all_to_all(slot_term, ('gx', 'gy'), split_axis=0, concat_axis=0, tile...  12.5 us
    ppermute x8, waiting for transfers between devices, exchange_halos(): lax.ppermute(first, axis, [(i + 1, i) for i in range(count - 1)])  9.86 us
    all_to_all x8, local copies, waits for them, and re-layouts, on_device(): lax.all_to_all(sent, ('gx', 'gy'), split_axis=0, concat_axis=0, tiled=True)  9.29 us
    select_n x1, other arithmetic, on_device(): coef_y = jnp.where(hit, fiber_table[2, klass], coef_y)  6.07 us
  transfers between devices with their start and end apart: 25, of which 4 were waited for; matrix products, arithmetic and copies ran while one was open for 15% of the time, Pallas kernels for 0%

profile of v5, /device:TPU:128, one launch (start us, length us, event | category | flops | bytes accessed | tf_op | source)
XLA Modules:
  0.0 196.4 jit_solution(3791051217500465789)
XLA Ops:
  0.6 1.4 slice_reduce_fusion
  2.1 3.4 %collective-permute-start.3 = (f32[4,128]{1,0:T(4,128)S(1)}, f32[4,128]{1,0:T(4,128)S(1)}, u32[]{:S(2)}, u32[]{:S(2)}) collective-permute-start(f32[4,128]{1,0:T(4,128)S(1)} %reshape_squeeze.6), channel_id=1, source_target_pairs={{0,2},{2,4},{4,6},{1,3},{3,5},{5,7},{8,10},{10,12},{12,14},{9,11},... | collective-permute-start | bytes 6152 | tf_op jit(solution)/shard_map/ppermute | solution.py:175
  5.6 1.3 collective-permute-start.4
  6.9 3.5 %collective-permute-start.1 = (f32[16,128]{1,0:T(8,128)S(1)}, f32[16,128]{1,0:T(8,128)S(1)}, u32[]{:S(2)}, u32[]{:S(2)}) collective-permute-start(f32[16,128]{1,0:T(8,128)S(1)} %bitcast.61), channel_id=1, source_target_pairs={{0,8},{8,16},{16,24},{24,32},{32,40},{40,48},{48,56},{56,64},{64,7... | collective-permute-start | bytes 24584 | tf_op jit(solution)/shard_map/ppermute | solution.py:175
  10.4 5.7 %collective-permute-start.2 = (f32[16,128]{1,0:T(8,128)S(1)}, f32[16,128]{1,0:T(8,128)S(1)}, u32[]{:S(2)}, u32[]{:S(2)}) collective-permute-start(f32[16,128]{1,0:T(8,128)S(1)} %bitcast.60), channel_id=1, source_target_pairs={{8,0},{16,8},{24,16},{32,24},{40,32},{48,40},{56,48},{64,56},{72,6... | collective-permute-start | bytes 24584 | tf_op jit(solution)/shard_map/ppermute | solution.py:176
  18.2 0.8 sub.7
  19.0 12.5 %all-to-all-start = ((s32[128,2,1]{1,2,0:T(1,128)}), s32[128,2,1]{1,2,0:T(1,128)S(1)}, u32[]{:S(2)}, u32[]{:S(2)}) async-start(s32[128,2,1]{1,2,0:T(1,128)} %bitcast.34), calls=%async_computation | async-start | bytes 131072 | tf_op jit(solution)/shard_map/all_to_all | solution.py:217
  34.3 0.7 fusion.1.oh_blk_ref
  35.0 0.8 fusion.oh_sblk_ref
  36.5 6.1 %select_select_fusion = (f32[16,32,128]{2,1,0:T(8,128)}, pred[16,32,128]{2,1,0:T(8,128)(4,1)S(1)}, pred[16,32,128]{2,1,0:T(8,128)(4,1)S(1)}, pred[16,32,128]{2,1...) fusion(f32[]{:T(128)} %bitcast.29, f32[]{:T(128)} %bitcast.28, ...), kind=kLoop, calls=%fused_computation.10 | loop fusion | flops 1048576 | bytes 1048608 | tf_op jit(solution)/shard_map/jit(_where)/select_n | solution.py:206
  42.6 5.9 %select_select_fusion.1.cx_ref = f32[16,32,128]{2,1,0:T(8,128)} fusion(pred[16,32,128]{2,1,0:T(8,128)(4,1)S(1)} %get-tuple-element.84, pred[16,32,128]{2,1,0:T(8,128)(4,1)S(1)} %get-tuple-element.83, pred[16,32,128]{2,1,0:T(8,128)(4,1)S(1)} %get-tuple-element.82, pred[16,32,128]{2,1,0:T(8,128)(4,1)S(1)} %get-tuple-element.81, ...), kind=kLoop, calls=%fused_computation.11 | loop fusion | flops 524288 | bytes 786464 | tf_op jit(solution)/shard_map/jit(_where)/select_n | solution.py:205
  49.2 0.7 gather_fusion
  51.4 0.8 reduce.9
  53.0 0.7 gather_fusion.1
  54.4 1.0 all_to_all.39
  55.4 13.7 %all-to-all-start.1 = ((f32[128,2,384]{2,1,0:T(2,128)}), f32[128,2,384]{2,1,0:T(2,128)S(1)}, u32[]{:S(2)}, u32[]{:S(2)}) async-start(f32[128,2,384]{2,1,0:T(2,128)} %all_to_all.39), calls=%async_computation.1 | async-start | bytes 786432 | tf_op jit(solution)/shard_map/all_to_all | solution.py:251
  69.2 5.9 %select_select_fusion.2.cz_ref = f32[16,32,128]{2,1,0:T(8,128)} fusion(pred[16,32,128]{2,1,0:T(8,128)(4,1)S(1)} %get-tuple-element.84, pred[16,32,128]{2,1,0:T(8,128)(4,1)S(1)} %get-tuple-element.83, pred[16,32,128]{2,1,0:T(8,128)(4,1)S(1)} %get-tuple-element.82, pred[16,32,128]{2,1,0:T(8,128)(4,1)S(1)} %get-tuple-element.81, ...), kind=kLoop, calls=%fused_computation.12 | loop fusion | flops 524288 | bytes 786464 | tf_op jit(solution)/shard_map/jit(_where)/select_n | solution.py:204
  75.0 0.7 fusion.4.oh_ids_t_ref
  76.4 4.8 %all-to-all-done.1 = f32[128,2,384]{2,1,0:T(2,128)S(1)} async-done(((f32[128,2,384]{2,1,0:T(2,128)}), f32[128,2,384]{2,1,0:T(2,128)S(1)}, u32[]{:S(2)}, u32[]{:S(2)}) %all-to-all-start.1) | async-done | bytes 393248 | tf_op jit(solution)/shard_map/all_to_all | solution.py:251
  81.5 1.2 gather_fusion.2
  83.5 4.2 %shard_map.138 = (f32[16,32,128]{2,1,0:T(8,128)}, f32[16,32,128]{2,1,0:T(8,128)}, f32[32,128]{1,0:T(8,128)}, f32[32,128]{1,0:T(8,128)}, f32[256,256]{1,0:T(8,128...) custom-call(s32[8]{0:T(128)} %convert_element_type.22.edge_ref, ...), custom_call_target="tpu_custom_call" | custom-call | tf_op jit(solution)/shard_map/pallas_call | solution.py:160
  87.7 1.8 all_to_all.42
  89.5 12.0 %all-to-all-start.2 = ((f32[128,2,256]{2,1,0:T(2,128)}), f32[128,2,256]{2,1,0:T(2,128)S(1)}, u32[]{:S(2)}, u32[]{:S(2)}) async-start(f32[128,2,256]{2,1,0:T(2,128)} %all_to_all.42), calls=%async_computation.2 | async-start | bytes 524288 | tf_op jit(solution)/shard_map/all_to_all | solution.py:251
  101.6 3.4 %collective-permute-start.6 = (f32[16,128]{1,0:T(8,128)S(1)}, f32[16,128]{1,0:T(8,128)S(1)}, u32[]{:S(2)}, u32[]{:S(2)}) collective-permute-start(f32[16,128]{1,0:T(8,128)S(1)} %copy-done.39), channel_id=1, source_target_pairs={{0,8},{8,16},{16,24},{24,32},{32,40},{40,48},{48,56},{56,64},{64,7... | collective-permute-start | bytes 24584 | tf_op jit(solution)/shard_map/ppermute | solution.py:175
  105.0 5.8 %collective-permute-start.7 = (f32[16,128]{1,0:T(8,128)S(1)}, f32[16,128]{1,0:T(8,128)S(1)}, u32[]{:S(2)}, u32[]{:S(2)}) collective-permute-start(f32[16,128]{1,0:T(8,128)S(1)} %copy-done.38), channel_id=1, source_target_pairs={{8,0},{16,8},{24,16},{32,24},{40,32},{48,40},{56,48},{64,56},{72,6... | collective-permute-start | bytes 24584 | tf_op jit(solution)/shard_map/ppermute | solution.py:176
  110.8 3.4 %collective-permute-start.8 = (f32[4,128]{1,0:T(4,128)S(1)}, f32[4,128]{1,0:T(4,128)S(1)}, u32[]{:S(2)}, u32[]{:S(2)}) collective-permute-start(f32[4,128]{1,0:T(4,128)S(1)} %copy-done.45), channel_id=1, source_target_pairs={{0,2},{2,4},{4,6},{1,3},{3,5},{5,7},{8,10},{10,12},{12,14},{9,11},... | collective-permute-start | bytes 6152 | tf_op jit(solution)/shard_map/ppermute | solution.py:175
  114.2 1.3 collective-permute-start.9
  115.5 0.9 all_to_all.44.recv_ref
  116.4 3.3 %collective-permute-done.9.yhi_ref = f32[4,128]{1,0:T(4,128)S(1)} collective-permute-done((f32[4,128]{1,0:T(4,128)S(1)}, f32[4,128]{1,0:T(4,128)S(1)}, u32[]{:S(2)}, u32[]{:S(2)}) %collective-permute-start.9) | collective-permute-done | bytes 2080 | tf_op jit(solution)/shard_map/ppermute | solution.py:176
  120.3 4.1 %shard_map.139 = (f32[16,32,128]{2,1,0:T(8,128)}, f32[16,32,128]{2,1,0:T(8,128)}, f32[32,128]{1,0:T(8,128)}, f32[32,128]{1,0:T(8,128)}, f32[256,256]{1,0:T(8,128...) custom-call(s32[8]{0:T(128)} %convert_element_type.22.edge_ref, ...), custom_call_target="tpu_custom_call" | custom-call | tf_op jit(solution)/shard_map/pallas_call | solution.py:160
  124.4 1.8 all_to_all.45
  126.2 11.1 %all-to-all-start.3 = ((f32[128,2,256]{2,1,0:T(2,128)}), f32[128,2,256]{2,1,0:T(2,128)S(1)}, u32[]{:S(2)}, u32[]{:S(2)}) async-start(f32[128,2,256]{2,1,0:T(2,128)} %all_to_all.45), calls=%async_computation.3 | async-start | bytes 524288 | tf_op jit(solution)/shard_map/all_to_all | solution.py:251
  137.5 3.4 %collective-permute-start.11 = (f32[16,128]{1,0:T(8,128)S(1)}, f32[16,128]{1,0:T(8,128)S(1)}, u32[]{:S(2)}, u32[]{:S(2)}) collective-permute-start(f32[16,128]{1,0:T(8,128)S(1)} %copy-done.36), channel_id=1, source_target_pairs={{0,8},{8,16},{16,24},{24,32},{32,40},{40,48},{48,56},{56,64},{64,7... | collective-permute-start | bytes 24584 | tf_op jit(solution)/shard_map/ppermute | solution.py:175
  140.9 5.8 %collective-permute-start.12 = (f32[16,128]{1,0:T(8,128)S(1)}, f32[16,128]{1,0:T(8,128)S(1)}, u32[]{:S(2)}, u32[]{:S(2)}) collective-permute-start(f32[16,128]{1,0:T(8,128)S(1)} %copy-done.34), channel_id=1, source_target_pairs={{8,0},{16,8},{24,16},{32,24},{40,32},{48,40},{56,48},{64,56},{72,6... | collective-permute-start | bytes 24584 | tf_op jit(solution)/shard_map/ppermute | solution.py:176
  146.7 3.4 %collective-permute-start.13 = (f32[4,128]{1,0:T(4,128)S(1)}, f32[4,128]{1,0:T(4,128)S(1)}, u32[]{:S(2)}, u32[]{:S(2)}) collective-permute-start(f32[4,128]{1,0:T(4,128)S(1)} %copy-done.42), channel_id=1, source_target_pairs={{0,2},{2,4},{4,6},{1,3},{3,5},{5,7},{8,10},{10,12},{12,14},{9,11},... | collective-permute-start | bytes 6152 | tf_op jit(solution)/shard_map/ppermute | solution.py:175
  150.1 1.3 collective-permute-start.14
  151.4 0.9 all_to_all.47.recv_ref
  152.3 3.3 %collective-permute-done.14.yhi_ref = f32[4,128]{1,0:T(4,128)S(1)} collective-permute-done((f32[4,128]{1,0:T(4,128)S(1)}, f32[4,128]{1,0:T(4,128)S(1)}, u32[]{:S(2)}, u32[]{:S(2)}) %collective-permute-start.14) | collective-permute-done | bytes 2080 | tf_op jit(solution)/shard_map/ppermute | solution.py:176
  156.2 4.1 %shard_map.140 = (f32[16,32,128]{2,1,0:T(8,128)}, f32[16,32,128]{2,1,0:T(8,128)}, f32[32,128]{1,0:T(8,128)}, f32[32,128]{1,0:T(8,128)}, f32[256,256]{1,0:T(8,128...) custom-call(s32[8]{0:T(128)} %convert_element_type.22.edge_ref, ...), custom_call_target="tpu_custom_call" | custom-call | tf_op jit(solution)/shard_map/pallas_call | solution.py:160
  160.3 1.8 all_to_all.48
  162.1 11.1 %all-to-all-start.4 = ((f32[128,2,256]{2,1,0:T(2,128)}), f32[128,2,256]{2,1,0:T(2,128)S(1)}, u32[]{:S(2)}, u32[]{:S(2)}) async-start(f32[128,2,256]{2,1,0:T(2,128)} %all_to_all.48), calls=%async_computation.4 | async-start | bytes 524288 | tf_op jit(solution)/shard_map/all_to_all | solution.py:251
  173.4 3.4 %collective-permute-start.16 = (f32[16,128]{1,0:T(8,128)S(1)}, f32[16,128]{1,0:T(8,128)S(1)}, u32[]{:S(2)}, u32[]{:S(2)}) collective-permute-start(f32[16,128]{1,0:T(8,128)S(1)} %copy-done.37), channel_id=1, source_target_pairs={{0,8},{8,16},{16,24},{24,32},{32,40},{40,48},{48,56},{56,64},{64,7... | collective-permute-start | bytes 24584 | tf_op jit(solution)/shard_map/ppermute | solution.py:175
  176.8 5.8 %collective-permute-start.17 = (f32[16,128]{1,0:T(8,128)S(1)}, f32[16,128]{1,0:T(8,128)S(1)}, u32[]{:S(2)}, u32[]{:S(2)}) collective-permute-start(f32[16,128]{1,0:T(8,128)S(1)} %copy-done.35), channel_id=1, source_target_pairs={{8,0},{16,8},{24,16},{32,24},{40,32},{48,40},{56,48},{64,56},{72,6... | collective-permute-start | bytes 24584 | tf_op jit(solution)/shard_map/ppermute | solution.py:176
  182.6 3.4 %collective-permute-start.18 = (f32[4,128]{1,0:T(4,128)S(1)}, f32[4,128]{1,0:T(4,128)S(1)}, u32[]{:S(2)}, u32[]{:S(2)}) collective-permute-start(f32[4,128]{1,0:T(4,128)S(1)} %copy-done.43), channel_id=1, source_target_pairs={{0,2},{2,4},{4,6},{1,3},{3,5},{5,7},{8,10},{10,12},{12,14},{9,11},... | collective-permute-start | bytes 6152 | tf_op jit(solution)/shard_map/ppermute | solution.py:175
  186.0 1.3 collective-permute-start.19
  187.3 0.9 all_to_all.50.recv_ref
  188.2 3.3 %collective-permute-done.19.yhi_ref = f32[4,128]{1,0:T(4,128)S(1)} collective-permute-done((f32[4,128]{1,0:T(4,128)S(1)}, f32[4,128]{1,0:T(4,128)S(1)}, u32[]{:S(2)}, u32[]{:S(2)}) %collective-permute-start.19) | collective-permute-done | bytes 2080 | tf_op jit(solution)/shard_map/ppermute | solution.py:176
  192.1 4.1 %shard_map.141 = (f32[16,32,128]{2,1,0:T(8,128)}, f32[16,32,128]{2,1,0:T(8,128)}, f32[32,128]{1,0:T(8,128)}, f32[32,128]{1,0:T(8,128)}, f32[256,256]{1,0:T(8,128...) custom-call(s32[8]{0:T(128)} %convert_element_type.22.edge_ref, ...), custom_call_target="tpu_custom_call" | custom-call | tf_op jit(solution)/shard_map/pallas_call | solution.py:160
  (149 shorter events, 13.1 us)
Async XLA Ops:
  0.6 6.2 %copy-start.1 = (f32[16,32,128]{2,1,0:T(8,128)S(1)}, f32[16,32,128]{2,1,0:T(8,128)}, u32[]{:S(2)}) copy-start(f32[16,32,128]{2,1,0:T(8,128)} %v_ref.1) | copy-start | bytes 786436
  2.1 80.6 %collective-permute-start.3 = (f32[4,128]{1,0:T(4,128)S(1)}, f32[4,128]{1,0:T(4,128)S(1)}, u32[]{:S(2)}, u32[]{:S(2)}) collective-permute-start(f32[4,128]{1,0:T(4,128)S(1)} %reshape_squeeze.6), channel_id=1, source_target_pairs={{0,2},{2,4},{4,6},{1,3},{3,5},{5,7},{8,10},{10,12},{12,14},{9,11},... | collective-permute-start | bytes 6152 | tf_op jit(solution)/shard_map/ppermute | solution.py:175
  5.6 77.1 %collective-permute-start.4 = (f32[4,128]{1,0:T(4,128)S(1)}, f32[4,128]{1,0:T(4,128)S(1)}, u32[]{:S(2)}, u32[]{:S(2)}) collective-permute-start(f32[4,128]{1,0:T(4,128)S(1)} %reshape_squeeze.7), channel_id=1, source_target_pairs={{2,0},{4,2},{6,4},{3,1},{5,3},{7,5},{10,8},{12,10},{14,12},{11,9},... | collective-permute-start | bytes 6152 | tf_op jit(solution)/shard_map/ppermute | solution.py:176
  6.9 75.8 %collective-permute-start.1 = (f32[16,128]{1,0:T(8,128)S(1)}, f32[16,128]{1,0:T(8,128)S(1)}, u32[]{:S(2)}, u32[]{:S(2)}) collective-permute-start(f32[16,128]{1,0:T(8,128)S(1)} %bitcast.61), channel_id=1, source_target_pairs={{0,8},{8,16},{16,24},{24,32},{32,40},{40,48},{48,56},{56,64},{64,7... | collective-permute-start | bytes 24584 | tf_op jit(solution)/shard_map/ppermute | solution.py:175
  10.4 72.4 %collective-permute-start.2 = (f32[16,128]{1,0:T(8,128)S(1)}, f32[16,128]{1,0:T(8,128)S(1)}, u32[]{:S(2)}, u32[]{:S(2)}) collective-permute-start(f32[16,128]{1,0:T(8,128)S(1)} %bitcast.60), channel_id=1, source_target_pairs={{8,0},{16,8},{24,16},{32,24},{40,32},{48,40},{56,48},{64,56},{72,6... | collective-permute-start | bytes 24584 | tf_op jit(solution)/shard_map/ppermute | solution.py:176
  16.1 66.7 %collective-permute-start = (f32[32,128]{1,0:T(8,128)S(1)}, f32[32,128]{1,0:T(8,128)S(1)}, u32[]{:S(2)}, u32[]{:S(2)}) collective-permute-start(f32[32,128]{1,0:T(8,128)S(1)} %select_bitcast_fusion), channel_id=1, source_target_pairs={{0,1},{1,0},{2,3},{3,2},{4,5},{5,4},{6,7},{7,6},{8,9},{9,8},{10,11... | collective-permute-start | bytes 49160 | tf_op jit(solution)/shard_map/ppermute | solution.py:172
  19.0 30.9 %all-to-all-start = ((s32[128,2,1]{1,2,0:T(1,128)}), s32[128,2,1]{1,2,0:T(1,128)S(1)}, u32[]{:S(2)}, u32[]{:S(2)}) async-start(s32[128,2,1]{1,2,0:T(1,128)} %bitcast.34), calls=%async_computation | async-start | bytes 131072 | tf_op jit(solution)/shard_map/all_to_all | solution.py:217
  34.3 2.2 %copy-start.4 = (s32[16,32,128]{2,1,0:T(8,128)S(1)}, s32[16,32,128]{2,1,0:T(8,128)}, u32[]{:S(2)}) copy-start(s32[16,32,128]{2,1,0:T(8,128)} %param.13) | copy-start | bytes 786436
  55.4 25.7 %all-to-all-start.1 = ((f32[128,2,384]{2,1,0:T(2,128)}), f32[128,2,384]{2,1,0:T(2,128)S(1)}, u32[]{:S(2)}, u32[]{:S(2)}) async-start(f32[128,2,384]{2,1,0:T(2,128)} %all_to_all.39), calls=%async_computation.1 | async-start | bytes 786432 | tf_op jit(solution)/shard_map/all_to_all | solution.py:251
  81.4 1.3 copy-start.3
  81.4 1.3 copy-start.30
  82.7 0.8 copy-start.20
  89.5 12.0 %copy-start.33 = (f32[32,128]{1,0:T(8,128)S(1)}, f32[32,128]{1,0:T(8,128)}, u32[]{:S(2)}) copy-start(f32[32,128]{1,0:T(8,128)} %get-tuple-element.43) | copy-start | bytes 49156
  89.5 12.1 %copy-start.39 = (f32[16,128]{1,0:T(8,128)S(1)}, f32[16,128]{1,0:T(8,128)}, u32[]{:S(2)}) copy-start(f32[16,128]{1,0:T(8,128)} %get-tuple-element.44) | copy-start | bytes 24580
  89.5 15.5 %copy-start.38 = (f32[16,128]{1,0:T(8,128)S(1)}, f32[16,128]{1,0:T(8,128)}, u32[]{:S(2)}) copy-start(f32[16,128]{1,0:T(8,128)} %get-tuple-element.45) | copy-start | bytes 24580
  89.5 26.0 %all-to-all-start.2 = ((f32[128,2,256]{2,1,0:T(2,128)}), f32[128,2,256]{2,1,0:T(2,128)S(1)}, u32[]{:S(2)}, u32[]{:S(2)}) async-start(f32[128,2,256]{2,1,0:T(2,128)} %all_to_all.42), calls=%async_computation.2 | async-start | bytes 524288 | tf_op jit(solution)/shard_map/all_to_all | solution.py:251
  101.5 18.2 %collective-permute-start.5 = (f32[32,128]{1,0:T(8,128)S(1)}, f32[32,128]{1,0:T(8,128)S(1)}, u32[]{:S(2)}, u32[]{:S(2)}) collective-permute-start(f32[32,128]{1,0:T(8,128)S(1)} %copy-done.33), channel_id=1, source_target_pairs={{0,1},{1,0},{2,3},{3,2},{4,5},{5,4},{6,7},{7,6},{8,9},{9,8},{10,11... | collective-permute-start | bytes 49160 | tf_op jit(solution)/shard_map/ppermute | solution.py:172
  101.6 9.2 %copy-start.45 = (f32[4,128]{1,0:T(4,128)S(1)}, f32[4,128]{1,0:T(4,128)}, u32[]{:S(2)}) copy-start(f32[4,128]{1,0:T(4,128)} %get-tuple-element.46) | copy-start | bytes 6148
  101.6 18.1 %collective-permute-start.6 = (f32[16,128]{1,0:T(8,128)S(1)}, f32[16,128]{1,0:T(8,128)S(1)}, u32[]{:S(2)}, u32[]{:S(2)}) collective-permute-start(f32[16,128]{1,0:T(8,128)S(1)} %copy-done.39), channel_id=1, source_target_pairs={{0,8},{8,16},{16,24},{24,32},{32,40},{40,48},{48,56},{56,64},{64,7... | collective-permute-start | bytes 24584 | tf_op jit(solution)/shard_map/ppermute | solution.py:175
  105.0 9.2 %copy-start.44 = (f32[4,128]{1,0:T(4,128)S(1)}, f32[4,128]{1,0:T(4,128)}, u32[]{:S(2)}) copy-start(f32[4,128]{1,0:T(4,128)} %get-tuple-element.47) | copy-start | bytes 6148
  105.0 14.7 %collective-permute-start.7 = (f32[16,128]{1,0:T(8,128)S(1)}, f32[16,128]{1,0:T(8,128)S(1)}, u32[]{:S(2)}, u32[]{:S(2)}) collective-permute-start(f32[16,128]{1,0:T(8,128)S(1)} %copy-done.38), channel_id=1, source_target_pairs={{8,0},{16,8},{24,16},{32,24},{40,32},{48,40},{56,48},{64,56},{72,6... | collective-permute-start | bytes 24584 | tf_op jit(solution)/shard_map/ppermute | solution.py:176
  110.8 5.6 %collective-permute-start.8 = (f32[4,128]{1,0:T(4,128)S(1)}, f32[4,128]{1,0:T(4,128)S(1)}, u32[]{:S(2)}, u32[]{:S(2)}) collective-permute-start(f32[4,128]{1,0:T(4,128)S(1)} %copy-done.45), channel_id=1, source_target_pairs={{0,2},{2,4},{4,6},{1,3},{3,5},{5,7},{8,10},{10,12},{12,14},{9,11},... | collective-permute-start | bytes 6152 | tf_op jit(solution)/shard_map/ppermute | solution.py:175
  114.2 5.5 %collective-permute-start.9 = (f32[4,128]{1,0:T(4,128)S(1)}, f32[4,128]{1,0:T(4,128)S(1)}, u32[]{:S(2)}, u32[]{:S(2)}) collective-permute-start(f32[4,128]{1,0:T(4,128)S(1)} %copy-done.44), channel_id=1, source_target_pairs={{2,0},{4,2},{6,4},{3,1},{5,3},{7,5},{10,8},{12,10},{14,12},{11,9},... | collective-permute-start | bytes 6152 | tf_op jit(solution)/shard_map/ppermute | solution.py:176
  116.4 3.3 %copy-start.24 = (f32[4,128]{1,0:T(4,128)}, f32[4,128]{1,0:T(4,128)S(1)}, u32[]{:S(2)}) copy-start(f32[4,128]{1,0:T(4,128)S(1)} %collective-permute-done.8.ylo_ref) | copy-start | bytes 6148
  126.2 11.1 %copy-start.31 = (f32[32,128]{1,0:T(8,128)S(1)}, f32[32,128]{1,0:T(8,128)}, u32[]{:S(2)}) copy-start(f32[32,128]{1,0:T(8,128)} %get-tuple-element.53) | copy-start | bytes 49156
  126.2 11.2 %copy-start.36 = (f32[16,128]{1,0:T(8,128)S(1)}, f32[16,128]{1,0:T(8,128)}, u32[]{:S(2)}) copy-start(f32[16,128]{1,0:T(8,128)} %get-tuple-element.54) | copy-start | bytes 24580
  126.2 14.7 %copy-start.34 = (f32[16,128]{1,0:T(8,128)S(1)}, f32[16,128]{1,0:T(8,128)}, u32[]{:S(2)}) copy-start(f32[16,128]{1,0:T(8,128)} %get-tuple-element.55) | copy-start | bytes 24580
  126.2 25.2 %all-to-all-start.3 = ((f32[128,2,256]{2,1,0:T(2,128)}), f32[128,2,256]{2,1,0:T(2,128)S(1)}, u32[]{:S(2)}, u32[]{:S(2)}) async-start(f32[128,2,256]{2,1,0:T(2,128)} %all_to_all.45), calls=%async_computation.3 | async-start | bytes 524288 | tf_op jit(solution)/shard_map/all_to_all | solution.py:251
  137.4 18.2 %collective-permute-start.10 = (f32[32,128]{1,0:T(8,128)S(1)}, f32[32,128]{1,0:T(8,128)S(1)}, u32[]{:S(2)}, u32[]{:S(2)}) collective-permute-start(f32[32,128]{1,0:T(8,128)S(1)} %copy-done.31), channel_id=1, source_target_pairs={{0,1},{1,0},{2,3},{3,2},{4,5},{5,4},{6,7},{7,6},{8,9},{9,8},{10,11... | collective-permute-start | bytes 49160 | tf_op jit(solution)/shard_map/ppermute | solution.py:172
  137.5 9.2 %copy-start.42 = (f32[4,128]{1,0:T(4,128)S(1)}, f32[4,128]{1,0:T(4,128)}, u32[]{:S(2)}) copy-start(f32[4,128]{1,0:T(4,128)} %get-tuple-element.56) | copy-start | bytes 6148
  137.5 18.1 %collective-permute-start.11 = (f32[16,128]{1,0:T(8,128)S(1)}, f32[16,128]{1,0:T(8,128)S(1)}, u32[]{:S(2)}, u32[]{:S(2)}) collective-permute-start(f32[16,128]{1,0:T(8,128)S(1)} %copy-done.36), channel_id=1, source_target_pairs={{0,8},{8,16},{16,24},{24,32},{32,40},{40,48},{48,56},{56,64},{64,7... | collective-permute-start | bytes 24584 | tf_op jit(solution)/shard_map/ppermute | solution.py:175
  140.9 9.2 %copy-start.40 = (f32[4,128]{1,0:T(4,128)S(1)}, f32[4,128]{1,0:T(4,128)}, u32[]{:S(2)}) copy-start(f32[4,128]{1,0:T(4,128)} %get-tuple-element.57) | copy-start | bytes 6148
  140.9 14.7 %collective-permute-start.12 = (f32[16,128]{1,0:T(8,128)S(1)}, f32[16,128]{1,0:T(8,128)S(1)}, u32[]{:S(2)}, u32[]{:S(2)}) collective-permute-start(f32[16,128]{1,0:T(8,128)S(1)} %copy-done.34), channel_id=1, source_target_pairs={{8,0},{16,8},{24,16},{32,24},{40,32},{48,40},{56,48},{64,56},{72,6... | collective-permute-start | bytes 24584 | tf_op jit(solution)/shard_map/ppermute | solution.py:176
  146.7 5.6 %collective-permute-start.13 = (f32[4,128]{1,0:T(4,128)S(1)}, f32[4,128]{1,0:T(4,128)S(1)}, u32[]{:S(2)}, u32[]{:S(2)}) collective-permute-start(f32[4,128]{1,0:T(4,128)S(1)} %copy-done.42), channel_id=1, source_target_pairs={{0,2},{2,4},{4,6},{1,3},{3,5},{5,7},{8,10},{10,12},{12,14},{9,11},... | collective-permute-start | bytes 6152 | tf_op jit(solution)/shard_map/ppermute | solution.py:175
  150.1 5.5 %collective-permute-start.14 = (f32[4,128]{1,0:T(4,128)S(1)}, f32[4,128]{1,0:T(4,128)S(1)}, u32[]{:S(2)}, u32[]{:S(2)}) collective-permute-start(f32[4,128]{1,0:T(4,128)S(1)} %copy-done.40), channel_id=1, source_target_pairs={{2,0},{4,2},{6,4},{3,1},{5,3},{7,5},{10,8},{12,10},{14,12},{11,9},... | collective-permute-start | bytes 6152 | tf_op jit(solution)/shard_map/ppermute | solution.py:176
  152.3 3.3 %copy-start.25 = (f32[4,128]{1,0:T(4,128)}, f32[4,128]{1,0:T(4,128)S(1)}, u32[]{:S(2)}) copy-start(f32[4,128]{1,0:T(4,128)S(1)} %collective-permute-done.13.ylo_ref) | copy-start | bytes 6148
  162.1 11.1 %copy-start.32 = (f32[32,128]{1,0:T(8,128)S(1)}, f32[32,128]{1,0:T(8,128)}, u32[]{:S(2)}) copy-start(f32[32,128]{1,0:T(8,128)} %get-tuple-element.63) | copy-start | bytes 49156
  162.1 11.2 %copy-start.37 = (f32[16,128]{1,0:T(8,128)S(1)}, f32[16,128]{1,0:T(8,128)}, u32[]{:S(2)}) copy-start(f32[16,128]{1,0:T(8,128)} %get-tuple-element.64) | copy-start | bytes 24580
  162.1 14.7 %copy-start.35 = (f32[16,128]{1,0:T(8,128)S(1)}, f32[16,128]{1,0:T(8,128)}, u32[]{:S(2)}) copy-start(f32[16,128]{1,0:T(8,128)} %get-tuple-element.65) | copy-start | bytes 24580
  162.1 25.2 %all-to-all-start.4 = ((f32[128,2,256]{2,1,0:T(2,128)}), f32[128,2,256]{2,1,0:T(2,128)S(1)}, u32[]{:S(2)}, u32[]{:S(2)}) async-start(f32[128,2,256]{2,1,0:T(2,128)} %all_to_all.48), calls=%async_computation.4 | async-start | bytes 524288 | tf_op jit(solution)/shard_map/all_to_all | solution.py:251
  173.3 18.2 %collective-permute-start.15 = (f32[32,128]{1,0:T(8,128)S(1)}, f32[32,128]{1,0:T(8,128)S(1)}, u32[]{:S(2)}, u32[]{:S(2)}) collective-permute-start(f32[32,128]{1,0:T(8,128)S(1)} %copy-done.32), channel_id=1, source_target_pairs={{0,1},{1,0},{2,3},{3,2},{4,5},{5,4},{6,7},{7,6},{8,9},{9,8},{10,11... | collective-permute-start | bytes 49160 | tf_op jit(solution)/shard_map/ppermute | solution.py:172
  173.4 9.2 %copy-start.43 = (f32[4,128]{1,0:T(4,128)S(1)}, f32[4,128]{1,0:T(4,128)}, u32[]{:S(2)}) copy-start(f32[4,128]{1,0:T(4,128)} %get-tuple-element.66) | copy-start | bytes 6148
  173.4 18.1 %collective-permute-start.16 = (f32[16,128]{1,0:T(8,128)S(1)}, f32[16,128]{1,0:T(8,128)S(1)}, u32[]{:S(2)}, u32[]{:S(2)}) collective-permute-start(f32[16,128]{1,0:T(8,128)S(1)} %copy-done.37), channel_id=1, source_target_pairs={{0,8},{8,16},{16,24},{24,32},{32,40},{40,48},{48,56},{56,64},{64,7... | collective-permute-start | bytes 24584 | tf_op jit(solution)/shard_map/ppermute | solution.py:175
  176.8 9.2 %copy-start.41 = (f32[4,128]{1,0:T(4,128)S(1)}, f32[4,128]{1,0:T(4,128)}, u32[]{:S(2)}) copy-start(f32[4,128]{1,0:T(4,128)} %get-tuple-element.67) | copy-start | bytes 6148
  176.8 14.7 %collective-permute-start.17 = (f32[16,128]{1,0:T(8,128)S(1)}, f32[16,128]{1,0:T(8,128)S(1)}, u32[]{:S(2)}, u32[]{:S(2)}) collective-permute-start(f32[16,128]{1,0:T(8,128)S(1)} %copy-done.35), channel_id=1, source_target_pairs={{8,0},{16,8},{24,16},{32,24},{40,32},{48,40},{56,48},{64,56},{72,6... | collective-permute-start | bytes 24584 | tf_op jit(solution)/shard_map/ppermute | solution.py:176
  182.6 5.6 %collective-permute-start.18 = (f32[4,128]{1,0:T(4,128)S(1)}, f32[4,128]{1,0:T(4,128)S(1)}, u32[]{:S(2)}, u32[]{:S(2)}) collective-permute-start(f32[4,128]{1,0:T(4,128)S(1)} %copy-done.43), channel_id=1, source_target_pairs={{0,2},{2,4},{4,6},{1,3},{3,5},{5,7},{8,10},{10,12},{12,14},{9,11},... | collective-permute-start | bytes 6152 | tf_op jit(solution)/shard_map/ppermute | solution.py:175
  186.0 5.5 %collective-permute-start.19 = (f32[4,128]{1,0:T(4,128)S(1)}, f32[4,128]{1,0:T(4,128)S(1)}, u32[]{:S(2)}, u32[]{:S(2)}) collective-permute-start(f32[4,128]{1,0:T(4,128)S(1)} %copy-done.41), channel_id=1, source_target_pairs={{2,0},{4,2},{6,4},{3,1},{5,3},{7,5},{10,8},{12,10},{14,12},{11,9},... | collective-permute-start | bytes 6152 | tf_op jit(solution)/shard_map/ppermute | solution.py:176
  188.2 3.3 %copy-start.22 = (f32[4,128]{1,0:T(4,128)}, f32[4,128]{1,0:T(4,128)S(1)}, u32[]{:S(2)}) copy-start(f32[4,128]{1,0:T(4,128)S(1)} %collective-permute-done.18.ylo_ref) | copy-start | bytes 6148
  (23 other events, 14.7 us)

commit v6 on v5

--- a/solution.py
+++ b/solution.py
@@ -135,6 +135,28 @@
     snd_ref[:, width:2 * width] = one_hot_dot(oh_ids_t_ref[...], ntv_ref[...])
 
 
+def coef_kernel(table_ref, cls_ref, cz_ref, cx_ref, cy_ref):
+    for z in range(cls_ref.shape[0]):
+        klass = cls_ref[z]
+        outs = [jnp.zeros(klass.shape, jnp.float32) for _ in range(3)]
+        for k in range(NCLASS):
+            hit = klass == k
+            outs = [jnp.where(hit, table_ref[d, k], outs[d]) for d in range(3)]
+        cz_ref[z], cx_ref[z], cy_ref[z] = outs
+
+
+def coefficients(fiber_class, fiber_table):
+    shape = jax.ShapeDtypeStruct(fiber_class.shape, jnp.float32)
+    vmem = pl.BlockSpec(memory_space=pltpu.VMEM)
+    return pl.pallas_call(
+        coef_kernel,
+        out_shape=(shape, shape, shape),
+        in_specs=[pl.BlockSpec(memory_space=pltpu.SMEM), vmem],
+        out_specs=[vmem] * 3,
+        interpret=INTERPRET,
+    )(fiber_table, fiber_class)
+
+
 def run_step(tables, state, recv, tile_gain, gains_rows, cable_rows, halos):
     volt, recovery, coef_z, coef_x, coef_y, term_volt, term_recovery = state
     depth, rows_x, width = volt.shape
@@ -196,14 +218,7 @@
     capacity = max(2, 2 * jcount // owners)
     slots_total = owners * capacity
     term_count = term_volt.shape[0]
-    coef_z = jnp.zeros(volt.shape, jnp.float32)
-    coef_x = jnp.zeros(volt.shape, jnp.float32)
-    coef_y = jnp.zeros(volt.shape, jnp.float32)
-    for klass in range(NCLASS):
-        hit = fiber_class == klass
-        coef_z = jnp.where(hit, fiber_table[0, klass], coef_z)
-        coef_x = jnp.where(hit, fiber_table[1, klass], coef_x)
-        coef_y = jnp.where(hit, fiber_table[2, klass], coef_y)
+    coef_z, coef_x, coef_y = coefficients(fiber_class, fiber_table)
 
     owner = junction_owner[:, 0]
     order = jnp.arange(jcount, dtype=jnp.int32)
@@ -245,6 +260,7 @@
         volt[:, :, 0].reshape(-1, width),
         volt[:, :, width - 1].reshape(-1, width),
     )
+    faces, sent = lax.optimization_barrier((faces, sent))
     tile_gain = None
     for step in range(STEPS):
         halos = exchange_halos(faces)

time: 198 us -> 180 us (0.909)
  other arithmetic: 24.1 us -> 6.18 us
  waiting for transfers between devices: 14.7 us -> 9.89 us
  starting transfers between devices: 116 us -> 120 us
  Pallas kernels: 16.5 us -> 18.7 us
    select_n x3 -> x0, other arithmetic: 17.8 us -> none  [the longest x1 6.07 us: on_device(): coef_y = jnp.where(hit, fiber_table[2, klass], coef_y)]
    all_to_all x4, waiting for transfers between devices: 4.77 us -> 0.01 us  [on_device(): lax.all_to_all(sent, ('gx', 'gy'), split_axis=0, concat_axis=0, tiled=True)]
    pallas_call x0 -> x1, Pallas kernels: none -> 2.17 us  [coefficients(): pl.pallas_call(coef_kernel, out_shape=(shape, shape, shape), in_specs=[pl...]
    unnamed x92 -> x88, local copies, waits for them, and re-layouts: 6.03 us -> 5.46 us
  transfers between devices with their start and end apart: 25 -> 25, of which waited for: 4 -> 3; matrix products, arithmetic and copies ran while one was open for 15% -> 5% of each run, Pallas kernels for 0% -> 1%
where the time goes in v6:
time: 180 us; the launch traced here: 178 us
  starting transfers between devices  120 us (67%)
  local copies, waits for them, and re-layouts  22.3 us (12%)
  Pallas kernels  18.7 us (10%)
  waiting for transfers between devices  9.89 us (5%)
  other arithmetic  6.18 us (3%)
    all_to_all x4, starting transfers between devices, on_device(): lax.all_to_all(sent, ('gx', 'gy'), split_axis=0, concat_axis=0, tiled=True)  49.8 us
    ppermute x8, starting transfers between devices, exchange_halos(): lax.ppermute(first, axis, [(i + 1, i) for i in range(count - 1)])  28.2 us
    ppermute x8, starting transfers between devices, exchange_halos(): lax.ppermute(last, axis, [(i, i + 1) for i in range(count - 1)])  27.1 us
    pallas_call x4, Pallas kernels, run_step(): pl.pallas_call(step_kernel, out_shape=out_shape, in_specs=[smem] + [vmem]...  16.5 us
    all_to_all x1, starting transfers between devices, on_device(): lax.all_to_all(slot_term, ('gx', 'gy'), split_axis=0, concat_axis=0, tile...  14 us
    ppermute x8, waiting for transfers between devices, exchange_halos(): lax.ppermute(first, axis, [(i + 1, i) for i in range(count - 1)])  9.84 us
    all_to_all x8, local copies, waits for them, and re-layouts, on_device(): lax.all_to_all(sent, ('gx', 'gy'), split_axis=0, concat_axis=0, tiled=True)  9.31 us
    unnamed x88, local copies, waits for them, and re-layouts  5.46 us
  transfers between devices with their start and end apart: 25, of which 3 were waited for; matrix products, arithmetic and copies ran while one was open for 5% of the time, Pallas kernels for 1%

profile of v6, /device:TPU:128, one launch (start us, length us, event | category | flops | bytes accessed | tf_op | source)
XLA Modules:
  0.0 178.2 jit_solution(5180831115100810264)
XLA Ops:
  2.8 0.8 sub.7
  3.5 14.0 %all-to-all-start = ((s32[128,2,1]{1,2,0:T(1,128)}), s32[128,2,1]{1,2,0:T(1,128)S(1)}, u32[]{:S(2)}, u32[]{:S(2)}) async-start(s32[128,2,1]{1,2,0:T(1,128)} %bitcast.13), calls=%async_computation | async-start | bytes 131072 | tf_op jit(solution)/shard_map/all_to_all | solution.py:232
  17.5 0.9 fusion.9
  18.4 1.4 slice_reduce_fusion
  19.8 0.7 fusion.2.oh_blk_t_ref
  20.5 0.7 fusion.1.oh_blk_ref
  21.2 0.7 fusion.3.oh_slot_ref
  22.7 0.7 gather_fusion
  23.5 2.2 %shard_map.138 = (f32[16,32,128]{2,1,0:T(8,128)}, f32[16,32,128]{2,1,0:T(8,128)}, f32[16,32,128]{2,1,0:T(8,128)}) custom-call(f32[3,8]{1,0:T(4,128)} %table_ref.1, s32[16,32,128]{2,1,0:T(8,128)} %cls_ref.1), custom_call_target="tpu_custom_call" | custom-call | tf_op jit(solution)/shard_map/pallas_call | solution.py:151
  27.1 0.8 reduce.9
  28.7 0.7 gather_fusion.1
  30.1 1.0 all_to_all.39
  31.1 13.7 %all-to-all-start.1 = ((f32[128,2,384]{2,1,0:T(2,128)}), f32[128,2,384]{2,1,0:T(2,128)S(1)}, u32[]{:S(2)}, u32[]{:S(2)}) async-start(f32[128,2,384]{2,1,0:T(2,128)} %all_to_all.39), calls=%async_computation.1 | async-start | bytes 786432 | tf_op jit(solution)/shard_map/all_to_all | solution.py:267
  44.9 0.8 fusion.oh_sblk_ref
  45.7 3.4 %collective-permute-start.3 = (f32[4,128]{1,0:T(4,128)S(1)}, f32[4,128]{1,0:T(4,128)S(1)}, u32[]{:S(2)}, u32[]{:S(2)}) collective-permute-start(f32[4,128]{1,0:T(4,128)S(1)} %reshape_squeeze.7), channel_id=1, source_target_pairs={{0,2},{2,4},{4,6},{1,3},{3,5},{5,7},{8,10},{10,12},{12,14},{9,11},... | collective-permute-start | bytes 6152 | tf_op jit(solution)/shard_map/ppermute | solution.py:197
  49.1 1.3 collective-permute-start.4
  50.4 3.4 %collective-permute-start.1 = (f32[16,128]{1,0:T(8,128)S(1)}, f32[16,128]{1,0:T(8,128)S(1)}, u32[]{:S(2)}, u32[]{:S(2)}) collective-permute-start(f32[16,128]{1,0:T(8,128)S(1)} %bitcast.37), channel_id=1, source_target_pairs={{0,8},{8,16},{16,24},{24,32},{32,40},{40,48},{48,56},{56,64},{64,7... | collective-permute-start | bytes 24584 | tf_op jit(solution)/shard_map/ppermute | solution.py:197
  53.8 5.8 %collective-permute-start.2 = (f32[16,128]{1,0:T(8,128)S(1)}, f32[16,128]{1,0:T(8,128)S(1)}, u32[]{:S(2)}, u32[]{:S(2)}) collective-permute-start(f32[16,128]{1,0:T(8,128)S(1)} %bitcast.36), channel_id=1, source_target_pairs={{8,0},{16,8},{24,16},{32,24},{40,32},{48,40},{56,48},{64,56},{72,6... | collective-permute-start | bytes 24584 | tf_op jit(solution)/shard_map/ppermute | solution.py:198
  59.6 0.7 fusion.4.oh_ids_t_ref
  61.3 1.2 gather_fusion.2
  63.3 4.2 %shard_map.139 = (f32[16,32,128]{2,1,0:T(8,128)}, f32[16,32,128]{2,1,0:T(8,128)}, f32[32,128]{1,0:T(8,128)}, f32[32,128]{1,0:T(8,128)}, f32[256,256]{1,0:T(8,128...) custom-call(s32[8]{0:T(128)} %convert_element_type.22.edge_ref, ...), custom_call_target="tpu_custom_call" | custom-call | tf_op jit(solution)/shard_map/pallas_call | solution.py:182
  67.5 1.8 %all_to_all.42 = f32[128,2,256]{2,1,0:T(2,128)} reshape(f32[256,256]{1,0:T(8,128)} %get-tuple-element.58) | data formatting | bytes 524288 | tf_op jit(solution)/shard_map/all_to_all | solution.py:267
  69.3 13.8 %all-to-all-start.2 = ((f32[128,2,256]{2,1,0:T(2,128)}), f32[128,2,256]{2,1,0:T(2,128)S(1)}, u32[]{:S(2)}, u32[]{:S(2)}) async-start(f32[128,2,256]{2,1,0:T(2,128)} %all_to_all.42), calls=%async_computation.2 | async-start | bytes 524288 | tf_op jit(solution)/shard_map/all_to_all | solution.py:267
  83.5 3.4 %collective-permute-start.6 = (f32[16,128]{1,0:T(8,128)S(1)}, f32[16,128]{1,0:T(8,128)S(1)}, u32[]{:S(2)}, u32[]{:S(2)}) collective-permute-start(f32[16,128]{1,0:T(8,128)S(1)} %copy-done.37), channel_id=1, source_target_pairs={{0,8},{8,16},{16,24},{24,32},{32,40},{40,48},{48,56},{56,64},{64,7... | collective-permute-start | bytes 24584 | tf_op jit(solution)/shard_map/ppermute | solution.py:197
  86.9 5.8 %collective-permute-start.7 = (f32[16,128]{1,0:T(8,128)S(1)}, f32[16,128]{1,0:T(8,128)S(1)}, u32[]{:S(2)}, u32[]{:S(2)}) collective-permute-start(f32[16,128]{1,0:T(8,128)S(1)} %copy-done.36), channel_id=1, source_target_pairs={{8,0},{16,8},{24,16},{32,24},{40,32},{48,40},{56,48},{64,56},{72,6... | collective-permute-start | bytes 24584 | tf_op jit(solution)/shard_map/ppermute | solution.py:198
  92.7 3.4 %collective-permute-start.8 = (f32[4,128]{1,0:T(4,128)S(1)}, f32[4,128]{1,0:T(4,128)S(1)}, u32[]{:S(2)}, u32[]{:S(2)}) collective-permute-start(f32[4,128]{1,0:T(4,128)S(1)} %copy-done.43), channel_id=1, source_target_pairs={{0,2},{2,4},{4,6},{1,3},{3,5},{5,7},{8,10},{10,12},{12,14},{9,11},... | collective-permute-start | bytes 6152 | tf_op jit(solution)/shard_map/ppermute | solution.py:197
  96.1 1.3 collective-permute-start.9
  97.4 0.9 all_to_all.44.recv_ref
  98.3 3.3 %collective-permute-done.9.yhi_ref = f32[4,128]{1,0:T(4,128)S(1)} collective-permute-done((f32[4,128]{1,0:T(4,128)S(1)}, f32[4,128]{1,0:T(4,128)S(1)}, u32[]{:S(2)}, u32[]{:S(2)}) %collective-permute-start.9) | collective-permute-done | bytes 2080 | tf_op jit(solution)/shard_map/ppermute | solution.py:198
  102.2 4.1 %shard_map.140 = (f32[16,32,128]{2,1,0:T(8,128)}, f32[16,32,128]{2,1,0:T(8,128)}, f32[32,128]{1,0:T(8,128)}, f32[32,128]{1,0:T(8,128)}, f32[256,256]{1,0:T(8,128...) custom-call(s32[8]{0:T(128)} %convert_element_type.22.edge_ref, ...), custom_call_target="tpu_custom_call" | custom-call | tf_op jit(solution)/shard_map/pallas_call | solution.py:182
  106.3 1.8 %all_to_all.45 = f32[128,2,256]{2,1,0:T(2,128)} reshape(f32[256,256]{1,0:T(8,128)} %get-tuple-element.68) | data formatting | bytes 524288 | tf_op jit(solution)/shard_map/all_to_all | solution.py:267
  108.1 11.1 %all-to-all-start.3 = ((f32[128,2,256]{2,1,0:T(2,128)}), f32[128,2,256]{2,1,0:T(2,128)S(1)}, u32[]{:S(2)}, u32[]{:S(2)}) async-start(f32[128,2,256]{2,1,0:T(2,128)} %all_to_all.45), calls=%async_computation.3 | async-start | bytes 524288 | tf_op jit(solution)/shard_map/all_to_all | solution.py:267
  119.4 3.4 %collective-permute-start.11 = (f32[16,128]{1,0:T(8,128)S(1)}, f32[16,128]{1,0:T(8,128)S(1)}, u32[]{:S(2)}, u32[]{:S(2)}) collective-permute-start(f32[16,128]{1,0:T(8,128)S(1)} %copy-done.34), channel_id=1, source_target_pairs={{0,8},{8,16},{16,24},{24,32},{32,40},{40,48},{48,56},{56,64},{64,7... | collective-permute-start | bytes 24584 | tf_op jit(solution)/shard_map/ppermute | solution.py:197
  122.8 5.8 %collective-permute-start.12 = (f32[16,128]{1,0:T(8,128)S(1)}, f32[16,128]{1,0:T(8,128)S(1)}, u32[]{:S(2)}, u32[]{:S(2)}) collective-permute-start(f32[16,128]{1,0:T(8,128)S(1)} %copy-done.32), channel_id=1, source_target_pairs={{8,0},{16,8},{24,16},{32,24},{40,32},{48,40},{56,48},{64,56},{72,6... | collective-permute-start | bytes 24584 | tf_op jit(solution)/shard_map/ppermute | solution.py:198
  128.6 3.4 %collective-permute-start.13 = (f32[4,128]{1,0:T(4,128)S(1)}, f32[4,128]{1,0:T(4,128)S(1)}, u32[]{:S(2)}, u32[]{:S(2)}) collective-permute-start(f32[4,128]{1,0:T(4,128)S(1)} %copy-done.40), channel_id=1, source_target_pairs={{0,2},{2,4},{4,6},{1,3},{3,5},{5,7},{8,10},{10,12},{12,14},{9,11},... | collective-permute-start | bytes 6152 | tf_op jit(solution)/shard_map/ppermute | solution.py:197
  132.0 1.3 collective-permute-start.14
  133.3 0.9 all_to_all.47.recv_ref
  134.2 3.3 %collective-permute-done.14.yhi_ref = f32[4,128]{1,0:T(4,128)S(1)} collective-permute-done((f32[4,128]{1,0:T(4,128)S(1)}, f32[4,128]{1,0:T(4,128)S(1)}, u32[]{:S(2)}, u32[]{:S(2)}) %collective-permute-start.14) | collective-permute-done | bytes 2080 | tf_op jit(solution)/shard_map/ppermute | solution.py:198
  138.1 4.1 %shard_map.141 = (f32[16,32,128]{2,1,0:T(8,128)}, f32[16,32,128]{2,1,0:T(8,128)}, f32[32,128]{1,0:T(8,128)}, f32[32,128]{1,0:T(8,128)}, f32[256,256]{1,0:T(8,128...) custom-call(s32[8]{0:T(128)} %convert_element_type.22.edge_ref, ...), custom_call_target="tpu_custom_call" | custom-call | tf_op jit(solution)/shard_map/pallas_call | solution.py:182
  142.2 1.8 %all_to_all.48 = f32[128,2,256]{2,1,0:T(2,128)} reshape(f32[256,256]{1,0:T(8,128)} %get-tuple-element.78) | data formatting | bytes 524288 | tf_op jit(solution)/shard_map/all_to_all | solution.py:267
  144.0 11.1 %all-to-all-start.4 = ((f32[128,2,256]{2,1,0:T(2,128)}), f32[128,2,256]{2,1,0:T(2,128)S(1)}, u32[]{:S(2)}, u32[]{:S(2)}) async-start(f32[128,2,256]{2,1,0:T(2,128)} %all_to_all.48), calls=%async_computation.4 | async-start | bytes 524288 | tf_op jit(solution)/shard_map/all_to_all | solution.py:267
  155.3 3.4 %collective-permute-start.16 = (f32[16,128]{1,0:T(8,128)S(1)}, f32[16,128]{1,0:T(8,128)S(1)}, u32[]{:S(2)}, u32[]{:S(2)}) collective-permute-start(f32[16,128]{1,0:T(8,128)S(1)} %copy-done.35), channel_id=1, source_target_pairs={{0,8},{8,16},{16,24},{24,32},{32,40},{40,48},{48,56},{56,64},{64,7... | collective-permute-start | bytes 24584 | tf_op jit(solution)/shard_map/ppermute | solution.py:197
  158.7 5.8 %collective-permute-start.17 = (f32[16,128]{1,0:T(8,128)S(1)}, f32[16,128]{1,0:T(8,128)S(1)}, u32[]{:S(2)}, u32[]{:S(2)}) collective-permute-start(f32[16,128]{1,0:T(8,128)S(1)} %copy-done.33), channel_id=1, source_target_pairs={{8,0},{16,8},{24,16},{32,24},{40,32},{48,40},{56,48},{64,56},{72,6... | collective-permute-start | bytes 24584 | tf_op jit(solution)/shard_map/ppermute | solution.py:198
  164.5 3.4 %collective-permute-start.18 = (f32[4,128]{1,0:T(4,128)S(1)}, f32[4,128]{1,0:T(4,128)S(1)}, u32[]{:S(2)}, u32[]{:S(2)}) collective-permute-start(f32[4,128]{1,0:T(4,128)S(1)} %copy-done.41), channel_id=1, source_target_pairs={{0,2},{2,4},{4,6},{1,3},{3,5},{5,7},{8,10},{10,12},{12,14},{9,11},... | collective-permute-start | bytes 6152 | tf_op jit(solution)/shard_map/ppermute | solution.py:197
  167.9 1.3 collective-permute-start.19
  169.2 0.9 all_to_all.50.recv_ref
  170.1 3.3 %collective-permute-done.19.yhi_ref = f32[4,128]{1,0:T(4,128)S(1)} collective-permute-done((f32[4,128]{1,0:T(4,128)S(1)}, f32[4,128]{1,0:T(4,128)S(1)}, u32[]{:S(2)}, u32[]{:S(2)}) %collective-permute-start.19) | collective-permute-done | bytes 2080 | tf_op jit(solution)/shard_map/ppermute | solution.py:198
  174.0 4.1 %shard_map.142 = (f32[16,32,128]{2,1,0:T(8,128)}, f32[16,32,128]{2,1,0:T(8,128)}, f32[32,128]{1,0:T(8,128)}, f32[32,128]{1,0:T(8,128)}, f32[256,256]{1,0:T(8,128...) custom-call(s32[8]{0:T(128)} %convert_element_type.22.edge_ref, ...), custom_call_target="tpu_custom_call" | custom-call | tf_op jit(solution)/shard_map/pallas_call | solution.py:182
  (141 shorter events, 9.9 us)
Async XLA Ops:
  3.5 22.1 %all-to-all-start = ((s32[128,2,1]{1,2,0:T(1,128)}), s32[128,2,1]{1,2,0:T(1,128)S(1)}, u32[]{:S(2)}, u32[]{:S(2)}) async-start(s32[128,2,1]{1,2,0:T(1,128)} %bitcast.13), calls=%async_computation | async-start | bytes 131072 | tf_op jit(solution)/shard_map/all_to_all | solution.py:232
  19.8 1.5 copy-start.1
  31.1 29.8 %all-to-all-start.1 = ((f32[128,2,384]{2,1,0:T(2,128)}), f32[128,2,384]{2,1,0:T(2,128)S(1)}, u32[]{:S(2)}, u32[]{:S(2)}) async-start(f32[128,2,384]{2,1,0:T(2,128)} %all_to_all.39), calls=%async_computation.1 | async-start | bytes 786432 | tf_op jit(solution)/shard_map/all_to_all | solution.py:267
  45.7 16.8 %collective-permute-start.3 = (f32[4,128]{1,0:T(4,128)S(1)}, f32[4,128]{1,0:T(4,128)S(1)}, u32[]{:S(2)}, u32[]{:S(2)}) collective-permute-start(f32[4,128]{1,0:T(4,128)S(1)} %reshape_squeeze.7), channel_id=1, source_target_pairs={{0,2},{2,4},{4,6},{1,3},{3,5},{5,7},{8,10},{10,12},{12,14},{9,11},... | collective-permute-start | bytes 6152 | tf_op jit(solution)/shard_map/ppermute | solution.py:197
  49.1 13.5 %collective-permute-start.4 = (f32[4,128]{1,0:T(4,128)S(1)}, f32[4,128]{1,0:T(4,128)S(1)}, u32[]{:S(2)}, u32[]{:S(2)}) collective-permute-start(f32[4,128]{1,0:T(4,128)S(1)} %reshape_squeeze.6), channel_id=1, source_target_pairs={{2,0},{4,2},{6,4},{3,1},{5,3},{7,5},{10,8},{12,10},{14,12},{11,9},... | collective-permute-start | bytes 6152 | tf_op jit(solution)/shard_map/ppermute | solution.py:198
  50.4 12.2 %collective-permute-start.1 = (f32[16,128]{1,0:T(8,128)S(1)}, f32[16,128]{1,0:T(8,128)S(1)}, u32[]{:S(2)}, u32[]{:S(2)}) collective-permute-start(f32[16,128]{1,0:T(8,128)S(1)} %bitcast.37), channel_id=1, source_target_pairs={{0,8},{8,16},{16,24},{24,32},{32,40},{40,48},{48,56},{56,64},{64,7... | collective-permute-start | bytes 24584 | tf_op jit(solution)/shard_map/ppermute | solution.py:197
  53.8 8.8 %collective-permute-start.2 = (f32[16,128]{1,0:T(8,128)S(1)}, f32[16,128]{1,0:T(8,128)S(1)}, u32[]{:S(2)}, u32[]{:S(2)}) collective-permute-start(f32[16,128]{1,0:T(8,128)S(1)} %bitcast.36), channel_id=1, source_target_pairs={{8,0},{16,8},{24,16},{32,24},{40,32},{48,40},{56,48},{64,56},{72,6... | collective-permute-start | bytes 24584 | tf_op jit(solution)/shard_map/ppermute | solution.py:198
  59.5 3.1 %collective-permute-start = (f32[32,128]{1,0:T(8,128)S(1)}, f32[32,128]{1,0:T(8,128)S(1)}, u32[]{:S(2)}, u32[]{:S(2)}) collective-permute-start(f32[32,128]{1,0:T(8,128)S(1)} %select_bitcast_fusion), channel_id=1, source_target_pairs={{0,1},{1,0},{2,3},{3,2},{4,5},{5,4},{6,7},{7,6},{8,9},{9,8},{10,11... | collective-permute-start | bytes 49160 | tf_op jit(solution)/shard_map/ppermute | solution.py:194
  61.2 1.3 copy-start.3
  61.3 1.3 copy-start.28
  62.5 0.8 copy-start.18
  62.5 0.8 copy-start.20
  69.3 13.8 %copy-start.31 = (f32[32,128]{1,0:T(8,128)S(1)}, f32[32,128]{1,0:T(8,128)}, u32[]{:S(2)}) copy-start(f32[32,128]{1,0:T(8,128)} %get-tuple-element.61) | copy-start | bytes 49156
  69.3 14.1 %copy-start.37 = (f32[16,128]{1,0:T(8,128)S(1)}, f32[16,128]{1,0:T(8,128)}, u32[]{:S(2)}) copy-start(f32[16,128]{1,0:T(8,128)} %get-tuple-element.62) | copy-start | bytes 24580
  69.3 17.5 %copy-start.36 = (f32[16,128]{1,0:T(8,128)S(1)}, f32[16,128]{1,0:T(8,128)}, u32[]{:S(2)}) copy-start(f32[16,128]{1,0:T(8,128)} %get-tuple-element.63) | copy-start | bytes 24580
  69.3 28.0 %all-to-all-start.2 = ((f32[128,2,256]{2,1,0:T(2,128)}), f32[128,2,256]{2,1,0:T(2,128)S(1)}, u32[]{:S(2)}, u32[]{:S(2)}) async-start(f32[128,2,256]{2,1,0:T(2,128)} %all_to_all.42), calls=%async_computation.2 | async-start | bytes 524288 | tf_op jit(solution)/shard_map/all_to_all | solution.py:267
  83.2 18.4 %collective-permute-start.5 = (f32[32,128]{1,0:T(8,128)S(1)}, f32[32,128]{1,0:T(8,128)S(1)}, u32[]{:S(2)}, u32[]{:S(2)}) collective-permute-start(f32[32,128]{1,0:T(8,128)S(1)} %copy-done.31), channel_id=1, source_target_pairs={{0,1},{1,0},{2,3},{3,2},{4,5},{5,4},{6,7},{7,6},{8,9},{9,8},{10,11... | collective-permute-start | bytes 49160 | tf_op jit(solution)/shard_map/ppermute | solution.py:194
  83.5 9.2 %copy-start.43 = (f32[4,128]{1,0:T(4,128)S(1)}, f32[4,128]{1,0:T(4,128)}, u32[]{:S(2)}) copy-start(f32[4,128]{1,0:T(4,128)} %get-tuple-element.64) | copy-start | bytes 6148
  83.5 18.1 %collective-permute-start.6 = (f32[16,128]{1,0:T(8,128)S(1)}, f32[16,128]{1,0:T(8,128)S(1)}, u32[]{:S(2)}, u32[]{:S(2)}) collective-permute-start(f32[16,128]{1,0:T(8,128)S(1)} %copy-done.37), channel_id=1, source_target_pairs={{0,8},{8,16},{16,24},{24,32},{32,40},{40,48},{48,56},{56,64},{64,7... | collective-permute-start | bytes 24584 | tf_op jit(solution)/shard_map/ppermute | solution.py:197
  86.9 9.2 %copy-start.42 = (f32[4,128]{1,0:T(4,128)S(1)}, f32[4,128]{1,0:T(4,128)}, u32[]{:S(2)}) copy-start(f32[4,128]{1,0:T(4,128)} %get-tuple-element.65) | copy-start | bytes 6148
  86.9 14.7 %collective-permute-start.7 = (f32[16,128]{1,0:T(8,128)S(1)}, f32[16,128]{1,0:T(8,128)S(1)}, u32[]{:S(2)}, u32[]{:S(2)}) collective-permute-start(f32[16,128]{1,0:T(8,128)S(1)} %copy-done.36), channel_id=1, source_target_pairs={{8,0},{16,8},{24,16},{32,24},{40,32},{48,40},{56,48},{64,56},{72,6... | collective-permute-start | bytes 24584 | tf_op jit(solution)/shard_map/ppermute | solution.py:198
  92.7 5.6 %collective-permute-start.8 = (f32[4,128]{1,0:T(4,128)S(1)}, f32[4,128]{1,0:T(4,128)S(1)}, u32[]{:S(2)}, u32[]{:S(2)}) collective-permute-start(f32[4,128]{1,0:T(4,128)S(1)} %copy-done.43), channel_id=1, source_target_pairs={{0,2},{2,4},{4,6},{1,3},{3,5},{5,7},{8,10},{10,12},{12,14},{9,11},... | collective-permute-start | bytes 6152 | tf_op jit(solution)/shard_map/ppermute | solution.py:197
  96.1 5.5 %collective-permute-start.9 = (f32[4,128]{1,0:T(4,128)S(1)}, f32[4,128]{1,0:T(4,128)S(1)}, u32[]{:S(2)}, u32[]{:S(2)}) collective-permute-start(f32[4,128]{1,0:T(4,128)S(1)} %copy-done.42), channel_id=1, source_target_pairs={{2,0},{4,2},{6,4},{3,1},{5,3},{7,5},{10,8},{12,10},{14,12},{11,9},... | collective-permute-start | bytes 6152 | tf_op jit(solution)/shard_map/ppermute | solution.py:198
  98.3 3.3 %copy-start.22 = (f32[4,128]{1,0:T(4,128)}, f32[4,128]{1,0:T(4,128)S(1)}, u32[]{:S(2)}) copy-start(f32[4,128]{1,0:T(4,128)S(1)} %collective-permute-done.8.ylo_ref) | copy-start | bytes 6148
  108.1 11.1 %copy-start.29 = (f32[32,128]{1,0:T(8,128)S(1)}, f32[32,128]{1,0:T(8,128)}, u32[]{:S(2)}) copy-start(f32[32,128]{1,0:T(8,128)} %get-tuple-element.71) | copy-start | bytes 49156
  108.1 11.3 %copy-start.34 = (f32[16,128]{1,0:T(8,128)S(1)}, f32[16,128]{1,0:T(8,128)}, u32[]{:S(2)}) copy-start(f32[16,128]{1,0:T(8,128)} %get-tuple-element.72) | copy-start | bytes 24580
  108.1 14.7 %copy-start.32 = (f32[16,128]{1,0:T(8,128)S(1)}, f32[16,128]{1,0:T(8,128)}, u32[]{:S(2)}) copy-start(f32[16,128]{1,0:T(8,128)} %get-tuple-element.73) | copy-start | bytes 24580
  108.1 25.2 %all-to-all-start.3 = ((f32[128,2,256]{2,1,0:T(2,128)}), f32[128,2,256]{2,1,0:T(2,128)S(1)}, u32[]{:S(2)}, u32[]{:S(2)}) async-start(f32[128,2,256]{2,1,0:T(2,128)} %all_to_all.45), calls=%async_computation.3 | async-start | bytes 524288 | tf_op jit(solution)/shard_map/all_to_all | solution.py:267
  119.3 18.2 %collective-permute-start.10 = (f32[32,128]{1,0:T(8,128)S(1)}, f32[32,128]{1,0:T(8,128)S(1)}, u32[]{:S(2)}, u32[]{:S(2)}) collective-permute-start(f32[32,128]{1,0:T(8,128)S(1)} %copy-done.29), channel_id=1, source_target_pairs={{0,1},{1,0},{2,3},{3,2},{4,5},{5,4},{6,7},{7,6},{8,9},{9,8},{10,11... | collective-permute-start | bytes 49160 | tf_op jit(solution)/shard_map/ppermute | solution.py:194
  119.4 9.2 %copy-start.40 = (f32[4,128]{1,0:T(4,128)S(1)}, f32[4,128]{1,0:T(4,128)}, u32[]{:S(2)}) copy-start(f32[4,128]{1,0:T(4,128)} %get-tuple-element.74) | copy-start | bytes 6148
  119.4 18.1 %collective-permute-start.11 = (f32[16,128]{1,0:T(8,128)S(1)}, f32[16,128]{1,0:T(8,128)S(1)}, u32[]{:S(2)}, u32[]{:S(2)}) collective-permute-start(f32[16,128]{1,0:T(8,128)S(1)} %copy-done.34), channel_id=1, source_target_pairs={{0,8},{8,16},{16,24},{24,32},{32,40},{40,48},{48,56},{56,64},{64,7... | collective-permute-start | bytes 24584 | tf_op jit(solution)/shard_map/ppermute | solution.py:197
  122.8 9.2 %copy-start.38 = (f32[4,128]{1,0:T(4,128)S(1)}, f32[4,128]{1,0:T(4,128)}, u32[]{:S(2)}) copy-start(f32[4,128]{1,0:T(4,128)} %get-tuple-element.75) | copy-start | bytes 6148
  122.8 14.7 %collective-permute-start.12 = (f32[16,128]{1,0:T(8,128)S(1)}, f32[16,128]{1,0:T(8,128)S(1)}, u32[]{:S(2)}, u32[]{:S(2)}) collective-permute-start(f32[16,128]{1,0:T(8,128)S(1)} %copy-done.32), channel_id=1, source_target_pairs={{8,0},{16,8},{24,16},{32,24},{40,32},{48,40},{56,48},{64,56},{72,6... | collective-permute-start | bytes 24584 | tf_op jit(solution)/shard_map/ppermute | solution.py:198
  128.6 5.6 %collective-permute-start.13 = (f32[4,128]{1,0:T(4,128)S(1)}, f32[4,128]{1,0:T(4,128)S(1)}, u32[]{:S(2)}, u32[]{:S(2)}) collective-permute-start(f32[4,128]{1,0:T(4,128)S(1)} %copy-done.40), channel_id=1, source_target_pairs={{0,2},{2,4},{4,6},{1,3},{3,5},{5,7},{8,10},{10,12},{12,14},{9,11},... | collective-permute-start | bytes 6152 | tf_op jit(solution)/shard_map/ppermute | solution.py:197
  132.0 5.5 %collective-permute-start.14 = (f32[4,128]{1,0:T(4,128)S(1)}, f32[4,128]{1,0:T(4,128)S(1)}, u32[]{:S(2)}, u32[]{:S(2)}) collective-permute-start(f32[4,128]{1,0:T(4,128)S(1)} %copy-done.38), channel_id=1, source_target_pairs={{2,0},{4,2},{6,4},{3,1},{5,3},{7,5},{10,8},{12,10},{14,12},{11,9},... | collective-permute-start | bytes 6152 | tf_op jit(solution)/shard_map/ppermute | solution.py:198
  134.2 3.3 %copy-start.23 = (f32[4,128]{1,0:T(4,128)}, f32[4,128]{1,0:T(4,128)S(1)}, u32[]{:S(2)}) copy-start(f32[4,128]{1,0:T(4,128)S(1)} %collective-permute-done.13.ylo_ref) | copy-start | bytes 6148
  144.0 11.1 %copy-start.30 = (f32[32,128]{1,0:T(8,128)S(1)}, f32[32,128]{1,0:T(8,128)}, u32[]{:S(2)}) copy-start(f32[32,128]{1,0:T(8,128)} %get-tuple-element.81) | copy-start | bytes 49156
  144.0 11.3 %copy-start.35 = (f32[16,128]{1,0:T(8,128)S(1)}, f32[16,128]{1,0:T(8,128)}, u32[]{:S(2)}) copy-start(f32[16,128]{1,0:T(8,128)} %get-tuple-element.82) | copy-start | bytes 24580
  144.0 14.7 %copy-start.33 = (f32[16,128]{1,0:T(8,128)S(1)}, f32[16,128]{1,0:T(8,128)}, u32[]{:S(2)}) copy-start(f32[16,128]{1,0:T(8,128)} %get-tuple-element.83) | copy-start | bytes 24580
  144.0 25.2 %all-to-all-start.4 = ((f32[128,2,256]{2,1,0:T(2,128)}), f32[128,2,256]{2,1,0:T(2,128)S(1)}, u32[]{:S(2)}, u32[]{:S(2)}) async-start(f32[128,2,256]{2,1,0:T(2,128)} %all_to_all.48), calls=%async_computation.4 | async-start | bytes 524288 | tf_op jit(solution)/shard_map/all_to_all | solution.py:267
  155.1 18.2 %collective-permute-start.15 = (f32[32,128]{1,0:T(8,128)S(1)}, f32[32,128]{1,0:T(8,128)S(1)}, u32[]{:S(2)}, u32[]{:S(2)}) collective-permute-start(f32[32,128]{1,0:T(8,128)S(1)} %copy-done.30), channel_id=1, source_target_pairs={{0,1},{1,0},{2,3},{3,2},{4,5},{5,4},{6,7},{7,6},{8,9},{9,8},{10,11... | collective-permute-start | bytes 49160 | tf_op jit(solution)/shard_map/ppermute | solution.py:194
  155.3 9.2 %copy-start.41 = (f32[4,128]{1,0:T(4,128)S(1)}, f32[4,128]{1,0:T(4,128)}, u32[]{:S(2)}) copy-start(f32[4,128]{1,0:T(4,128)} %get-tuple-element.84) | copy-start | bytes 6148
  155.3 18.1 %collective-permute-start.16 = (f32[16,128]{1,0:T(8,128)S(1)}, f32[16,128]{1,0:T(8,128)S(1)}, u32[]{:S(2)}, u32[]{:S(2)}) collective-permute-start(f32[16,128]{1,0:T(8,128)S(1)} %copy-done.35), channel_id=1, source_target_pairs={{0,8},{8,16},{16,24},{24,32},{32,40},{40,48},{48,56},{56,64},{64,7... | collective-permute-start | bytes 24584 | tf_op jit(solution)/shard_map/ppermute | solution.py:197
  158.7 9.2 %copy-start.39 = (f32[4,128]{1,0:T(4,128)S(1)}, f32[4,128]{1,0:T(4,128)}, u32[]{:S(2)}) copy-start(f32[4,128]{1,0:T(4,128)} %get-tuple-element.85) | copy-start | bytes 6148
  158.7 14.7 %collective-permute-start.17 = (f32[16,128]{1,0:T(8,128)S(1)}, f32[16,128]{1,0:T(8,128)S(1)}, u32[]{:S(2)}, u32[]{:S(2)}) collective-permute-start(f32[16,128]{1,0:T(8,128)S(1)} %copy-done.33), channel_id=1, source_target_pairs={{8,0},{16,8},{24,16},{32,24},{40,32},{48,40},{56,48},{64,56},{72,6... | collective-permute-start | bytes 24584 | tf_op jit(solution)/shard_map/ppermute | solution.py:198
  164.5 5.6 %collective-permute-start.18 = (f32[4,128]{1,0:T(4,128)S(1)}, f32[4,128]{1,0:T(4,128)S(1)}, u32[]{:S(2)}, u32[]{:S(2)}) collective-permute-start(f32[4,128]{1,0:T(4,128)S(1)} %copy-done.41), channel_id=1, source_target_pairs={{0,2},{2,4},{4,6},{1,3},{3,5},{5,7},{8,10},{10,12},{12,14},{9,11},... | collective-permute-start | bytes 6152 | tf_op jit(solution)/shard_map/ppermute | solution.py:197
  167.9 5.5 %collective-permute-start.19 = (f32[4,128]{1,0:T(4,128)S(1)}, f32[4,128]{1,0:T(4,128)S(1)}, u32[]{:S(2)}, u32[]{:S(2)}) collective-permute-start(f32[4,128]{1,0:T(4,128)S(1)} %copy-done.39), channel_id=1, source_target_pairs={{2,0},{4,2},{6,4},{3,1},{5,3},{7,5},{10,8},{12,10},{14,12},{11,9},... | collective-permute-start | bytes 6152 | tf_op jit(solution)/shard_map/ppermute | solution.py:198
  170.1 3.3 %copy-start.19 = (f32[4,128]{1,0:T(4,128)}, f32[4,128]{1,0:T(4,128)S(1)}, u32[]{:S(2)}) copy-start(f32[4,128]{1,0:T(4,128)S(1)} %collective-permute-done.18.ylo_ref) | copy-start | bytes 6148
  (21 other events, 13.3 us)

commit v7 on v6

--- a/solution.py
+++ b/solution.py
@@ -1,3 +1,5 @@
+import functools
+
 import jax
 import jax.numpy as jnp
 from jax import lax
@@ -47,36 +49,11 @@
     return (dot(a) + dot(b)) + dot(c)
 
 
-def step_kernel(
-    edge_ref,
-    v_ref, w_ref, cz_ref, cx_ref, cy_ref, recv_ref, tg_ref, g_ref,
-    tv_ref, tr_ref, cg_ref, zr_ref, xlo_ref, xhi_ref, ylo_ref, yhi_ref,
-    oh_blk_ref, oh_blk_t_ref, oh_slot_ref, oh_ids_ref, oh_ids_t_ref, oh_sblk_ref,
-    nv_ref, nw_ref, ntv_ref, ntr_ref, snd_ref, zs_ref, xf_ref, xl_ref, yf_ref, yl_ref,
+def slab_kernel(
+    edge_ref, v_ref, w_ref, cz_ref, cx_ref, cy_ref, zr_ref, xlo_ref, xhi_ref, ylo_ref, yhi_ref,
+    base_ref, react_ref, nw_ref,
 ):
     depth, rows_x, width = v_ref.shape
-
-    v_flat = v_ref[...].reshape(depth * rows_x, width)
-    rows = one_hot_dot(oh_blk_ref[...], v_flat)
-    far = one_hot_dot(oh_slot_ref[...], recv_ref[:, width:2 * width])
-    tile_current = tg_ref[...] * (far - rows)
-    into_voxel = one_hot_dot(oh_blk_t_ref[...], tile_current)
-
-    far_volt = one_hot_dot(oh_ids_t_ref[...], tv_ref[...])
-    current = g_ref[...] * (far_volt - recv_ref[:, 0:width])
-    into_term = one_hot_dot(oh_ids_ref[...], -current)
-
-    u = tv_ref[...]
-    r = tr_ref[...]
-    u_minus, u_plus = shifted(u, 1)
-    lane_t = lax.broadcasted_iota(jnp.int32, u.shape, 1)
-    u_minus = jnp.where(lane_t == 0, u, u_minus)
-    u_plus = jnp.where(lane_t == width - 1, u, u_plus)
-    lap_k = u_plus + u_minus - 2.0 * u
-    react_u, new_r = cell_kinetics(u, r, 0.1 * into_term)
-    ntv_ref[...] = u + cg_ref[...] * lap_k + react_u
-    ntr_ref[...] = new_r
-
     plane = (rows_x, width)
     sub = lax.broadcasted_iota(jnp.int32, plane, 0)
     lane = lax.broadcasted_iota(jnp.int32, plane, 1)
@@ -87,8 +64,6 @@
     y_low = flag(edge_ref, 4, (rows_x, 1))
     y_high = flag(edge_ref, 5, (rows_x, 1))
     per_row = width // rows_x
-    y_first = [jnp.zeros((1, width), jnp.float32) for _ in range(yf_ref.shape[0])]
-    y_last = [jnp.zeros((1, width), jnp.float32) for _ in range(yf_ref.shape[0])]
     for z in range(depth):
         vz = v_ref[z]
         if z == 0:
@@ -116,23 +91,70 @@
         lap_z = zp + zm - 2.0 * vz
         lap_x = xp + xm - 2.0 * vz
         lap_y = yp + ym - 2.0 * vz
-        react_v, new_w = cell_kinetics(vz, w_ref[z], into_voxel[z * rows_x:(z + 1) * rows_x])
-        nv = vz + (cz_ref[z] * lap_z + cx_ref[z] * lap_x + cy_ref[z] * lap_y) + react_v
-        nv_ref[z] = nv
-        nw_ref[z] = new_w
-        xf_ref[z:z + 1, :] = nv[0:1, :]
-        xl_ref[z:z + 1, :] = nv[rows_x - 1:rows_x, :]
+        wz = w_ref[z]
+        base_ref[z] = vz + (cz_ref[z] * lap_z + cx_ref[z] * lap_x + cy_ref[z] * lap_y)
+        react_ref[z] = -8.0 * vz * (vz - 0.15) * (vz - 1.0) - vz * wz
+        nw_ref[z] = wz + 0.01 * (-wz - 8.0 * vz * (vz - 1.15))
+
+
+def junction_kernel(
+    edge_ref,
+    v_ref, base_ref, react_ref, recv_ref, tg_ref, g_ref, tv_ref, tr_ref, cg_ref,
+    oh_blk_ref, oh_blk_t_ref, oh_slot_ref, oh_ids_ref, oh_ids_t_ref, oh_sblk_ref,
+    nv_ref, ntv_ref, ntr_ref, *tail, pack,
+):
+    depth, rows_x, width = v_ref.shape
+
+    v_flat = v_ref[...].reshape(depth * rows_x, width)
+    rows = one_hot_dot(oh_blk_ref[...], v_flat)
+    far = one_hot_dot(oh_slot_ref[...], recv_ref[:, width:2 * width])
+    tile_current = tg_ref[...] * (far - rows)
+    into_voxel = one_hot_dot(oh_blk_t_ref[...], tile_current).reshape(depth, rows_x, width)
+    nv = base_ref[...] + 0.1 * (react_ref[...] + into_voxel)
+    nv_ref[...] = nv
+
+    far_volt = one_hot_dot(oh_ids_t_ref[...], tv_ref[...])
+    current = g_ref[...] * (far_volt - recv_ref[:, 0:width])
+    into_term = one_hot_dot(oh_ids_ref[...], -current)
+
+    u = tv_ref[...]
+    r = tr_ref[...]
+    u_minus, u_plus = shifted(u, 1)
+    lane_t = lax.broadcasted_iota(jnp.int32, u.shape, 1)
+    u_minus = jnp.where(lane_t == 0, u, u_minus)
+    u_plus = jnp.where(lane_t == width - 1, u, u_plus)
+    lap_k = u_plus + u_minus - 2.0 * u
+    react_u, new_r = cell_kinetics(u, r, 0.1 * into_term)
+    ntv = u + cg_ref[...] * lap_k + react_u
+    ntv_ref[...] = ntv
+    ntr_ref[...] = new_r
+    if not pack:
+        return
+    snd_ref, zs_ref, xf_ref, xl_ref, yf_ref, yl_ref = tail
+
+    plane = (rows_x, width)
+    sub = lax.broadcasted_iota(jnp.int32, plane, 0)
+    lane = lax.broadcasted_iota(jnp.int32, plane, 1)
+    per_row = width // rows_x
+    y_first = [jnp.zeros((1, width), jnp.float32) for _ in range(yf_ref.shape[0])]
+    y_last = [jnp.zeros((1, width), jnp.float32) for _ in range(yf_ref.shape[0])]
+    for z in range(depth):
+        nz = nv[z]
+        xf_ref[z:z + 1, :] = nz[0:1, :]
+        xl_ref[z:z + 1, :] = nz[rows_x - 1:rows_x, :]
+        row_at, lane_at = z // per_row, (z % per_row) * rows_x
+        pick = lane == sub + lane_at
         y_first[row_at] = y_first[row_at] + jnp.sum(
-            jnp.where(pick, nv[:, 0:1], 0.0), axis=0, keepdims=True)
+            jnp.where(pick, nz[:, 0:1], 0.0), axis=0, keepdims=True)
         y_last[row_at] = y_last[row_at] + jnp.sum(
-            jnp.where(pick, nv[:, width - 1:width], 0.0), axis=0, keepdims=True)
+            jnp.where(pick, nz[:, width - 1:width], 0.0), axis=0, keepdims=True)
     for i in range(yf_ref.shape[0]):
         yf_ref[i:i + 1, :] = y_first[i]
         yl_ref[i:i + 1, :] = y_last[i]
-    zs_ref[...] = jnp.where(z_low, nv_ref[depth - 1], nv_ref[0])
-
-    snd_ref[:, 0:width] = one_hot_dot(oh_sblk_ref[...], nv_ref[...].reshape(depth * rows_x, width))
-    snd_ref[:, width:2 * width] = one_hot_dot(oh_ids_t_ref[...], ntv_ref[...])
+    zs_ref[...] = jnp.where(flag(edge_ref, 0, plane), nv[depth - 1], nv[0])
+
+    snd_ref[:, 0:width] = one_hot_dot(oh_sblk_ref[...], nv.reshape(depth * rows_x, width))
+    snd_ref[:, width:2 * width] = one_hot_dot(oh_ids_t_ref[...], ntv)
 
 
 def coef_kernel(table_ref, cls_ref, cz_ref, cx_ref, cy_ref):
@@ -157,35 +179,44 @@
     )(fiber_table, fiber_class)
 
 
-def run_step(tables, state, recv, tile_gain, gains_rows, cable_rows, halos):
+def run_step(tables, state, recv, tile_gain, gains_rows, cable_rows, halos, pack):
     volt, recovery, coef_z, coef_x, coef_y, term_volt, term_recovery = state
     depth, rows_x, width = volt.shape
     slots = recv.shape[0]
+    edges, one_hots = tables
     f32 = jnp.float32
     smem = pl.BlockSpec(memory_space=pltpu.SMEM)
     vmem = pl.BlockSpec(memory_space=pltpu.VMEM)
-    out_shape = (
-        jax.ShapeDtypeStruct(volt.shape, f32),
-        jax.ShapeDtypeStruct(volt.shape, f32),
-        jax.ShapeDtypeStruct(term_volt.shape, f32),
-        jax.ShapeDtypeStruct(term_volt.shape, f32),
-        jax.ShapeDtypeStruct((slots, 2 * width), f32),
-        jax.ShapeDtypeStruct((rows_x, width), f32),
-        jax.ShapeDtypeStruct((depth, width), f32),
-        jax.ShapeDtypeStruct((depth, width), f32),
-        jax.ShapeDtypeStruct((depth * rows_x // width, width), f32),
-        jax.ShapeDtypeStruct((depth * rows_x // width, width), f32),
-    )
-    edges, one_hots = tables
-    operands = (edges, volt, recovery, coef_z, coef_x, coef_y, recv, tile_gain,
-                gains_rows, term_volt, term_recovery, cable_rows) + tuple(halos) + tuple(one_hots)
-    return pl.pallas_call(
-        step_kernel,
+    slab = jax.ShapeDtypeStruct(volt.shape, f32)
+    operands = (edges, volt, recovery, coef_z, coef_x, coef_y) + tuple(halos)
+    base, react, new_w = pl.pallas_call(
+        slab_kernel,
+        out_shape=(slab, slab, slab),
+        in_specs=[smem] + [vmem] * (len(operands) - 1),
+        out_specs=[vmem] * 3,
+        interpret=INTERPRET,
+    )(*operands)
+    term = jax.ShapeDtypeStruct(term_volt.shape, f32)
+    out_shape = (slab, term, term)
+    if pack:
+        out_shape += (
+            jax.ShapeDtypeStruct((slots, 2 * width), f32),
+            jax.ShapeDtypeStruct((rows_x, width), f32),
+            jax.ShapeDtypeStruct((depth, width), f32),
+            jax.ShapeDtypeStruct((depth, width), f32),
+            jax.ShapeDtypeStruct((depth * rows_x // width, width), f32),
+            jax.ShapeDtypeStruct((depth * rows_x // width, width), f32),
+        )
+    operands = (edges, volt, base, react, recv, tile_gain, gains_rows, term_volt, term_recovery,
+                cable_rows) + tuple(one_hots)
+    outs = pl.pallas_call(
+        functools.partial(junction_kernel, pack=pack),
         out_shape=out_shape,
         in_specs=[smem] + [vmem] * (len(operands) - 1),
         out_specs=[vmem] * len(out_shape),
         interpret=INTERPRET,
     )(*operands)
+    return (outs[0], new_w) + tuple(outs[1:])
 
 
 def exchange_halos(faces):
@@ -268,9 +299,9 @@
         if step == 0:
             tile_gain = received[:, 2 * width:3 * width][slot]
         state = (volt, recovery, coef_z, coef_x, coef_y, term_volt, term_recovery)
-        outs = run_step(tables, state, received, tile_gain, gain_rows, cable_rows, halos)
-        volt, recovery, term_volt, term_recovery, sent = outs[:5]
-        faces = outs[5:]
+        outs = run_step(tables, state, received, tile_gain, gain_rows, cable_rows, halos, step < STEPS - 1)
+        volt, recovery, term_volt, term_recovery = outs[:4]
+        sent, faces = (outs[4], outs[5:]) if step < STEPS - 1 else (None, None)
     return (volt, recovery, term_volt, term_recovery)
 
 

time: 180 us -> 193 us (1.072)
  Pallas kernels: 18.7 us -> 26.9 us
  waiting for transfers between devices: 9.89 us -> 12.5 us
    pallas_call x4 -> x8, Pallas kernels: 16.5 us -> 24.7 us  [the longest x4 12.8 us: run_step(): pl.pallas_call(functools.partial(junction_kernel, pack=pack), out_shape=o...]
    ppermute x8, waiting for transfers between devices: 9.84 us -> 12.5 us  [exchange_halos(): lax.ppermute(first, axis, [(i + 1, i) for i in range(count - 1)])]
  transfers between devices with their start and end apart: 25 -> 25, of which waited for: 3 -> 3; matrix products, arithmetic and copies ran while one was open for 5% -> 4% of each run, Pallas kernels for 1% -> 7%
where the time goes in v7:
time: 193 us; the launch traced here: 191 us
  starting transfers between devices  121 us (63%)
  Pallas kernels  26.9 us (14%)
  local copies, waits for them, and re-layouts  23 us (12%)
  waiting for transfers between devices  12.5 us (6%)
  other arithmetic  6.18 us (3%)
    all_to_all x4, starting transfers between devices, on_device(): lax.all_to_all(sent, ('gx', 'gy'), split_axis=0, concat_axis=0, tiled=True)  51.4 us
    ppermute x8, starting transfers between devices, exchange_halos(): lax.ppermute(first, axis, [(i + 1, i) for i in range(count - 1)])  28.2 us
    ppermute x8, starting transfers between devices, exchange_halos(): lax.ppermute(last, axis, [(i, i + 1) for i in range(count - 1)])  27.1 us
    all_to_all x1, starting transfers between devices, on_device(): lax.all_to_all(slot_term, ('gx', 'gy'), split_axis=0, concat_axis=0, tile...  14 us
    pallas_call x4, Pallas kernels, run_step(): pl.pallas_call(functools.partial(junction_kernel, pack=pack), out_shape=o...  12.8 us
    ppermute x8, waiting for transfers between devices, exchange_halos(): lax.ppermute(first, axis, [(i + 1, i) for i in range(count - 1)])  12.5 us
    pallas_call x4, Pallas kernels, run_step(): pl.pallas_call(slab_kernel, out_shape=(slab, slab, slab), in_specs=[smem]...  12 us
    all_to_all x8, local copies, waits for them, and re-layouts, on_device(): lax.all_to_all(sent, ('gx', 'gy'), split_axis=0, concat_axis=0, tiled=True)  9.39 us
  transfers between devices with their start and end apart: 25, of which 3 were waited for; matrix products, arithmetic and copies ran while one was open for 4% of the time, Pallas kernels for 7%

profile of v7, /device:TPU:128, one launch (start us, length us, event | category | flops | bytes accessed | tf_op | source)
XLA Modules:
  0.0 191.2 jit_solution(18250761398672648286)
XLA Ops:
  2.8 0.8 sub.7
  3.5 14.0 %all-to-all-start = ((s32[128,2,1]{1,2,0:T(1,128)}), s32[128,2,1]{1,2,0:T(1,128)S(1)}, u32[]{:S(2)}, u32[]{:S(2)}) async-start(s32[128,2,1]{1,2,0:T(1,128)} %bitcast.13), calls=%async_computation | async-start | bytes 131072 | tf_op jit(solution)/shard_map/all_to_all | solution.py:263
  17.5 0.9 fusion.9
  18.4 1.4 slice_reduce_fusion
  20.5 0.7 fusion.1.oh_blk_ref
  23.5 2.2 %shard_map.138 = (f32[16,32,128]{2,1,0:T(8,128)}, f32[16,32,128]{2,1,0:T(8,128)}, f32[16,32,128]{2,1,0:T(8,128)}) custom-call(f32[3,8]{1,0:T(4,128)} %table_ref.1, s32[16,32,128]{2,1,0:T(8,128)} %cls_ref.1), custom_call_target="tpu_custom_call" | custom-call | tf_op jit(solution)/shard_map/pallas_call | solution.py:173
  27.1 0.8 reduce.9
  28.7 0.7 gather_fusion.1
  30.1 1.0 all_to_all.39
  31.1 13.7 %all-to-all-start.1 = ((f32[128,2,384]{2,1,0:T(2,128)}), f32[128,2,384]{2,1,0:T(2,128)S(1)}, u32[]{:S(2)}, u32[]{:S(2)}) async-start(f32[128,2,384]{2,1,0:T(2,128)} %all_to_all.39), calls=%async_computation.1 | async-start | bytes 786432 | tf_op jit(solution)/shard_map/all_to_all | solution.py:298
  44.9 0.8 fusion.oh_sblk_ref
  45.7 3.4 %collective-permute-start.3 = (f32[4,128]{1,0:T(4,128)S(1)}, f32[4,128]{1,0:T(4,128)S(1)}, u32[]{:S(2)}, u32[]{:S(2)}) collective-permute-start(f32[4,128]{1,0:T(4,128)S(1)} %reshape_squeeze.7), channel_id=1, source_target_pairs={{0,2},{2,4},{4,6},{1,3},{3,5},{5,7},{8,10},{10,12},{12,14},{9,11},... | collective-permute-start | bytes 6152 | tf_op jit(solution)/shard_map/ppermute | solution.py:228
  49.1 1.3 collective-permute-start.4
  50.4 3.4 %collective-permute-start.1 = (f32[16,128]{1,0:T(8,128)S(1)}, f32[16,128]{1,0:T(8,128)S(1)}, u32[]{:S(2)}, u32[]{:S(2)}) collective-permute-start(f32[16,128]{1,0:T(8,128)S(1)} %bitcast.37), channel_id=1, source_target_pairs={{0,8},{8,16},{16,24},{24,32},{32,40},{40,48},{48,56},{56,64},{64,7... | collective-permute-start | bytes 24584 | tf_op jit(solution)/shard_map/ppermute | solution.py:228
  53.8 5.8 %collective-permute-start.2 = (f32[16,128]{1,0:T(8,128)S(1)}, f32[16,128]{1,0:T(8,128)S(1)}, u32[]{:S(2)}, u32[]{:S(2)}) collective-permute-start(f32[16,128]{1,0:T(8,128)S(1)} %bitcast.36), channel_id=1, source_target_pairs={{8,0},{16,8},{24,16},{32,24},{40,32},{48,40},{56,48},{64,56},{72,6... | collective-permute-start | bytes 24584 | tf_op jit(solution)/shard_map/ppermute | solution.py:229
  61.7 3.0 %shard_map.139 = (f32[16,32,128]{2,1,0:T(8,128)}, f32[16,32,128]{2,1,0:T(8,128)}, f32[16,32,128]{2,1,0:T(8,128)}) custom-call(s32[8]{0:T(128)} %convert_element_type.22.edge_ref, f32[16,32,128]{2,1,0:T(8,128)} %v_ref.3, f32[16,32,128]{2,1,0:T(8,128)} %w_ref.1, f32[16,32,128]{2,1,0:T(8,128)} %get-tuple-element.55.cz_ref, ...), custom_call_target="tpu_custom_call" | custom-call | tf_op jit(solution)/shard_map/pallas_call | solution.py:192
  65.0 1.2 gather_fusion.2
  66.9 3.3 %shard_map.140 = (f32[16,32,128]{2,1,0:T(8,128)}, f32[32,128]{1,0:T(8,128)}, f32[32,128]{1,0:T(8,128)}, f32[256,256]{1,0:T(8,128)}, f32[32,128]{1,0:T(8,128)}, /...) custom-call(s32[8]{0:T(128)} %convert_element_type.22.edge_ref, ...), custom_call_target="tpu_custom_call" | custom-call | tf_op jit(solution)/shard_map/pallas_call | solution.py:212
  70.2 1.8 all_to_all.42
  72.0 15.4 %all-to-all-start.2 = ((f32[128,2,256]{2,1,0:T(2,128)}), f32[128,2,256]{2,1,0:T(2,128)S(1)}, u32[]{:S(2)}, u32[]{:S(2)}) async-start(f32[128,2,256]{2,1,0:T(2,128)} %all_to_all.42), calls=%async_computation.2 | async-start | bytes 524288 | tf_op jit(solution)/shard_map/all_to_all | solution.py:298
  87.7 3.4 %collective-permute-start.6 = (f32[16,128]{1,0:T(8,128)S(1)}, f32[16,128]{1,0:T(8,128)S(1)}, u32[]{:S(2)}, u32[]{:S(2)}) collective-permute-start(f32[16,128]{1,0:T(8,128)S(1)} %copy-done.37), channel_id=1, source_target_pairs={{0,8},{8,16},{16,24},{24,32},{32,40},{40,48},{48,56},{56,64},{64,7... | collective-permute-start | bytes 24584 | tf_op jit(solution)/shard_map/ppermute | solution.py:228
  91.1 5.8 %collective-permute-start.7 = (f32[16,128]{1,0:T(8,128)S(1)}, f32[16,128]{1,0:T(8,128)S(1)}, u32[]{:S(2)}, u32[]{:S(2)}) collective-permute-start(f32[16,128]{1,0:T(8,128)S(1)} %copy-done.34), channel_id=1, source_target_pairs={{8,0},{16,8},{24,16},{32,24},{40,32},{48,40},{56,48},{64,56},{72,6... | collective-permute-start | bytes 24584 | tf_op jit(solution)/shard_map/ppermute | solution.py:229
  96.9 3.4 %collective-permute-start.8 = (f32[4,128]{1,0:T(4,128)S(1)}, f32[4,128]{1,0:T(4,128)S(1)}, u32[]{:S(2)}, u32[]{:S(2)}) collective-permute-start(f32[4,128]{1,0:T(4,128)S(1)} %copy-done.43), channel_id=1, source_target_pairs={{0,2},{2,4},{4,6},{1,3},{3,5},{5,7},{8,10},{10,12},{12,14},{9,11},... | collective-permute-start | bytes 6152 | tf_op jit(solution)/shard_map/ppermute | solution.py:228
  100.3 1.3 collective-permute-start.9
  101.6 4.2 %collective-permute-done.9.yhi_ref = f32[4,128]{1,0:T(4,128)S(1)} collective-permute-done((f32[4,128]{1,0:T(4,128)S(1)}, f32[4,128]{1,0:T(4,128)S(1)}, u32[]{:S(2)}, u32[]{:S(2)}) %collective-permute-start.9) | collective-permute-done | bytes 2080 | tf_op jit(solution)/shard_map/ppermute | solution.py:229
  106.4 3.0 %shard_map.141 = (f32[16,32,128]{2,1,0:T(8,128)}, f32[16,32,128]{2,1,0:T(8,128)}, f32[16,32,128]{2,1,0:T(8,128)}) custom-call(s32[8]{0:T(128)} %convert_element_type.22.edge_ref, f32[16,32,128]{2,1,0:T(8,128)} %get-tuple-element.66.v_ref, f32[16,32,128]{2,1,0:T(8,128)} %get-tuple-element.67.w_ref, f32[16,32,128]{2,1,0:T(8,128)} %get-tuple-element.55.cz_ref, ...), custom_call_target="tpu_custom_call" | custom-call | tf_op jit(solution)/shard_map/pallas_call | solution.py:192
  109.4 0.9 all_to_all.44.recv_ref
  110.3 3.3 %shard_map.142 = (f32[16,32,128]{2,1,0:T(8,128)}, f32[32,128]{1,0:T(8,128)}, f32[32,128]{1,0:T(8,128)}, f32[256,256]{1,0:T(8,128)}, f32[32,128]{1,0:T(8,128)}, /...) custom-call(s32[8]{0:T(128)} %convert_element_type.22.edge_ref, ...), custom_call_target="tpu_custom_call" | custom-call | tf_op jit(solution)/shard_map/pallas_call | solution.py:212
  113.6 1.8 all_to_all.45
  115.4 11.1 %all-to-all-start.3 = ((f32[128,2,256]{2,1,0:T(2,128)}), f32[128,2,256]{2,1,0:T(2,128)S(1)}, u32[]{:S(2)}, u32[]{:S(2)}) async-start(f32[128,2,256]{2,1,0:T(2,128)} %all_to_all.45), calls=%async_computation.3 | async-start | bytes 524288 | tf_op jit(solution)/shard_map/all_to_all | solution.py:298
  126.7 3.4 %collective-permute-start.11 = (f32[16,128]{1,0:T(8,128)S(1)}, f32[16,128]{1,0:T(8,128)S(1)}, u32[]{:S(2)}, u32[]{:S(2)}) collective-permute-start(f32[16,128]{1,0:T(8,128)S(1)} %copy-done.35), channel_id=1, source_target_pairs={{0,8},{8,16},{16,24},{24,32},{32,40},{40,48},{48,56},{56,64},{64,7... | collective-permute-start | bytes 24584 | tf_op jit(solution)/shard_map/ppermute | solution.py:228
  130.1 5.8 %collective-permute-start.12 = (f32[16,128]{1,0:T(8,128)S(1)}, f32[16,128]{1,0:T(8,128)S(1)}, u32[]{:S(2)}, u32[]{:S(2)}) collective-permute-start(f32[16,128]{1,0:T(8,128)S(1)} %copy-done.32), channel_id=1, source_target_pairs={{8,0},{16,8},{24,16},{32,24},{40,32},{48,40},{56,48},{64,56},{72,6... | collective-permute-start | bytes 24584 | tf_op jit(solution)/shard_map/ppermute | solution.py:229
  135.9 3.4 %collective-permute-start.13 = (f32[4,128]{1,0:T(4,128)S(1)}, f32[4,128]{1,0:T(4,128)S(1)}, u32[]{:S(2)}, u32[]{:S(2)}) collective-permute-start(f32[4,128]{1,0:T(4,128)S(1)} %copy-done.41), channel_id=1, source_target_pairs={{0,2},{2,4},{4,6},{1,3},{3,5},{5,7},{8,10},{10,12},{12,14},{9,11},... | collective-permute-start | bytes 6152 | tf_op jit(solution)/shard_map/ppermute | solution.py:228
  139.3 1.3 collective-permute-start.14
  140.6 4.2 %collective-permute-done.14.yhi_ref = f32[4,128]{1,0:T(4,128)S(1)} collective-permute-done((f32[4,128]{1,0:T(4,128)S(1)}, f32[4,128]{1,0:T(4,128)S(1)}, u32[]{:S(2)}, u32[]{:S(2)}) %collective-permute-start.14) | collective-permute-done | bytes 2080 | tf_op jit(solution)/shard_map/ppermute | solution.py:229
  145.4 3.0 %shard_map.143 = (f32[16,32,128]{2,1,0:T(8,128)}, f32[16,32,128]{2,1,0:T(8,128)}, f32[16,32,128]{2,1,0:T(8,128)}) custom-call(s32[8]{0:T(128)} %convert_element_type.22.edge_ref, f32[16,32,128]{2,1,0:T(8,128)} %get-tuple-element.78.v_ref, f32[16,32,128]{2,1,0:T(8,128)} %get-tuple-element.79.w_ref, f32[16,32,128]{2,1,0:T(8,128)} %get-tuple-element.55.cz_ref, ...), custom_call_target="tpu_custom_call" | custom-call | tf_op jit(solution)/shard_map/pallas_call | solution.py:192
  148.4 0.9 all_to_all.47.recv_ref
  149.3 3.3 %shard_map.144 = (f32[16,32,128]{2,1,0:T(8,128)}, f32[32,128]{1,0:T(8,128)}, f32[32,128]{1,0:T(8,128)}, f32[256,256]{1,0:T(8,128)}, f32[32,128]{1,0:T(8,128)}, /...) custom-call(s32[8]{0:T(128)} %convert_element_type.22.edge_ref, ...), custom_call_target="tpu_custom_call" | custom-call | tf_op jit(solution)/shard_map/pallas_call | solution.py:212
  152.6 1.8 all_to_all.48
  154.4 11.1 %all-to-all-start.4 = ((f32[128,2,256]{2,1,0:T(2,128)}), f32[128,2,256]{2,1,0:T(2,128)S(1)}, u32[]{:S(2)}, u32[]{:S(2)}) async-start(f32[128,2,256]{2,1,0:T(2,128)} %all_to_all.48), calls=%async_computation.4 | async-start | bytes 524288 | tf_op jit(solution)/shard_map/all_to_all | solution.py:298
  165.7 3.4 %collective-permute-start.16 = (f32[16,128]{1,0:T(8,128)S(1)}, f32[16,128]{1,0:T(8,128)S(1)}, u32[]{:S(2)}, u32[]{:S(2)}) collective-permute-start(f32[16,128]{1,0:T(8,128)S(1)} %copy-done.36), channel_id=1, source_target_pairs={{0,8},{8,16},{16,24},{24,32},{32,40},{40,48},{48,56},{56,64},{64,7... | collective-permute-start | bytes 24584 | tf_op jit(solution)/shard_map/ppermute | solution.py:228
  169.1 5.8 %collective-permute-start.17 = (f32[16,128]{1,0:T(8,128)S(1)}, f32[16,128]{1,0:T(8,128)S(1)}, u32[]{:S(2)}, u32[]{:S(2)}) collective-permute-start(f32[16,128]{1,0:T(8,128)S(1)} %copy-done.33), channel_id=1, source_target_pairs={{8,0},{16,8},{24,16},{32,24},{40,32},{48,40},{56,48},{64,56},{72,6... | collective-permute-start | bytes 24584 | tf_op jit(solution)/shard_map/ppermute | solution.py:229
  174.9 3.4 %collective-permute-start.18 = (f32[4,128]{1,0:T(4,128)S(1)}, f32[4,128]{1,0:T(4,128)S(1)}, u32[]{:S(2)}, u32[]{:S(2)}) collective-permute-start(f32[4,128]{1,0:T(4,128)S(1)} %copy-done.42), channel_id=1, source_target_pairs={{0,2},{2,4},{4,6},{1,3},{3,5},{5,7},{8,10},{10,12},{12,14},{9,11},... | collective-permute-start | bytes 6152 | tf_op jit(solution)/shard_map/ppermute | solution.py:228
  178.3 1.3 collective-permute-start.19
  179.6 4.2 %collective-permute-done.19.yhi_ref = f32[4,128]{1,0:T(4,128)S(1)} collective-permute-done((f32[4,128]{1,0:T(4,128)S(1)}, f32[4,128]{1,0:T(4,128)S(1)}, u32[]{:S(2)}, u32[]{:S(2)}) %collective-permute-start.19) | collective-permute-done | bytes 2080 | tf_op jit(solution)/shard_map/ppermute | solution.py:229
  184.4 3.0 %shard_map.145 = (f32[16,32,128]{2,1,0:T(8,128)}, f32[16,32,128]{2,1,0:T(8,128)}, f32[16,32,128]{2,1,0:T(8,128)}) custom-call(s32[8]{0:T(128)} %convert_element_type.22.edge_ref, f32[16,32,128]{2,1,0:T(8,128)} %get-tuple-element.90.v_ref, f32[16,32,128]{2,1,0:T(8,128)} %get-tuple-element.91.w_ref, f32[16,32,128]{2,1,0:T(8,128)} %get-tuple-element.55.cz_ref, ...), custom_call_target="tpu_custom_call" | custom-call | tf_op jit(solution)/shard_map/pallas_call | solution.py:192
  187.4 0.9 all_to_all.50.recv_ref
  188.3 2.9 %shard_map.146 = (f32[16,32,128]{2,1,0:T(8,128)}, f32[32,128]{1,0:T(8,128)}, f32[32,128]{1,0:T(8,128)}) custom-call(s32[8]{0:T(128)} %convert_element_type.22.edge_ref, f32[16,32,128]{2,1,0:T(8,128)} %get-tuple-element.90.v_ref, f32[16,32,128]{2,1,0:T(8,128)} %get-tuple-element.97.base_ref, f32[16,32,128]{2,1,0:T(8,128)} %get-tuple-element.98.react_ref, ...), custom_call_target="tpu_custom_call" | custom-call | tf_op jit(solution)/shard_map/pallas_call | solution.py:212
  (145 shorter events, 13.3 us)
Async XLA Ops:
  3.5 22.1 %all-to-all-start = ((s32[128,2,1]{1,2,0:T(1,128)}), s32[128,2,1]{1,2,0:T(1,128)S(1)}, u32[]{:S(2)}, u32[]{:S(2)}) async-start(s32[128,2,1]{1,2,0:T(1,128)} %bitcast.13), calls=%async_computation | async-start | bytes 131072 | tf_op jit(solution)/shard_map/all_to_all | solution.py:263
  19.8 1.5 copy-start.1
  25.8 0.7 copy-start.27
  27.9 0.7 copy-start
  31.1 33.5 %all-to-all-start.1 = ((f32[128,2,384]{2,1,0:T(2,128)}), f32[128,2,384]{2,1,0:T(2,128)S(1)}, u32[]{:S(2)}, u32[]{:S(2)}) async-start(f32[128,2,384]{2,1,0:T(2,128)} %all_to_all.39), calls=%async_computation.1 | async-start | bytes 786432 | tf_op jit(solution)/shard_map/all_to_all | solution.py:298
  45.7 15.3 %collective-permute-start.3 = (f32[4,128]{1,0:T(4,128)S(1)}, f32[4,128]{1,0:T(4,128)S(1)}, u32[]{:S(2)}, u32[]{:S(2)}) collective-permute-start(f32[4,128]{1,0:T(4,128)S(1)} %reshape_squeeze.7), channel_id=1, source_target_pairs={{0,2},{2,4},{4,6},{1,3},{3,5},{5,7},{8,10},{10,12},{12,14},{9,11},... | collective-permute-start | bytes 6152 | tf_op jit(solution)/shard_map/ppermute | solution.py:228
  49.1 11.9 %collective-permute-start.4 = (f32[4,128]{1,0:T(4,128)S(1)}, f32[4,128]{1,0:T(4,128)S(1)}, u32[]{:S(2)}, u32[]{:S(2)}) collective-permute-start(f32[4,128]{1,0:T(4,128)S(1)} %reshape_squeeze.6), channel_id=1, source_target_pairs={{2,0},{4,2},{6,4},{3,1},{5,3},{7,5},{10,8},{12,10},{14,12},{11,9},... | collective-permute-start | bytes 6152 | tf_op jit(solution)/shard_map/ppermute | solution.py:229
  50.4 10.6 %collective-permute-start.1 = (f32[16,128]{1,0:T(8,128)S(1)}, f32[16,128]{1,0:T(8,128)S(1)}, u32[]{:S(2)}, u32[]{:S(2)}) collective-permute-start(f32[16,128]{1,0:T(8,128)S(1)} %bitcast.37), channel_id=1, source_target_pairs={{0,8},{8,16},{16,24},{24,32},{32,40},{40,48},{48,56},{56,64},{64,7... | collective-permute-start | bytes 24584 | tf_op jit(solution)/shard_map/ppermute | solution.py:228
  53.8 7.2 %collective-permute-start.2 = (f32[16,128]{1,0:T(8,128)S(1)}, f32[16,128]{1,0:T(8,128)S(1)}, u32[]{:S(2)}, u32[]{:S(2)}) collective-permute-start(f32[16,128]{1,0:T(8,128)S(1)} %bitcast.36), channel_id=1, source_target_pairs={{8,0},{16,8},{24,16},{32,24},{40,32},{48,40},{56,48},{64,56},{72,6... | collective-permute-start | bytes 24584 | tf_op jit(solution)/shard_map/ppermute | solution.py:229
  59.5 1.5 collective-permute-start
  64.9 1.3 copy-start.3
  65.0 1.2 copy-start.28
  72.0 15.4 %copy-start.31 = (f32[32,128]{1,0:T(8,128)S(1)}, f32[32,128]{1,0:T(8,128)}, u32[]{:S(2)}) copy-start(f32[32,128]{1,0:T(8,128)} %get-tuple-element.68) | copy-start | bytes 49156
  72.0 15.7 %copy-start.37 = (f32[16,128]{1,0:T(8,128)S(1)}, f32[16,128]{1,0:T(8,128)}, u32[]{:S(2)}) copy-start(f32[16,128]{1,0:T(8,128)} %get-tuple-element.69) | copy-start | bytes 24580
  72.0 19.1 %copy-start.34 = (f32[16,128]{1,0:T(8,128)S(1)}, f32[16,128]{1,0:T(8,128)}, u32[]{:S(2)}) copy-start(f32[16,128]{1,0:T(8,128)} %get-tuple-element.70) | copy-start | bytes 24580
  72.0 37.4 %all-to-all-start.2 = ((f32[128,2,256]{2,1,0:T(2,128)}), f32[128,2,256]{2,1,0:T(2,128)S(1)}, u32[]{:S(2)}, u32[]{:S(2)}) async-start(f32[128,2,256]{2,1,0:T(2,128)} %all_to_all.42), calls=%async_computation.2 | async-start | bytes 524288 | tf_op jit(solution)/shard_map/all_to_all | solution.py:298
  87.4 18.4 %collective-permute-start.5 = (f32[32,128]{1,0:T(8,128)S(1)}, f32[32,128]{1,0:T(8,128)S(1)}, u32[]{:S(2)}, u32[]{:S(2)}) collective-permute-start(f32[32,128]{1,0:T(8,128)S(1)} %copy-done.31), channel_id=1, source_target_pairs={{0,1},{1,0},{2,3},{3,2},{4,5},{5,4},{6,7},{7,6},{8,9},{9,8},{10,11... | collective-permute-start | bytes 49160 | tf_op jit(solution)/shard_map/ppermute | solution.py:225
  87.7 9.2 %copy-start.43 = (f32[4,128]{1,0:T(4,128)S(1)}, f32[4,128]{1,0:T(4,128)}, u32[]{:S(2)}) copy-start(f32[4,128]{1,0:T(4,128)} %get-tuple-element.71) | copy-start | bytes 6148
  87.7 18.1 %collective-permute-start.6 = (f32[16,128]{1,0:T(8,128)S(1)}, f32[16,128]{1,0:T(8,128)S(1)}, u32[]{:S(2)}, u32[]{:S(2)}) collective-permute-start(f32[16,128]{1,0:T(8,128)S(1)} %copy-done.37), channel_id=1, source_target_pairs={{0,8},{8,16},{16,24},{24,32},{32,40},{40,48},{48,56},{56,64},{64,7... | collective-permute-start | bytes 24584 | tf_op jit(solution)/shard_map/ppermute | solution.py:228
  91.1 9.2 %copy-start.40 = (f32[4,128]{1,0:T(4,128)S(1)}, f32[4,128]{1,0:T(4,128)}, u32[]{:S(2)}) copy-start(f32[4,128]{1,0:T(4,128)} %get-tuple-element.72) | copy-start | bytes 6148
  91.1 14.7 %collective-permute-start.7 = (f32[16,128]{1,0:T(8,128)S(1)}, f32[16,128]{1,0:T(8,128)S(1)}, u32[]{:S(2)}, u32[]{:S(2)}) collective-permute-start(f32[16,128]{1,0:T(8,128)S(1)} %copy-done.34), channel_id=1, source_target_pairs={{8,0},{16,8},{24,16},{32,24},{40,32},{48,40},{56,48},{64,56},{72,6... | collective-permute-start | bytes 24584 | tf_op jit(solution)/shard_map/ppermute | solution.py:229
  96.9 4.7 %collective-permute-start.8 = (f32[4,128]{1,0:T(4,128)S(1)}, f32[4,128]{1,0:T(4,128)S(1)}, u32[]{:S(2)}, u32[]{:S(2)}) collective-permute-start(f32[4,128]{1,0:T(4,128)S(1)} %copy-done.43), channel_id=1, source_target_pairs={{0,2},{2,4},{4,6},{1,3},{3,5},{5,7},{8,10},{10,12},{12,14},{9,11},... | collective-permute-start | bytes 6152 | tf_op jit(solution)/shard_map/ppermute | solution.py:228
  100.3 5.5 %collective-permute-start.9 = (f32[4,128]{1,0:T(4,128)S(1)}, f32[4,128]{1,0:T(4,128)S(1)}, u32[]{:S(2)}, u32[]{:S(2)}) collective-permute-start(f32[4,128]{1,0:T(4,128)S(1)} %copy-done.40), channel_id=1, source_target_pairs={{2,0},{4,2},{6,4},{3,1},{5,3},{7,5},{10,8},{12,10},{14,12},{11,9},... | collective-permute-start | bytes 6152 | tf_op jit(solution)/shard_map/ppermute | solution.py:229
  101.6 4.2 %copy-start.20 = (f32[4,128]{1,0:T(4,128)}, f32[4,128]{1,0:T(4,128)S(1)}, u32[]{:S(2)}) copy-start(f32[4,128]{1,0:T(4,128)S(1)} %collective-permute-done.8.ylo_ref) | copy-start | bytes 6148
  115.4 11.1 %copy-start.29 = (f32[32,128]{1,0:T(8,128)S(1)}, f32[32,128]{1,0:T(8,128)}, u32[]{:S(2)}) copy-start(f32[32,128]{1,0:T(8,128)} %get-tuple-element.80) | copy-start | bytes 49156
  115.4 11.3 %copy-start.35 = (f32[16,128]{1,0:T(8,128)S(1)}, f32[16,128]{1,0:T(8,128)}, u32[]{:S(2)}) copy-start(f32[16,128]{1,0:T(8,128)} %get-tuple-element.81) | copy-start | bytes 24580
  115.4 14.7 %copy-start.32 = (f32[16,128]{1,0:T(8,128)S(1)}, f32[16,128]{1,0:T(8,128)}, u32[]{:S(2)}) copy-start(f32[16,128]{1,0:T(8,128)} %get-tuple-element.82) | copy-start | bytes 24580
  115.4 33.0 %all-to-all-start.3 = ((f32[128,2,256]{2,1,0:T(2,128)}), f32[128,2,256]{2,1,0:T(2,128)S(1)}, u32[]{:S(2)}, u32[]{:S(2)}) async-start(f32[128,2,256]{2,1,0:T(2,128)} %all_to_all.45), calls=%async_computation.3 | async-start | bytes 524288 | tf_op jit(solution)/shard_map/all_to_all | solution.py:298
  126.6 18.2 %collective-permute-start.10 = (f32[32,128]{1,0:T(8,128)S(1)}, f32[32,128]{1,0:T(8,128)S(1)}, u32[]{:S(2)}, u32[]{:S(2)}) collective-permute-start(f32[32,128]{1,0:T(8,128)S(1)} %copy-done.29), channel_id=1, source_target_pairs={{0,1},{1,0},{2,3},{3,2},{4,5},{5,4},{6,7},{7,6},{8,9},{9,8},{10,11... | collective-permute-start | bytes 49160 | tf_op jit(solution)/shard_map/ppermute | solution.py:225
  126.7 9.2 %copy-start.41 = (f32[4,128]{1,0:T(4,128)S(1)}, f32[4,128]{1,0:T(4,128)}, u32[]{:S(2)}) copy-start(f32[4,128]{1,0:T(4,128)} %get-tuple-element.83) | copy-start | bytes 6148
  126.7 18.1 %collective-permute-start.11 = (f32[16,128]{1,0:T(8,128)S(1)}, f32[16,128]{1,0:T(8,128)S(1)}, u32[]{:S(2)}, u32[]{:S(2)}) collective-permute-start(f32[16,128]{1,0:T(8,128)S(1)} %copy-done.35), channel_id=1, source_target_pairs={{0,8},{8,16},{16,24},{24,32},{32,40},{40,48},{48,56},{56,64},{64,7... | collective-permute-start | bytes 24584 | tf_op jit(solution)/shard_map/ppermute | solution.py:228
  130.1 9.2 %copy-start.38 = (f32[4,128]{1,0:T(4,128)S(1)}, f32[4,128]{1,0:T(4,128)}, u32[]{:S(2)}) copy-start(f32[4,128]{1,0:T(4,128)} %get-tuple-element.84) | copy-start | bytes 6148
  130.1 14.7 %collective-permute-start.12 = (f32[16,128]{1,0:T(8,128)S(1)}, f32[16,128]{1,0:T(8,128)S(1)}, u32[]{:S(2)}, u32[]{:S(2)}) collective-permute-start(f32[16,128]{1,0:T(8,128)S(1)} %copy-done.32), channel_id=1, source_target_pairs={{8,0},{16,8},{24,16},{32,24},{40,32},{48,40},{56,48},{64,56},{72,6... | collective-permute-start | bytes 24584 | tf_op jit(solution)/shard_map/ppermute | solution.py:229
  135.9 4.7 %collective-permute-start.13 = (f32[4,128]{1,0:T(4,128)S(1)}, f32[4,128]{1,0:T(4,128)S(1)}, u32[]{:S(2)}, u32[]{:S(2)}) collective-permute-start(f32[4,128]{1,0:T(4,128)S(1)} %copy-done.41), channel_id=1, source_target_pairs={{0,2},{2,4},{4,6},{1,3},{3,5},{5,7},{8,10},{10,12},{12,14},{9,11},... | collective-permute-start | bytes 6152 | tf_op jit(solution)/shard_map/ppermute | solution.py:228
  139.3 5.5 %collective-permute-start.14 = (f32[4,128]{1,0:T(4,128)S(1)}, f32[4,128]{1,0:T(4,128)S(1)}, u32[]{:S(2)}, u32[]{:S(2)}) collective-permute-start(f32[4,128]{1,0:T(4,128)S(1)} %copy-done.38), channel_id=1, source_target_pairs={{2,0},{4,2},{6,4},{3,1},{5,3},{7,5},{10,8},{12,10},{14,12},{11,9},... | collective-permute-start | bytes 6152 | tf_op jit(solution)/shard_map/ppermute | solution.py:229
  140.6 4.2 %copy-start.21 = (f32[4,128]{1,0:T(4,128)}, f32[4,128]{1,0:T(4,128)S(1)}, u32[]{:S(2)}) copy-start(f32[4,128]{1,0:T(4,128)S(1)} %collective-permute-done.13.ylo_ref) | copy-start | bytes 6148
  154.4 11.1 %copy-start.30 = (f32[32,128]{1,0:T(8,128)S(1)}, f32[32,128]{1,0:T(8,128)}, u32[]{:S(2)}) copy-start(f32[32,128]{1,0:T(8,128)} %get-tuple-element.92) | copy-start | bytes 49156
  154.4 11.2 %copy-start.36 = (f32[16,128]{1,0:T(8,128)S(1)}, f32[16,128]{1,0:T(8,128)}, u32[]{:S(2)}) copy-start(f32[16,128]{1,0:T(8,128)} %get-tuple-element.93) | copy-start | bytes 24580
  154.4 14.7 %copy-start.33 = (f32[16,128]{1,0:T(8,128)S(1)}, f32[16,128]{1,0:T(8,128)}, u32[]{:S(2)}) copy-start(f32[16,128]{1,0:T(8,128)} %get-tuple-element.94) | copy-start | bytes 24580
  154.4 33.0 %all-to-all-start.4 = ((f32[128,2,256]{2,1,0:T(2,128)}), f32[128,2,256]{2,1,0:T(2,128)S(1)}, u32[]{:S(2)}, u32[]{:S(2)}) async-start(f32[128,2,256]{2,1,0:T(2,128)} %all_to_all.48), calls=%async_computation.4 | async-start | bytes 524288 | tf_op jit(solution)/shard_map/all_to_all | solution.py:298
  165.6 18.2 %collective-permute-start.15 = (f32[32,128]{1,0:T(8,128)S(1)}, f32[32,128]{1,0:T(8,128)S(1)}, u32[]{:S(2)}, u32[]{:S(2)}) collective-permute-start(f32[32,128]{1,0:T(8,128)S(1)} %copy-done.30), channel_id=1, source_target_pairs={{0,1},{1,0},{2,3},{3,2},{4,5},{5,4},{6,7},{7,6},{8,9},{9,8},{10,11... | collective-permute-start | bytes 49160 | tf_op jit(solution)/shard_map/ppermute | solution.py:225
  165.7 9.2 %copy-start.42 = (f32[4,128]{1,0:T(4,128)S(1)}, f32[4,128]{1,0:T(4,128)}, u32[]{:S(2)}) copy-start(f32[4,128]{1,0:T(4,128)} %get-tuple-element.95) | copy-start | bytes 6148
  165.7 18.1 %collective-permute-start.16 = (f32[16,128]{1,0:T(8,128)S(1)}, f32[16,128]{1,0:T(8,128)S(1)}, u32[]{:S(2)}, u32[]{:S(2)}) collective-permute-start(f32[16,128]{1,0:T(8,128)S(1)} %copy-done.36), channel_id=1, source_target_pairs={{0,8},{8,16},{16,24},{24,32},{32,40},{40,48},{48,56},{56,64},{64,7... | collective-permute-start | bytes 24584 | tf_op jit(solution)/shard_map/ppermute | solution.py:228
  169.1 9.2 %copy-start.39 = (f32[4,128]{1,0:T(4,128)S(1)}, f32[4,128]{1,0:T(4,128)}, u32[]{:S(2)}) copy-start(f32[4,128]{1,0:T(4,128)} %get-tuple-element.96) | copy-start | bytes 6148
  169.1 14.7 %collective-permute-start.17 = (f32[16,128]{1,0:T(8,128)S(1)}, f32[16,128]{1,0:T(8,128)S(1)}, u32[]{:S(2)}, u32[]{:S(2)}) collective-permute-start(f32[16,128]{1,0:T(8,128)S(1)} %copy-done.33), channel_id=1, source_target_pairs={{8,0},{16,8},{24,16},{32,24},{40,32},{48,40},{56,48},{64,56},{72,6... | collective-permute-start | bytes 24584 | tf_op jit(solution)/shard_map/ppermute | solution.py:229
  174.9 4.7 %collective-permute-start.18 = (f32[4,128]{1,0:T(4,128)S(1)}, f32[4,128]{1,0:T(4,128)S(1)}, u32[]{:S(2)}, u32[]{:S(2)}) collective-permute-start(f32[4,128]{1,0:T(4,128)S(1)} %copy-done.42), channel_id=1, source_target_pairs={{0,2},{2,4},{4,6},{1,3},{3,5},{5,7},{8,10},{10,12},{12,14},{9,11},... | collective-permute-start | bytes 6152 | tf_op jit(solution)/shard_map/ppermute | solution.py:228
  178.3 5.5 %collective-permute-start.19 = (f32[4,128]{1,0:T(4,128)S(1)}, f32[4,128]{1,0:T(4,128)S(1)}, u32[]{:S(2)}, u32[]{:S(2)}) collective-permute-start(f32[4,128]{1,0:T(4,128)S(1)} %copy-done.39), channel_id=1, source_target_pairs={{2,0},{4,2},{6,4},{3,1},{5,3},{7,5},{10,8},{12,10},{14,12},{11,9},... | collective-permute-start | bytes 6152 | tf_op jit(solution)/shard_map/ppermute | solution.py:229
  179.6 4.2 %copy-start.19 = (f32[4,128]{1,0:T(4,128)}, f32[4,128]{1,0:T(4,128)S(1)}, u32[]{:S(2)}) copy-start(f32[4,128]{1,0:T(4,128)S(1)} %collective-permute-done.18.ylo_ref) | copy-start | bytes 6148
  (21 other events, 12.7 us)

commit v8 on v6

--- a/solution.py
+++ b/solution.py
@@ -1,3 +1,5 @@
+import functools
+
 import jax
 import jax.numpy as jnp
 from jax import lax
@@ -47,19 +49,26 @@
     return (dot(a) + dot(b)) + dot(c)
 
 
-def step_kernel(
-    edge_ref,
-    v_ref, w_ref, cz_ref, cx_ref, cy_ref, recv_ref, tg_ref, g_ref,
-    tv_ref, tr_ref, cg_ref, zr_ref, xlo_ref, xhi_ref, ylo_ref, yhi_ref,
-    oh_blk_ref, oh_blk_t_ref, oh_slot_ref, oh_ids_ref, oh_ids_t_ref, oh_sblk_ref,
-    nv_ref, nw_ref, ntv_ref, ntr_ref, snd_ref, zs_ref, xf_ref, xl_ref, yf_ref, yl_ref,
-):
+def step_kernel(*refs, first, pack):
+    refs = iter(refs)
+    edge_ref, v_ref, w_ref, cz_ref, cx_ref, cy_ref, recv_ref = (next(refs) for _ in range(7))
+    tg_ref = None if first else next(refs)
+    g_ref, tv_ref, tr_ref, cg_ref, zr_ref, xlo_ref, xhi_ref, ylo_ref, yhi_ref = (next(refs) for _ in range(9))
+    oh_blk_ref, oh_blk_t_ref, oh_slot_ref, oh_ids_ref, oh_ids_t_ref, oh_sblk_ref = (next(refs) for _ in range(6))
+    nv_ref, nw_ref, ntv_ref, ntr_ref = (next(refs) for _ in range(4))
+    if pack:
+        snd_ref, zs_ref, xf_ref, xl_ref, yf_ref, yl_ref = (next(refs) for _ in range(6))
     depth, rows_x, width = v_ref.shape
+    if first:
+        tile_gain = one_hot_dot(oh_slot_ref[...], recv_ref[:, 2 * width:3 * width])
+        next(refs)[...] = tile_gain
+    else:
+        tile_gain = tg_ref[...]
 
     v_flat = v_ref[...].reshape(depth * rows_x, width)
     rows = one_hot_dot(oh_blk_ref[...], v_flat)
     far = one_hot_dot(oh_slot_ref[...], recv_ref[:, width:2 * width])
-    tile_current = tg_ref[...] * (far - rows)
+    tile_current = tile_gain * (far - rows)
     into_voxel = one_hot_dot(oh_blk_t_ref[...], tile_current)
 
     far_volt = one_hot_dot(oh_ids_t_ref[...], tv_ref[...])
@@ -87,8 +96,9 @@
     y_low = flag(edge_ref, 4, (rows_x, 1))
     y_high = flag(edge_ref, 5, (rows_x, 1))
     per_row = width // rows_x
-    y_first = [jnp.zeros((1, width), jnp.float32) for _ in range(yf_ref.shape[0])]
-    y_last = [jnp.zeros((1, width), jnp.float32) for _ in range(yf_ref.shape[0])]
+    face_rows = depth * rows_x // width
+    y_first = [jnp.zeros((1, width), jnp.float32) for _ in range(face_rows)]
+    y_last = [jnp.zeros((1, width), jnp.float32) for _ in range(face_rows)]
     for z in range(depth):
         vz = v_ref[z]
         if z == 0:
@@ -120,13 +130,17 @@
         nv = vz + (cz_ref[z] * lap_z + cx_ref[z] * lap_x + cy_ref[z] * lap_y) + react_v
         nv_ref[z] = nv
         nw_ref[z] = new_w
+        if not pack:
+            continue
         xf_ref[z:z + 1, :] = nv[0:1, :]
         xl_ref[z:z + 1, :] = nv[rows_x - 1:rows_x, :]
         y_first[row_at] = y_first[row_at] + jnp.sum(
             jnp.where(pick, nv[:, 0:1], 0.0), axis=0, keepdims=True)
         y_last[row_at] = y_last[row_at] + jnp.sum(
             jnp.where(pick, nv[:, width - 1:width], 0.0), axis=0, keepdims=True)
-    for i in range(yf_ref.shape[0]):
+    if not pack:
+        return
+    for i in range(face_rows):
         yf_ref[i:i + 1, :] = y_first[i]
         yl_ref[i:i + 1, :] = y_last[i]
     zs_ref[...] = jnp.where(z_low, nv_ref[depth - 1], nv_ref[0])
@@ -157,10 +171,11 @@
     )(fiber_table, fiber_class)
 
 
-def run_step(tables, state, recv, tile_gain, gains_rows, cable_rows, halos):
+def run_step(tables, state, recv, tile_gain, gains_rows, cable_rows, halos, pack):
     volt, recovery, coef_z, coef_x, coef_y, term_volt, term_recovery = state
     depth, rows_x, width = volt.shape
     slots = recv.shape[0]
+    first = tile_gain is None
     f32 = jnp.float32
     smem = pl.BlockSpec(memory_space=pltpu.SMEM)
     vmem = pl.BlockSpec(memory_space=pltpu.VMEM)
@@ -169,23 +184,29 @@
         jax.ShapeDtypeStruct(volt.shape, f32),
         jax.ShapeDtypeStruct(term_volt.shape, f32),
         jax.ShapeDtypeStruct(term_volt.shape, f32),
-        jax.ShapeDtypeStruct((slots, 2 * width), f32),
-        jax.ShapeDtypeStruct((rows_x, width), f32),
-        jax.ShapeDtypeStruct((depth, width), f32),
-        jax.ShapeDtypeStruct((depth, width), f32),
-        jax.ShapeDtypeStruct((depth * rows_x // width, width), f32),
-        jax.ShapeDtypeStruct((depth * rows_x // width, width), f32),
     )
+    if pack:
+        out_shape += (
+            jax.ShapeDtypeStruct((slots, 2 * width), f32),
+            jax.ShapeDtypeStruct((rows_x, width), f32),
+            jax.ShapeDtypeStruct((depth, width), f32),
+            jax.ShapeDtypeStruct((depth, width), f32),
+            jax.ShapeDtypeStruct((depth * rows_x // width, width), f32),
+            jax.ShapeDtypeStruct((depth * rows_x // width, width), f32),
+        )
+    if first:
+        out_shape += (jax.ShapeDtypeStruct((tables[1][2].shape[0], width), f32),)
     edges, one_hots = tables
-    operands = (edges, volt, recovery, coef_z, coef_x, coef_y, recv, tile_gain,
-                gains_rows, term_volt, term_recovery, cable_rows) + tuple(halos) + tuple(one_hots)
-    return pl.pallas_call(
-        step_kernel,
+    operands = ((edges, volt, recovery, coef_z, coef_x, coef_y, recv) + (() if first else (tile_gain,))
+                + (gains_rows, term_volt, term_recovery, cable_rows) + tuple(halos) + tuple(one_hots))
+    outs = pl.pallas_call(
+        functools.partial(step_kernel, first=first, pack=pack),
         out_shape=out_shape,
         in_specs=[smem] + [vmem] * (len(operands) - 1),
         out_specs=[vmem] * len(out_shape),
         interpret=INTERPRET,
     )(*operands)
+    return outs
 
 
 def exchange_halos(faces):
@@ -265,12 +286,14 @@
     for step in range(STEPS):
         halos = exchange_halos(faces)
         received = lax.all_to_all(sent, ("gx", "gy"), split_axis=0, concat_axis=0, tiled=True)
+        state = (volt, recovery, coef_z, coef_x, coef_y, term_volt, term_recovery)
+        pack = step < STEPS - 1
+        outs = run_step(tables, state, received, tile_gain, gain_rows, cable_rows, halos, pack)
         if step == 0:
-            tile_gain = received[:, 2 * width:3 * width][slot]
-        state = (volt, recovery, coef_z, coef_x, coef_y, term_volt, term_recovery)
-        outs = run_step(tables, state, received, tile_gain, gain_rows, cable_rows, halos)
-        volt, recovery, term_volt, term_recovery, sent = outs[:5]
-        faces = outs[5:]
+            tile_gain = outs[-1]
+        volt, recovery, term_volt, term_recovery = outs[:4]
+        if pack:
+            sent, faces = outs[4], outs[5:10]
     return (volt, recovery, term_volt, term_recovery)
 
 

time: 180 us -> 179 us (level)
  waiting for transfers between devices: 9.89 us -> 12.3 us
  starting transfers between devices: 120 us -> 118 us
    all_to_all x1, waiting for transfers between devices: 0.01 us -> 2.43 us  [on_device(): lax.all_to_all(slot_term, ('gx', 'gy'), split_axis=0, concat_axis=0, tile...]
    all_to_all x4, starting transfers between devices: 49.8 us -> 47.9 us  [on_device(): lax.all_to_all(sent, ('gx', 'gy'), split_axis=0, concat_axis=0, tiled=True)]
    unnamed x88 -> x86, local copies, waits for them, and re-layouts: 5.46 us -> 5.46 us
  transfers between devices with their start and end apart: 25 -> 25, of which waited for: 3 -> 4; matrix products, arithmetic and copies ran while one was open for 5% -> 5% of each run, Pallas kernels for 1% -> 1%
where the time goes in v8:
time: 179 us; the launch traced here: 177 us
  starting transfers between devices  118 us (66%)
  local copies, waits for them, and re-layouts  21.8 us (12%)
  Pallas kernels  17.9 us (10%)
  waiting for transfers between devices  12.3 us (7%)
  other arithmetic  6.25 us (3%)
    all_to_all x4, starting transfers between devices, on_device(): lax.all_to_all(sent, ('gx', 'gy'), split_axis=0, concat_axis=0, tiled=True)  47.9 us
    ppermute x8, starting transfers between devices, exchange_halos(): lax.ppermute(first, axis, [(i + 1, i) for i in range(count - 1)])  28.2 us
    ppermute x8, starting transfers between devices, exchange_halos(): lax.ppermute(last, axis, [(i, i + 1) for i in range(count - 1)])  27.1 us
    pallas_call x4, Pallas kernels, run_step(): pl.pallas_call(functools.partial(step_kernel, first=first, pack=pack), ou...  15.7 us
    all_to_all x1, starting transfers between devices, on_device(): lax.all_to_all(slot_term, ('gx', 'gy'), split_axis=0, concat_axis=0, tile...  14 us
    all_to_all x8, local copies, waits for them, and re-layouts, on_device(): lax.all_to_all(sent, ('gx', 'gy'), split_axis=0, concat_axis=0, tiled=True)  10 us
    ppermute x8, waiting for transfers between devices, exchange_halos(): lax.ppermute(first, axis, [(i + 1, i) for i in range(count - 1)])  9.87 us
    unnamed x86, local copies, waits for them, and re-layouts  5.46 us
  transfers between devices with their start and end apart: 25, of which 4 were waited for; matrix products, arithmetic and copies ran while one was open for 5% of the time, Pallas kernels for 1%

profile of v8, /device:TPU:128, one launch (start us, length us, event | category | flops | bytes accessed | tf_op | source)
XLA Modules:
  0.0 177.3 jit_solution(12576122433413839627)
XLA Ops:
  2.8 0.8 sub.7
  3.5 14.0 %all-to-all-start = ((s32[128,2,1]{1,2,0:T(1,128)}), s32[128,2,1]{1,2,0:T(1,128)S(1)}, u32[]{:S(2)}, u32[]{:S(2)}) async-start(s32[128,2,1]{1,2,0:T(1,128)} %bitcast.13), calls=%async_computation | async-start | bytes 131072 | tf_op jit(solution)/shard_map/all_to_all | solution.py:253
  17.5 0.9 fusion.8
  18.4 1.4 slice_reduce_fusion
  20.5 0.7 fusion.1.refs_16_.refs_17_
  21.4 0.7 gather_fusion
  22.1 2.4 %all-to-all-done = s32[128,2,1]{1,2,0:T(1,128)S(1)} async-done(((s32[128,2,1]{1,2,0:T(1,128)}), s32[128,2,1]{1,2,0:T(1,128)S(1)}, u32[]{:S(2)}, u32[]{:S(2)}) %all-to-all-start) | async-done | bytes 1056 | tf_op jit(solution)/shard_map/all_to_all | solution.py:253
  26.1 0.8 reduce.9
  27.6 0.7 gather_fusion.1
  29.1 1.0 all_to_all.39
  30.1 11.3 %all-to-all-start.1 = ((f32[128,2,384]{2,1,0:T(2,128)}), f32[128,2,384]{2,1,0:T(2,128)S(1)}, u32[]{:S(2)}, u32[]{:S(2)}) async-start(f32[128,2,384]{2,1,0:T(2,128)} %all_to_all.39), calls=%async_computation.1 | async-start | bytes 786432 | tf_op jit(solution)/shard_map/all_to_all | solution.py:288
  41.4 0.7 fusion.3.refs_18_.refs_19_
  42.8 2.1 %shard_map.138 = (f32[16,32,128]{2,1,0:T(8,128)}, f32[16,32,128]{2,1,0:T(8,128)}, f32[16,32,128]{2,1,0:T(8,128)}) custom-call(f32[3,8]{1,0:T(4,128)} %table_ref.1, s32[16,32,128]{2,1,0:T(8,128)} %cls_ref.1), custom_call_target="tpu_custom_call" | custom-call | tf_op jit(solution)/shard_map/pallas_call | solution.py:165
  44.9 0.8 fusion.refs_21_.refs_22_
  45.7 3.4 %collective-permute-start.3 = (f32[4,128]{1,0:T(4,128)S(1)}, f32[4,128]{1,0:T(4,128)S(1)}, u32[]{:S(2)}, u32[]{:S(2)}) collective-permute-start(f32[4,128]{1,0:T(4,128)S(1)} %reshape_squeeze.7), channel_id=1, source_target_pairs={{0,2},{2,4},{4,6},{1,3},{3,5},{5,7},{8,10},{10,12},{12,14},{9,11},... | collective-permute-start | bytes 6152 | tf_op jit(solution)/shard_map/ppermute | solution.py:218
  49.1 1.3 collective-permute-start.4
  50.4 3.4 %collective-permute-start.1 = (f32[16,128]{1,0:T(8,128)S(1)}, f32[16,128]{1,0:T(8,128)S(1)}, u32[]{:S(2)}, u32[]{:S(2)}) collective-permute-start(f32[16,128]{1,0:T(8,128)S(1)} %bitcast.33), channel_id=1, source_target_pairs={{0,8},{8,16},{16,24},{24,32},{32,40},{40,48},{48,56},{56,64},{64,7... | collective-permute-start | bytes 24584 | tf_op jit(solution)/shard_map/ppermute | solution.py:218
  53.8 5.8 %collective-permute-start.2 = (f32[16,128]{1,0:T(8,128)S(1)}, f32[16,128]{1,0:T(8,128)S(1)}, u32[]{:S(2)}, u32[]{:S(2)}) collective-permute-start(f32[16,128]{1,0:T(8,128)S(1)} %bitcast.32), channel_id=1, source_target_pairs={{8,0},{16,8},{24,16},{32,24},{40,32},{48,40},{56,48},{64,56},{72,6... | collective-permute-start | bytes 24584 | tf_op jit(solution)/shard_map/ppermute | solution.py:219
  59.7 0.7 fusion.4.refs_20_.refs_21_
  61.0 1.0 all_to_all.41.refs_6_
  62.8 4.0 %shard_map.139 = (f32[16,32,128]{2,1,0:T(8,128)}, f32[16,32,128]{2,1,0:T(8,128)}, f32[32,128]{1,0:T(8,128)}, f32[32,128]{1,0:T(8,128)}, f32[256,256]{1,0:T(8,128...) custom-call(s32[8]{0:T(128)} %convert_element_type.22.refs_0_, ...), custom_call_target="tpu_custom_call" | custom-call | tf_op jit(solution)/shard_map/pallas_call | solution.py:202
  66.9 1.8 %all_to_all.42 = f32[128,2,256]{2,1,0:T(2,128)} reshape(f32[256,256]{1,0:T(8,128)} %get-tuple-element.55) | data formatting | bytes 524288 | tf_op jit(solution)/shard_map/all_to_all | solution.py:288
  68.7 14.3 %all-to-all-start.2 = ((f32[128,2,256]{2,1,0:T(2,128)}), f32[128,2,256]{2,1,0:T(2,128)S(1)}, u32[]{:S(2)}, u32[]{:S(2)}) async-start(f32[128,2,256]{2,1,0:T(2,128)} %all_to_all.42), calls=%async_computation.2 | async-start | bytes 524288 | tf_op jit(solution)/shard_map/all_to_all | solution.py:288
  83.2 3.4 %collective-permute-start.6 = (f32[16,128]{1,0:T(8,128)S(1)}, f32[16,128]{1,0:T(8,128)S(1)}, u32[]{:S(2)}, u32[]{:S(2)}) collective-permute-start(f32[16,128]{1,0:T(8,128)S(1)} %copy-done.36), channel_id=1, source_target_pairs={{0,8},{8,16},{16,24},{24,32},{32,40},{40,48},{48,56},{56,64},{64,7... | collective-permute-start | bytes 24584 | tf_op jit(solution)/shard_map/ppermute | solution.py:218
  86.6 5.8 %collective-permute-start.7 = (f32[16,128]{1,0:T(8,128)S(1)}, f32[16,128]{1,0:T(8,128)S(1)}, u32[]{:S(2)}, u32[]{:S(2)}) collective-permute-start(f32[16,128]{1,0:T(8,128)S(1)} %copy-done.33), channel_id=1, source_target_pairs={{8,0},{16,8},{24,16},{32,24},{40,32},{48,40},{56,48},{64,56},{72,6... | collective-permute-start | bytes 24584 | tf_op jit(solution)/shard_map/ppermute | solution.py:219
  92.4 3.4 %collective-permute-start.8 = (f32[4,128]{1,0:T(4,128)S(1)}, f32[4,128]{1,0:T(4,128)S(1)}, u32[]{:S(2)}, u32[]{:S(2)}) collective-permute-start(f32[4,128]{1,0:T(4,128)S(1)} %copy-done.42), channel_id=1, source_target_pairs={{0,2},{2,4},{4,6},{1,3},{3,5},{5,7},{8,10},{10,12},{12,14},{9,11},... | collective-permute-start | bytes 6152 | tf_op jit(solution)/shard_map/ppermute | solution.py:218
  95.8 1.3 collective-permute-start.9
  97.1 0.9 all_to_all.44.refs_6_
  98.0 3.3 %collective-permute-done.9.refs_16_ = f32[4,128]{1,0:T(4,128)S(1)} collective-permute-done((f32[4,128]{1,0:T(4,128)S(1)}, f32[4,128]{1,0:T(4,128)S(1)}, u32[]{:S(2)}, u32[]{:S(2)}) %collective-permute-start.9) | collective-permute-done | bytes 2080 | tf_op jit(solution)/shard_map/ppermute | solution.py:219
  101.9 4.1 %shard_map.140 = (f32[16,32,128]{2,1,0:T(8,128)}, f32[16,32,128]{2,1,0:T(8,128)}, f32[32,128]{1,0:T(8,128)}, f32[32,128]{1,0:T(8,128)}, f32[256,256]{1,0:T(8,128...) custom-call(s32[8]{0:T(128)} %convert_element_type.22.refs_0_, ...), custom_call_target="tpu_custom_call" | custom-call | tf_op jit(solution)/shard_map/pallas_call | solution.py:202
  106.0 1.8 %all_to_all.45 = f32[128,2,256]{2,1,0:T(2,128)} reshape(f32[256,256]{1,0:T(8,128)} %get-tuple-element.66) | data formatting | bytes 524288 | tf_op jit(solution)/shard_map/all_to_all | solution.py:288
  107.8 11.1 %all-to-all-start.3 = ((f32[128,2,256]{2,1,0:T(2,128)}), f32[128,2,256]{2,1,0:T(2,128)S(1)}, u32[]{:S(2)}, u32[]{:S(2)}) async-start(f32[128,2,256]{2,1,0:T(2,128)} %all_to_all.45), calls=%async_computation.3 | async-start | bytes 524288 | tf_op jit(solution)/shard_map/all_to_all | solution.py:288
  119.1 3.4 %collective-permute-start.11 = (f32[16,128]{1,0:T(8,128)S(1)}, f32[16,128]{1,0:T(8,128)S(1)}, u32[]{:S(2)}, u32[]{:S(2)}) collective-permute-start(f32[16,128]{1,0:T(8,128)S(1)} %copy-done.34), channel_id=1, source_target_pairs={{0,8},{8,16},{16,24},{24,32},{32,40},{40,48},{48,56},{56,64},{64,7... | collective-permute-start | bytes 24584 | tf_op jit(solution)/shard_map/ppermute | solution.py:218
  122.5 5.8 %collective-permute-start.12 = (f32[16,128]{1,0:T(8,128)S(1)}, f32[16,128]{1,0:T(8,128)S(1)}, u32[]{:S(2)}, u32[]{:S(2)}) collective-permute-start(f32[16,128]{1,0:T(8,128)S(1)} %copy-done.31), channel_id=1, source_target_pairs={{8,0},{16,8},{24,16},{32,24},{40,32},{48,40},{56,48},{64,56},{72,6... | collective-permute-start | bytes 24584 | tf_op jit(solution)/shard_map/ppermute | solution.py:219
  128.3 3.4 %collective-permute-start.13 = (f32[4,128]{1,0:T(4,128)S(1)}, f32[4,128]{1,0:T(4,128)S(1)}, u32[]{:S(2)}, u32[]{:S(2)}) collective-permute-start(f32[4,128]{1,0:T(4,128)S(1)} %copy-done.40), channel_id=1, source_target_pairs={{0,2},{2,4},{4,6},{1,3},{3,5},{5,7},{8,10},{10,12},{12,14},{9,11},... | collective-permute-start | bytes 6152 | tf_op jit(solution)/shard_map/ppermute | solution.py:218
  131.7 1.3 collective-permute-start.14
  133.0 0.9 all_to_all.47.refs_6_
  133.9 3.3 %collective-permute-done.14.refs_16_ = f32[4,128]{1,0:T(4,128)S(1)} collective-permute-done((f32[4,128]{1,0:T(4,128)S(1)}, f32[4,128]{1,0:T(4,128)S(1)}, u32[]{:S(2)}, u32[]{:S(2)}) %collective-permute-start.14) | collective-permute-done | bytes 2080 | tf_op jit(solution)/shard_map/ppermute | solution.py:219
  137.8 4.1 %shard_map.141 = (f32[16,32,128]{2,1,0:T(8,128)}, f32[16,32,128]{2,1,0:T(8,128)}, f32[32,128]{1,0:T(8,128)}, f32[32,128]{1,0:T(8,128)}, f32[256,256]{1,0:T(8,128...) custom-call(s32[8]{0:T(128)} %convert_element_type.22.refs_0_, ...), custom_call_target="tpu_custom_call" | custom-call | tf_op jit(solution)/shard_map/pallas_call | solution.py:202
  141.9 1.8 %all_to_all.48 = f32[128,2,256]{2,1,0:T(2,128)} reshape(f32[256,256]{1,0:T(8,128)} %get-tuple-element.76) | data formatting | bytes 524288 | tf_op jit(solution)/shard_map/all_to_all | solution.py:288
  143.7 11.1 %all-to-all-start.4 = ((f32[128,2,256]{2,1,0:T(2,128)}), f32[128,2,256]{2,1,0:T(2,128)S(1)}, u32[]{:S(2)}, u32[]{:S(2)}) async-start(f32[128,2,256]{2,1,0:T(2,128)} %all_to_all.48), calls=%async_computation.4 | async-start | bytes 524288 | tf_op jit(solution)/shard_map/all_to_all | solution.py:288
  155.0 3.4 %collective-permute-start.16 = (f32[16,128]{1,0:T(8,128)S(1)}, f32[16,128]{1,0:T(8,128)S(1)}, u32[]{:S(2)}, u32[]{:S(2)}) collective-permute-start(f32[16,128]{1,0:T(8,128)S(1)} %copy-done.35), channel_id=1, source_target_pairs={{0,8},{8,16},{16,24},{24,32},{32,40},{40,48},{48,56},{56,64},{64,7... | collective-permute-start | bytes 24584 | tf_op jit(solution)/shard_map/ppermute | solution.py:218
  158.4 5.8 %collective-permute-start.17 = (f32[16,128]{1,0:T(8,128)S(1)}, f32[16,128]{1,0:T(8,128)S(1)}, u32[]{:S(2)}, u32[]{:S(2)}) collective-permute-start(f32[16,128]{1,0:T(8,128)S(1)} %copy-done.32), channel_id=1, source_target_pairs={{8,0},{16,8},{24,16},{32,24},{40,32},{48,40},{56,48},{64,56},{72,6... | collective-permute-start | bytes 24584 | tf_op jit(solution)/shard_map/ppermute | solution.py:219
  164.2 3.4 %collective-permute-start.18 = (f32[4,128]{1,0:T(4,128)S(1)}, f32[4,128]{1,0:T(4,128)S(1)}, u32[]{:S(2)}, u32[]{:S(2)}) collective-permute-start(f32[4,128]{1,0:T(4,128)S(1)} %copy-done.41), channel_id=1, source_target_pairs={{0,2},{2,4},{4,6},{1,3},{3,5},{5,7},{8,10},{10,12},{12,14},{9,11},... | collective-permute-start | bytes 6152 | tf_op jit(solution)/shard_map/ppermute | solution.py:218
  167.6 1.3 collective-permute-start.19
  168.9 0.9 all_to_all.50.refs_6_
  169.8 3.3 %collective-permute-done.19.refs_16_ = f32[4,128]{1,0:T(4,128)S(1)} collective-permute-done((f32[4,128]{1,0:T(4,128)S(1)}, f32[4,128]{1,0:T(4,128)S(1)}, u32[]{:S(2)}, u32[]{:S(2)}) %collective-permute-start.19) | collective-permute-done | bytes 2080 | tf_op jit(solution)/shard_map/ppermute | solution.py:219
  173.7 3.5 %shard_map.142 = (f32[16,32,128]{2,1,0:T(8,128)}, f32[16,32,128]{2,1,0:T(8,128)}, f32[32,128]{1,0:T(8,128)}, f32[32,128]{1,0:T(8,128)}) custom-call(s32[8]{0:T(128)} %convert_element_type.22.refs_0_, f32[16,32,128]{2,1,0:T(8,128)} %get-tuple-element.74.refs_1_, f32[16,32,128]{2,1,0:T(8,128)} %get-tuple-element.75.refs_2_, ...), custom_call_target="tpu_custom_call" | custom-call | tf_op jit(solution)/shard_map/pallas_call | solution.py:202
  (136 shorter events, 10.2 us)
Async XLA Ops:
  3.5 21.0 %all-to-all-start = ((s32[128,2,1]{1,2,0:T(1,128)}), s32[128,2,1]{1,2,0:T(1,128)S(1)}, u32[]{:S(2)}, u32[]{:S(2)}) async-start(s32[128,2,1]{1,2,0:T(1,128)} %bitcast.13), calls=%async_computation | async-start | bytes 131072 | tf_op jit(solution)/shard_map/all_to_all | solution.py:253
  19.8 1.4 copy-start.1
  30.1 31.0 %all-to-all-start.1 = ((f32[128,2,384]{2,1,0:T(2,128)}), f32[128,2,384]{2,1,0:T(2,128)S(1)}, u32[]{:S(2)}, u32[]{:S(2)}) async-start(f32[128,2,384]{2,1,0:T(2,128)} %all_to_all.39), calls=%async_computation.1 | async-start | bytes 786432 | tf_op jit(solution)/shard_map/all_to_all | solution.py:288
  45.7 16.3 %collective-permute-start.3 = (f32[4,128]{1,0:T(4,128)S(1)}, f32[4,128]{1,0:T(4,128)S(1)}, u32[]{:S(2)}, u32[]{:S(2)}) collective-permute-start(f32[4,128]{1,0:T(4,128)S(1)} %reshape_squeeze.7), channel_id=1, source_target_pairs={{0,2},{2,4},{4,6},{1,3},{3,5},{5,7},{8,10},{10,12},{12,14},{9,11},... | collective-permute-start | bytes 6152 | tf_op jit(solution)/shard_map/ppermute | solution.py:218
  49.1 13.0 %collective-permute-start.4 = (f32[4,128]{1,0:T(4,128)S(1)}, f32[4,128]{1,0:T(4,128)S(1)}, u32[]{:S(2)}, u32[]{:S(2)}) collective-permute-start(f32[4,128]{1,0:T(4,128)S(1)} %reshape_squeeze.6), channel_id=1, source_target_pairs={{2,0},{4,2},{6,4},{3,1},{5,3},{7,5},{10,8},{12,10},{14,12},{11,9},... | collective-permute-start | bytes 6152 | tf_op jit(solution)/shard_map/ppermute | solution.py:219
  50.4 11.7 %collective-permute-start.1 = (f32[16,128]{1,0:T(8,128)S(1)}, f32[16,128]{1,0:T(8,128)S(1)}, u32[]{:S(2)}, u32[]{:S(2)}) collective-permute-start(f32[16,128]{1,0:T(8,128)S(1)} %bitcast.33), channel_id=1, source_target_pairs={{0,8},{8,16},{16,24},{24,32},{32,40},{40,48},{48,56},{56,64},{64,7... | collective-permute-start | bytes 24584 | tf_op jit(solution)/shard_map/ppermute | solution.py:218
  53.8 8.3 %collective-permute-start.2 = (f32[16,128]{1,0:T(8,128)S(1)}, f32[16,128]{1,0:T(8,128)S(1)}, u32[]{:S(2)}, u32[]{:S(2)}) collective-permute-start(f32[16,128]{1,0:T(8,128)S(1)} %bitcast.32), channel_id=1, source_target_pairs={{8,0},{16,8},{24,16},{32,24},{40,32},{48,40},{56,48},{64,56},{72,6... | collective-permute-start | bytes 24584 | tf_op jit(solution)/shard_map/ppermute | solution.py:219
  59.6 2.5 %collective-permute-start = (f32[32,128]{1,0:T(8,128)S(1)}, f32[32,128]{1,0:T(8,128)S(1)}, u32[]{:S(2)}, u32[]{:S(2)}) collective-permute-start(f32[32,128]{1,0:T(8,128)S(1)} %select_bitcast_fusion), channel_id=1, source_target_pairs={{0,1},{1,0},{2,3},{3,2},{4,5},{5,4},{6,7},{7,6},{8,9},{9,8},{10,11... | collective-permute-start | bytes 49160 | tf_op jit(solution)/shard_map/ppermute | solution.py:215
  61.0 1.1 copy-start.27
  62.1 0.8 copy-start.16
  62.1 0.8 copy-start.17
  62.1 0.7 copy-start.11
  68.7 14.3 %copy-start.30 = (f32[32,128]{1,0:T(8,128)S(1)}, f32[32,128]{1,0:T(8,128)}, u32[]{:S(2)}) copy-start(f32[32,128]{1,0:T(8,128)} %get-tuple-element.59) | copy-start | bytes 49156
  68.7 14.5 %copy-start.36 = (f32[16,128]{1,0:T(8,128)S(1)}, f32[16,128]{1,0:T(8,128)}, u32[]{:S(2)}) copy-start(f32[16,128]{1,0:T(8,128)} %get-tuple-element.60) | copy-start | bytes 24580
  68.7 17.9 %copy-start.33 = (f32[16,128]{1,0:T(8,128)S(1)}, f32[16,128]{1,0:T(8,128)}, u32[]{:S(2)}) copy-start(f32[16,128]{1,0:T(8,128)} %get-tuple-element.61) | copy-start | bytes 24580
  68.7 28.4 %all-to-all-start.2 = ((f32[128,2,256]{2,1,0:T(2,128)}), f32[128,2,256]{2,1,0:T(2,128)S(1)}, u32[]{:S(2)}, u32[]{:S(2)}) async-start(f32[128,2,256]{2,1,0:T(2,128)} %all_to_all.42), calls=%async_computation.2 | async-start | bytes 524288 | tf_op jit(solution)/shard_map/all_to_all | solution.py:288
  83.1 18.2 %collective-permute-start.5 = (f32[32,128]{1,0:T(8,128)S(1)}, f32[32,128]{1,0:T(8,128)S(1)}, u32[]{:S(2)}, u32[]{:S(2)}) collective-permute-start(f32[32,128]{1,0:T(8,128)S(1)} %copy-done.30), channel_id=1, source_target_pairs={{0,1},{1,0},{2,3},{3,2},{4,5},{5,4},{6,7},{7,6},{8,9},{9,8},{10,11... | collective-permute-start | bytes 49160 | tf_op jit(solution)/shard_map/ppermute | solution.py:215
  83.2 9.2 %copy-start.42 = (f32[4,128]{1,0:T(4,128)S(1)}, f32[4,128]{1,0:T(4,128)}, u32[]{:S(2)}) copy-start(f32[4,128]{1,0:T(4,128)} %get-tuple-element.62) | copy-start | bytes 6148
  83.2 18.1 %collective-permute-start.6 = (f32[16,128]{1,0:T(8,128)S(1)}, f32[16,128]{1,0:T(8,128)S(1)}, u32[]{:S(2)}, u32[]{:S(2)}) collective-permute-start(f32[16,128]{1,0:T(8,128)S(1)} %copy-done.36), channel_id=1, source_target_pairs={{0,8},{8,16},{16,24},{24,32},{32,40},{40,48},{48,56},{56,64},{64,7... | collective-permute-start | bytes 24584 | tf_op jit(solution)/shard_map/ppermute | solution.py:218
  86.6 9.2 %copy-start.39 = (f32[4,128]{1,0:T(4,128)S(1)}, f32[4,128]{1,0:T(4,128)}, u32[]{:S(2)}) copy-start(f32[4,128]{1,0:T(4,128)} %get-tuple-element.63) | copy-start | bytes 6148
  86.6 14.7 %collective-permute-start.7 = (f32[16,128]{1,0:T(8,128)S(1)}, f32[16,128]{1,0:T(8,128)S(1)}, u32[]{:S(2)}, u32[]{:S(2)}) collective-permute-start(f32[16,128]{1,0:T(8,128)S(1)} %copy-done.33), channel_id=1, source_target_pairs={{8,0},{16,8},{24,16},{32,24},{40,32},{48,40},{56,48},{64,56},{72,6... | collective-permute-start | bytes 24584 | tf_op jit(solution)/shard_map/ppermute | solution.py:219
  92.4 5.6 %collective-permute-start.8 = (f32[4,128]{1,0:T(4,128)S(1)}, f32[4,128]{1,0:T(4,128)S(1)}, u32[]{:S(2)}, u32[]{:S(2)}) collective-permute-start(f32[4,128]{1,0:T(4,128)S(1)} %copy-done.42), channel_id=1, source_target_pairs={{0,2},{2,4},{4,6},{1,3},{3,5},{5,7},{8,10},{10,12},{12,14},{9,11},... | collective-permute-start | bytes 6152 | tf_op jit(solution)/shard_map/ppermute | solution.py:218
  95.8 5.5 %collective-permute-start.9 = (f32[4,128]{1,0:T(4,128)S(1)}, f32[4,128]{1,0:T(4,128)S(1)}, u32[]{:S(2)}, u32[]{:S(2)}) collective-permute-start(f32[4,128]{1,0:T(4,128)S(1)} %copy-done.39), channel_id=1, source_target_pairs={{2,0},{4,2},{6,4},{3,1},{5,3},{7,5},{10,8},{12,10},{14,12},{11,9},... | collective-permute-start | bytes 6152 | tf_op jit(solution)/shard_map/ppermute | solution.py:219
  98.0 3.3 %copy-start.20 = (f32[4,128]{1,0:T(4,128)}, f32[4,128]{1,0:T(4,128)S(1)}, u32[]{:S(2)}) copy-start(f32[4,128]{1,0:T(4,128)S(1)} %collective-permute-done.8.refs_15_) | copy-start | bytes 6148
  107.8 11.1 %copy-start.28 = (f32[32,128]{1,0:T(8,128)S(1)}, f32[32,128]{1,0:T(8,128)}, u32[]{:S(2)}) copy-start(f32[32,128]{1,0:T(8,128)} %get-tuple-element.69) | copy-start | bytes 49156
  107.8 11.3 %copy-start.34 = (f32[16,128]{1,0:T(8,128)S(1)}, f32[16,128]{1,0:T(8,128)}, u32[]{:S(2)}) copy-start(f32[16,128]{1,0:T(8,128)} %get-tuple-element.70) | copy-start | bytes 24580
  107.8 14.7 %copy-start.31 = (f32[16,128]{1,0:T(8,128)S(1)}, f32[16,128]{1,0:T(8,128)}, u32[]{:S(2)}) copy-start(f32[16,128]{1,0:T(8,128)} %get-tuple-element.71) | copy-start | bytes 24580
  107.8 25.2 %all-to-all-start.3 = ((f32[128,2,256]{2,1,0:T(2,128)}), f32[128,2,256]{2,1,0:T(2,128)S(1)}, u32[]{:S(2)}, u32[]{:S(2)}) async-start(f32[128,2,256]{2,1,0:T(2,128)} %all_to_all.45), calls=%async_computation.3 | async-start | bytes 524288 | tf_op jit(solution)/shard_map/all_to_all | solution.py:288
  119.0 18.2 %collective-permute-start.10 = (f32[32,128]{1,0:T(8,128)S(1)}, f32[32,128]{1,0:T(8,128)S(1)}, u32[]{:S(2)}, u32[]{:S(2)}) collective-permute-start(f32[32,128]{1,0:T(8,128)S(1)} %copy-done.28), channel_id=1, source_target_pairs={{0,1},{1,0},{2,3},{3,2},{4,5},{5,4},{6,7},{7,6},{8,9},{9,8},{10,11... | collective-permute-start | bytes 49160 | tf_op jit(solution)/shard_map/ppermute | solution.py:215
  119.1 9.2 %copy-start.40 = (f32[4,128]{1,0:T(4,128)S(1)}, f32[4,128]{1,0:T(4,128)}, u32[]{:S(2)}) copy-start(f32[4,128]{1,0:T(4,128)} %get-tuple-element.72) | copy-start | bytes 6148
  119.1 18.1 %collective-permute-start.11 = (f32[16,128]{1,0:T(8,128)S(1)}, f32[16,128]{1,0:T(8,128)S(1)}, u32[]{:S(2)}, u32[]{:S(2)}) collective-permute-start(f32[16,128]{1,0:T(8,128)S(1)} %copy-done.34), channel_id=1, source_target_pairs={{0,8},{8,16},{16,24},{24,32},{32,40},{40,48},{48,56},{56,64},{64,7... | collective-permute-start | bytes 24584 | tf_op jit(solution)/shard_map/ppermute | solution.py:218
  122.5 9.2 %copy-start.37 = (f32[4,128]{1,0:T(4,128)S(1)}, f32[4,128]{1,0:T(4,128)}, u32[]{:S(2)}) copy-start(f32[4,128]{1,0:T(4,128)} %get-tuple-element.73) | copy-start | bytes 6148
  122.5 14.7 %collective-permute-start.12 = (f32[16,128]{1,0:T(8,128)S(1)}, f32[16,128]{1,0:T(8,128)S(1)}, u32[]{:S(2)}, u32[]{:S(2)}) collective-permute-start(f32[16,128]{1,0:T(8,128)S(1)} %copy-done.31), channel_id=1, source_target_pairs={{8,0},{16,8},{24,16},{32,24},{40,32},{48,40},{56,48},{64,56},{72,6... | collective-permute-start | bytes 24584 | tf_op jit(solution)/shard_map/ppermute | solution.py:219
  128.3 5.6 %collective-permute-start.13 = (f32[4,128]{1,0:T(4,128)S(1)}, f32[4,128]{1,0:T(4,128)S(1)}, u32[]{:S(2)}, u32[]{:S(2)}) collective-permute-start(f32[4,128]{1,0:T(4,128)S(1)} %copy-done.40), channel_id=1, source_target_pairs={{0,2},{2,4},{4,6},{1,3},{3,5},{5,7},{8,10},{10,12},{12,14},{9,11},... | collective-permute-start | bytes 6152 | tf_op jit(solution)/shard_map/ppermute | solution.py:218
  131.7 5.5 %collective-permute-start.14 = (f32[4,128]{1,0:T(4,128)S(1)}, f32[4,128]{1,0:T(4,128)S(1)}, u32[]{:S(2)}, u32[]{:S(2)}) collective-permute-start(f32[4,128]{1,0:T(4,128)S(1)} %copy-done.37), channel_id=1, source_target_pairs={{2,0},{4,2},{6,4},{3,1},{5,3},{7,5},{10,8},{12,10},{14,12},{11,9},... | collective-permute-start | bytes 6152 | tf_op jit(solution)/shard_map/ppermute | solution.py:219
  133.9 3.3 %copy-start.21 = (f32[4,128]{1,0:T(4,128)}, f32[4,128]{1,0:T(4,128)S(1)}, u32[]{:S(2)}) copy-start(f32[4,128]{1,0:T(4,128)S(1)} %collective-permute-done.13.refs_15_) | copy-start | bytes 6148
  143.7 11.1 %copy-start.29 = (f32[32,128]{1,0:T(8,128)S(1)}, f32[32,128]{1,0:T(8,128)}, u32[]{:S(2)}) copy-start(f32[32,128]{1,0:T(8,128)} %get-tuple-element.79) | copy-start | bytes 49156
  143.7 11.2 %copy-start.35 = (f32[16,128]{1,0:T(8,128)S(1)}, f32[16,128]{1,0:T(8,128)}, u32[]{:S(2)}) copy-start(f32[16,128]{1,0:T(8,128)} %get-tuple-element.80) | copy-start | bytes 24580
  143.7 14.7 %copy-start.32 = (f32[16,128]{1,0:T(8,128)S(1)}, f32[16,128]{1,0:T(8,128)}, u32[]{:S(2)}) copy-start(f32[16,128]{1,0:T(8,128)} %get-tuple-element.81) | copy-start | bytes 24580
  143.7 25.2 %all-to-all-start.4 = ((f32[128,2,256]{2,1,0:T(2,128)}), f32[128,2,256]{2,1,0:T(2,128)S(1)}, u32[]{:S(2)}, u32[]{:S(2)}) async-start(f32[128,2,256]{2,1,0:T(2,128)} %all_to_all.48), calls=%async_computation.4 | async-start | bytes 524288 | tf_op jit(solution)/shard_map/all_to_all | solution.py:288
  154.8 18.2 %collective-permute-start.15 = (f32[32,128]{1,0:T(8,128)S(1)}, f32[32,128]{1,0:T(8,128)S(1)}, u32[]{:S(2)}, u32[]{:S(2)}) collective-permute-start(f32[32,128]{1,0:T(8,128)S(1)} %copy-done.29), channel_id=1, source_target_pairs={{0,1},{1,0},{2,3},{3,2},{4,5},{5,4},{6,7},{7,6},{8,9},{9,8},{10,11... | collective-permute-start | bytes 49160 | tf_op jit(solution)/shard_map/ppermute | solution.py:215
  155.0 9.2 %copy-start.41 = (f32[4,128]{1,0:T(4,128)S(1)}, f32[4,128]{1,0:T(4,128)}, u32[]{:S(2)}) copy-start(f32[4,128]{1,0:T(4,128)} %get-tuple-element.82) | copy-start | bytes 6148
  155.0 18.1 %collective-permute-start.16 = (f32[16,128]{1,0:T(8,128)S(1)}, f32[16,128]{1,0:T(8,128)S(1)}, u32[]{:S(2)}, u32[]{:S(2)}) collective-permute-start(f32[16,128]{1,0:T(8,128)S(1)} %copy-done.35), channel_id=1, source_target_pairs={{0,8},{8,16},{16,24},{24,32},{32,40},{40,48},{48,56},{56,64},{64,7... | collective-permute-start | bytes 24584 | tf_op jit(solution)/shard_map/ppermute | solution.py:218
  158.4 9.2 %copy-start.38 = (f32[4,128]{1,0:T(4,128)S(1)}, f32[4,128]{1,0:T(4,128)}, u32[]{:S(2)}) copy-start(f32[4,128]{1,0:T(4,128)} %get-tuple-element.83) | copy-start | bytes 6148
  158.4 14.7 %collective-permute-start.17 = (f32[16,128]{1,0:T(8,128)S(1)}, f32[16,128]{1,0:T(8,128)S(1)}, u32[]{:S(2)}, u32[]{:S(2)}) collective-permute-start(f32[16,128]{1,0:T(8,128)S(1)} %copy-done.32), channel_id=1, source_target_pairs={{8,0},{16,8},{24,16},{32,24},{40,32},{48,40},{56,48},{64,56},{72,6... | collective-permute-start | bytes 24584 | tf_op jit(solution)/shard_map/ppermute | solution.py:219
  164.2 5.6 %collective-permute-start.18 = (f32[4,128]{1,0:T(4,128)S(1)}, f32[4,128]{1,0:T(4,128)S(1)}, u32[]{:S(2)}, u32[]{:S(2)}) collective-permute-start(f32[4,128]{1,0:T(4,128)S(1)} %copy-done.41), channel_id=1, source_target_pairs={{0,2},{2,4},{4,6},{1,3},{3,5},{5,7},{8,10},{10,12},{12,14},{9,11},... | collective-permute-start | bytes 6152 | tf_op jit(solution)/shard_map/ppermute | solution.py:218
  167.6 5.5 %collective-permute-start.19 = (f32[4,128]{1,0:T(4,128)S(1)}, f32[4,128]{1,0:T(4,128)S(1)}, u32[]{:S(2)}, u32[]{:S(2)}) collective-permute-start(f32[4,128]{1,0:T(4,128)S(1)} %copy-done.38), channel_id=1, source_target_pairs={{2,0},{4,2},{6,4},{3,1},{5,3},{7,5},{10,8},{12,10},{14,12},{11,9},... | collective-permute-start | bytes 6152 | tf_op jit(solution)/shard_map/ppermute | solution.py:219
  169.8 3.3 %copy-start.18 = (f32[4,128]{1,0:T(4,128)}, f32[4,128]{1,0:T(4,128)S(1)}, u32[]{:S(2)}) copy-start(f32[4,128]{1,0:T(4,128)S(1)} %collective-permute-done.18.refs_15_) | copy-start | bytes 6148
  (20 other events, 12.6 us)

commit v9 on v8

--- a/solution.py
+++ b/solution.py
@@ -145,8 +145,10 @@
         yl_ref[i:i + 1, :] = y_last[i]
     zs_ref[...] = jnp.where(z_low, nv_ref[depth - 1], nv_ref[0])
 
-    snd_ref[:, 0:width] = one_hot_dot(oh_sblk_ref[...], nv_ref[...].reshape(depth * rows_x, width))
-    snd_ref[:, width:2 * width] = one_hot_dot(oh_ids_t_ref[...], ntv_ref[...])
+    dests, capacity = snd_ref.shape[0], snd_ref.shape[1]
+    sel_rows = one_hot_dot(oh_sblk_ref[...], nv_ref[...].reshape(depth * rows_x, width))
+    sel_volt = one_hot_dot(oh_ids_t_ref[...], ntv_ref[...])
+    snd_ref[...] = jnp.concatenate([sel_rows, sel_volt], axis=1).reshape(dests, capacity, 2 * width)
 
 
 def coef_kernel(table_ref, cls_ref, cz_ref, cx_ref, cy_ref):
@@ -187,7 +189,7 @@
     )
     if pack:
         out_shape += (
-            jax.ShapeDtypeStruct((slots, 2 * width), f32),
+            jax.ShapeDtypeStruct((slots // 2, 2, 2 * width), f32),
             jax.ShapeDtypeStruct((rows_x, width), f32),
             jax.ShapeDtypeStruct((depth, width), f32),
             jax.ShapeDtypeStruct((depth, width), f32),
@@ -293,7 +295,7 @@
             tile_gain = outs[-1]
         volt, recovery, term_volt, term_recovery = outs[:4]
         if pack:
-            sent, faces = outs[4], outs[5:10]
+            sent, faces = outs[4].reshape(slots_total, 2 * width), outs[5:10]
     return (volt, recovery, term_volt, term_recovery)
 
 

time: 179 us -> 173 us (0.966)
  local copies, waits for them, and re-layouts: 21.8 us -> 16.4 us
    all_to_all x8 -> x5, local copies, waits for them, and re-layouts: 10 us -> 4.63 us  [on_device(): lax.all_to_all(sent, ('gx', 'gy'), split_axis=0, concat_axis=0, tiled=True)]
where the time goes in v9:
time: 173 us; the launch traced here: 172 us
  starting transfers between devices  118 us (68%)
  Pallas kernels  17.7 us (10%)
  local copies, waits for them, and re-layouts  16.4 us (9%)
  waiting for transfers between devices  12.3 us (7%)
  other arithmetic  6.27 us (4%)
    all_to_all x4, starting transfers between devices, on_device(): lax.all_to_all(sent, ('gx', 'gy'), split_axis=0, concat_axis=0, tiled=True)  47.9 us
    ppermute x8, starting transfers between devices, exchange_halos(): lax.ppermute(first, axis, [(i + 1, i) for i in range(count - 1)])  28.4 us
    ppermute x8, starting transfers between devices, exchange_halos(): lax.ppermute(last, axis, [(i, i + 1) for i in range(count - 1)])  27.1 us
    pallas_call x4, Pallas kernels, run_step(): pl.pallas_call(functools.partial(step_kernel, first=first, pack=pack), ou...  15.6 us
    all_to_all x1, starting transfers between devices, on_device(): lax.all_to_all(slot_term, ('gx', 'gy'), split_axis=0, concat_axis=0, tile...  14 us
    ppermute x8, waiting for transfers between devices, exchange_halos(): lax.ppermute(first, axis, [(i + 1, i) for i in range(count - 1)])  9.87 us
    unnamed x86, local copies, waits for them, and re-layouts  5.46 us
    all_to_all x5, local copies, waits for them, and re-layouts, on_device(): lax.all_to_all(sent, ('gx', 'gy'), split_axis=0, concat_axis=0, tiled=True)  4.63 us
  transfers between devices with their start and end apart: 25, of which 4 were waited for; matrix products, arithmetic and copies ran while one was open for 5% of the time, Pallas kernels for 1%

profile of v9, /device:TPU:128, one launch (start us, length us, event | category | flops | bytes accessed | tf_op | source)
XLA Modules:
  0.0 172.1 jit_solution(12880669339685505144)
XLA Ops:
  1.9 0.7 copy-done.15
  2.8 0.8 sub.7
  3.5 14.0 %all-to-all-start = ((s32[128,2,1]{1,2,0:T(1,128)}), s32[128,2,1]{1,2,0:T(1,128)S(1)}, u32[]{:S(2)}, u32[]{:S(2)}) async-start(s32[128,2,1]{1,2,0:T(1,128)} %bitcast.13), calls=%async_computation | async-start | bytes 131072 | tf_op jit(solution)/shard_map/all_to_all | solution.py:255
  17.5 0.9 fusion.8
  18.4 1.4 slice_reduce_fusion
  19.8 0.7 fusion.2.refs_17_.refs_18_
  20.5 0.7 fusion.1.refs_16_.refs_17_
  21.4 0.7 gather_fusion
  22.1 2.4 %all-to-all-done = s32[128,2,1]{1,2,0:T(1,128)S(1)} async-done(((s32[128,2,1]{1,2,0:T(1,128)}), s32[128,2,1]{1,2,0:T(1,128)S(1)}, u32[]{:S(2)}, u32[]{:S(2)}) %all-to-all-start) | async-done | bytes 1056 | tf_op jit(solution)/shard_map/all_to_all | solution.py:255
  26.1 0.8 reduce.9
  27.6 0.7 gather_fusion.1
  29.1 1.0 all_to_all.33
  30.1 11.3 %all-to-all-start.1 = ((f32[128,2,384]{2,1,0:T(2,128)}), f32[128,2,384]{2,1,0:T(2,128)S(1)}, u32[]{:S(2)}, u32[]{:S(2)}) async-start(f32[128,2,384]{2,1,0:T(2,128)} %all_to_all.33), calls=%async_computation.1 | async-start | bytes 786432 | tf_op jit(solution)/shard_map/all_to_all | solution.py:290
  41.4 0.7 fusion.3.refs_18_.refs_19_
  42.8 2.1 %shard_map.138 = (f32[16,32,128]{2,1,0:T(8,128)}, f32[16,32,128]{2,1,0:T(8,128)}, f32[16,32,128]{2,1,0:T(8,128)}) custom-call(f32[3,8]{1,0:T(4,128)} %table_ref.1, s32[16,32,128]{2,1,0:T(8,128)} %cls_ref.1), custom_call_target="tpu_custom_call" | custom-call | tf_op jit(solution)/shard_map/pallas_call | solution.py:167
  44.9 0.8 fusion.refs_21_.refs_22_
  45.7 3.4 %collective-permute-start.3 = (f32[4,128]{1,0:T(4,128)S(1)}, f32[4,128]{1,0:T(4,128)S(1)}, u32[]{:S(2)}, u32[]{:S(2)}) collective-permute-start(f32[4,128]{1,0:T(4,128)S(1)} %reshape_squeeze.7), channel_id=1, source_target_pairs={{0,2},{2,4},{4,6},{1,3},{3,5},{5,7},{8,10},{10,12},{12,14},{9,11},... | collective-permute-start | bytes 6152 | tf_op jit(solution)/shard_map/ppermute | solution.py:220
  49.1 1.3 collective-permute-start.4
  50.4 3.4 %collective-permute-start.1 = (f32[16,128]{1,0:T(8,128)S(1)}, f32[16,128]{1,0:T(8,128)S(1)}, u32[]{:S(2)}, u32[]{:S(2)}) collective-permute-start(f32[16,128]{1,0:T(8,128)S(1)} %bitcast.33), channel_id=1, source_target_pairs={{0,8},{8,16},{16,24},{24,32},{32,40},{40,48},{48,56},{56,64},{64,7... | collective-permute-start | bytes 24584 | tf_op jit(solution)/shard_map/ppermute | solution.py:220
  53.8 5.8 %collective-permute-start.2 = (f32[16,128]{1,0:T(8,128)S(1)}, f32[16,128]{1,0:T(8,128)S(1)}, u32[]{:S(2)}, u32[]{:S(2)}) collective-permute-start(f32[16,128]{1,0:T(8,128)S(1)} %bitcast.32), channel_id=1, source_target_pairs={{8,0},{16,8},{24,16},{32,24},{40,32},{48,40},{56,48},{64,56},{72,6... | collective-permute-start | bytes 24584 | tf_op jit(solution)/shard_map/ppermute | solution.py:221
  59.7 0.7 fusion.4.refs_20_.refs_21_
  61.0 1.0 all_to_all.35.refs_6_
  62.1 0.7 broadcast_in_dim.74.refs_10_.refs_11_
  62.8 4.0 %shard_map.139 = (f32[16,32,128]{2,1,0:T(8,128)}, f32[16,32,128]{2,1,0:T(8,128)}, f32[32,128]{1,0:T(8,128)}, f32[32,128]{1,0:T(8,128)}, f32[128,2,256]{2,1,0:T(2...) custom-call(s32[8]{0:T(128)} %convert_element_type.22.refs_0_, ...), custom_call_target="tpu_custom_call" | custom-call | tf_op jit(solution)/shard_map/pallas_call | solution.py:204
  66.9 14.3 %all-to-all-start.2 = ((f32[128,2,256]{2,1,0:T(2,128)}), f32[128,2,256]{2,1,0:T(2,128)S(1)}, u32[]{:S(2)}, u32[]{:S(2)}) async-start(f32[128,2,256]{2,1,0:T(2,128)} %get-tuple-element.55), calls=%async_computation.2 | async-start | bytes 524288 | tf_op jit(solution)/shard_map/all_to_all | solution.py:290
  81.4 3.4 %collective-permute-start.6 = (f32[16,128]{1,0:T(8,128)S(1)}, f32[16,128]{1,0:T(8,128)S(1)}, u32[]{:S(2)}, u32[]{:S(2)}) collective-permute-start(f32[16,128]{1,0:T(8,128)S(1)} %copy-done.36), channel_id=1, source_target_pairs={{0,8},{8,16},{16,24},{24,32},{32,40},{40,48},{48,56},{56,64},{64,7... | collective-permute-start | bytes 24584 | tf_op jit(solution)/shard_map/ppermute | solution.py:220
  84.8 5.8 %collective-permute-start.7 = (f32[16,128]{1,0:T(8,128)S(1)}, f32[16,128]{1,0:T(8,128)S(1)}, u32[]{:S(2)}, u32[]{:S(2)}) collective-permute-start(f32[16,128]{1,0:T(8,128)S(1)} %copy-done.33), channel_id=1, source_target_pairs={{8,0},{16,8},{24,16},{32,24},{40,32},{48,40},{56,48},{64,56},{72,6... | collective-permute-start | bytes 24584 | tf_op jit(solution)/shard_map/ppermute | solution.py:221
  90.6 3.4 %collective-permute-start.8 = (f32[4,128]{1,0:T(4,128)S(1)}, f32[4,128]{1,0:T(4,128)S(1)}, u32[]{:S(2)}, u32[]{:S(2)}) collective-permute-start(f32[4,128]{1,0:T(4,128)S(1)} %copy-done.42), channel_id=1, source_target_pairs={{0,2},{2,4},{4,6},{1,3},{3,5},{5,7},{8,10},{10,12},{12,14},{9,11},... | collective-permute-start | bytes 6152 | tf_op jit(solution)/shard_map/ppermute | solution.py:220
  94.0 1.5 collective-permute-start.9
  95.5 0.9 all_to_all.37.refs_6_
  96.3 3.3 %collective-permute-done.9.refs_16_ = f32[4,128]{1,0:T(4,128)S(1)} collective-permute-done((f32[4,128]{1,0:T(4,128)S(1)}, f32[4,128]{1,0:T(4,128)S(1)}, u32[]{:S(2)}, u32[]{:S(2)}) %collective-permute-start.9) | collective-permute-done | bytes 2080 | tf_op jit(solution)/shard_map/ppermute | solution.py:221
  100.3 4.0 %shard_map.140 = (f32[16,32,128]{2,1,0:T(8,128)}, f32[16,32,128]{2,1,0:T(8,128)}, f32[32,128]{1,0:T(8,128)}, f32[32,128]{1,0:T(8,128)}, f32[128,2,256]{2,1,0:T(2...) custom-call(s32[8]{0:T(128)} %convert_element_type.22.refs_0_, ...), custom_call_target="tpu_custom_call" | custom-call | tf_op jit(solution)/shard_map/pallas_call | solution.py:204
  104.3 11.1 %all-to-all-start.3 = ((f32[128,2,256]{2,1,0:T(2,128)}), f32[128,2,256]{2,1,0:T(2,128)S(1)}, u32[]{:S(2)}, u32[]{:S(2)}) async-start(f32[128,2,256]{2,1,0:T(2,128)} %get-tuple-element.66), calls=%async_computation.3 | async-start | bytes 524288 | tf_op jit(solution)/shard_map/all_to_all | solution.py:290
  115.6 3.4 %collective-permute-start.11 = (f32[16,128]{1,0:T(8,128)S(1)}, f32[16,128]{1,0:T(8,128)S(1)}, u32[]{:S(2)}, u32[]{:S(2)}) collective-permute-start(f32[16,128]{1,0:T(8,128)S(1)} %copy-done.34), channel_id=1, source_target_pairs={{0,8},{8,16},{16,24},{24,32},{32,40},{40,48},{48,56},{56,64},{64,7... | collective-permute-start | bytes 24584 | tf_op jit(solution)/shard_map/ppermute | solution.py:220
  119.0 5.8 %collective-permute-start.12 = (f32[16,128]{1,0:T(8,128)S(1)}, f32[16,128]{1,0:T(8,128)S(1)}, u32[]{:S(2)}, u32[]{:S(2)}) collective-permute-start(f32[16,128]{1,0:T(8,128)S(1)} %copy-done.31), channel_id=1, source_target_pairs={{8,0},{16,8},{24,16},{32,24},{40,32},{48,40},{56,48},{64,56},{72,6... | collective-permute-start | bytes 24584 | tf_op jit(solution)/shard_map/ppermute | solution.py:221
  124.8 3.4 %collective-permute-start.13 = (f32[4,128]{1,0:T(4,128)S(1)}, f32[4,128]{1,0:T(4,128)S(1)}, u32[]{:S(2)}, u32[]{:S(2)}) collective-permute-start(f32[4,128]{1,0:T(4,128)S(1)} %copy-done.40), channel_id=1, source_target_pairs={{0,2},{2,4},{4,6},{1,3},{3,5},{5,7},{8,10},{10,12},{12,14},{9,11},... | collective-permute-start | bytes 6152 | tf_op jit(solution)/shard_map/ppermute | solution.py:220
  128.2 1.3 collective-permute-start.14
  129.5 0.9 all_to_all.39.refs_6_
  130.4 3.3 %collective-permute-done.14.refs_16_ = f32[4,128]{1,0:T(4,128)S(1)} collective-permute-done((f32[4,128]{1,0:T(4,128)S(1)}, f32[4,128]{1,0:T(4,128)S(1)}, u32[]{:S(2)}, u32[]{:S(2)}) %collective-permute-start.14) | collective-permute-done | bytes 2080 | tf_op jit(solution)/shard_map/ppermute | solution.py:221
  134.3 4.0 %shard_map.141 = (f32[16,32,128]{2,1,0:T(8,128)}, f32[16,32,128]{2,1,0:T(8,128)}, f32[32,128]{1,0:T(8,128)}, f32[32,128]{1,0:T(8,128)}, f32[128,2,256]{2,1,0:T(2...) custom-call(s32[8]{0:T(128)} %convert_element_type.22.refs_0_, ...), custom_call_target="tpu_custom_call" | custom-call | tf_op jit(solution)/shard_map/pallas_call | solution.py:204
  138.4 11.1 %all-to-all-start.4 = ((f32[128,2,256]{2,1,0:T(2,128)}), f32[128,2,256]{2,1,0:T(2,128)S(1)}, u32[]{:S(2)}, u32[]{:S(2)}) async-start(f32[128,2,256]{2,1,0:T(2,128)} %get-tuple-element.76), calls=%async_computation.4 | async-start | bytes 524288 | tf_op jit(solution)/shard_map/all_to_all | solution.py:290
  149.7 3.4 %collective-permute-start.16 = (f32[16,128]{1,0:T(8,128)S(1)}, f32[16,128]{1,0:T(8,128)S(1)}, u32[]{:S(2)}, u32[]{:S(2)}) collective-permute-start(f32[16,128]{1,0:T(8,128)S(1)} %copy-done.35), channel_id=1, source_target_pairs={{0,8},{8,16},{16,24},{24,32},{32,40},{40,48},{48,56},{56,64},{64,7... | collective-permute-start | bytes 24584 | tf_op jit(solution)/shard_map/ppermute | solution.py:220
  153.1 5.8 %collective-permute-start.17 = (f32[16,128]{1,0:T(8,128)S(1)}, f32[16,128]{1,0:T(8,128)S(1)}, u32[]{:S(2)}, u32[]{:S(2)}) collective-permute-start(f32[16,128]{1,0:T(8,128)S(1)} %copy-done.32), channel_id=1, source_target_pairs={{8,0},{16,8},{24,16},{32,24},{40,32},{48,40},{56,48},{64,56},{72,6... | collective-permute-start | bytes 24584 | tf_op jit(solution)/shard_map/ppermute | solution.py:221
  158.9 3.4 %collective-permute-start.18 = (f32[4,128]{1,0:T(4,128)S(1)}, f32[4,128]{1,0:T(4,128)S(1)}, u32[]{:S(2)}, u32[]{:S(2)}) collective-permute-start(f32[4,128]{1,0:T(4,128)S(1)} %copy-done.41), channel_id=1, source_target_pairs={{0,2},{2,4},{4,6},{1,3},{3,5},{5,7},{8,10},{10,12},{12,14},{9,11},... | collective-permute-start | bytes 6152 | tf_op jit(solution)/shard_map/ppermute | solution.py:220
  162.3 1.3 collective-permute-start.19
  163.6 0.9 all_to_all.41.refs_6_
  164.5 3.3 %collective-permute-done.19.refs_16_ = f32[4,128]{1,0:T(4,128)S(1)} collective-permute-done((f32[4,128]{1,0:T(4,128)S(1)}, f32[4,128]{1,0:T(4,128)S(1)}, u32[]{:S(2)}, u32[]{:S(2)}) %collective-permute-start.19) | collective-permute-done | bytes 2080 | tf_op jit(solution)/shard_map/ppermute | solution.py:221
  168.4 3.5 %shard_map.142 = (f32[16,32,128]{2,1,0:T(8,128)}, f32[16,32,128]{2,1,0:T(8,128)}, f32[32,128]{1,0:T(8,128)}, f32[32,128]{1,0:T(8,128)}) custom-call(s32[8]{0:T(128)} %convert_element_type.22.refs_0_, f32[16,32,128]{2,1,0:T(8,128)} %get-tuple-element.74.refs_1_, f32[16,32,128]{2,1,0:T(8,128)} %get-tuple-element.75.refs_2_, ...), custom_call_target="tpu_custom_call" | custom-call | tf_op jit(solution)/shard_map/pallas_call | solution.py:204
  (133 shorter events, 8.2 us)
Async XLA Ops:
  3.5 21.0 %all-to-all-start = ((s32[128,2,1]{1,2,0:T(1,128)}), s32[128,2,1]{1,2,0:T(1,128)S(1)}, u32[]{:S(2)}, u32[]{:S(2)}) async-start(s32[128,2,1]{1,2,0:T(1,128)} %bitcast.13), calls=%async_computation | async-start | bytes 131072 | tf_op jit(solution)/shard_map/all_to_all | solution.py:255
  19.8 1.4 copy-start.1
  30.1 31.0 %all-to-all-start.1 = ((f32[128,2,384]{2,1,0:T(2,128)}), f32[128,2,384]{2,1,0:T(2,128)S(1)}, u32[]{:S(2)}, u32[]{:S(2)}) async-start(f32[128,2,384]{2,1,0:T(2,128)} %all_to_all.33), calls=%async_computation.1 | async-start | bytes 786432 | tf_op jit(solution)/shard_map/all_to_all | solution.py:290
  45.7 16.3 %collective-permute-start.3 = (f32[4,128]{1,0:T(4,128)S(1)}, f32[4,128]{1,0:T(4,128)S(1)}, u32[]{:S(2)}, u32[]{:S(2)}) collective-permute-start(f32[4,128]{1,0:T(4,128)S(1)} %reshape_squeeze.7), channel_id=1, source_target_pairs={{0,2},{2,4},{4,6},{1,3},{3,5},{5,7},{8,10},{10,12},{12,14},{9,11},... | collective-permute-start | bytes 6152 | tf_op jit(solution)/shard_map/ppermute | solution.py:220
  49.1 13.0 %collective-permute-start.4 = (f32[4,128]{1,0:T(4,128)S(1)}, f32[4,128]{1,0:T(4,128)S(1)}, u32[]{:S(2)}, u32[]{:S(2)}) collective-permute-start(f32[4,128]{1,0:T(4,128)S(1)} %reshape_squeeze.6), channel_id=1, source_target_pairs={{2,0},{4,2},{6,4},{3,1},{5,3},{7,5},{10,8},{12,10},{14,12},{11,9},... | collective-permute-start | bytes 6152 | tf_op jit(solution)/shard_map/ppermute | solution.py:221
  50.4 11.7 %collective-permute-start.1 = (f32[16,128]{1,0:T(8,128)S(1)}, f32[16,128]{1,0:T(8,128)S(1)}, u32[]{:S(2)}, u32[]{:S(2)}) collective-permute-start(f32[16,128]{1,0:T(8,128)S(1)} %bitcast.33), channel_id=1, source_target_pairs={{0,8},{8,16},{16,24},{24,32},{32,40},{40,48},{48,56},{56,64},{64,7... | collective-permute-start | bytes 24584 | tf_op jit(solution)/shard_map/ppermute | solution.py:220
  53.8 8.3 %collective-permute-start.2 = (f32[16,128]{1,0:T(8,128)S(1)}, f32[16,128]{1,0:T(8,128)S(1)}, u32[]{:S(2)}, u32[]{:S(2)}) collective-permute-start(f32[16,128]{1,0:T(8,128)S(1)} %bitcast.32), channel_id=1, source_target_pairs={{8,0},{16,8},{24,16},{32,24},{40,32},{48,40},{56,48},{64,56},{72,6... | collective-permute-start | bytes 24584 | tf_op jit(solution)/shard_map/ppermute | solution.py:221
  59.6 2.5 %collective-permute-start = (f32[32,128]{1,0:T(8,128)S(1)}, f32[32,128]{1,0:T(8,128)S(1)}, u32[]{:S(2)}, u32[]{:S(2)}) collective-permute-start(f32[32,128]{1,0:T(8,128)S(1)} %select_bitcast_fusion), channel_id=1, source_target_pairs={{0,1},{1,0},{2,3},{3,2},{4,5},{5,4},{6,7},{7,6},{8,9},{9,8},{10,11... | collective-permute-start | bytes 49160 | tf_op jit(solution)/shard_map/ppermute | solution.py:217
  61.0 1.1 copy-start.27
  62.1 0.8 copy-start.16
  62.1 0.8 copy-start.17
  62.1 0.7 copy-start.11
  66.8 14.4 %copy-start.30 = (f32[32,128]{1,0:T(8,128)S(1)}, f32[32,128]{1,0:T(8,128)}, u32[]{:S(2)}) copy-start(f32[32,128]{1,0:T(8,128)} %get-tuple-element.59) | copy-start | bytes 49156
  66.9 14.5 %copy-start.36 = (f32[16,128]{1,0:T(8,128)S(1)}, f32[16,128]{1,0:T(8,128)}, u32[]{:S(2)}) copy-start(f32[16,128]{1,0:T(8,128)} %get-tuple-element.60) | copy-start | bytes 24580
  66.9 17.9 %copy-start.33 = (f32[16,128]{1,0:T(8,128)S(1)}, f32[16,128]{1,0:T(8,128)}, u32[]{:S(2)}) copy-start(f32[16,128]{1,0:T(8,128)} %get-tuple-element.61) | copy-start | bytes 24580
  66.9 28.6 %all-to-all-start.2 = ((f32[128,2,256]{2,1,0:T(2,128)}), f32[128,2,256]{2,1,0:T(2,128)S(1)}, u32[]{:S(2)}, u32[]{:S(2)}) async-start(f32[128,2,256]{2,1,0:T(2,128)} %get-tuple-element.55), calls=%async_computation.2 | async-start | bytes 524288 | tf_op jit(solution)/shard_map/all_to_all | solution.py:290
  81.2 18.4 %collective-permute-start.5 = (f32[32,128]{1,0:T(8,128)S(1)}, f32[32,128]{1,0:T(8,128)S(1)}, u32[]{:S(2)}, u32[]{:S(2)}) collective-permute-start(f32[32,128]{1,0:T(8,128)S(1)} %copy-done.30), channel_id=1, source_target_pairs={{0,1},{1,0},{2,3},{3,2},{4,5},{5,4},{6,7},{7,6},{8,9},{9,8},{10,11... | collective-permute-start | bytes 49160 | tf_op jit(solution)/shard_map/ppermute | solution.py:217
  81.3 9.2 %copy-start.42 = (f32[4,128]{1,0:T(4,128)S(1)}, f32[4,128]{1,0:T(4,128)}, u32[]{:S(2)}) copy-start(f32[4,128]{1,0:T(4,128)} %get-tuple-element.62) | copy-start | bytes 6148
  81.4 18.3 %collective-permute-start.6 = (f32[16,128]{1,0:T(8,128)S(1)}, f32[16,128]{1,0:T(8,128)S(1)}, u32[]{:S(2)}, u32[]{:S(2)}) collective-permute-start(f32[16,128]{1,0:T(8,128)S(1)} %copy-done.36), channel_id=1, source_target_pairs={{0,8},{8,16},{16,24},{24,32},{32,40},{40,48},{48,56},{56,64},{64,7... | collective-permute-start | bytes 24584 | tf_op jit(solution)/shard_map/ppermute | solution.py:220
  84.8 9.2 %copy-start.39 = (f32[4,128]{1,0:T(4,128)S(1)}, f32[4,128]{1,0:T(4,128)}, u32[]{:S(2)}) copy-start(f32[4,128]{1,0:T(4,128)} %get-tuple-element.63) | copy-start | bytes 6148
  84.8 14.8 %collective-permute-start.7 = (f32[16,128]{1,0:T(8,128)S(1)}, f32[16,128]{1,0:T(8,128)S(1)}, u32[]{:S(2)}, u32[]{:S(2)}) collective-permute-start(f32[16,128]{1,0:T(8,128)S(1)} %copy-done.33), channel_id=1, source_target_pairs={{8,0},{16,8},{24,16},{32,24},{40,32},{48,40},{56,48},{64,56},{72,6... | collective-permute-start | bytes 24584 | tf_op jit(solution)/shard_map/ppermute | solution.py:221
  90.6 5.8 %collective-permute-start.8 = (f32[4,128]{1,0:T(4,128)S(1)}, f32[4,128]{1,0:T(4,128)S(1)}, u32[]{:S(2)}, u32[]{:S(2)}) collective-permute-start(f32[4,128]{1,0:T(4,128)S(1)} %copy-done.42), channel_id=1, source_target_pairs={{0,2},{2,4},{4,6},{1,3},{3,5},{5,7},{8,10},{10,12},{12,14},{9,11},... | collective-permute-start | bytes 6152 | tf_op jit(solution)/shard_map/ppermute | solution.py:220
  94.0 5.7 %collective-permute-start.9 = (f32[4,128]{1,0:T(4,128)S(1)}, f32[4,128]{1,0:T(4,128)S(1)}, u32[]{:S(2)}, u32[]{:S(2)}) collective-permute-start(f32[4,128]{1,0:T(4,128)S(1)} %copy-done.39), channel_id=1, source_target_pairs={{2,0},{4,2},{6,4},{3,1},{5,3},{7,5},{10,8},{12,10},{14,12},{11,9},... | collective-permute-start | bytes 6152 | tf_op jit(solution)/shard_map/ppermute | solution.py:221
  96.3 3.3 %copy-start.20 = (f32[4,128]{1,0:T(4,128)}, f32[4,128]{1,0:T(4,128)S(1)}, u32[]{:S(2)}) copy-start(f32[4,128]{1,0:T(4,128)S(1)} %collective-permute-done.8.refs_15_) | copy-start | bytes 6148
  104.3 11.2 %copy-start.28 = (f32[32,128]{1,0:T(8,128)S(1)}, f32[32,128]{1,0:T(8,128)}, u32[]{:S(2)}) copy-start(f32[32,128]{1,0:T(8,128)} %get-tuple-element.69) | copy-start | bytes 49156
  104.3 11.3 %copy-start.34 = (f32[16,128]{1,0:T(8,128)S(1)}, f32[16,128]{1,0:T(8,128)}, u32[]{:S(2)}) copy-start(f32[16,128]{1,0:T(8,128)} %get-tuple-element.70) | copy-start | bytes 24580
  104.3 14.7 %copy-start.31 = (f32[16,128]{1,0:T(8,128)S(1)}, f32[16,128]{1,0:T(8,128)}, u32[]{:S(2)}) copy-start(f32[16,128]{1,0:T(8,128)} %get-tuple-element.71) | copy-start | bytes 24580
  104.3 25.2 %all-to-all-start.3 = ((f32[128,2,256]{2,1,0:T(2,128)}), f32[128,2,256]{2,1,0:T(2,128)S(1)}, u32[]{:S(2)}, u32[]{:S(2)}) async-start(f32[128,2,256]{2,1,0:T(2,128)} %get-tuple-element.66), calls=%async_computation.3 | async-start | bytes 524288 | tf_op jit(solution)/shard_map/all_to_all | solution.py:290
  115.5 18.2 %collective-permute-start.10 = (f32[32,128]{1,0:T(8,128)S(1)}, f32[32,128]{1,0:T(8,128)S(1)}, u32[]{:S(2)}, u32[]{:S(2)}) collective-permute-start(f32[32,128]{1,0:T(8,128)S(1)} %copy-done.28), channel_id=1, source_target_pairs={{0,1},{1,0},{2,3},{3,2},{4,5},{5,4},{6,7},{7,6},{8,9},{9,8},{10,11... | collective-permute-start | bytes 49160 | tf_op jit(solution)/shard_map/ppermute | solution.py:217
  115.6 9.2 %copy-start.40 = (f32[4,128]{1,0:T(4,128)S(1)}, f32[4,128]{1,0:T(4,128)}, u32[]{:S(2)}) copy-start(f32[4,128]{1,0:T(4,128)} %get-tuple-element.72) | copy-start | bytes 6148
  115.6 18.1 %collective-permute-start.11 = (f32[16,128]{1,0:T(8,128)S(1)}, f32[16,128]{1,0:T(8,128)S(1)}, u32[]{:S(2)}, u32[]{:S(2)}) collective-permute-start(f32[16,128]{1,0:T(8,128)S(1)} %copy-done.34), channel_id=1, source_target_pairs={{0,8},{8,16},{16,24},{24,32},{32,40},{40,48},{48,56},{56,64},{64,7... | collective-permute-start | bytes 24584 | tf_op jit(solution)/shard_map/ppermute | solution.py:220
  119.0 9.2 %copy-start.37 = (f32[4,128]{1,0:T(4,128)S(1)}, f32[4,128]{1,0:T(4,128)}, u32[]{:S(2)}) copy-start(f32[4,128]{1,0:T(4,128)} %get-tuple-element.73) | copy-start | bytes 6148
  119.0 14.7 %collective-permute-start.12 = (f32[16,128]{1,0:T(8,128)S(1)}, f32[16,128]{1,0:T(8,128)S(1)}, u32[]{:S(2)}, u32[]{:S(2)}) collective-permute-start(f32[16,128]{1,0:T(8,128)S(1)} %copy-done.31), channel_id=1, source_target_pairs={{8,0},{16,8},{24,16},{32,24},{40,32},{48,40},{56,48},{64,56},{72,6... | collective-permute-start | bytes 24584 | tf_op jit(solution)/shard_map/ppermute | solution.py:221
  124.8 5.6 %collective-permute-start.13 = (f32[4,128]{1,0:T(4,128)S(1)}, f32[4,128]{1,0:T(4,128)S(1)}, u32[]{:S(2)}, u32[]{:S(2)}) collective-permute-start(f32[4,128]{1,0:T(4,128)S(1)} %copy-done.40), channel_id=1, source_target_pairs={{0,2},{2,4},{4,6},{1,3},{3,5},{5,7},{8,10},{10,12},{12,14},{9,11},... | collective-permute-start | bytes 6152 | tf_op jit(solution)/shard_map/ppermute | solution.py:220
  128.2 5.5 %collective-permute-start.14 = (f32[4,128]{1,0:T(4,128)S(1)}, f32[4,128]{1,0:T(4,128)S(1)}, u32[]{:S(2)}, u32[]{:S(2)}) collective-permute-start(f32[4,128]{1,0:T(4,128)S(1)} %copy-done.37), channel_id=1, source_target_pairs={{2,0},{4,2},{6,4},{3,1},{5,3},{7,5},{10,8},{12,10},{14,12},{11,9},... | collective-permute-start | bytes 6152 | tf_op jit(solution)/shard_map/ppermute | solution.py:221
  130.4 3.3 %copy-start.21 = (f32[4,128]{1,0:T(4,128)}, f32[4,128]{1,0:T(4,128)S(1)}, u32[]{:S(2)}) copy-start(f32[4,128]{1,0:T(4,128)S(1)} %collective-permute-done.13.refs_15_) | copy-start | bytes 6148
  138.4 11.2 %copy-start.29 = (f32[32,128]{1,0:T(8,128)S(1)}, f32[32,128]{1,0:T(8,128)}, u32[]{:S(2)}) copy-start(f32[32,128]{1,0:T(8,128)} %get-tuple-element.79) | copy-start | bytes 49156
  138.4 11.3 %copy-start.35 = (f32[16,128]{1,0:T(8,128)S(1)}, f32[16,128]{1,0:T(8,128)}, u32[]{:S(2)}) copy-start(f32[16,128]{1,0:T(8,128)} %get-tuple-element.80) | copy-start | bytes 24580
  138.4 14.7 %copy-start.32 = (f32[16,128]{1,0:T(8,128)S(1)}, f32[16,128]{1,0:T(8,128)}, u32[]{:S(2)}) copy-start(f32[16,128]{1,0:T(8,128)} %get-tuple-element.81) | copy-start | bytes 24580
  138.4 25.2 %all-to-all-start.4 = ((f32[128,2,256]{2,1,0:T(2,128)}), f32[128,2,256]{2,1,0:T(2,128)S(1)}, u32[]{:S(2)}, u32[]{:S(2)}) async-start(f32[128,2,256]{2,1,0:T(2,128)} %get-tuple-element.76), calls=%async_computation.4 | async-start | bytes 524288 | tf_op jit(solution)/shard_map/all_to_all | solution.py:290
  149.6 18.2 %collective-permute-start.15 = (f32[32,128]{1,0:T(8,128)S(1)}, f32[32,128]{1,0:T(8,128)S(1)}, u32[]{:S(2)}, u32[]{:S(2)}) collective-permute-start(f32[32,128]{1,0:T(8,128)S(1)} %copy-done.29), channel_id=1, source_target_pairs={{0,1},{1,0},{2,3},{3,2},{4,5},{5,4},{6,7},{7,6},{8,9},{9,8},{10,11... | collective-permute-start | bytes 49160 | tf_op jit(solution)/shard_map/ppermute | solution.py:217
  149.7 9.2 %copy-start.41 = (f32[4,128]{1,0:T(4,128)S(1)}, f32[4,128]{1,0:T(4,128)}, u32[]{:S(2)}) copy-start(f32[4,128]{1,0:T(4,128)} %get-tuple-element.82) | copy-start | bytes 6148
  149.7 18.1 %collective-permute-start.16 = (f32[16,128]{1,0:T(8,128)S(1)}, f32[16,128]{1,0:T(8,128)S(1)}, u32[]{:S(2)}, u32[]{:S(2)}) collective-permute-start(f32[16,128]{1,0:T(8,128)S(1)} %copy-done.35), channel_id=1, source_target_pairs={{0,8},{8,16},{16,24},{24,32},{32,40},{40,48},{48,56},{56,64},{64,7... | collective-permute-start | bytes 24584 | tf_op jit(solution)/shard_map/ppermute | solution.py:220
  153.1 9.2 %copy-start.38 = (f32[4,128]{1,0:T(4,128)S(1)}, f32[4,128]{1,0:T(4,128)}, u32[]{:S(2)}) copy-start(f32[4,128]{1,0:T(4,128)} %get-tuple-element.83) | copy-start | bytes 6148
  153.1 14.7 %collective-permute-start.17 = (f32[16,128]{1,0:T(8,128)S(1)}, f32[16,128]{1,0:T(8,128)S(1)}, u32[]{:S(2)}, u32[]{:S(2)}) collective-permute-start(f32[16,128]{1,0:T(8,128)S(1)} %copy-done.32), channel_id=1, source_target_pairs={{8,0},{16,8},{24,16},{32,24},{40,32},{48,40},{56,48},{64,56},{72,6... | collective-permute-start | bytes 24584 | tf_op jit(solution)/shard_map/ppermute | solution.py:221
  158.9 5.6 %collective-permute-start.18 = (f32[4,128]{1,0:T(4,128)S(1)}, f32[4,128]{1,0:T(4,128)S(1)}, u32[]{:S(2)}, u32[]{:S(2)}) collective-permute-start(f32[4,128]{1,0:T(4,128)S(1)} %copy-done.41), channel_id=1, source_target_pairs={{0,2},{2,4},{4,6},{1,3},{3,5},{5,7},{8,10},{10,12},{12,14},{9,11},... | collective-permute-start | bytes 6152 | tf_op jit(solution)/shard_map/ppermute | solution.py:220
  162.3 5.5 %collective-permute-start.19 = (f32[4,128]{1,0:T(4,128)S(1)}, f32[4,128]{1,0:T(4,128)S(1)}, u32[]{:S(2)}, u32[]{:S(2)}) collective-permute-start(f32[4,128]{1,0:T(4,128)S(1)} %copy-done.38), channel_id=1, source_target_pairs={{2,0},{4,2},{6,4},{3,1},{5,3},{7,5},{10,8},{12,10},{14,12},{11,9},... | collective-permute-start | bytes 6152 | tf_op jit(solution)/shard_map/ppermute | solution.py:221
  164.5 3.3 %copy-start.18 = (f32[4,128]{1,0:T(4,128)}, f32[4,128]{1,0:T(4,128)S(1)}, u32[]{:S(2)}) copy-start(f32[4,128]{1,0:T(4,128)S(1)} %collective-permute-done.18.refs_15_) | copy-start | bytes 6148
  (20 other events, 12.6 us)

commit v10 on v9

--- a/solution.py
+++ b/solution.py
@@ -59,20 +59,22 @@
     if pack:
         snd_ref, zs_ref, xf_ref, xl_ref, yf_ref, yl_ref = (next(refs) for _ in range(6))
     depth, rows_x, width = v_ref.shape
+    recv = recv_ref[...]
+    recv = recv.reshape(recv.shape[0] * recv.shape[1], recv.shape[2])
     if first:
-        tile_gain = one_hot_dot(oh_slot_ref[...], recv_ref[:, 2 * width:3 * width])
+        tile_gain = one_hot_dot(oh_slot_ref[...], recv[:, 2 * width:3 * width])
         next(refs)[...] = tile_gain
     else:
         tile_gain = tg_ref[...]
 
     v_flat = v_ref[...].reshape(depth * rows_x, width)
     rows = one_hot_dot(oh_blk_ref[...], v_flat)
-    far = one_hot_dot(oh_slot_ref[...], recv_ref[:, width:2 * width])
+    far = one_hot_dot(oh_slot_ref[...], recv[:, width:2 * width])
     tile_current = tile_gain * (far - rows)
     into_voxel = one_hot_dot(oh_blk_t_ref[...], tile_current)
 
     far_volt = one_hot_dot(oh_ids_t_ref[...], tv_ref[...])
-    current = g_ref[...] * (far_volt - recv_ref[:, 0:width])
+    current = g_ref[...] * (far_volt - recv[:, 0:width])
     into_term = one_hot_dot(oh_ids_ref[...], -current)
 
     u = tv_ref[...]
@@ -176,7 +178,7 @@
 def run_step(tables, state, recv, tile_gain, gains_rows, cable_rows, halos, pack):
     volt, recovery, coef_z, coef_x, coef_y, term_volt, term_recovery = state
     depth, rows_x, width = volt.shape
-    slots = recv.shape[0]
+    slots = recv.shape[0] * recv.shape[1]
     first = tile_gain is None
     f32 = jnp.float32
     smem = pl.BlockSpec(memory_space=pltpu.SMEM)
@@ -287,6 +289,7 @@
     tile_gain = None
     for step in range(STEPS):
         halos = exchange_halos(faces)
+        sent = sent.reshape(owners, capacity, sent.shape[-1])
         received = lax.all_to_all(sent, ("gx", "gy"), split_axis=0, concat_axis=0, tiled=True)
         state = (volt, recovery, coef_z, coef_x, coef_y, term_volt, term_recovery)
         pack = step < STEPS - 1
@@ -295,7 +298,7 @@
             tile_gain = outs[-1]
         volt, recovery, term_volt, term_recovery = outs[:4]
         if pack:
-            sent, faces = outs[4].reshape(slots_total, 2 * width), outs[5:10]
+            sent, faces = outs[4], outs[5:10]
     return (volt, recovery, term_volt, term_recovery)
 
 

time: 173 us -> 174 us (level)
  local copies, waits for them, and re-layouts: 16.4 us -> 13.1 us
  waiting for transfers between devices: 12.3 us -> 14.9 us
    all_to_all x5 -> x0, local copies, waits for them, and re-layouts: 4.63 us -> none  [on_device(): lax.all_to_all(sent, ('gx', 'gy'), split_axis=0, concat_axis=0, tiled=True)]
    ppermute x8, waiting for transfers between devices: 9.87 us -> 12.5 us  [exchange_halos(): lax.ppermute(first, axis, [(i + 1, i) for i in range(count - 1)])]
    unnamed x86 -> x94, local copies, waits for them, and re-layouts: 5.46 us -> 5.78 us
where the time goes in v10:
time: 174 us; the launch traced here: 173 us
  starting transfers between devices  119 us (68%)
  Pallas kernels  18.3 us (11%)
  waiting for transfers between devices  14.9 us (9%)
  local copies, waits for them, and re-layouts  13.1 us (8%)
  other arithmetic  6.25 us (4%)
    all_to_all x4, starting transfers between devices, on_device(): lax.all_to_all(sent, ('gx', 'gy'), split_axis=0, concat_axis=0, tiled=True)  49 us
    ppermute x8, starting transfers between devices, exchange_halos(): lax.ppermute(first, axis, [(i + 1, i) for i in range(count - 1)])  28.4 us
    ppermute x8, starting transfers between devices, exchange_halos(): lax.ppermute(last, axis, [(i, i + 1) for i in range(count - 1)])  27.1 us
    pallas_call x4, Pallas kernels, run_step(): pl.pallas_call(functools.partial(step_kernel, first=first, pack=pack), ou...  16.1 us
    all_to_all x1, starting transfers between devices, on_device(): lax.all_to_all(slot_term, ('gx', 'gy'), split_axis=0, concat_axis=0, tile...  14 us
    ppermute x8, waiting for transfers between devices, exchange_halos(): lax.ppermute(first, axis, [(i + 1, i) for i in range(count - 1)])  12.5 us
    unnamed x94, local copies, waits for them, and re-layouts  5.78 us
  transfers between devices with their start and end apart: 25, of which 4 were waited for; matrix products, arithmetic and copies ran while one was open for 5% of the time, Pallas kernels for 1%

profile of v10, /device:TPU:128, one launch (start us, length us, event | category | flops | bytes accessed | tf_op | source)
XLA Modules:
  0.0 173.1 jit_solution(18331361487824208307)
XLA Ops:
  0.6 0.6 copy-done.29
  1.9 0.7 copy-done.19
  2.8 0.8 sub.7
  3.5 14.0 %all-to-all-start = ((s32[128,2,1]{1,2,0:T(1,128)}), s32[128,2,1]{1,2,0:T(1,128)S(1)}, u32[]{:S(2)}, u32[]{:S(2)}) async-start(s32[128,2,1]{1,2,0:T(1,128)} %bitcast.13), calls=%async_computation | async-start | bytes 131072 | tf_op jit(solution)/shard_map/all_to_all | solution.py:257
  17.5 0.9 fusion.8
  18.4 1.4 slice_reduce_fusion
  19.8 0.7 fusion.2.refs_17_.refs_18_
  20.5 0.8 fusion.1.refs_16_.refs_17_
  21.4 0.7 gather_fusion
  22.1 2.4 %all-to-all-done = s32[128,2,1]{1,2,0:T(1,128)S(1)} async-done(((s32[128,2,1]{1,2,0:T(1,128)}), s32[128,2,1]{1,2,0:T(1,128)S(1)}, u32[]{:S(2)}, u32[]{:S(2)}) %all-to-all-start) | async-done | bytes 1056 | tf_op jit(solution)/shard_map/all_to_all | solution.py:257
  24.7 0.6 copy-done.30
  26.1 0.8 reduce.9
  27.6 0.7 gather_fusion.1
  28.5 0.6 copy-done.2
  29.1 1.0 reshape.109
  30.1 11.3 %all-to-all-start.1 = ((f32[128,2,384]{2,1,0:T(2,128)}), f32[128,2,384]{2,1,0:T(2,128)S(1)}, u32[]{:S(2)}, u32[]{:S(2)}) async-start(f32[128,2,384]{2,1,0:T(2,128)} %reshape.109), calls=%async_computation.1 | async-start | bytes 786432 | tf_op jit(solution)/shard_map/all_to_all | solution.py:293
  41.4 0.7 fusion.3.refs_18_.refs_19_
  42.8 2.2 %shard_map.138 = (f32[16,32,128]{2,1,0:T(8,128)}, f32[16,32,128]{2,1,0:T(8,128)}, f32[16,32,128]{2,1,0:T(8,128)}) custom-call(f32[3,8]{1,0:T(4,128)} %table_ref.1, s32[16,32,128]{2,1,0:T(8,128)} %cls_ref.1), custom_call_target="tpu_custom_call" | custom-call | tf_op jit(solution)/shard_map/pallas_call | solution.py:169
  44.9 0.8 fusion.refs_21_.refs_22_
  45.7 3.4 %collective-permute-start.3 = (f32[4,128]{1,0:T(4,128)S(1)}, f32[4,128]{1,0:T(4,128)S(1)}, u32[]{:S(2)}, u32[]{:S(2)}) collective-permute-start(f32[4,128]{1,0:T(4,128)S(1)} %reshape_squeeze.7), channel_id=1, source_target_pairs={{0,2},{2,4},{4,6},{1,3},{3,5},{5,7},{8,10},{10,12},{12,14},{9,11},... | collective-permute-start | bytes 6152 | tf_op jit(solution)/shard_map/ppermute | solution.py:222
  49.1 1.3 collective-permute-start.4
  50.4 3.4 %collective-permute-start.1 = (f32[16,128]{1,0:T(8,128)S(1)}, f32[16,128]{1,0:T(8,128)S(1)}, u32[]{:S(2)}, u32[]{:S(2)}) collective-permute-start(f32[16,128]{1,0:T(8,128)S(1)} %bitcast.33), channel_id=1, source_target_pairs={{0,8},{8,16},{16,24},{24,32},{32,40},{40,48},{48,56},{56,64},{64,7... | collective-permute-start | bytes 24584 | tf_op jit(solution)/shard_map/ppermute | solution.py:222
  53.8 5.8 %collective-permute-start.2 = (f32[16,128]{1,0:T(8,128)S(1)}, f32[16,128]{1,0:T(8,128)S(1)}, u32[]{:S(2)}, u32[]{:S(2)}) collective-permute-start(f32[16,128]{1,0:T(8,128)S(1)} %bitcast.32), channel_id=1, source_target_pairs={{8,0},{16,8},{24,16},{32,24},{40,32},{48,40},{56,48},{64,56},{72,6... | collective-permute-start | bytes 24584 | tf_op jit(solution)/shard_map/ppermute | solution.py:223
  59.7 0.7 fusion.4.refs_20_.refs_21_
  60.4 0.6 fusion.6.refs_19_.refs_20_
  61.1 0.7 broadcast_in_dim.74.refs_10_.refs_11_
  61.9 4.3 %shard_map.139 = (f32[16,32,128]{2,1,0:T(8,128)}, f32[16,32,128]{2,1,0:T(8,128)}, f32[32,128]{1,0:T(8,128)}, f32[32,128]{1,0:T(8,128)}, f32[128,2,256]{2,1,0:T(2...) custom-call(s32[8]{0:T(128)} %convert_element_type.22.refs_0_, ...), custom_call_target="tpu_custom_call" | custom-call | tf_op jit(solution)/shard_map/pallas_call | solution.py:206
  66.2 15.4 %all-to-all-start.2 = ((f32[128,2,256]{2,1,0:T(2,128)}), f32[128,2,256]{2,1,0:T(2,128)S(1)}, u32[]{:S(2)}, u32[]{:S(2)}) async-start(f32[128,2,256]{2,1,0:T(2,128)} %get-tuple-element.55), calls=%async_computation.2 | async-start | bytes 524288 | tf_op jit(solution)/shard_map/all_to_all | solution.py:293
  81.7 3.4 %collective-permute-start.6 = (f32[16,128]{1,0:T(8,128)S(1)}, f32[16,128]{1,0:T(8,128)S(1)}, u32[]{:S(2)}, u32[]{:S(2)}) collective-permute-start(f32[16,128]{1,0:T(8,128)S(1)} %copy-done.40), channel_id=1, source_target_pairs={{0,8},{8,16},{16,24},{24,32},{32,40},{40,48},{48,56},{56,64},{64,7... | collective-permute-start | bytes 24584 | tf_op jit(solution)/shard_map/ppermute | solution.py:222
  85.2 5.8 %collective-permute-start.7 = (f32[16,128]{1,0:T(8,128)S(1)}, f32[16,128]{1,0:T(8,128)S(1)}, u32[]{:S(2)}, u32[]{:S(2)}) collective-permute-start(f32[16,128]{1,0:T(8,128)S(1)} %copy-done.37), channel_id=1, source_target_pairs={{8,0},{16,8},{24,16},{32,24},{40,32},{48,40},{56,48},{64,56},{72,6... | collective-permute-start | bytes 24584 | tf_op jit(solution)/shard_map/ppermute | solution.py:223
  90.9 3.4 %collective-permute-start.8 = (f32[4,128]{1,0:T(4,128)S(1)}, f32[4,128]{1,0:T(4,128)S(1)}, u32[]{:S(2)}, u32[]{:S(2)}) collective-permute-start(f32[4,128]{1,0:T(4,128)S(1)} %copy-done.46), channel_id=1, source_target_pairs={{0,2},{2,4},{4,6},{1,3},{3,5},{5,7},{8,10},{10,12},{12,14},{9,11},... | collective-permute-start | bytes 6152 | tf_op jit(solution)/shard_map/ppermute | solution.py:222
  94.3 1.5 collective-permute-start.9
  95.8 4.2 %collective-permute-done.9.refs_16_ = f32[4,128]{1,0:T(4,128)S(1)} collective-permute-done((f32[4,128]{1,0:T(4,128)S(1)}, f32[4,128]{1,0:T(4,128)S(1)}, u32[]{:S(2)}, u32[]{:S(2)}) %collective-permute-start.9) | collective-permute-done | bytes 2080 | tf_op jit(solution)/shard_map/ppermute | solution.py:223
  100.8 4.1 %shard_map.140 = (f32[16,32,128]{2,1,0:T(8,128)}, f32[16,32,128]{2,1,0:T(8,128)}, f32[32,128]{1,0:T(8,128)}, f32[32,128]{1,0:T(8,128)}, f32[128,2,256]{2,1,0:T(2...) custom-call(s32[8]{0:T(128)} %convert_element_type.22.refs_0_, ...), custom_call_target="tpu_custom_call" | custom-call | tf_op jit(solution)/shard_map/pallas_call | solution.py:206
  104.9 11.1 %all-to-all-start.3 = ((f32[128,2,256]{2,1,0:T(2,128)}), f32[128,2,256]{2,1,0:T(2,128)S(1)}, u32[]{:S(2)}, u32[]{:S(2)}) async-start(f32[128,2,256]{2,1,0:T(2,128)} %get-tuple-element.66), calls=%async_computation.3 | async-start | bytes 524288 | tf_op jit(solution)/shard_map/all_to_all | solution.py:293
  116.2 3.4 %collective-permute-start.11 = (f32[16,128]{1,0:T(8,128)S(1)}, f32[16,128]{1,0:T(8,128)S(1)}, u32[]{:S(2)}, u32[]{:S(2)}) collective-permute-start(f32[16,128]{1,0:T(8,128)S(1)} %copy-done.38), channel_id=1, source_target_pairs={{0,8},{8,16},{16,24},{24,32},{32,40},{40,48},{48,56},{56,64},{64,7... | collective-permute-start | bytes 24584 | tf_op jit(solution)/shard_map/ppermute | solution.py:222
  119.6 5.8 %collective-permute-start.12 = (f32[16,128]{1,0:T(8,128)S(1)}, f32[16,128]{1,0:T(8,128)S(1)}, u32[]{:S(2)}, u32[]{:S(2)}) collective-permute-start(f32[16,128]{1,0:T(8,128)S(1)} %copy-done.35), channel_id=1, source_target_pairs={{8,0},{16,8},{24,16},{32,24},{40,32},{48,40},{56,48},{64,56},{72,6... | collective-permute-start | bytes 24584 | tf_op jit(solution)/shard_map/ppermute | solution.py:223
  125.4 3.4 %collective-permute-start.13 = (f32[4,128]{1,0:T(4,128)S(1)}, f32[4,128]{1,0:T(4,128)S(1)}, u32[]{:S(2)}, u32[]{:S(2)}) collective-permute-start(f32[4,128]{1,0:T(4,128)S(1)} %copy-done.44), channel_id=1, source_target_pairs={{0,2},{2,4},{4,6},{1,3},{3,5},{5,7},{8,10},{10,12},{12,14},{9,11},... | collective-permute-start | bytes 6152 | tf_op jit(solution)/shard_map/ppermute | solution.py:222
  128.8 1.3 collective-permute-start.14
  130.1 4.2 %collective-permute-done.14.refs_16_ = f32[4,128]{1,0:T(4,128)S(1)} collective-permute-done((f32[4,128]{1,0:T(4,128)S(1)}, f32[4,128]{1,0:T(4,128)S(1)}, u32[]{:S(2)}, u32[]{:S(2)}) %collective-permute-start.14) | collective-permute-done | bytes 2080 | tf_op jit(solution)/shard_map/ppermute | solution.py:223
  135.0 4.1 %shard_map.141 = (f32[16,32,128]{2,1,0:T(8,128)}, f32[16,32,128]{2,1,0:T(8,128)}, f32[32,128]{1,0:T(8,128)}, f32[32,128]{1,0:T(8,128)}, f32[128,2,256]{2,1,0:T(2...) custom-call(s32[8]{0:T(128)} %convert_element_type.22.refs_0_, ...), custom_call_target="tpu_custom_call" | custom-call | tf_op jit(solution)/shard_map/pallas_call | solution.py:206
  139.2 11.1 %all-to-all-start.4 = ((f32[128,2,256]{2,1,0:T(2,128)}), f32[128,2,256]{2,1,0:T(2,128)S(1)}, u32[]{:S(2)}, u32[]{:S(2)}) async-start(f32[128,2,256]{2,1,0:T(2,128)} %get-tuple-element.76), calls=%async_computation.4 | async-start | bytes 524288 | tf_op jit(solution)/shard_map/all_to_all | solution.py:293
  150.5 3.4 %collective-permute-start.16 = (f32[16,128]{1,0:T(8,128)S(1)}, f32[16,128]{1,0:T(8,128)S(1)}, u32[]{:S(2)}, u32[]{:S(2)}) collective-permute-start(f32[16,128]{1,0:T(8,128)S(1)} %copy-done.39), channel_id=1, source_target_pairs={{0,8},{8,16},{16,24},{24,32},{32,40},{40,48},{48,56},{56,64},{64,7... | collective-permute-start | bytes 24584 | tf_op jit(solution)/shard_map/ppermute | solution.py:222
  153.9 5.8 %collective-permute-start.17 = (f32[16,128]{1,0:T(8,128)S(1)}, f32[16,128]{1,0:T(8,128)S(1)}, u32[]{:S(2)}, u32[]{:S(2)}) collective-permute-start(f32[16,128]{1,0:T(8,128)S(1)} %copy-done.36), channel_id=1, source_target_pairs={{8,0},{16,8},{24,16},{32,24},{40,32},{48,40},{56,48},{64,56},{72,6... | collective-permute-start | bytes 24584 | tf_op jit(solution)/shard_map/ppermute | solution.py:223
  159.7 3.4 %collective-permute-start.18 = (f32[4,128]{1,0:T(4,128)S(1)}, f32[4,128]{1,0:T(4,128)S(1)}, u32[]{:S(2)}, u32[]{:S(2)}) collective-permute-start(f32[4,128]{1,0:T(4,128)S(1)} %copy-done.45), channel_id=1, source_target_pairs={{0,2},{2,4},{4,6},{1,3},{3,5},{5,7},{8,10},{10,12},{12,14},{9,11},... | collective-permute-start | bytes 6152 | tf_op jit(solution)/shard_map/ppermute | solution.py:222
  163.1 1.3 collective-permute-start.19
  164.4 4.2 %collective-permute-done.19.refs_16_ = f32[4,128]{1,0:T(4,128)S(1)} collective-permute-done((f32[4,128]{1,0:T(4,128)S(1)}, f32[4,128]{1,0:T(4,128)S(1)}, u32[]{:S(2)}, u32[]{:S(2)}) %collective-permute-start.19) | collective-permute-done | bytes 2080 | tf_op jit(solution)/shard_map/ppermute | solution.py:223
  169.3 3.6 %shard_map.142 = (f32[16,32,128]{2,1,0:T(8,128)}, f32[16,32,128]{2,1,0:T(8,128)}, f32[32,128]{1,0:T(8,128)}, f32[32,128]{1,0:T(8,128)}) custom-call(s32[8]{0:T(128)} %convert_element_type.22.refs_0_, f32[16,32,128]{2,1,0:T(8,128)} %get-tuple-element.74.refs_1_, f32[16,32,128]{2,1,0:T(8,128)} %get-tuple-element.75.refs_2_, ...), custom_call_target="tpu_custom_call" | custom-call | tf_op jit(solution)/shard_map/pallas_call | solution.py:206
  (137 shorter events, 5.9 us)
Async XLA Ops:
  3.5 21.0 %all-to-all-start = ((s32[128,2,1]{1,2,0:T(1,128)}), s32[128,2,1]{1,2,0:T(1,128)S(1)}, u32[]{:S(2)}, u32[]{:S(2)}) async-start(s32[128,2,1]{1,2,0:T(1,128)} %bitcast.13), calls=%async_computation | async-start | bytes 131072 | tf_op jit(solution)/shard_map/all_to_all | solution.py:257
  19.8 1.5 copy-start.1
  30.1 31.1 %all-to-all-start.1 = ((f32[128,2,384]{2,1,0:T(2,128)}), f32[128,2,384]{2,1,0:T(2,128)S(1)}, u32[]{:S(2)}, u32[]{:S(2)}) async-start(f32[128,2,384]{2,1,0:T(2,128)} %reshape.109), calls=%async_computation.1 | async-start | bytes 786432 | tf_op jit(solution)/shard_map/all_to_all | solution.py:293
  45.7 15.3 %collective-permute-start.3 = (f32[4,128]{1,0:T(4,128)S(1)}, f32[4,128]{1,0:T(4,128)S(1)}, u32[]{:S(2)}, u32[]{:S(2)}) collective-permute-start(f32[4,128]{1,0:T(4,128)S(1)} %reshape_squeeze.7), channel_id=1, source_target_pairs={{0,2},{2,4},{4,6},{1,3},{3,5},{5,7},{8,10},{10,12},{12,14},{9,11},... | collective-permute-start | bytes 6152 | tf_op jit(solution)/shard_map/ppermute | solution.py:222
  49.1 11.9 %collective-permute-start.4 = (f32[4,128]{1,0:T(4,128)S(1)}, f32[4,128]{1,0:T(4,128)S(1)}, u32[]{:S(2)}, u32[]{:S(2)}) collective-permute-start(f32[4,128]{1,0:T(4,128)S(1)} %reshape_squeeze.6), channel_id=1, source_target_pairs={{2,0},{4,2},{6,4},{3,1},{5,3},{7,5},{10,8},{12,10},{14,12},{11,9},... | collective-permute-start | bytes 6152 | tf_op jit(solution)/shard_map/ppermute | solution.py:223
  50.4 10.6 %collective-permute-start.1 = (f32[16,128]{1,0:T(8,128)S(1)}, f32[16,128]{1,0:T(8,128)S(1)}, u32[]{:S(2)}, u32[]{:S(2)}) collective-permute-start(f32[16,128]{1,0:T(8,128)S(1)} %bitcast.33), channel_id=1, source_target_pairs={{0,8},{8,16},{16,24},{24,32},{32,40},{40,48},{48,56},{56,64},{64,7... | collective-permute-start | bytes 24584 | tf_op jit(solution)/shard_map/ppermute | solution.py:222
  53.8 7.2 %collective-permute-start.2 = (f32[16,128]{1,0:T(8,128)S(1)}, f32[16,128]{1,0:T(8,128)S(1)}, u32[]{:S(2)}, u32[]{:S(2)}) collective-permute-start(f32[16,128]{1,0:T(8,128)S(1)} %bitcast.32), channel_id=1, source_target_pairs={{8,0},{16,8},{24,16},{32,24},{40,32},{48,40},{56,48},{64,56},{72,6... | collective-permute-start | bytes 24584 | tf_op jit(solution)/shard_map/ppermute | solution.py:223
  59.6 1.5 collective-permute-start
  61.0 0.8 copy-start.20
  61.0 0.8 copy-start.21
  61.1 0.8 copy-start.15
  61.1 0.8 copy-start.18
  66.2 15.4 %copy-start.34 = (f32[32,128]{1,0:T(8,128)S(1)}, f32[32,128]{1,0:T(8,128)}, u32[]{:S(2)}) copy-start(f32[32,128]{1,0:T(8,128)} %get-tuple-element.59) | copy-start | bytes 49156
  66.2 15.5 %copy-start.40 = (f32[16,128]{1,0:T(8,128)S(1)}, f32[16,128]{1,0:T(8,128)}, u32[]{:S(2)}) copy-start(f32[16,128]{1,0:T(8,128)} %get-tuple-element.60) | copy-start | bytes 24580
  66.2 18.9 %copy-start.37 = (f32[16,128]{1,0:T(8,128)S(1)}, f32[16,128]{1,0:T(8,128)}, u32[]{:S(2)}) copy-start(f32[16,128]{1,0:T(8,128)} %get-tuple-element.61) | copy-start | bytes 24580
  66.2 33.8 %all-to-all-start.2 = ((f32[128,2,256]{2,1,0:T(2,128)}), f32[128,2,256]{2,1,0:T(2,128)S(1)}, u32[]{:S(2)}, u32[]{:S(2)}) async-start(f32[128,2,256]{2,1,0:T(2,128)} %get-tuple-element.55), calls=%async_computation.2 | async-start | bytes 524288 | tf_op jit(solution)/shard_map/all_to_all | solution.py:293
  81.6 18.4 %collective-permute-start.5 = (f32[32,128]{1,0:T(8,128)S(1)}, f32[32,128]{1,0:T(8,128)S(1)}, u32[]{:S(2)}, u32[]{:S(2)}) collective-permute-start(f32[32,128]{1,0:T(8,128)S(1)} %copy-done.34), channel_id=1, source_target_pairs={{0,1},{1,0},{2,3},{3,2},{4,5},{5,4},{6,7},{7,6},{8,9},{9,8},{10,11... | collective-permute-start | bytes 49160 | tf_op jit(solution)/shard_map/ppermute | solution.py:219
  81.7 9.2 %copy-start.46 = (f32[4,128]{1,0:T(4,128)S(1)}, f32[4,128]{1,0:T(4,128)}, u32[]{:S(2)}) copy-start(f32[4,128]{1,0:T(4,128)} %get-tuple-element.62) | copy-start | bytes 6148
  81.7 18.3 %collective-permute-start.6 = (f32[16,128]{1,0:T(8,128)S(1)}, f32[16,128]{1,0:T(8,128)S(1)}, u32[]{:S(2)}, u32[]{:S(2)}) collective-permute-start(f32[16,128]{1,0:T(8,128)S(1)} %copy-done.40), channel_id=1, source_target_pairs={{0,8},{8,16},{16,24},{24,32},{32,40},{40,48},{48,56},{56,64},{64,7... | collective-permute-start | bytes 24584 | tf_op jit(solution)/shard_map/ppermute | solution.py:222
  85.1 9.2 %copy-start.43 = (f32[4,128]{1,0:T(4,128)S(1)}, f32[4,128]{1,0:T(4,128)}, u32[]{:S(2)}) copy-start(f32[4,128]{1,0:T(4,128)} %get-tuple-element.63) | copy-start | bytes 6148
  85.2 14.8 %collective-permute-start.7 = (f32[16,128]{1,0:T(8,128)S(1)}, f32[16,128]{1,0:T(8,128)S(1)}, u32[]{:S(2)}, u32[]{:S(2)}) collective-permute-start(f32[16,128]{1,0:T(8,128)S(1)} %copy-done.37), channel_id=1, source_target_pairs={{8,0},{16,8},{24,16},{32,24},{40,32},{48,40},{56,48},{64,56},{72,6... | collective-permute-start | bytes 24584 | tf_op jit(solution)/shard_map/ppermute | solution.py:223
  90.9 4.9 %collective-permute-start.8 = (f32[4,128]{1,0:T(4,128)S(1)}, f32[4,128]{1,0:T(4,128)S(1)}, u32[]{:S(2)}, u32[]{:S(2)}) collective-permute-start(f32[4,128]{1,0:T(4,128)S(1)} %copy-done.46), channel_id=1, source_target_pairs={{0,2},{2,4},{4,6},{1,3},{3,5},{5,7},{8,10},{10,12},{12,14},{9,11},... | collective-permute-start | bytes 6152 | tf_op jit(solution)/shard_map/ppermute | solution.py:222
  94.3 5.7 %collective-permute-start.9 = (f32[4,128]{1,0:T(4,128)S(1)}, f32[4,128]{1,0:T(4,128)S(1)}, u32[]{:S(2)}, u32[]{:S(2)}) collective-permute-start(f32[4,128]{1,0:T(4,128)S(1)} %copy-done.43), channel_id=1, source_target_pairs={{2,0},{4,2},{6,4},{3,1},{5,3},{7,5},{10,8},{12,10},{14,12},{11,9},... | collective-permute-start | bytes 6152 | tf_op jit(solution)/shard_map/ppermute | solution.py:223
  95.8 4.2 %copy-start.24 = (f32[4,128]{1,0:T(4,128)}, f32[4,128]{1,0:T(4,128)S(1)}, u32[]{:S(2)}) copy-start(f32[4,128]{1,0:T(4,128)S(1)} %collective-permute-done.8.refs_15_) | copy-start | bytes 6148
  104.9 11.2 %copy-start.32 = (f32[32,128]{1,0:T(8,128)S(1)}, f32[32,128]{1,0:T(8,128)}, u32[]{:S(2)}) copy-start(f32[32,128]{1,0:T(8,128)} %get-tuple-element.69) | copy-start | bytes 49156
  104.9 11.3 %copy-start.38 = (f32[16,128]{1,0:T(8,128)S(1)}, f32[16,128]{1,0:T(8,128)}, u32[]{:S(2)}) copy-start(f32[16,128]{1,0:T(8,128)} %get-tuple-element.70) | copy-start | bytes 24580
  104.9 14.7 %copy-start.35 = (f32[16,128]{1,0:T(8,128)S(1)}, f32[16,128]{1,0:T(8,128)}, u32[]{:S(2)}) copy-start(f32[16,128]{1,0:T(8,128)} %get-tuple-element.71) | copy-start | bytes 24580
  104.9 29.4 %all-to-all-start.3 = ((f32[128,2,256]{2,1,0:T(2,128)}), f32[128,2,256]{2,1,0:T(2,128)S(1)}, u32[]{:S(2)}, u32[]{:S(2)}) async-start(f32[128,2,256]{2,1,0:T(2,128)} %get-tuple-element.66), calls=%async_computation.3 | async-start | bytes 524288 | tf_op jit(solution)/shard_map/all_to_all | solution.py:293
  116.1 18.2 %collective-permute-start.10 = (f32[32,128]{1,0:T(8,128)S(1)}, f32[32,128]{1,0:T(8,128)S(1)}, u32[]{:S(2)}, u32[]{:S(2)}) collective-permute-start(f32[32,128]{1,0:T(8,128)S(1)} %copy-done.32), channel_id=1, source_target_pairs={{0,1},{1,0},{2,3},{3,2},{4,5},{5,4},{6,7},{7,6},{8,9},{9,8},{10,11... | collective-permute-start | bytes 49160 | tf_op jit(solution)/shard_map/ppermute | solution.py:219
  116.2 9.2 %copy-start.44 = (f32[4,128]{1,0:T(4,128)S(1)}, f32[4,128]{1,0:T(4,128)}, u32[]{:S(2)}) copy-start(f32[4,128]{1,0:T(4,128)} %get-tuple-element.72) | copy-start | bytes 6148
  116.2 18.1 %collective-permute-start.11 = (f32[16,128]{1,0:T(8,128)S(1)}, f32[16,128]{1,0:T(8,128)S(1)}, u32[]{:S(2)}, u32[]{:S(2)}) collective-permute-start(f32[16,128]{1,0:T(8,128)S(1)} %copy-done.38), channel_id=1, source_target_pairs={{0,8},{8,16},{16,24},{24,32},{32,40},{40,48},{48,56},{56,64},{64,7... | collective-permute-start | bytes 24584 | tf_op jit(solution)/shard_map/ppermute | solution.py:222
  119.6 9.2 %copy-start.41 = (f32[4,128]{1,0:T(4,128)S(1)}, f32[4,128]{1,0:T(4,128)}, u32[]{:S(2)}) copy-start(f32[4,128]{1,0:T(4,128)} %get-tuple-element.73) | copy-start | bytes 6148
  119.6 14.7 %collective-permute-start.12 = (f32[16,128]{1,0:T(8,128)S(1)}, f32[16,128]{1,0:T(8,128)S(1)}, u32[]{:S(2)}, u32[]{:S(2)}) collective-permute-start(f32[16,128]{1,0:T(8,128)S(1)} %copy-done.35), channel_id=1, source_target_pairs={{8,0},{16,8},{24,16},{32,24},{40,32},{48,40},{56,48},{64,56},{72,6... | collective-permute-start | bytes 24584 | tf_op jit(solution)/shard_map/ppermute | solution.py:223
  125.4 4.7 %collective-permute-start.13 = (f32[4,128]{1,0:T(4,128)S(1)}, f32[4,128]{1,0:T(4,128)S(1)}, u32[]{:S(2)}, u32[]{:S(2)}) collective-permute-start(f32[4,128]{1,0:T(4,128)S(1)} %copy-done.44), channel_id=1, source_target_pairs={{0,2},{2,4},{4,6},{1,3},{3,5},{5,7},{8,10},{10,12},{12,14},{9,11},... | collective-permute-start | bytes 6152 | tf_op jit(solution)/shard_map/ppermute | solution.py:222
  128.8 5.5 %collective-permute-start.14 = (f32[4,128]{1,0:T(4,128)S(1)}, f32[4,128]{1,0:T(4,128)S(1)}, u32[]{:S(2)}, u32[]{:S(2)}) collective-permute-start(f32[4,128]{1,0:T(4,128)S(1)} %copy-done.41), channel_id=1, source_target_pairs={{2,0},{4,2},{6,4},{3,1},{5,3},{7,5},{10,8},{12,10},{14,12},{11,9},... | collective-permute-start | bytes 6152 | tf_op jit(solution)/shard_map/ppermute | solution.py:223
  130.1 4.2 %copy-start.25 = (f32[4,128]{1,0:T(4,128)}, f32[4,128]{1,0:T(4,128)S(1)}, u32[]{:S(2)}) copy-start(f32[4,128]{1,0:T(4,128)S(1)} %collective-permute-done.13.refs_15_) | copy-start | bytes 6148
  139.1 11.2 %copy-start.33 = (f32[32,128]{1,0:T(8,128)S(1)}, f32[32,128]{1,0:T(8,128)}, u32[]{:S(2)}) copy-start(f32[32,128]{1,0:T(8,128)} %get-tuple-element.79) | copy-start | bytes 49156
  139.2 11.3 %copy-start.39 = (f32[16,128]{1,0:T(8,128)S(1)}, f32[16,128]{1,0:T(8,128)}, u32[]{:S(2)}) copy-start(f32[16,128]{1,0:T(8,128)} %get-tuple-element.80) | copy-start | bytes 24580
  139.2 14.7 %copy-start.36 = (f32[16,128]{1,0:T(8,128)S(1)}, f32[16,128]{1,0:T(8,128)}, u32[]{:S(2)}) copy-start(f32[16,128]{1,0:T(8,128)} %get-tuple-element.81) | copy-start | bytes 24580
  139.2 29.4 %all-to-all-start.4 = ((f32[128,2,256]{2,1,0:T(2,128)}), f32[128,2,256]{2,1,0:T(2,128)S(1)}, u32[]{:S(2)}, u32[]{:S(2)}) async-start(f32[128,2,256]{2,1,0:T(2,128)} %get-tuple-element.76), calls=%async_computation.4 | async-start | bytes 524288 | tf_op jit(solution)/shard_map/all_to_all | solution.py:293
  150.3 18.2 %collective-permute-start.15 = (f32[32,128]{1,0:T(8,128)S(1)}, f32[32,128]{1,0:T(8,128)S(1)}, u32[]{:S(2)}, u32[]{:S(2)}) collective-permute-start(f32[32,128]{1,0:T(8,128)S(1)} %copy-done.33), channel_id=1, source_target_pairs={{0,1},{1,0},{2,3},{3,2},{4,5},{5,4},{6,7},{7,6},{8,9},{9,8},{10,11... | collective-permute-start | bytes 49160 | tf_op jit(solution)/shard_map/ppermute | solution.py:219
  150.4 9.2 %copy-start.45 = (f32[4,128]{1,0:T(4,128)S(1)}, f32[4,128]{1,0:T(4,128)}, u32[]{:S(2)}) copy-start(f32[4,128]{1,0:T(4,128)} %get-tuple-element.82) | copy-start | bytes 6148
  150.5 18.1 %collective-permute-start.16 = (f32[16,128]{1,0:T(8,128)S(1)}, f32[16,128]{1,0:T(8,128)S(1)}, u32[]{:S(2)}, u32[]{:S(2)}) collective-permute-start(f32[16,128]{1,0:T(8,128)S(1)} %copy-done.39), channel_id=1, source_target_pairs={{0,8},{8,16},{16,24},{24,32},{32,40},{40,48},{48,56},{56,64},{64,7... | collective-permute-start | bytes 24584 | tf_op jit(solution)/shard_map/ppermute | solution.py:222
  153.9 9.2 %copy-start.42 = (f32[4,128]{1,0:T(4,128)S(1)}, f32[4,128]{1,0:T(4,128)}, u32[]{:S(2)}) copy-start(f32[4,128]{1,0:T(4,128)} %get-tuple-element.83) | copy-start | bytes 6148
  153.9 14.7 %collective-permute-start.17 = (f32[16,128]{1,0:T(8,128)S(1)}, f32[16,128]{1,0:T(8,128)S(1)}, u32[]{:S(2)}, u32[]{:S(2)}) collective-permute-start(f32[16,128]{1,0:T(8,128)S(1)} %copy-done.36), channel_id=1, source_target_pairs={{8,0},{16,8},{24,16},{32,24},{40,32},{48,40},{56,48},{64,56},{72,6... | collective-permute-start | bytes 24584 | tf_op jit(solution)/shard_map/ppermute | solution.py:223
  159.7 4.7 %collective-permute-start.18 = (f32[4,128]{1,0:T(4,128)S(1)}, f32[4,128]{1,0:T(4,128)S(1)}, u32[]{:S(2)}, u32[]{:S(2)}) collective-permute-start(f32[4,128]{1,0:T(4,128)S(1)} %copy-done.45), channel_id=1, source_target_pairs={{0,2},{2,4},{4,6},{1,3},{3,5},{5,7},{8,10},{10,12},{12,14},{9,11},... | collective-permute-start | bytes 6152 | tf_op jit(solution)/shard_map/ppermute | solution.py:222
  163.1 5.5 %collective-permute-start.19 = (f32[4,128]{1,0:T(4,128)S(1)}, f32[4,128]{1,0:T(4,128)S(1)}, u32[]{:S(2)}, u32[]{:S(2)}) collective-permute-start(f32[4,128]{1,0:T(4,128)S(1)} %copy-done.42), channel_id=1, source_target_pairs={{2,0},{4,2},{6,4},{3,1},{5,3},{7,5},{10,8},{12,10},{14,12},{11,9},... | collective-permute-start | bytes 6152 | tf_op jit(solution)/shard_map/ppermute | solution.py:223
  164.4 4.2 %copy-start.22 = (f32[4,128]{1,0:T(4,128)}, f32[4,128]{1,0:T(4,128)S(1)}, u32[]{:S(2)}) copy-start(f32[4,128]{1,0:T(4,128)S(1)} %collective-permute-done.18.refs_15_) | copy-start | bytes 6148
  (24 other events, 15.5 us)
